TPU v7x, 512 devices: a whole 4x4x16 slice. The times are simulated.
512 devices in a mesh: depth: 128 (over z, x, core), dp: 4 (over y).
Axes of the slice: x: 4, y: 4, z: 16, core: 2. Of those that a mesh axis runs over, the one named last changes fastest.
Arguments:
- cpoints: float32 [128, 4, 64, 256], P('depth', 'dp'), may hold values from -6 to 6, as said below
- weights: bfloat16 [512, 64, 576], P('depth'), may hold values from -12 to 12
- coarse_gain: float32 [128, 64], P('depth'), may hold values from 0.04 to 1
- cotangent: float32 [128, 4, 64, 256], P('depth', 'dp'), may hold values from -0.6 to 0.6
Outputs:
- corrected: float32 [128, 4, 64, 256], P('depth', 'dp')
- grad_cpoints: float32 [128, 4, 64, 256], P('depth', 'dp')
- grad_weights: float32 [512, 64, 576], P('depth')
Inputs may be any that keep to these rules, and one draw needn't show every extreme that they name: cpoints[0] holds the network input; cpoints[d] the current guess of the state entering block d.
All inputs are finite; a program needn't handle non-finite values.
Results may differ from a plain program's by a relative error of at most 0.0041.
Values sent between devices are 32-bit elements; how exact they have to be, the bound alone decides.
No kernel may reach another device: no remote copies, remote signals or barrier semaphores. Data moves between devices by JAX's collectives and lax.ppermute only.
A program may use at most 64 MiB of HBM per device.

v0:
```python
import jax
import jax.numpy as jnp
from jax import lax
from jax.sharding import PartitionSpec as P

WID = 16


TAP_OFFSETS = [(-1, -1), (-1, 0), (-1, 1), (0, -1), (0, 0), (0, 1), (1, -1), (1, 0), (1, 1)]


def prefix(part, axis, combine, identity, reverse):
    count = lax.axis_size(axis)
    place = lax.axis_index(axis)
    ahead = count - 1 - place if reverse else place
    gathered = jax.tree.map(lambda a: lax.all_gather(a, axis), part)
    state = jax.tree.map(lambda a, e: jnp.zeros_like(a) + jnp.asarray(e, a.dtype), part, identity)

    def one(hop, state):
        source = count - 1 - hop if reverse else hop
        return combine(
            state, jax.tree.map(lambda a: lax.dynamic_index_in_dim(a, source, 0, False), gathered)
        )

    return lax.fori_loop(0, ahead, one, state)


def passed_along(block, axis, distance):
    devices = range(lax.axis_size(axis))
    route = [(i - distance, i) for i in devices if i - distance in devices]
    return lax.ppermute(block, axis, route)


def shift_pixels(values, shift_down, shift_right, row_width):
    pixel_count = values.shape[-1]
    offset = shift_down * row_width + shift_right
    padded = jnp.pad(values, [(0, 0)] * (values.ndim - 1) + [(row_width + 1, row_width + 1)])
    shifted = lax.slice_in_dim(
        padded, row_width + 1 + offset, row_width + 1 + offset + pixel_count, axis=values.ndim - 1
    )
    column = jnp.arange(pixel_count) % row_width + shift_right
    inside = (column >= 0) & (column < row_width)
    return jnp.where(inside, shifted, jnp.zeros_like(shifted))


def unfold(values, row_width):
    return jnp.concatenate([shift_pixels(values, a, b, row_width) for a, b in TAP_OFFSETS], axis=1)


def fold_taps(tap_grads, row_width):
    channels = tap_grads.shape[1] // 9
    accumulated = jnp.zeros((tap_grads.shape[0], channels, tap_grads.shape[2]), jnp.float32)
    for tap_index, (a, b) in enumerate(TAP_OFFSETS):
        piece = tap_grads[:, tap_index * channels : (tap_index + 1) * channels]
        accumulated = accumulated + shift_pixels(piece, -a, -b, row_width)
    return accumulated


def run_block(current, block_weights, step_size):
    inputs_kept = []
    for layer in range(block_weights.shape[0]):
        inputs_kept.append(current)
        squashed = jnp.tanh(current)
        patches = unfold(squashed.astype(jnp.bfloat16), WID)
        mixed = jnp.einsum(
            "ok,bkp->bop", block_weights[layer], patches, preferred_element_type=jnp.float32
        )
        current = current + step_size * mixed
    return (current, inputs_kept)


def back_block(inputs_kept, block_weights, upstream, step_size):
    layer_count = block_weights.shape[0]
    layer_grads = [None] * layer_count
    for layer in reversed(range(layer_count)):
        squashed = jnp.tanh(inputs_kept[layer])
        patches = unfold(squashed.astype(jnp.bfloat16), WID)
        scaled = (step_size * upstream).astype(jnp.bfloat16)
        layer_grads[layer] = jnp.einsum(
            "bop,bkp->ok", scaled, patches, preferred_element_type=jnp.float32
        )
        spread = jnp.einsum(
            "ok,bop->bkp", block_weights[layer], scaled, preferred_element_type=jnp.float32
        )
        upstream = upstream + (1.0 - squashed * squashed) * fold_taps(spread, WID)
    return (upstream, jnp.stack(layer_grads))


def compose_maps(earlier, later):
    return (later[0] * earlier[0], later[0][None, :, None] * earlier[1] + later[1])


def adjoint_carry(rate_vec, incoming):
    identity_maps = (jnp.ones_like(rate_vec), jnp.zeros_like(incoming))
    _, passed_in = prefix(
        (rate_vec, rate_vec[None, :, None] * incoming), "depth", compose_maps, identity_maps, True
    )
    return passed_in


def body(cpoints, weights, coarse_gain, cotangent):
    step_size = 1.0 / (weights.shape[0] * lax.axis_size("depth"))
    own_state = cpoints[0]
    rate_vec = coarse_gain[0]
    cot_here = cotangent[0]
    leading = lax.axis_index("depth") == 0
    relaxed, own_kept = run_block(own_state, weights, step_size)
    arriving = passed_along(relaxed, "depth", 1)
    start_state = jnp.where(leading, own_state, arriving)
    propagated, start_kept = run_block(start_state, weights, step_size)
    gained_start = rate_vec[None, :, None] * start_state
    offset = propagated - jnp.where(leading, jnp.zeros_like(gained_start), gained_start)
    identity_maps = (jnp.ones_like(rate_vec), jnp.zeros_like(offset))
    _, previous_out = prefix((rate_vec, offset), "depth", compose_maps, identity_maps, False)
    corrected = rate_vec[None, :, None] * previous_out + offset
    passed_in = adjoint_carry(rate_vec, cot_here)
    adjoint_here = cot_here + passed_in
    back_start, start_grads = back_block(start_kept, weights, adjoint_here, step_size)
    arriving_bar = passed_along(back_start, "depth", -1)
    relaxed_bar = arriving_bar - passed_in
    back_own, own_grads = back_block(own_kept, weights, relaxed_bar, step_size)
    grad_cpoints = jnp.where(leading, back_own + back_start, back_own)
    grad_weights = lax.psum(start_grads + own_grads, "dp")
    return (corrected[None], grad_cpoints[None], grad_weights)


def solution(mesh):
    placed = (
        P("depth", "dp", None, None),
        P("depth", None, None),
        P("depth", None),
        P("depth", "dp", None, None),
    )
    return jax.shard_map(
        body,
        mesh=mesh,
        in_specs=placed,
        out_specs=(
            P("depth", "dp", None, None),
            P("depth", "dp", None, None),
            P("depth", None, None),
        ),
        check_vma=False,
    )
```

profile of v0, /device:TPU:495, one launch (start us, length us, event | category | flops | bytes accessed | tf_op | source)
XLA Modules:
  0.0 549.2 jit_solution(12237711900461175792)
XLA Ops:
  7.2 1.6 broadcast_multiply_fusion
  11.3 1.1 tanh_convert_fusion.6
  13.1 1.1 tanh_convert_fusion.5
  14.9 1.1 tanh_convert_fusion.4
  16.7 1.1 fusion.11
  17.8 1.3 collective-permute-start
  19.1 72.5 %all-gather.1 = f32[128,1,64]{2,1,0:T(1,128)S(1)} all-gather(f32[1,1,64]{2,1,0:T(1,128)} %bitcast.280), channel_id=1, replica_groups=mesh['depth'=128,'dp'=4] {'depth'}, dimensions={0}, use_global_device_ids=true | all-gather | bytes 33024 | tf_op jit(solution)/shard_map/all_gather | solution.py:16
  93.1 1.1 tanh_convert_fusion.2
  94.9 1.1 tanh_convert_fusion.1
  96.7 58.0 %all-gather.5.cloned.1.call-done = f32[128,1,64,256]{3,2,1,0:T(8,128)} async-done(((f32[1,1,64,256]{3,2,1,0:T(8,128)}), f32[128,1,64,256]{3,2,1,0:T(8,128)}) %all-gather.5.cloned.1.call-update) | async-done | bytes 8388624 | tf_op jit(solution)/shard_map/all_gather | solution.py:16
  158.6 3.3 collective-permute-start.1
  167.4 249.2 %all-gather.7.cloned.1.call-done = f32[128,64,256]{2,1,0:T(8,128)} async-done(((f32[1,64,256]{2,1,0:T(8,128)}), f32[128,64,256]{2,1,0:T(8,128)}) %all-gather.7.cloned.1.call-update) | async-done | bytes 8388624 | tf_op jit(solution)/shard_map/all_gather | solution.py:16
  416.6 123.4 %while.26 = (s32[]{:T(128)}, f32[1,64,256]{2,1,0:T(8,128)S(1)}, s32[]{:T(128)}, f32[128,64]{1,0:T(8,128)S(1)}, f32[128,1,64,256]{3,2,1,0:T(8,128)}, /*index=5*/s32[]{:T(128)}, s32[]{:T(128)}, s32[]{:T(128)}) while((s32[]{:T(128)}, f32[1,64,256]{2,1,0:T(8,128)S(1)}, s32[]{:T(128)}, f32[128,64]{1,0:T(8,128)S(1)}, f32[128,1,64,256]{3,2,1,0:T(8,128)}, ...), condition=%wide.region_1.2_spmd, body=%wide.region_0.1_spmd.sunk | while | flops 32773 | bytes 197503 | solution.py:25
  416.6 0.9 bitcast_add_fusion.5
  417.6 0.9 bitcast_add_fusion.5
  418.6 0.9 bitcast_add_fusion.5
  419.5 0.9 bitcast_add_fusion.5
  420.5 0.9 bitcast_add_fusion.5
  421.5 0.9 bitcast_add_fusion.5
  422.5 0.9 bitcast_add_fusion.5
  423.4 0.9 bitcast_add_fusion.5
  424.4 0.9 bitcast_add_fusion.5
  425.4 0.9 bitcast_add_fusion.5
  426.3 0.9 bitcast_add_fusion.5
  427.3 0.9 bitcast_add_fusion.5
  428.3 0.9 bitcast_add_fusion.5
  429.3 0.9 bitcast_add_fusion.5
  430.2 0.9 bitcast_add_fusion.5
  431.2 0.9 bitcast_add_fusion.5
  432.2 0.9 bitcast_add_fusion.5
  433.2 0.9 bitcast_add_fusion.5
  434.1 0.9 bitcast_add_fusion.5
  435.1 0.9 bitcast_add_fusion.5
  436.1 0.9 bitcast_add_fusion.5
  437.0 0.9 bitcast_add_fusion.5
  438.0 0.9 bitcast_add_fusion.5
  439.0 0.9 bitcast_add_fusion.5
  440.0 0.9 bitcast_add_fusion.5
  440.9 0.9 bitcast_add_fusion.5
  441.9 0.9 bitcast_add_fusion.5
  442.9 0.9 bitcast_add_fusion.5
  443.8 0.9 bitcast_add_fusion.5
  444.8 0.9 bitcast_add_fusion.5
  445.8 0.9 bitcast_add_fusion.5
  446.8 0.9 bitcast_add_fusion.5
  461.3 0.9 bitcast_add_fusion.5
  462.3 0.9 bitcast_add_fusion.5
  463.3 0.9 bitcast_add_fusion.5
  464.3 0.9 bitcast_add_fusion.5
  468.1 0.9 bitcast_add_fusion.5
  469.1 0.9 bitcast_add_fusion.5
  481.7 0.9 bitcast_add_fusion.5
  482.7 0.9 bitcast_add_fusion.5
  483.7 0.9 bitcast_add_fusion.5
  500.2 0.9 bitcast_add_fusion.5
  501.2 0.9 bitcast_add_fusion.5
  502.2 0.9 bitcast_add_fusion.5
  518.7 0.9 bitcast_add_fusion.5
  519.6 0.9 bitcast_add_fusion.5
  520.6 0.9 bitcast_add_fusion.5
  537.1 0.9 bitcast_add_fusion.5
  538.1 0.9 bitcast_add_fusion.5
  539.1 0.9 bitcast_add_fusion.5
  540.7 2.0 copy.86
  (339 shorter events, 89.7 us)
Async XLA Ops:
  7.2 148.9 %copy-start.4 = (f32[1,64]{1,0:T(1,128)S(1)}, f32[1,64]{1,0:T(1,128)}, u32[]{:S(2)}) copy-start(f32[1,64]{1,0:T(1,128)} %param.10) | copy-start | bytes 772
  7.2 147.6 %copy-start.3 = (f32[1,1,64,256]{3,2,1,0:T(8,128)S(1)}, f32[1,1,64,256]{3,2,1,0:T(8,128)}, u32[]{:S(2)}) copy-start(f32[1,1,64,256]{3,2,1,0:T(8,128)} %param.11) | copy-start | bytes 196612
  7.2 147.6 %copy-start = (bf16[4,64,576]{2,1,0:T(8,128)(2,1)S(1)}, bf16[4,64,576]{2,1,0:T(8,128)(2,1)}, u32[]{:S(2)}) copy-start(bf16[4,64,576]{2,1,0:T(8,128)(2,1)} %param.9) | copy-start | bytes 884740
  7.2 147.5 %all-gather.5.cloned.1.call-start = ((), (), s32[]{:S(2)}) async-start(), calls=%async_computation | async-start | bytes 8454144 | tf_op jit(solution)/shard_map/all_gather | solution.py:16
  8.9 407.7 %all-gather.7.cloned.1.call-start = ((), (), s32[]{:S(2)}) async-start(), calls=%async_computation.2 | async-start | bytes 8454144 | tf_op jit(solution)/shard_map/all_gather | solution.py:16
  17.8 73.8 %collective-permute-start = (f32[1,64,256]{2,1,0:T(8,128)S(1)}, f32[1,64,256]{2,1,0:T(8,128)S(1)}, u32[]{:S(2)}, u32[]{:S(2)}) collective-permute-start(f32[1,64,256]{2,1,0:T(8,128)S(1)} %fusion.11), channel_id=1, source_target_pairs={{0,4},{4,8},{8,12},{12,16},{16,20},{20,24},{24,28},{28,32},{32,36}... | collective-permute-start | bytes 196616 | tf_op jit(solution)/shard_map/ppermute | solution.py:31
  156.9 383.9 %all-reduce.74.cloned.1.call-start = ((), (), s32[]{:S(2)}) async-start(), calls=%async_computation.1 | async-start | bytes 1310720 | tf_op jit(solution)/shard_map/psum | solution.py:123
  158.6 7.9 %copy-start.1 = (f32[1,1,64,256]{3,2,1,0:T(8,128)S(1)}, f32[1,1,64,256]{3,2,1,0:T(8,128)}, u32[]{:S(2)}) copy-start(f32[1,1,64,256]{3,2,1,0:T(8,128)} %param.8) | copy-start | bytes 196612
  158.6 4.1 collective-permute-start.1
  162.7 377.3 %copy-start.2 = (f32[1,64,256]{2,1,0:T(8,128)S(1)}, f32[1,64,256]{2,1,0:T(8,128)}, u32[]{:S(2)}) copy-start(f32[1,64,256]{2,1,0:T(8,128)} %select_subtract_fusion) | copy-start | bytes 196612
Sparse Core Ops, SparseCore 0:
  11.7 142.9 all-gather.4
  158.4 258.1 all-gather.6
  419.5 54.7 all-reduce.73
where the time goes:
time: 556 us; the launch traced here: 549 us
  waiting for transfers between devices  307 us (55%)
  other arithmetic  131 us (24%)
  blocking collectives  72.5 us (13%)
  between operations  14.3 us (3%)
  matrix products  11.5 us (2%)
    all_gather x2, waiting for transfers between devices, prefix(): gathered = jax.tree.map(lambda a: lax.all_gather(a, axis), part)  307 us
    add x127, other arithmetic, compose_maps(): later[0][None, :, None] * earlier[1] + later[1]  118 us
    all_gather x1, blocking collectives, prefix(): gathered = jax.tree.map(lambda a: lax.all_gather(a, axis), part)  72.5 us
  transfers between devices with their start and end apart: 5, of which 2 were waited for; matrix products, arithmetic and copies ran while one was open for 26% of the time, Pallas kernels for 0%

commit v1 on v0

--- a/solution.py
+++ b/solution.py
@@ -9,20 +9,32 @@
 TAP_OFFSETS = [(-1, -1), (-1, 0), (-1, 1), (0, -1), (0, 0), (0, 1), (1, -1), (1, 0), (1, 1)]
 
 
-def prefix(part, axis, combine, identity, reverse):
+def pack(gain, state):
+    row = jnp.pad(gain, (0, state.shape[-1] - gain.shape[0]))
+    return jnp.concatenate([state.reshape(-1, state.shape[-1]), row[None]], axis=0)
+
+
+def scan_along(gain, state, axis, reverse):
     count = lax.axis_size(axis)
-    place = lax.axis_index(axis)
-    ahead = count - 1 - place if reverse else place
-    gathered = jax.tree.map(lambda a: lax.all_gather(a, axis), part)
-    state = jax.tree.map(lambda a, e: jnp.zeros_like(a) + jnp.asarray(e, a.dtype), part, identity)
-
-    def one(hop, state):
-        source = count - 1 - hop if reverse else hop
-        return combine(
-            state, jax.tree.map(lambda a: lax.dynamic_index_in_dim(a, source, 0, False), gathered)
-        )
-
-    return lax.fori_loop(0, ahead, one, state)
+    rows = state.shape[-2]
+    carried = jnp.zeros_like(state)
+    total = state
+    distance = 1
+    while distance < count:
+        final = 2 * distance >= count
+        step = -distance if reverse else distance
+        message = total if final else pack(gain, total)
+        arrived = passed_along(message, axis, step)
+        if final:
+            part = arrived
+        else:
+            part = arrived[:rows].reshape(state.shape)
+        carried = carried + gain[:, None] * part
+        total = state + carried
+        if not final:
+            gain = gain * arrived[rows, : gain.shape[0]]
+        distance *= 2
+    return total, carried
 
 
 def passed_along(block, axis, distance):
@@ -86,35 +98,21 @@
     return (upstream, jnp.stack(layer_grads))
 
 
-def compose_maps(earlier, later):
-    return (later[0] * earlier[0], later[0][None, :, None] * earlier[1] + later[1])
-
-
-def adjoint_carry(rate_vec, incoming):
-    identity_maps = (jnp.ones_like(rate_vec), jnp.zeros_like(incoming))
-    _, passed_in = prefix(
-        (rate_vec, rate_vec[None, :, None] * incoming), "depth", compose_maps, identity_maps, True
-    )
-    return passed_in
-
-
 def body(cpoints, weights, coarse_gain, cotangent):
     step_size = 1.0 / (weights.shape[0] * lax.axis_size("depth"))
     own_state = cpoints[0]
     rate_vec = coarse_gain[0]
     cot_here = cotangent[0]
     leading = lax.axis_index("depth") == 0
+    next_rate = passed_along(rate_vec, "depth", -1)
+    adjoint_here, passed_in = scan_along(next_rate, cot_here, "depth", True)
     relaxed, own_kept = run_block(own_state, weights, step_size)
     arriving = passed_along(relaxed, "depth", 1)
     start_state = jnp.where(leading, own_state, arriving)
     propagated, start_kept = run_block(start_state, weights, step_size)
     gained_start = rate_vec[None, :, None] * start_state
     offset = propagated - jnp.where(leading, jnp.zeros_like(gained_start), gained_start)
-    identity_maps = (jnp.ones_like(rate_vec), jnp.zeros_like(offset))
-    _, previous_out = prefix((rate_vec, offset), "depth", compose_maps, identity_maps, False)
-    corrected = rate_vec[None, :, None] * previous_out + offset
-    passed_in = adjoint_carry(rate_vec, cot_here)
-    adjoint_here = cot_here + passed_in
+    corrected, _ = scan_along(rate_vec, offset, "depth", False)
     back_start, start_grads = back_block(start_kept, weights, adjoint_here, step_size)
     arriving_bar = passed_along(back_start, "depth", -1)
     relaxed_bar = arriving_bar - passed_in

time: 556 us -> 189 us (0.34)
  the two profiles are of different devices: /device:TPU:495 before, /device:TPU:2 now
where the time goes in v1:
time: 189 us; the launch traced here: 188 us
  starting transfers between devices  77.6 us (41%)
  waiting for transfers between devices  75.6 us (40%)
  between operations  14.9 us (8%)
  other arithmetic  11.2 us (6%)
  matrix products  5.53 us (3%)
  local copies, waits for them, and re-layouts  3.21 us (2%)
    ppermute x17, starting transfers between devices, passed_along(): return lax.ppermute(block, axis, route)  77.6 us
    ppermute x17, waiting for transfers between devices, passed_along(): return lax.ppermute(block, axis, route)  58.1 us
    psum x1, waiting for transfers between devices, body(): grad_weights = lax.psum(start_grads + own_grads, 'dp')  17.4 us
    unnamed x64, other arithmetic  4.68 us
  transfers between devices with their start and end apart: 18, of which 14 were waited for; matrix products, arithmetic and copies ran while one was open for 7% of the time, Pallas kernels for 0%

profile of v1, /device:TPU:2, one launch (start us, length us, event | category | flops | bytes accessed | tf_op | source)
XLA Modules:
  0.0 188.1 jit_solution(49535777164816162)
XLA Ops:
  7.2 0.6 copy-done.3
  7.8 1.9 %collective-permute-start.8 = (f32[64]{0:T(128)S(1)}, f32[64]{0:T(128)S(1)}, u32[]{:S(2)}, u32[]{:S(2)}) collective-permute-start(f32[64]{0:T(128)S(1)} %bitcast.368), channel_id=1, source_target_pairs={{4,0},{8,4},{12,8},{16,12},{20,16},{24,20},{28,24},{32,28},{36,32}... | collective-permute-start | bytes 776 | tf_op jit(solution)/shard_map/ppermute | solution.py:43
  9.8 0.9 fusion.209
  11.4 0.3 copy-done.1
  12.6 0.2 tanh_convert_fusion.5
  14.6 2.4 %collective-permute-start = (f32[1,64,256]{2,1,0:T(8,128)S(1)}, f32[1,64,256]{2,1,0:T(8,128)S(1)}, u32[]{:S(2)}, u32[]{:S(2)}) collective-permute-start(f32[1,64,256]{2,1,0:T(8,128)S(1)} %fusion.11), channel_id=1, source_target_pairs={{0,4},{4,8},{8,12},{12,16},{16,20},{20,24},{24,28},{28,32},{32,36}... | collective-permute-start | bytes 196616 | tf_op jit(solution)/shard_map/ppermute | solution.py:43
  17.0 7.4 %collective-permute-start.9 = (f32[65,256]{1,0:T(8,128)S(1)}, f32[65,256]{1,0:T(8,128)S(1)}, u32[]{:S(2)}, u32[]{:S(2)}) collective-permute-start(f32[65,256]{1,0:T(8,128)S(1)} %pad_maximum_fusion.6), channel_id=1, source_target_pairs={{4,0},{8,4},{12,8},{16,12},{20,16},{24,20},{28,24},{32,28},{36,32}... | collective-permute-start | bytes 199688 | tf_op jit(solution)/shard_map/ppermute | solution.py:43
  25.2 0.2 tanh_convert_fusion.2
  26.1 0.2 tanh_convert_fusion.1
  26.8 1.9 %collective-permute-start.10 = (f32[65,256]{1,0:T(8,128)S(1)}, f32[65,256]{1,0:T(8,128)S(1)}, u32[]{:S(2)}, u32[]{:S(2)}) collective-permute-start(f32[65,256]{1,0:T(8,128)S(1)} %pad_maximum_fusion.7), channel_id=1, source_target_pairs={{8,0},{12,4},{16,8},{20,12},{24,16},{28,20},{32,24},{36,28},{40,32... | collective-permute-start | bytes 199688 | tf_op jit(solution)/shard_map/ppermute | solution.py:43
  28.7 4.3 %collective-permute-done.10 = f32[65,256]{1,0:T(8,128)S(1)} collective-permute-done((f32[65,256]{1,0:T(8,128)S(1)}, f32[65,256]{1,0:T(8,128)S(1)}, u32[]{:S(2)}, u32[]{:S(2)}) %collective-permute-start.10) | collective-permute-done | bytes 66592 | tf_op jit(solution)/shard_map/ppermute | solution.py:43
  33.1 1.3 collective-permute-start.11
  34.5 7.0 %collective-permute-done.11 = f32[65,256]{1,0:T(8,128)S(1)} collective-permute-done((f32[65,256]{1,0:T(8,128)S(1)}, f32[65,256]{1,0:T(8,128)S(1)}, u32[]{:S(2)}, u32[]{:S(2)}) %collective-permute-start.11) | collective-permute-done | bytes 66592 | tf_op jit(solution)/shard_map/ppermute | solution.py:43
  41.6 1.3 collective-permute-start.12
  43.0 4.9 %collective-permute-done.12 = f32[65,256]{1,0:T(8,128)S(1)} collective-permute-done((f32[65,256]{1,0:T(8,128)S(1)}, f32[65,256]{1,0:T(8,128)S(1)}, u32[]{:S(2)}, u32[]{:S(2)}) %collective-permute-start.12) | collective-permute-done | bytes 66592 | tf_op jit(solution)/shard_map/ppermute | solution.py:43
  48.0 1.3 collective-permute-start.13
  49.4 5.8 %collective-permute-done.13 = f32[65,256]{1,0:T(8,128)S(1)} collective-permute-done((f32[65,256]{1,0:T(8,128)S(1)}, f32[65,256]{1,0:T(8,128)S(1)}, u32[]{:S(2)}, u32[]{:S(2)}) %collective-permute-start.13) | collective-permute-done | bytes 66592 | tf_op jit(solution)/shard_map/ppermute | solution.py:43
  55.3 1.3 collective-permute-start.14
  56.7 10.1 %collective-permute-done.14 = f32[65,256]{1,0:T(8,128)S(1)} collective-permute-done((f32[65,256]{1,0:T(8,128)S(1)}, f32[65,256]{1,0:T(8,128)S(1)}, u32[]{:S(2)}, u32[]{:S(2)}) %collective-permute-start.14) | collective-permute-done | bytes 66592 | tf_op jit(solution)/shard_map/ppermute | solution.py:43
  66.9 1.3 collective-permute-start.15
  68.2 13.8 %collective-permute-done.15 = f32[1,64,256]{2,1,0:T(8,128)S(1)} collective-permute-done((f32[1,64,256]{2,1,0:T(8,128)S(1)}, f32[1,64,256]{2,1,0:T(8,128)S(1)}, u32[]{:S(2)}, u32[]{:S(2)}) %collective-permute-start.15) | collective-permute-done | bytes 65568 | tf_op jit(solution)/shard_map/ppermute | solution.py:43
  82.1 0.3 convolution_bitcast_fusion.7
  82.4 0.2 fusion.58
  82.7 0.2 convolution_bitcast_fusion.13
  82.9 0.3 convolution_bitcast_fusion.6
  83.2 0.2 fusion.76
  83.4 0.2 convolution_bitcast_fusion.14
  83.7 0.3 convolution_bitcast_fusion.5
  84.0 0.2 fusion.94
  84.2 0.2 convolution_bitcast_fusion.15
  84.4 0.3 convolution_bitcast_fusion.4
  85.6 6.3 %collective-permute-start.1 = (f32[65,256]{1,0:T(8,128)S(1)}, f32[65,256]{1,0:T(8,128)S(1)}, u32[]{:S(2)}, u32[]{:S(2)}) collective-permute-start(f32[65,256]{1,0:T(8,128)S(1)} %pad_maximum_fusion), channel_id=1, source_target_pairs={{0,4},{4,8},{8,12},{12,16},{16,20},{20,24},{24,28},{28,32},{32,36}... | collective-permute-start | bytes 199688 | tf_op jit(solution)/shard_map/ppermute | solution.py:43
  92.0 0.2 fusion.112
  92.2 1.9 %collective-permute-start.16 = (f32[1,64,256]{2,1,0:T(8,128)S(1)}, f32[1,64,256]{2,1,0:T(8,128)S(1)}, u32[]{:S(2)}, u32[]{:S(2)}) collective-permute-start(f32[1,64,256]{2,1,0:T(8,128)S(1)} %fusion.112), channel_id=1, source_target_pairs={{4,0},{8,4},{12,8},{16,12},{20,16},{24,20},{28,24},{32,28},{36,32}... | collective-permute-start | bytes 196616 | tf_op jit(solution)/shard_map/ppermute | solution.py:43
  94.2 0.2 convolution_bitcast_fusion.12
  94.4 1.7 collective-permute-done.16
  96.1 0.2 convolution_bitcast_fusion.8
  96.3 0.3 convolution_bitcast_fusion.3
  96.6 0.2 fusion.130
  96.8 0.2 convolution_bitcast_fusion.9
  97.0 0.3 convolution_bitcast_fusion.2
  97.4 0.2 fusion.148
  97.6 0.3 convolution_bitcast_fusion.1
  97.9 0.2 fusion.166
  98.1 0.2 convolution_bitcast_fusion.10
  98.5 3.5 %collective-permute-start.2 = (f32[65,256]{1,0:T(8,128)S(1)}, f32[65,256]{1,0:T(8,128)S(1)}, u32[]{:S(2)}, u32[]{:S(2)}) collective-permute-start(f32[65,256]{1,0:T(8,128)S(1)} %pad_maximum_fusion.1), channel_id=1, source_target_pairs={{0,8},{4,12},{8,16},{12,20},{16,24},{20,28},{24,32},{28,36},{32,40... | collective-permute-start | bytes 199688 | tf_op jit(solution)/shard_map/ppermute | solution.py:43
  102.0 0.2 convolution_bitcast_fusion.11
  102.2 2.5 %collective-permute-done.2 = f32[65,256]{1,0:T(8,128)S(1)} collective-permute-done((f32[65,256]{1,0:T(8,128)S(1)}, f32[65,256]{1,0:T(8,128)S(1)}, u32[]{:S(2)}, u32[]{:S(2)}) %collective-permute-start.2) | collective-permute-done | bytes 66592 | tf_op jit(solution)/shard_map/ppermute | solution.py:43
  104.8 8.5 %collective-permute-start.3 = (f32[65,256]{1,0:T(8,128)S(1)}, f32[65,256]{1,0:T(8,128)S(1)}, u32[]{:S(2)}, u32[]{:S(2)}) collective-permute-start(f32[65,256]{1,0:T(8,128)S(1)} %pad_maximum_fusion.2), channel_id=1, source_target_pairs={{0,16},{4,20},{8,24},{12,28},{16,32},{20,36},{24,40},{28,44},{32,4... | collective-permute-start | bytes 199688 | tf_op jit(solution)/shard_map/ppermute | solution.py:43
  113.4 0.9 maximum_add_fusion
  114.3 1.4 collective-permute-done.3
  115.9 5.0 %collective-permute-start.4 = (f32[65,256]{1,0:T(8,128)S(1)}, f32[65,256]{1,0:T(8,128)S(1)}, u32[]{:S(2)}, u32[]{:S(2)}) collective-permute-start(f32[65,256]{1,0:T(8,128)S(1)} %pad_maximum_fusion.3), channel_id=1, source_target_pairs={{0,32},{4,36},{8,40},{12,44},{16,48},{20,52},{24,56},{28,60},{32,6... | collective-permute-start | bytes 199688 | tf_op jit(solution)/shard_map/ppermute | solution.py:43
  120.8 0.3 convolution_bitcast_fusion
  121.1 1.7 collective-permute-done.4
  122.9 7.1 %collective-permute-start.5 = (f32[65,256]{1,0:T(8,128)S(1)}, f32[65,256]{1,0:T(8,128)S(1)}, u32[]{:S(2)}, u32[]{:S(2)}) collective-permute-start(f32[65,256]{1,0:T(8,128)S(1)} %pad_maximum_fusion.4), channel_id=1, source_target_pairs={{0,64},{4,68},{8,72},{12,76},{16,80},{20,84},{24,88},{28,92},{32,9... | collective-permute-start | bytes 199688 | tf_op jit(solution)/shard_map/ppermute | solution.py:43
  130.1 1.9 %collective-permute-done.5 = f32[65,256]{1,0:T(8,128)S(1)} collective-permute-done((f32[65,256]{1,0:T(8,128)S(1)}, f32[65,256]{1,0:T(8,128)S(1)}, u32[]{:S(2)}, u32[]{:S(2)}) %collective-permute-start.5) | collective-permute-done | bytes 66592 | tf_op jit(solution)/shard_map/ppermute | solution.py:43
  132.2 12.0 %collective-permute-start.6 = (f32[65,256]{1,0:T(8,128)S(1)}, f32[65,256]{1,0:T(8,128)S(1)}, u32[]{:S(2)}, u32[]{:S(2)}) collective-permute-start(f32[65,256]{1,0:T(8,128)S(1)} %pad_maximum_fusion.5), channel_id=1, source_target_pairs={{0,128},{4,132},{8,136},{12,140},{16,144},{20,148},{24,152},{28,15... | collective-permute-start | bytes 199688 | tf_op jit(solution)/shard_map/ppermute | solution.py:43
  144.2 0.8 fusion.208
  145.0 1.1 collective-permute-done.6
  146.2 13.0 %collective-permute-start.7 = (f32[1,64,256]{2,1,0:T(8,128)S(1)}, f32[1,64,256]{2,1,0:T(8,128)S(1)}, u32[]{:S(2)}, u32[]{:S(2)}) collective-permute-start(f32[1,64,256]{2,1,0:T(8,128)S(1)} %fusion.303), channel_id=1, source_target_pairs={{0,256},{4,260},{8,264},{12,268},{16,272},{20,276},{24,280},{28,28... | collective-permute-start | bytes 196616 | tf_op jit(solution)/shard_map/ppermute | solution.py:43
  159.3 1.9 collective-permute-done.7
  161.1 0.7 add_bitcast_fusion.1
  161.8 17.4 %all-reduce.86.cloned.1.call-done = f32[4,64,576]{2,1,0:T(8,128)} async-done(((f32[4,64,576]{2,1,0:T(8,128)}), f32[4,64,576]{2,1,0:T(8,128)}) %all-reduce.86.cloned.1.call-update) | async-done | bytes 589840 | tf_op jit(solution)/shard_map/psum | solution.py:121
  179.3 2.0 %copy.72 = f32[4,64,576]{2,1,0:T(8,128)} copy(f32[4,64,576]{2,1,0:T(8,128)} %all-reduce.86.cloned.1.call-done) | data formatting | bytes 1179648
  (149 shorter events, 7.8 us)
Async XLA Ops:
  7.2 0.7 copy-start.3
  7.2 172.1 %all-reduce.86.cloned.1.call-start = ((), (), s32[]{:S(2)}) async-start(), calls=%async_computation | async-start | bytes 1310720 | tf_op jit(solution)/shard_map/psum | solution.py:121
  7.8 9.2 %collective-permute-start.8 = (f32[64]{0:T(128)S(1)}, f32[64]{0:T(128)S(1)}, u32[]{:S(2)}, u32[]{:S(2)}) collective-permute-start(f32[64]{0:T(128)S(1)} %bitcast.368), channel_id=1, source_target_pairs={{4,0},{8,4},{12,8},{16,12},{20,16},{24,20},{28,24},{32,28},{36,32}... | collective-permute-start | bytes 776 | tf_op jit(solution)/shard_map/ppermute | solution.py:43
  9.8 1.3 copy-start.2
  10.7 1.0 copy-start.1
  14.4 2.7 %copy-start = (f32[1,1,64,256]{3,2,1,0:T(8,128)S(1)}, f32[1,1,64,256]{3,2,1,0:T(8,128)}, u32[]{:S(2)}) copy-start(f32[1,1,64,256]{3,2,1,0:T(8,128)} %param.7) | copy-start | bytes 196612
  14.6 9.9 %collective-permute-start = (f32[1,64,256]{2,1,0:T(8,128)S(1)}, f32[1,64,256]{2,1,0:T(8,128)S(1)}, u32[]{:S(2)}, u32[]{:S(2)}) collective-permute-start(f32[1,64,256]{2,1,0:T(8,128)S(1)} %fusion.11), channel_id=1, source_target_pairs={{0,4},{4,8},{8,12},{12,16},{16,20},{20,24},{24,28},{28,32},{32,36}... | collective-permute-start | bytes 196616 | tf_op jit(solution)/shard_map/ppermute | solution.py:43
  17.0 9.6 %collective-permute-start.9 = (f32[65,256]{1,0:T(8,128)S(1)}, f32[65,256]{1,0:T(8,128)S(1)}, u32[]{:S(2)}, u32[]{:S(2)}) collective-permute-start(f32[65,256]{1,0:T(8,128)S(1)} %pad_maximum_fusion.6), channel_id=1, source_target_pairs={{4,0},{8,4},{12,8},{16,12},{20,16},{24,20},{28,24},{32,28},{36,32}... | collective-permute-start | bytes 199688 | tf_op jit(solution)/shard_map/ppermute | solution.py:43
  26.8 6.2 %collective-permute-start.10 = (f32[65,256]{1,0:T(8,128)S(1)}, f32[65,256]{1,0:T(8,128)S(1)}, u32[]{:S(2)}, u32[]{:S(2)}) collective-permute-start(f32[65,256]{1,0:T(8,128)S(1)} %pad_maximum_fusion.7), channel_id=1, source_target_pairs={{8,0},{12,4},{16,8},{20,12},{24,16},{28,20},{32,24},{36,28},{40,32... | collective-permute-start | bytes 199688 | tf_op jit(solution)/shard_map/ppermute | solution.py:43
  33.1 8.3 %collective-permute-start.11 = (f32[65,256]{1,0:T(8,128)S(1)}, f32[65,256]{1,0:T(8,128)S(1)}, u32[]{:S(2)}, u32[]{:S(2)}) collective-permute-start(f32[65,256]{1,0:T(8,128)S(1)} %pad_maximum_fusion.8), channel_id=1, source_target_pairs={{16,0},{20,4},{24,8},{28,12},{32,16},{36,20},{40,24},{44,28},{48,3... | collective-permute-start | bytes 199688 | tf_op jit(solution)/shard_map/ppermute | solution.py:43
  41.6 6.2 %collective-permute-start.12 = (f32[65,256]{1,0:T(8,128)S(1)}, f32[65,256]{1,0:T(8,128)S(1)}, u32[]{:S(2)}, u32[]{:S(2)}) collective-permute-start(f32[65,256]{1,0:T(8,128)S(1)} %pad_maximum_fusion.9), channel_id=1, source_target_pairs={{32,0},{36,4},{40,8},{44,12},{48,16},{52,20},{56,24},{60,28},{64,3... | collective-permute-start | bytes 199688 | tf_op jit(solution)/shard_map/ppermute | solution.py:43
  48.0 7.2 %collective-permute-start.13 = (f32[65,256]{1,0:T(8,128)S(1)}, f32[65,256]{1,0:T(8,128)S(1)}, u32[]{:S(2)}, u32[]{:S(2)}) collective-permute-start(f32[65,256]{1,0:T(8,128)S(1)} %pad_maximum_fusion.10), channel_id=1, source_target_pairs={{64,0},{68,4},{72,8},{76,12},{80,16},{84,20},{88,24},{92,28},{96,3... | collective-permute-start | bytes 199688 | tf_op jit(solution)/shard_map/ppermute | solution.py:43
  55.3 11.5 %collective-permute-start.14 = (f32[65,256]{1,0:T(8,128)S(1)}, f32[65,256]{1,0:T(8,128)S(1)}, u32[]{:S(2)}, u32[]{:S(2)}) collective-permute-start(f32[65,256]{1,0:T(8,128)S(1)} %pad_maximum_fusion.11), channel_id=1, source_target_pairs={{128,0},{132,4},{136,8},{140,12},{144,16},{148,20},{152,24},{156,2... | collective-permute-start | bytes 199688 | tf_op jit(solution)/shard_map/ppermute | solution.py:43
  66.9 15.1 %collective-permute-start.15 = (f32[1,64,256]{2,1,0:T(8,128)S(1)}, f32[1,64,256]{2,1,0:T(8,128)S(1)}, u32[]{:S(2)}, u32[]{:S(2)}) collective-permute-start(f32[1,64,256]{2,1,0:T(8,128)S(1)} %get-tuple-element.5), channel_id=1, source_target_pairs={{256,0},{260,4},{264,8},{268,12},{272,16},{276,20},{280,24},{284,2... | collective-permute-start | bytes 196616 | tf_op jit(solution)/shard_map/ppermute | solution.py:43
  85.6 12.7 %collective-permute-start.1 = (f32[65,256]{1,0:T(8,128)S(1)}, f32[65,256]{1,0:T(8,128)S(1)}, u32[]{:S(2)}, u32[]{:S(2)}) collective-permute-start(f32[65,256]{1,0:T(8,128)S(1)} %pad_maximum_fusion), channel_id=1, source_target_pairs={{0,4},{4,8},{8,12},{12,16},{16,20},{20,24},{24,28},{28,32},{32,36}... | collective-permute-start | bytes 199688 | tf_op jit(solution)/shard_map/ppermute | solution.py:43
  92.2 3.8 %collective-permute-start.16 = (f32[1,64,256]{2,1,0:T(8,128)S(1)}, f32[1,64,256]{2,1,0:T(8,128)S(1)}, u32[]{:S(2)}, u32[]{:S(2)}) collective-permute-start(f32[1,64,256]{2,1,0:T(8,128)S(1)} %fusion.112), channel_id=1, source_target_pairs={{4,0},{8,4},{12,8},{16,12},{20,16},{24,20},{28,24},{32,28},{36,32}... | collective-permute-start | bytes 196616 | tf_op jit(solution)/shard_map/ppermute | solution.py:43
  98.5 6.2 %collective-permute-start.2 = (f32[65,256]{1,0:T(8,128)S(1)}, f32[65,256]{1,0:T(8,128)S(1)}, u32[]{:S(2)}, u32[]{:S(2)}) collective-permute-start(f32[65,256]{1,0:T(8,128)S(1)} %pad_maximum_fusion.1), channel_id=1, source_target_pairs={{0,8},{4,12},{8,16},{12,20},{16,24},{20,28},{24,32},{28,36},{32,40... | collective-permute-start | bytes 199688 | tf_op jit(solution)/shard_map/ppermute | solution.py:43
  104.8 10.9 %collective-permute-start.3 = (f32[65,256]{1,0:T(8,128)S(1)}, f32[65,256]{1,0:T(8,128)S(1)}, u32[]{:S(2)}, u32[]{:S(2)}) collective-permute-start(f32[65,256]{1,0:T(8,128)S(1)} %pad_maximum_fusion.2), channel_id=1, source_target_pairs={{0,16},{4,20},{8,24},{12,28},{16,32},{20,36},{24,40},{28,44},{32,4... | collective-permute-start | bytes 199688 | tf_op jit(solution)/shard_map/ppermute | solution.py:43
  115.9 6.9 %collective-permute-start.4 = (f32[65,256]{1,0:T(8,128)S(1)}, f32[65,256]{1,0:T(8,128)S(1)}, u32[]{:S(2)}, u32[]{:S(2)}) collective-permute-start(f32[65,256]{1,0:T(8,128)S(1)} %pad_maximum_fusion.3), channel_id=1, source_target_pairs={{0,32},{4,36},{8,40},{12,44},{16,48},{20,52},{24,56},{28,60},{32,6... | collective-permute-start | bytes 199688 | tf_op jit(solution)/shard_map/ppermute | solution.py:43
  122.9 9.1 %collective-permute-start.5 = (f32[65,256]{1,0:T(8,128)S(1)}, f32[65,256]{1,0:T(8,128)S(1)}, u32[]{:S(2)}, u32[]{:S(2)}) collective-permute-start(f32[65,256]{1,0:T(8,128)S(1)} %pad_maximum_fusion.4), channel_id=1, source_target_pairs={{0,64},{4,68},{8,72},{12,76},{16,80},{20,84},{24,88},{28,92},{32,9... | collective-permute-start | bytes 199688 | tf_op jit(solution)/shard_map/ppermute | solution.py:43
  132.2 14.0 %collective-permute-start.6 = (f32[65,256]{1,0:T(8,128)S(1)}, f32[65,256]{1,0:T(8,128)S(1)}, u32[]{:S(2)}, u32[]{:S(2)}) collective-permute-start(f32[65,256]{1,0:T(8,128)S(1)} %pad_maximum_fusion.5), channel_id=1, source_target_pairs={{0,128},{4,132},{8,136},{12,140},{16,144},{20,148},{24,152},{28,15... | collective-permute-start | bytes 199688 | tf_op jit(solution)/shard_map/ppermute | solution.py:43
  146.2 14.9 %collective-permute-start.7 = (f32[1,64,256]{2,1,0:T(8,128)S(1)}, f32[1,64,256]{2,1,0:T(8,128)S(1)}, u32[]{:S(2)}, u32[]{:S(2)}) collective-permute-start(f32[1,64,256]{2,1,0:T(8,128)S(1)} %fusion.303), channel_id=1, source_target_pairs={{0,256},{4,260},{8,264},{12,268},{16,272},{20,276},{24,280},{28,28... | collective-permute-start | bytes 196616 | tf_op jit(solution)/shard_map/ppermute | solution.py:43
Sparse Core Ops, SparseCore 0:
  114.5 64.7 all-reduce.85

commit v2 on v1

--- a/solution.py
+++ b/solution.py
@@ -14,27 +14,35 @@
     return jnp.concatenate([state.reshape(-1, state.shape[-1]), row[None]], axis=0)
 
 
-def scan_along(gain, state, axis, reverse):
+def exchange(gain, state, axis, bit):
     count = lax.axis_size(axis)
+    arrived = lax.ppermute(pack(gain, state), axis, [(i, i ^ (1 << bit)) for i in range(count)])
     rows = state.shape[-2]
-    carried = jnp.zeros_like(state)
-    total = state
-    distance = 1
-    while distance < count:
-        final = 2 * distance >= count
-        step = -distance if reverse else distance
-        message = total if final else pack(gain, total)
-        arrived = passed_along(message, axis, step)
-        if final:
-            part = arrived
-        else:
-            part = arrived[:rows].reshape(state.shape)
-        carried = carried + gain[:, None] * part
-        total = state + carried
-        if not final:
-            gain = gain * arrived[rows, : gain.shape[0]]
-        distance *= 2
-    return total, carried
+    return arrived[rows, : gain.shape[0]], arrived[:rows].reshape(state.shape)
+
+
+def scan_round(scan, arrived, partner_first, bit, last):
+    part_gain, part_state, whole_gain, whole_state = scan
+    got_gain, got_state = arrived
+    take = partner_first(bit)
+    part_state = jnp.where(take, part_state + part_gain[:, None] * got_state, part_state)
+    part_gain = jnp.where(take, part_gain * got_gain, part_gain)
+    if not last:
+        whole_state = jnp.where(
+            take,
+            whole_state + whole_gain[:, None] * got_state,
+            got_state + got_gain[:, None] * whole_state,
+        )
+        whole_gain = whole_gain * got_gain
+    return (part_gain, part_state, whole_gain, whole_state)
+
+
+def dp_sum(terms, axis):
+    count = lax.axis_size(axis)
+    if count != 4:
+        return lax.psum(terms, axis)
+    got = [lax.ppermute(terms, axis, [(i, i ^ k) for i in range(count)]) for k in (1, 2, 3)]
+    return (terms + got[0]) + (got[1] + got[2])
 
 
 def passed_along(block, axis, distance):
@@ -100,25 +108,51 @@
 
 def body(cpoints, weights, coarse_gain, cotangent):
     step_size = 1.0 / (weights.shape[0] * lax.axis_size("depth"))
+    rounds = (lax.axis_size("depth") - 1).bit_length()
+    place = lax.axis_index("depth")
     own_state = cpoints[0]
     rate_vec = coarse_gain[0]
     cot_here = cotangent[0]
-    leading = lax.axis_index("depth") == 0
-    next_rate = passed_along(rate_vec, "depth", -1)
-    adjoint_here, passed_in = scan_along(next_rate, cot_here, "depth", True)
+    leading = place == 0
+
+    def before(bit):
+        return (place >> bit) % 2 == 1
+
+    def after(bit):
+        return (place >> bit) % 2 == 0
+
+    reverse = (jnp.ones_like(rate_vec), jnp.zeros_like(cot_here), rate_vec, rate_vec[None, :, None] * cot_here)
+    lag = min(3, rounds - 1)
+    for bit in range(lag):
+        reverse = scan_round(reverse, exchange(reverse[2], reverse[3], "depth", bit), after, bit, bit == rounds - 1)
     relaxed, own_kept = run_block(own_state, weights, step_size)
     arriving = passed_along(relaxed, "depth", 1)
     start_state = jnp.where(leading, own_state, arriving)
     propagated, start_kept = run_block(start_state, weights, step_size)
     gained_start = rate_vec[None, :, None] * start_state
     offset = propagated - jnp.where(leading, jnp.zeros_like(gained_start), gained_start)
-    corrected, _ = scan_along(rate_vec, offset, "depth", False)
-    back_start, start_grads = back_block(start_kept, weights, adjoint_here, step_size)
-    arriving_bar = passed_along(back_start, "depth", -1)
-    relaxed_bar = arriving_bar - passed_in
-    back_own, own_grads = back_block(own_kept, weights, relaxed_bar, step_size)
+    forward = (rate_vec, offset, rate_vec, offset)
+    for bit in range(rounds):
+        rbit = bit + lag
+        if rbit < rounds:
+            reverse, forward = lax.optimization_barrier((reverse, forward))
+            got_r = exchange(reverse[2], reverse[3], "depth", rbit)
+            got_f = exchange(forward[2], forward[3], "depth", bit)
+            reverse = scan_round(reverse, got_r, after, rbit, rbit == rounds - 1)
+        else:
+            got_f = exchange(forward[2], forward[3], "depth", bit)
+        forward = scan_round(forward, got_f, before, bit, bit == rounds - 1)
+        if rbit == rounds - 1:
+            passed_in = reverse[1]
+            adjoint_here = cot_here + passed_in
+            back_start, start_grads = back_block(start_kept, weights, adjoint_here, step_size)
+            start_sum = dp_sum(start_grads, "dp")
+            arriving_bar = passed_along(back_start, "depth", -1)
+            relaxed_bar = arriving_bar - passed_in
+            back_own, own_grads = back_block(own_kept, weights, relaxed_bar, step_size)
+    corrected = forward[1]
     grad_cpoints = jnp.where(leading, back_own + back_start, back_own)
-    grad_weights = lax.psum(start_grads + own_grads, "dp")
+    grad_weights = start_sum + dp_sum(own_grads, "dp")
     return (corrected[None], grad_cpoints[None], grad_weights)
 
 

time: 189 us -> 165 us (0.87)
  the two profiles are of different devices: /device:TPU:2 before, /device:TPU:8 now
where the time goes in v2:
time: 165 us
  starting transfers between devices  86.9 us (53%)
  waiting for transfers between devices  57.7 us (35%)
  other arithmetic  12 us (7%)
  matrix products  5.52 us (3%)
  between operations  1.85 us (1%)
    ppermute x14, starting transfers between devices, exchange(): lax.ppermute(pack(gain, state), axis, [(i, i ^ 1 << bit) for i in range(c...  64.4 us
    ppermute x14, waiting for transfers between devices, exchange(): lax.ppermute(pack(gain, state), axis, [(i, i ^ 1 << bit) for i in range(c...  43.8 us
    ppermute x6, starting transfers between devices, dp_sum(): lax.ppermute(terms, axis, [(i, i ^ k) for i in range(count)])  19.5 us
    ppermute x6, waiting for transfers between devices, dp_sum(): lax.ppermute(terms, axis, [(i, i ^ k) for i in range(count)])  13.9 us
    unnamed x64, other arithmetic  4.68 us
  transfers between devices with their start and end apart: 22, of which 14 were waited for; matrix products, arithmetic and copies ran while one was open for 7% of the time, Pallas kernels for 0%

profile of v2, /device:TPU:8, one launch (start us, length us, event | category | flops | bytes accessed | tf_op | source)
XLA Modules:
  0.0 164.6 jit_solution(16879764140644978556)
XLA Ops:
  0.7 0.9 fusion.207
  2.3 0.3 copy-done
  5.5 1.7 %collective-permute-start.3 = (f32[1,64,256]{2,1,0:T(8,128)S(1)}, f32[1,64,256]{2,1,0:T(8,128)S(1)}, u32[]{:S(2)}, u32[]{:S(2)}) collective-permute-start(f32[1,64,256]{2,1,0:T(8,128)S(1)} %fusion.11), channel_id=1, source_target_pairs={{0,4},{4,8},{8,12},{12,16},{16,20},{20,24},{24,28},{28,32},{32,36}... | collective-permute-start | bytes 196616 | tf_op jit(solution)/shard_map/ppermute | solution.py:51
  7.3 3.7 %collective-permute-start = (f32[65,256]{1,0:T(8,128)S(1)}, f32[65,256]{1,0:T(8,128)S(1)}, u32[]{:S(2)}, u32[]{:S(2)}) collective-permute-start(f32[65,256]{1,0:T(8,128)S(1)} %pad_maximum_fusion.2), channel_id=1, source_target_pairs={{0,4},{4,0},{8,12},{12,8},{16,20},{20,16},{24,28},{28,24},{32,36},... | collective-permute-start | bytes 199688 | tf_op jit(solution)/shard_map/ppermute | solution.py:19
  14.6 3.4 %collective-permute-start.1 = (f32[65,256]{1,0:T(8,128)S(1)}, f32[65,256]{1,0:T(8,128)S(1)}, u32[]{:S(2)}, u32[]{:S(2)}) collective-permute-start(f32[65,256]{1,0:T(8,128)S(1)} %pad_maximum_fusion.3), channel_id=1, source_target_pairs={{0,8},{4,12},{8,0},{12,4},{16,24},{20,28},{24,16},{28,20},{32,40},... | collective-permute-start | bytes 199688 | tf_op jit(solution)/shard_map/ppermute | solution.py:19
  18.1 2.8 %collective-permute-done.1 = f32[65,256]{1,0:T(8,128)S(1)} collective-permute-done((f32[65,256]{1,0:T(8,128)S(1)}, f32[65,256]{1,0:T(8,128)S(1)}, u32[]{:S(2)}, u32[]{:S(2)}) %collective-permute-start.1) | collective-permute-done | bytes 66592 | tf_op jit(solution)/shard_map/ppermute | solution.py:19
  21.0 4.9 %collective-permute-start.2 = (f32[65,256]{1,0:T(8,128)S(1)}, f32[65,256]{1,0:T(8,128)S(1)}, u32[]{:S(2)}, u32[]{:S(2)}) collective-permute-start(f32[65,256]{1,0:T(8,128)S(1)} %pad_maximum_fusion.4), channel_id=1, source_target_pairs={{0,16},{4,20},{8,24},{12,28},{16,0},{20,4},{24,8},{28,12},{32,48},... | collective-permute-start | bytes 199688 | tf_op jit(solution)/shard_map/ppermute | solution.py:19
  26.0 2.7 %collective-permute-done.2 = f32[65,256]{1,0:T(8,128)S(1)} collective-permute-done((f32[65,256]{1,0:T(8,128)S(1)}, f32[65,256]{1,0:T(8,128)S(1)}, u32[]{:S(2)}, u32[]{:S(2)}) %collective-permute-start.2) | collective-permute-done | bytes 66592 | tf_op jit(solution)/shard_map/ppermute | solution.py:19
  28.9 5.9 %collective-permute-start.4 = (f32[65,256]{1,0:T(8,128)S(1)}, f32[65,256]{1,0:T(8,128)S(1)}, u32[]{:S(2)}, u32[]{:S(2)}) collective-permute-start(f32[65,256]{1,0:T(8,128)S(1)} %pad_maximum_fusion.5), channel_id=1, source_target_pairs={{0,32},{4,36},{8,40},{12,44},{16,48},{20,52},{24,56},{28,60},{32,0... | collective-permute-start | bytes 199688 | tf_op jit(solution)/shard_map/ppermute | solution.py:19
  34.8 1.9 %collective-permute-start.5 = (f32[65,256]{1,0:T(8,128)S(1)}, f32[65,256]{1,0:T(8,128)S(1)}, u32[]{:S(2)}, u32[]{:S(2)}) collective-permute-start(f32[65,256]{1,0:T(8,128)S(1)} %pad_maximum_fusion.6), channel_id=1, source_target_pairs={{0,4},{4,0},{8,12},{12,8},{16,20},{20,16},{24,28},{28,24},{32,36},... | collective-permute-start | bytes 199688 | tf_op jit(solution)/shard_map/ppermute | solution.py:19
  36.7 0.4 collective-permute-done.4
  37.1 0.9 collective-permute-done.5
  38.2 5.2 %collective-permute-start.6 = (f32[65,256]{1,0:T(8,128)S(1)}, f32[65,256]{1,0:T(8,128)S(1)}, u32[]{:S(2)}, u32[]{:S(2)}) collective-permute-start(f32[65,256]{1,0:T(8,128)S(1)} %pad_maximum_fusion.7), channel_id=1, source_target_pairs={{0,64},{4,68},{8,72},{12,76},{16,80},{20,84},{24,88},{28,92},{32,9... | collective-permute-start | bytes 199688 | tf_op jit(solution)/shard_map/ppermute | solution.py:19
  43.4 1.9 %collective-permute-start.7 = (f32[65,256]{1,0:T(8,128)S(1)}, f32[65,256]{1,0:T(8,128)S(1)}, u32[]{:S(2)}, u32[]{:S(2)}) collective-permute-start(f32[65,256]{1,0:T(8,128)S(1)} %pad_maximum_fusion.8), channel_id=1, source_target_pairs={{0,8},{4,12},{8,0},{12,4},{16,24},{20,28},{24,16},{28,20},{32,40},... | collective-permute-start | bytes 199688 | tf_op jit(solution)/shard_map/ppermute | solution.py:19
  45.3 1.7 %collective-permute-done.6 = f32[65,256]{1,0:T(8,128)S(1)} collective-permute-done((f32[65,256]{1,0:T(8,128)S(1)}, f32[65,256]{1,0:T(8,128)S(1)}, u32[]{:S(2)}, u32[]{:S(2)}) %collective-permute-start.6) | collective-permute-done | bytes 66592 | tf_op jit(solution)/shard_map/ppermute | solution.py:19
  47.1 2.6 %collective-permute-done.7 = f32[65,256]{1,0:T(8,128)S(1)} collective-permute-done((f32[65,256]{1,0:T(8,128)S(1)}, f32[65,256]{1,0:T(8,128)S(1)}, u32[]{:S(2)}, u32[]{:S(2)}) %collective-permute-start.7) | collective-permute-done | bytes 66592 | tf_op jit(solution)/shard_map/ppermute | solution.py:19
  49.9 9.1 %collective-permute-start.8 = (f32[65,256]{1,0:T(8,128)S(1)}, f32[65,256]{1,0:T(8,128)S(1)}, u32[]{:S(2)}, u32[]{:S(2)}) collective-permute-start(f32[65,256]{1,0:T(8,128)S(1)} %pad_maximum_fusion.9), channel_id=1, source_target_pairs={{0,128},{4,132},{8,136},{12,140},{16,144},{20,148},{24,152},{28,15... | collective-permute-start | bytes 199688 | tf_op jit(solution)/shard_map/ppermute | solution.py:19
  59.0 3.7 %collective-permute-start.9 = (f32[65,256]{1,0:T(8,128)S(1)}, f32[65,256]{1,0:T(8,128)S(1)}, u32[]{:S(2)}, u32[]{:S(2)}) collective-permute-start(f32[65,256]{1,0:T(8,128)S(1)} %pad_maximum_fusion.10), channel_id=1, source_target_pairs={{0,16},{4,20},{8,24},{12,28},{16,0},{20,4},{24,8},{28,12},{32,48},... | collective-permute-start | bytes 199688 | tf_op jit(solution)/shard_map/ppermute | solution.py:19
  62.8 1.7 %collective-permute-done.8 = f32[65,256]{1,0:T(8,128)S(1)} collective-permute-done((f32[65,256]{1,0:T(8,128)S(1)}, f32[65,256]{1,0:T(8,128)S(1)}, u32[]{:S(2)}, u32[]{:S(2)}) %collective-permute-start.8) | collective-permute-done | bytes 66592 | tf_op jit(solution)/shard_map/ppermute | solution.py:19
  64.4 2.3 %collective-permute-done.9 = f32[65,256]{1,0:T(8,128)S(1)} collective-permute-done((f32[65,256]{1,0:T(8,128)S(1)}, f32[65,256]{1,0:T(8,128)S(1)}, u32[]{:S(2)}, u32[]{:S(2)}) %collective-permute-start.9) | collective-permute-done | bytes 66592 | tf_op jit(solution)/shard_map/ppermute | solution.py:19
  67.0 9.9 %collective-permute-start.14 = (f32[65,256]{1,0:T(8,128)S(1)}, f32[65,256]{1,0:T(8,128)S(1)}, u32[]{:S(2)}, u32[]{:S(2)}) collective-permute-start(f32[65,256]{1,0:T(8,128)S(1)} %pad_maximum_fusion.15), channel_id=1, source_target_pairs={{0,256},{4,260},{8,264},{12,268},{16,272},{20,276},{24,280},{28,28... | collective-permute-start | bytes 199688 | tf_op jit(solution)/shard_map/ppermute | solution.py:19
  77.0 1.9 %collective-permute-start.10 = (f32[65,256]{1,0:T(8,128)S(1)}, f32[65,256]{1,0:T(8,128)S(1)}, u32[]{:S(2)}, u32[]{:S(2)}) collective-permute-start(f32[65,256]{1,0:T(8,128)S(1)} %pad_maximum_fusion.11), channel_id=1, source_target_pairs={{0,32},{4,36},{8,40},{12,44},{16,48},{20,52},{24,56},{28,60},{32,0... | collective-permute-start | bytes 199688 | tf_op jit(solution)/shard_map/ppermute | solution.py:19
  78.9 5.3 %collective-permute-done.14 = f32[65,256]{1,0:T(8,128)S(1)} collective-permute-done((f32[65,256]{1,0:T(8,128)S(1)}, f32[65,256]{1,0:T(8,128)S(1)}, u32[]{:S(2)}, u32[]{:S(2)}) %collective-permute-start.14) | collective-permute-done | bytes 66592 | tf_op jit(solution)/shard_map/ppermute | solution.py:19
  84.3 0.2 convolution_bitcast_fusion.12
  84.5 0.3 convolution_bitcast_fusion.7
  84.9 0.2 fusion.60
  85.1 0.2 convolution_bitcast_fusion.13
  85.3 0.3 convolution_bitcast_fusion.6
  85.6 0.2 fusion.78
  85.8 0.2 convolution_bitcast_fusion.14
  86.0 0.3 convolution_bitcast_fusion.5
  86.4 0.2 fusion.96
  86.6 0.2 convolution_bitcast_fusion.15
  86.9 4.2 %collective-permute-start.17 = (f32[4,64,576]{2,1,0:T(8,128)S(1)}, f32[4,64,576]{2,1,0:T(8,128)S(1)}, u32[]{:S(2)}, u32[]{:S(2)}) collective-permute-start(f32[4,64,576]{2,1,0:T(8,128)S(1)} %pad_maximum_fusion), channel_id=1, source_target_pairs={{0,2},{1,3},{2,0},{3,1},{4,6},{5,7},{6,4},{7,5},{8,10},{9,11},{10,... | collective-permute-start | bytes 1769480 | tf_op jit(solution)/shard_map/ppermute | solution.py:44
  91.1 1.9 %collective-permute-start.18 = (f32[4,64,576]{2,1,0:T(8,128)S(1)}, f32[4,64,576]{2,1,0:T(8,128)S(1)}, u32[]{:S(2)}, u32[]{:S(2)}) collective-permute-start(f32[4,64,576]{2,1,0:T(8,128)S(1)} %pad_maximum_fusion), channel_id=1, source_target_pairs={{0,3},{1,2},{2,1},{3,0},{4,7},{5,6},{6,5},{7,4},{8,11},{9,10},{10,... | collective-permute-start | bytes 1769480 | tf_op jit(solution)/shard_map/ppermute | solution.py:44
  93.0 4.3 %collective-permute-start.16 = (f32[4,64,576]{2,1,0:T(8,128)S(1)}, f32[4,64,576]{2,1,0:T(8,128)S(1)}, u32[]{:S(2)}, u32[]{:S(2)}) collective-permute-start(f32[4,64,576]{2,1,0:T(8,128)S(1)} %pad_maximum_fusion), channel_id=1, source_target_pairs={{0,1},{1,0},{2,3},{3,2},{4,5},{5,4},{6,7},{7,6},{8,9},{9,8},{10,11... | collective-permute-start | bytes 1769480 | tf_op jit(solution)/shard_map/ppermute | solution.py:44
  97.3 0.3 convolution_bitcast_fusion.4
  97.7 0.2 fusion.114
  97.9 1.3 collective-permute-start.15
  99.3 1.9 %collective-permute-start.11 = (f32[65,256]{1,0:T(8,128)S(1)}, f32[65,256]{1,0:T(8,128)S(1)}, u32[]{:S(2)}, u32[]{:S(2)}) collective-permute-start(f32[65,256]{1,0:T(8,128)S(1)} %pad_maximum_fusion.12), channel_id=1, source_target_pairs={{0,64},{4,68},{8,72},{12,76},{16,80},{20,84},{24,88},{28,92},{32,9... | collective-permute-start | bytes 199688 | tf_op jit(solution)/shard_map/ppermute | solution.py:19
  101.3 0.2 convolution_bitcast_fusion.8
  101.5 0.3 convolution_bitcast_fusion.3
  101.8 0.2 fusion.132
  102.1 0.2 convolution_bitcast_fusion.9
  102.3 0.3 convolution_bitcast_fusion.2
  102.6 0.2 fusion.150
  102.8 0.2 convolution_bitcast_fusion.10
  103.0 0.3 convolution_bitcast_fusion.1
  103.4 0.2 fusion.168
  103.6 0.2 convolution_bitcast_fusion.11
  103.8 4.9 %collective-permute-done.11 = f32[65,256]{1,0:T(8,128)S(1)} collective-permute-done((f32[65,256]{1,0:T(8,128)S(1)}, f32[65,256]{1,0:T(8,128)S(1)}, u32[]{:S(2)}, u32[]{:S(2)}) %collective-permute-start.11) | collective-permute-done | bytes 66592 | tf_op jit(solution)/shard_map/ppermute | solution.py:19
  108.8 2.4 %collective-permute-start.12 = (f32[65,256]{1,0:T(8,128)S(1)}, f32[65,256]{1,0:T(8,128)S(1)}, u32[]{:S(2)}, u32[]{:S(2)}) collective-permute-start(f32[65,256]{1,0:T(8,128)S(1)} %pad_maximum_fusion.13), channel_id=1, source_target_pairs={{0,128},{4,132},{8,136},{12,140},{16,144},{20,148},{24,152},{28,15... | collective-permute-start | bytes 199688 | tf_op jit(solution)/shard_map/ppermute | solution.py:19
  111.3 3.0 %collective-permute-start.20 = (f32[4,64,576]{2,1,0:T(8,128)S(1)}, f32[4,64,576]{2,1,0:T(8,128)S(1)}, u32[]{:S(2)}, u32[]{:S(2)}) collective-permute-start(f32[4,64,576]{2,1,0:T(8,128)S(1)} %pad_maximum_fusion.1), channel_id=1, source_target_pairs={{0,2},{1,3},{2,0},{3,1},{4,6},{5,7},{6,4},{7,5},{8,10},{9,11},{10,... | collective-permute-start | bytes 1769480 | tf_op jit(solution)/shard_map/ppermute | solution.py:44
  114.3 8.0 %collective-permute-done.12 = f32[65,256]{1,0:T(8,128)S(1)} collective-permute-done((f32[65,256]{1,0:T(8,128)S(1)}, f32[65,256]{1,0:T(8,128)S(1)}, u32[]{:S(2)}, u32[]{:S(2)}) %collective-permute-start.12) | collective-permute-done | bytes 66592 | tf_op jit(solution)/shard_map/ppermute | solution.py:19
  122.4 8.6 %collective-permute-start.13 = (f32[65,256]{1,0:T(8,128)S(1)}, f32[65,256]{1,0:T(8,128)S(1)}, u32[]{:S(2)}, u32[]{:S(2)}) collective-permute-start(f32[65,256]{1,0:T(8,128)S(1)} %pad_maximum_fusion.14), channel_id=1, source_target_pairs={{0,256},{4,260},{8,264},{12,268},{16,272},{20,276},{24,280},{28,28... | collective-permute-start | bytes 199688 | tf_op jit(solution)/shard_map/ppermute | solution.py:19
  131.0 0.3 convolution_bitcast_fusion
  131.3 10.6 %collective-permute-done.13 = f32[65,256]{1,0:T(8,128)S(1)} collective-permute-done((f32[65,256]{1,0:T(8,128)S(1)}, f32[65,256]{1,0:T(8,128)S(1)}, u32[]{:S(2)}, u32[]{:S(2)}) %collective-permute-start.13) | collective-permute-done | bytes 66592 | tf_op jit(solution)/shard_map/ppermute | solution.py:19
  141.9 3.5 %collective-permute-start.21 = (f32[4,64,576]{2,1,0:T(8,128)S(1)}, f32[4,64,576]{2,1,0:T(8,128)S(1)}, u32[]{:S(2)}, u32[]{:S(2)}) collective-permute-start(f32[4,64,576]{2,1,0:T(8,128)S(1)} %pad_maximum_fusion.1), channel_id=1, source_target_pairs={{0,3},{1,2},{2,1},{3,0},{4,7},{5,6},{6,5},{7,4},{8,11},{9,10},{10,... | collective-permute-start | bytes 1769480 | tf_op jit(solution)/shard_map/ppermute | solution.py:44
  145.4 2.6 %collective-permute-start.19 = (f32[4,64,576]{2,1,0:T(8,128)S(1)}, f32[4,64,576]{2,1,0:T(8,128)S(1)}, u32[]{:S(2)}, u32[]{:S(2)}) collective-permute-start(f32[4,64,576]{2,1,0:T(8,128)S(1)} %pad_maximum_fusion.1), channel_id=1, source_target_pairs={{0,1},{1,0},{2,3},{3,2},{4,5},{5,4},{6,7},{7,6},{8,9},{9,8},{10,11... | collective-permute-start | bytes 1769480 | tf_op jit(solution)/shard_map/ppermute | solution.py:44
  148.0 0.8 fusion.206
  148.9 0.7 fusion.49
  149.6 10.7 %collective-permute-done.21 = f32[4,64,576]{2,1,0:T(8,128)S(1)} collective-permute-done((f32[4,64,576]{2,1,0:T(8,128)S(1)}, f32[4,64,576]{2,1,0:T(8,128)S(1)}, u32[]{:S(2)}, u32[]{:S(2)}) %collective-permute-start.21) | collective-permute-done | bytes 589856 | tf_op jit(solution)/shard_map/ppermute | solution.py:44
  160.3 3.2 %collective-permute-done.19 = f32[4,64,576]{2,1,0:T(8,128)S(1)} collective-permute-done((f32[4,64,576]{2,1,0:T(8,128)S(1)}, f32[4,64,576]{2,1,0:T(8,128)S(1)}, u32[]{:S(2)}, u32[]{:S(2)}) %collective-permute-start.19) | collective-permute-done | bytes 589856 | tf_op jit(solution)/shard_map/ppermute | solution.py:44
  163.5 1.1 add_add_fusion
  (175 shorter events, 8.9 us)
Async XLA Ops:
  0.7 1.3 copy-start.1
  1.6 1.0 copy-start
  5.2 2.0 %copy-start.2 = (f32[1,1,64,256]{3,2,1,0:T(8,128)S(1)}, f32[1,1,64,256]{3,2,1,0:T(8,128)}, u32[]{:S(2)}) copy-start(f32[1,1,64,256]{3,2,1,0:T(8,128)} %param.7) | copy-start | bytes 196612
  5.4 1.8 %copy-start.3 = (f32[1,64]{1,0:T(1,128)S(1)}, f32[1,64]{1,0:T(1,128)}, u32[]{:S(2)}) copy-start(f32[1,64]{1,0:T(1,128)} %param.6) | copy-start | bytes 772
  5.5 5.6 %collective-permute-start.3 = (f32[1,64,256]{2,1,0:T(8,128)S(1)}, f32[1,64,256]{2,1,0:T(8,128)S(1)}, u32[]{:S(2)}, u32[]{:S(2)}) collective-permute-start(f32[1,64,256]{2,1,0:T(8,128)S(1)} %fusion.11), channel_id=1, source_target_pairs={{0,4},{4,8},{8,12},{12,16},{16,20},{20,24},{24,28},{28,32},{32,36}... | collective-permute-start | bytes 196616 | tf_op jit(solution)/shard_map/ppermute | solution.py:51
  7.3 7.1 %collective-permute-start = (f32[65,256]{1,0:T(8,128)S(1)}, f32[65,256]{1,0:T(8,128)S(1)}, u32[]{:S(2)}, u32[]{:S(2)}) collective-permute-start(f32[65,256]{1,0:T(8,128)S(1)} %pad_maximum_fusion.2), channel_id=1, source_target_pairs={{0,4},{4,0},{8,12},{12,8},{16,20},{20,16},{24,28},{28,24},{32,36},... | collective-permute-start | bytes 199688 | tf_op jit(solution)/shard_map/ppermute | solution.py:19
  14.6 6.2 %collective-permute-start.1 = (f32[65,256]{1,0:T(8,128)S(1)}, f32[65,256]{1,0:T(8,128)S(1)}, u32[]{:S(2)}, u32[]{:S(2)}) collective-permute-start(f32[65,256]{1,0:T(8,128)S(1)} %pad_maximum_fusion.3), channel_id=1, source_target_pairs={{0,8},{4,12},{8,0},{12,4},{16,24},{20,28},{24,16},{28,20},{32,40},... | collective-permute-start | bytes 199688 | tf_op jit(solution)/shard_map/ppermute | solution.py:19
  21.0 7.8 %collective-permute-start.2 = (f32[65,256]{1,0:T(8,128)S(1)}, f32[65,256]{1,0:T(8,128)S(1)}, u32[]{:S(2)}, u32[]{:S(2)}) collective-permute-start(f32[65,256]{1,0:T(8,128)S(1)} %pad_maximum_fusion.4), channel_id=1, source_target_pairs={{0,16},{4,20},{8,24},{12,28},{16,0},{20,4},{24,8},{28,12},{32,48},... | collective-permute-start | bytes 199688 | tf_op jit(solution)/shard_map/ppermute | solution.py:19
  28.9 8.2 %collective-permute-start.4 = (f32[65,256]{1,0:T(8,128)S(1)}, f32[65,256]{1,0:T(8,128)S(1)}, u32[]{:S(2)}, u32[]{:S(2)}) collective-permute-start(f32[65,256]{1,0:T(8,128)S(1)} %pad_maximum_fusion.5), channel_id=1, source_target_pairs={{0,32},{4,36},{8,40},{12,44},{16,48},{20,52},{24,56},{28,60},{32,0... | collective-permute-start | bytes 199688 | tf_op jit(solution)/shard_map/ppermute | solution.py:19
  34.8 3.2 %collective-permute-start.5 = (f32[65,256]{1,0:T(8,128)S(1)}, f32[65,256]{1,0:T(8,128)S(1)}, u32[]{:S(2)}, u32[]{:S(2)}) collective-permute-start(f32[65,256]{1,0:T(8,128)S(1)} %pad_maximum_fusion.6), channel_id=1, source_target_pairs={{0,4},{4,0},{8,12},{12,8},{16,20},{20,16},{24,28},{28,24},{32,36},... | collective-permute-start | bytes 199688 | tf_op jit(solution)/shard_map/ppermute | solution.py:19
  38.2 8.9 %collective-permute-start.6 = (f32[65,256]{1,0:T(8,128)S(1)}, f32[65,256]{1,0:T(8,128)S(1)}, u32[]{:S(2)}, u32[]{:S(2)}) collective-permute-start(f32[65,256]{1,0:T(8,128)S(1)} %pad_maximum_fusion.7), channel_id=1, source_target_pairs={{0,64},{4,68},{8,72},{12,76},{16,80},{20,84},{24,88},{28,92},{32,9... | collective-permute-start | bytes 199688 | tf_op jit(solution)/shard_map/ppermute | solution.py:19
  43.4 6.2 %collective-permute-start.7 = (f32[65,256]{1,0:T(8,128)S(1)}, f32[65,256]{1,0:T(8,128)S(1)}, u32[]{:S(2)}, u32[]{:S(2)}) collective-permute-start(f32[65,256]{1,0:T(8,128)S(1)} %pad_maximum_fusion.8), channel_id=1, source_target_pairs={{0,8},{4,12},{8,0},{12,4},{16,24},{20,28},{24,16},{28,20},{32,40},... | collective-permute-start | bytes 199688 | tf_op jit(solution)/shard_map/ppermute | solution.py:19
  49.9 14.5 %collective-permute-start.8 = (f32[65,256]{1,0:T(8,128)S(1)}, f32[65,256]{1,0:T(8,128)S(1)}, u32[]{:S(2)}, u32[]{:S(2)}) collective-permute-start(f32[65,256]{1,0:T(8,128)S(1)} %pad_maximum_fusion.9), channel_id=1, source_target_pairs={{0,128},{4,132},{8,136},{12,140},{16,144},{20,148},{24,152},{28,15... | collective-permute-start | bytes 199688 | tf_op jit(solution)/shard_map/ppermute | solution.py:19
  59.0 7.8 %collective-permute-start.9 = (f32[65,256]{1,0:T(8,128)S(1)}, f32[65,256]{1,0:T(8,128)S(1)}, u32[]{:S(2)}, u32[]{:S(2)}) collective-permute-start(f32[65,256]{1,0:T(8,128)S(1)} %pad_maximum_fusion.10), channel_id=1, source_target_pairs={{0,16},{4,20},{8,24},{12,28},{16,0},{20,4},{24,8},{28,12},{32,48},... | collective-permute-start | bytes 199688 | tf_op jit(solution)/shard_map/ppermute | solution.py:19
  67.0 17.2 %collective-permute-start.14 = (f32[65,256]{1,0:T(8,128)S(1)}, f32[65,256]{1,0:T(8,128)S(1)}, u32[]{:S(2)}, u32[]{:S(2)}) collective-permute-start(f32[65,256]{1,0:T(8,128)S(1)} %pad_maximum_fusion.15), channel_id=1, source_target_pairs={{0,256},{4,260},{8,264},{12,268},{16,272},{20,276},{24,280},{28,28... | collective-permute-start | bytes 199688 | tf_op jit(solution)/shard_map/ppermute | solution.py:19
  77.0 20.7 %collective-permute-start.10 = (f32[65,256]{1,0:T(8,128)S(1)}, f32[65,256]{1,0:T(8,128)S(1)}, u32[]{:S(2)}, u32[]{:S(2)}) collective-permute-start(f32[65,256]{1,0:T(8,128)S(1)} %pad_maximum_fusion.11), channel_id=1, source_target_pairs={{0,32},{4,36},{8,40},{12,44},{16,48},{20,52},{24,56},{28,60},{32,0... | collective-permute-start | bytes 199688 | tf_op jit(solution)/shard_map/ppermute | solution.py:19
  86.9 58.5 %collective-permute-start.17 = (f32[4,64,576]{2,1,0:T(8,128)S(1)}, f32[4,64,576]{2,1,0:T(8,128)S(1)}, u32[]{:S(2)}, u32[]{:S(2)}) collective-permute-start(f32[4,64,576]{2,1,0:T(8,128)S(1)} %pad_maximum_fusion), channel_id=1, source_target_pairs={{0,2},{1,3},{2,0},{3,1},{4,6},{5,7},{6,4},{7,5},{8,10},{9,11},{10,... | collective-permute-start | bytes 1769480 | tf_op jit(solution)/shard_map/ppermute | solution.py:44
  91.1 58.5 %collective-permute-start.18 = (f32[4,64,576]{2,1,0:T(8,128)S(1)}, f32[4,64,576]{2,1,0:T(8,128)S(1)}, u32[]{:S(2)}, u32[]{:S(2)}) collective-permute-start(f32[4,64,576]{2,1,0:T(8,128)S(1)} %pad_maximum_fusion), channel_id=1, source_target_pairs={{0,3},{1,2},{2,1},{3,0},{4,7},{5,6},{6,5},{7,4},{8,11},{9,10},{10,... | collective-permute-start | bytes 1769480 | tf_op jit(solution)/shard_map/ppermute | solution.py:44
  93.0 56.6 %collective-permute-start.16 = (f32[4,64,576]{2,1,0:T(8,128)S(1)}, f32[4,64,576]{2,1,0:T(8,128)S(1)}, u32[]{:S(2)}, u32[]{:S(2)}) collective-permute-start(f32[4,64,576]{2,1,0:T(8,128)S(1)} %pad_maximum_fusion), channel_id=1, source_target_pairs={{0,1},{1,0},{2,3},{3,2},{4,5},{5,4},{6,7},{7,6},{8,9},{9,8},{10,11... | collective-permute-start | bytes 1769480 | tf_op jit(solution)/shard_map/ppermute | solution.py:44
  97.9 3.4 %collective-permute-start.15 = (f32[1,64,256]{2,1,0:T(8,128)S(1)}, f32[1,64,256]{2,1,0:T(8,128)S(1)}, u32[]{:S(2)}, u32[]{:S(2)}) collective-permute-start(f32[1,64,256]{2,1,0:T(8,128)S(1)} %fusion.114), channel_id=1, source_target_pairs={{4,0},{8,4},{12,8},{16,12},{20,16},{24,20},{28,24},{32,28},{36,32}... | collective-permute-start | bytes 196616 | tf_op jit(solution)/shard_map/ppermute | solution.py:51
  99.3 9.4 %collective-permute-start.11 = (f32[65,256]{1,0:T(8,128)S(1)}, f32[65,256]{1,0:T(8,128)S(1)}, u32[]{:S(2)}, u32[]{:S(2)}) collective-permute-start(f32[65,256]{1,0:T(8,128)S(1)} %pad_maximum_fusion.12), channel_id=1, source_target_pairs={{0,64},{4,68},{8,72},{12,76},{16,80},{20,84},{24,88},{28,92},{32,9... | collective-permute-start | bytes 199688 | tf_op jit(solution)/shard_map/ppermute | solution.py:19
  108.8 13.4 %collective-permute-start.12 = (f32[65,256]{1,0:T(8,128)S(1)}, f32[65,256]{1,0:T(8,128)S(1)}, u32[]{:S(2)}, u32[]{:S(2)}) collective-permute-start(f32[65,256]{1,0:T(8,128)S(1)} %pad_maximum_fusion.13), channel_id=1, source_target_pairs={{0,128},{4,132},{8,136},{12,140},{16,144},{20,148},{24,152},{28,15... | collective-permute-start | bytes 199688 | tf_op jit(solution)/shard_map/ppermute | solution.py:19
  111.3 38.3 %collective-permute-start.20 = (f32[4,64,576]{2,1,0:T(8,128)S(1)}, f32[4,64,576]{2,1,0:T(8,128)S(1)}, u32[]{:S(2)}, u32[]{:S(2)}) collective-permute-start(f32[4,64,576]{2,1,0:T(8,128)S(1)} %pad_maximum_fusion.1), channel_id=1, source_target_pairs={{0,2},{1,3},{2,0},{3,1},{4,6},{5,7},{6,4},{7,5},{8,10},{9,11},{10,... | collective-permute-start | bytes 1769480 | tf_op jit(solution)/shard_map/ppermute | solution.py:44
  122.4 19.5 %collective-permute-start.13 = (f32[65,256]{1,0:T(8,128)S(1)}, f32[65,256]{1,0:T(8,128)S(1)}, u32[]{:S(2)}, u32[]{:S(2)}) collective-permute-start(f32[65,256]{1,0:T(8,128)S(1)} %pad_maximum_fusion.14), channel_id=1, source_target_pairs={{0,256},{4,260},{8,264},{12,268},{16,272},{20,276},{24,280},{28,28... | collective-permute-start | bytes 199688 | tf_op jit(solution)/shard_map/ppermute | solution.py:19
  141.9 18.4 %collective-permute-start.21 = (f32[4,64,576]{2,1,0:T(8,128)S(1)}, f32[4,64,576]{2,1,0:T(8,128)S(1)}, u32[]{:S(2)}, u32[]{:S(2)}) collective-permute-start(f32[4,64,576]{2,1,0:T(8,128)S(1)} %pad_maximum_fusion.1), channel_id=1, source_target_pairs={{0,3},{1,2},{2,1},{3,0},{4,7},{5,6},{6,5},{7,4},{8,11},{9,10},{10,... | collective-permute-start | bytes 1769480 | tf_op jit(solution)/shard_map/ppermute | solution.py:44
  145.4 18.1 %collective-permute-start.19 = (f32[4,64,576]{2,1,0:T(8,128)S(1)}, f32[4,64,576]{2,1,0:T(8,128)S(1)}, u32[]{:S(2)}, u32[]{:S(2)}) collective-permute-start(f32[4,64,576]{2,1,0:T(8,128)S(1)} %pad_maximum_fusion.1), channel_id=1, source_target_pairs={{0,1},{1,0},{2,3},{3,2},{4,5},{5,4},{6,7},{7,6},{8,9},{9,8},{10,11... | collective-permute-start | bytes 1769480 | tf_op jit(solution)/shard_map/ppermute | solution.py:44

commit v3 on v2

--- a/solution.py
+++ b/solution.py
@@ -17,7 +17,7 @@
 def exchange(gain, state, axis, bit):
     count = lax.axis_size(axis)
     arrived = lax.ppermute(pack(gain, state), axis, [(i, i ^ (1 << bit)) for i in range(count)])
-    rows = state.shape[-2]
+    rows = state.size // state.shape[-1]
     return arrived[rows, : gain.shape[0]], arrived[:rows].reshape(state.shape)
 
 
@@ -37,12 +37,16 @@
     return (part_gain, part_state, whole_gain, whole_state)
 
 
-def dp_sum(terms, axis):
+def gather_images(block, axis):
     count = lax.axis_size(axis)
-    if count != 4:
-        return lax.psum(terms, axis)
-    got = [lax.ppermute(terms, axis, [(i, i ^ k) for i in range(count)]) for k in (1, 2, 3)]
-    return (terms + got[0]) + (got[1] + got[2])
+    got = [lax.ppermute(block, axis, [(i, i ^ k) for i in range(count)]) for k in range(1, count)]
+    return jnp.stack([block] + got)
+
+
+def symmetric_sum(slots):
+    while slots.shape[0] > 1:
+        slots = slots[0::2] + slots[1::2]
+    return slots[0]
 
 
 def passed_along(block, axis, distance):
@@ -97,22 +101,23 @@
         patches = unfold(squashed.astype(jnp.bfloat16), WID)
         scaled = (step_size * upstream).astype(jnp.bfloat16)
         layer_grads[layer] = jnp.einsum(
-            "bop,bkp->ok", scaled, patches, preferred_element_type=jnp.float32
+            "bop,bkp->bok", scaled, patches, preferred_element_type=jnp.float32
         )
         spread = jnp.einsum(
             "ok,bop->bkp", block_weights[layer], scaled, preferred_element_type=jnp.float32
         )
         upstream = upstream + (1.0 - squashed * squashed) * fold_taps(spread, WID)
-    return (upstream, jnp.stack(layer_grads))
+    return (upstream, jnp.stack(layer_grads, axis=1))
 
 
 def body(cpoints, weights, coarse_gain, cotangent):
     step_size = 1.0 / (weights.shape[0] * lax.axis_size("depth"))
     rounds = (lax.axis_size("depth") - 1).bit_length()
     place = lax.axis_index("depth")
-    own_state = cpoints[0]
+    images = gather_images(jnp.stack([cpoints[0, 0], cotangent[0, 0]]), "dp")
+    own_state = images[:, 0]
     rate_vec = coarse_gain[0]
-    cot_here = cotangent[0]
+    cot_here = images[:, 1]
     leading = place == 0
 
     def before(bit):
@@ -146,13 +151,12 @@
             passed_in = reverse[1]
             adjoint_here = cot_here + passed_in
             back_start, start_grads = back_block(start_kept, weights, adjoint_here, step_size)
-            start_sum = dp_sum(start_grads, "dp")
             arriving_bar = passed_along(back_start, "depth", -1)
             relaxed_bar = arriving_bar - passed_in
             back_own, own_grads = back_block(own_kept, weights, relaxed_bar, step_size)
-    corrected = forward[1]
-    grad_cpoints = jnp.where(leading, back_own + back_start, back_own)
-    grad_weights = start_sum + dp_sum(own_grads, "dp")
+    corrected = forward[1][:1]
+    grad_cpoints = jnp.where(leading, back_own[:1] + back_start[:1], back_own[:1])
+    grad_weights = symmetric_sum(start_grads + own_grads)
     return (corrected[None], grad_cpoints[None], grad_weights)
 
 

time: 165 us -> 267 us (1.62)
  the two profiles are of different devices: /device:TPU:8 before, /device:TPU:2 now
where the time goes in v3:
time: 267 us; the launch traced here: 265 us
  waiting for transfers between devices  118 us (44%)
  starting transfers between devices  76.1 us (29%)
  other arithmetic  34.7 us (13%)
  local copies, waits for them, and re-layouts  22.4 us (8%)
  matrix products  11.3 us (4%)
    ppermute x14, waiting for transfers between devices, exchange(): lax.ppermute(pack(gain, state), axis, [(i, i ^ 1 << bit) for i in range(c...  112 us
    ppermute x14, starting transfers between devices, exchange(): lax.ppermute(pack(gain, state), axis, [(i, i ^ 1 << bit) for i in range(c...  62.3 us
    unnamed x84, local copies, waits for them, and re-layouts  11.9 us
    ppermute x3, starting transfers between devices, gather_images(): lax.ppermute(block, axis, [(i, i ^ k) for i in range(count)])  9.99 us
    unnamed x64, other arithmetic  6.08 us
    concatenate x14, other arithmetic, pack(): jnp.concatenate([state.reshape(-1, state.shape[-1]), row[None]], axis=0)  5.78 us
  transfers between devices with their start and end apart: 19, of which 12 were waited for; matrix products, arithmetic and copies ran while one was open for 13% of the time, Pallas kernels for 0%

profile of v3, /device:TPU:2, one launch (start us, length us, event | category | flops | bytes accessed | tf_op | source)
XLA Modules:
  0.0 265.1 jit_solution(8385422861032573503)
XLA Ops:
  0.6 0.9 fusion.283
  1.5 5.1 %collective-permute-start.1 = (f32[2,64,256]{2,1,0:T(8,128)S(1)}, f32[2,64,256]{2,1,0:T(8,128)S(1)}, u32[]{:S(2)}, u32[]{:S(2)}) collective-permute-start(f32[2,64,256]{2,1,0:T(8,128)S(1)} %get-tuple-element.181), channel_id=1, source_target_pairs={{0,2},{1,3},{2,0},{3,1},{4,6},{5,7},{6,4},{7,5},{8,10},{9,11},{10,... | collective-permute-start | bytes 393224 | tf_op jit(solution)/shard_map/ppermute | solution.py:42
  6.6 2.6 collective-permute-start
  9.2 2.3 collective-permute-start.2
  13.5 3.8 %collective-permute-done.2 = f32[2,64,256]{2,1,0:T(8,128)S(1)} collective-permute-done((f32[2,64,256]{2,1,0:T(8,128)S(1)}, f32[2,64,256]{2,1,0:T(8,128)S(1)}, u32[]{:S(2)}, u32[]{:S(2)}) %collective-permute-start.2) | collective-permute-done | bytes 131104 | tf_op jit(solution)/shard_map/ppermute | solution.py:42
  17.5 1.9 collective-permute-start.3
  26.4 1.1 fusion.294
  27.4 0.7 pad_maximum_fusion.2
  28.2 4.8 %collective-permute-start.4 = (f32[257,256]{1,0:T(8,128)}, f32[257,256]{1,0:T(8,128)}, u32[]{:S(2)}, u32[]{:S(2)}) collective-permute-start(f32[257,256]{1,0:T(8,128)} %pad_maximum_fusion.2), channel_id=1, source_target_pairs={{0,8},{4,12},{8,0},{12,4},{16,24},{20,28},{24,16},{28,20},{32,40},... | collective-permute-start | bytes 789512 | tf_op jit(solution)/shard_map/ppermute | solution.py:19
  33.3 7.1 %collective-permute-done.4 = f32[257,256]{1,0:T(8,128)} collective-permute-done((f32[257,256]{1,0:T(8,128)}, f32[257,256]{1,0:T(8,128)}, u32[]{:S(2)}, u32[]{:S(2)}) %collective-permute-start.4) | collective-permute-done | bytes 263200 | tf_op jit(solution)/shard_map/ppermute | solution.py:19
  41.9 1.1 fusion.295
  43.0 2.9 %collective-permute-start.5 = (f32[257,256]{1,0:T(8,128)S(1)}, f32[257,256]{1,0:T(8,128)S(1)}, u32[]{:S(2)}, u32[]{:S(2)}) collective-permute-start(f32[257,256]{1,0:T(8,128)S(1)} %pad_maximum_fusion.3), channel_id=1, source_target_pairs={{0,16},{4,20},{8,24},{12,28},{16,0},{20,4},{24,8},{28,12},{32,48},... | collective-permute-start | bytes 789512 | tf_op jit(solution)/shard_map/ppermute | solution.py:19
  46.2 1.9 collective-permute-start.6
  48.1 6.5 %collective-permute-done.5 = f32[257,256]{1,0:T(8,128)S(1)} collective-permute-done((f32[257,256]{1,0:T(8,128)S(1)}, f32[257,256]{1,0:T(8,128)S(1)}, u32[]{:S(2)}, u32[]{:S(2)}) %collective-permute-start.5) | collective-permute-done | bytes 263200 | tf_op jit(solution)/shard_map/ppermute | solution.py:19
  54.7 0.7 broadcast_select_fusion.8
  55.4 0.7 collective-permute-done.6
  56.1 1.1 tanh_convert_fusion.3
  63.5 1.0 fusion.2
  64.6 0.7 pad_maximum_fusion.4
  65.3 3.9 %collective-permute-start.7 = (f32[257,256]{1,0:T(8,128)}, f32[257,256]{1,0:T(8,128)}, u32[]{:S(2)}, u32[]{:S(2)}) collective-permute-start(f32[257,256]{1,0:T(8,128)} %pad_maximum_fusion.4), channel_id=1, source_target_pairs={{0,32},{4,36},{8,40},{12,44},{16,48},{20,52},{24,56},{28,60},{32,0... | collective-permute-start | bytes 789512 | tf_op jit(solution)/shard_map/ppermute | solution.py:19
  69.2 1.0 pad_maximum_fusion.5
  70.2 1.9 collective-permute-start.8
  72.1 3.0 %collective-permute-done.7 = f32[257,256]{1,0:T(8,128)} collective-permute-done((f32[257,256]{1,0:T(8,128)}, f32[257,256]{1,0:T(8,128)}, u32[]{:S(2)}, u32[]{:S(2)}) %collective-permute-start.7) | collective-permute-done | bytes 263200 | tf_op jit(solution)/shard_map/ppermute | solution.py:19
  75.8 1.0 slice.1068
  76.9 0.8 add_select_fusion.18
  77.7 0.8 add_select_fusion.17
  79.3 0.7 pad_maximum_fusion.6
  80.0 5.2 %collective-permute-start.9 = (f32[257,256]{1,0:T(8,128)}, f32[257,256]{1,0:T(8,128)}, u32[]{:S(2)}, u32[]{:S(2)}) collective-permute-start(f32[257,256]{1,0:T(8,128)} %pad_maximum_fusion.6), channel_id=1, source_target_pairs={{0,64},{4,68},{8,72},{12,76},{16,80},{20,84},{24,88},{28,92},{32,9... | collective-permute-start | bytes 789512 | tf_op jit(solution)/shard_map/ppermute | solution.py:19
  85.3 2.6 collective-permute-start.10
  87.9 8.3 %collective-permute-done.9 = f32[257,256]{1,0:T(8,128)} collective-permute-done((f32[257,256]{1,0:T(8,128)}, f32[257,256]{1,0:T(8,128)}, u32[]{:S(2)}, u32[]{:S(2)}) %collective-permute-start.9) | collective-permute-done | bytes 263200 | tf_op jit(solution)/shard_map/ppermute | solution.py:19
  96.9 1.0 slice.1072
  98.0 0.8 add_select_fusion.16
  98.9 0.9 add_select_fusion.15
  99.8 0.7 fusion.276
  100.5 0.7 pad_maximum_fusion.8
  101.2 9.1 %collective-permute-start.11 = (f32[257,256]{1,0:T(8,128)}, f32[257,256]{1,0:T(8,128)}, u32[]{:S(2)}, u32[]{:S(2)}) collective-permute-start(f32[257,256]{1,0:T(8,128)} %pad_maximum_fusion.8), channel_id=1, source_target_pairs={{0,128},{4,132},{8,136},{12,140},{16,144},{20,148},{24,152},{28,15... | collective-permute-start | bytes 789512 | tf_op jit(solution)/shard_map/ppermute | solution.py:19
  110.4 1.0 pad_maximum_fusion.9
  111.4 5.1 %collective-permute-start.12 = (f32[257,256]{1,0:T(8,128)S(1)}, f32[257,256]{1,0:T(8,128)S(1)}, u32[]{:S(2)}, u32[]{:S(2)}) collective-permute-start(f32[257,256]{1,0:T(8,128)S(1)} %pad_maximum_fusion.9), channel_id=1, source_target_pairs={{0,16},{4,20},{8,24},{12,28},{16,0},{20,4},{24,8},{28,12},{32,48},... | collective-permute-start | bytes 789512 | tf_op jit(solution)/shard_map/ppermute | solution.py:19
  116.5 16.1 %collective-permute-done.11 = f32[257,256]{1,0:T(8,128)} collective-permute-done((f32[257,256]{1,0:T(8,128)}, f32[257,256]{1,0:T(8,128)}, u32[]{:S(2)}, u32[]{:S(2)}) %collective-permute-start.11) | collective-permute-done | bytes 263200 | tf_op jit(solution)/shard_map/ppermute | solution.py:19
  133.3 1.0 slice.1076
  134.3 0.8 add_select_fusion.14
  135.2 0.8 add_select_fusion.13
  136.7 0.7 pad_maximum_fusion.14
  137.4 13.3 %collective-permute-start.17 = (f32[257,256]{1,0:T(8,128)}, f32[257,256]{1,0:T(8,128)}, u32[]{:S(2)}, u32[]{:S(2)}) collective-permute-start(f32[257,256]{1,0:T(8,128)} %pad_maximum_fusion.14), channel_id=1, source_target_pairs={{0,256},{4,260},{8,264},{12,268},{16,272},{20,276},{24,280},{28,28... | collective-permute-start | bytes 789512 | tf_op jit(solution)/shard_map/ppermute | solution.py:19
  150.8 2.2 collective-permute-start.13
  153.0 20.0 %collective-permute-done.17 = f32[257,256]{1,0:T(8,128)} collective-permute-done((f32[257,256]{1,0:T(8,128)}, f32[257,256]{1,0:T(8,128)}, u32[]{:S(2)}, u32[]{:S(2)}) %collective-permute-start.17) | collective-permute-done | bytes 263200 | tf_op jit(solution)/shard_map/ppermute | solution.py:19
  173.0 1.0 slice.1090
  175.4 0.7 copy-done.32
  178.6 0.7 copy-done.30
  181.8 0.7 copy-done.28
  183.9 0.7 copy-done.14
  185.3 1.9 collective-permute-start.18
  187.4 2.1 collective-permute-start.14
  190.0 1.1 collective-permute-done.18
  192.3 0.8 copy-done.22
  195.5 0.7 copy-done.26
  198.7 0.7 copy-done.24
  203.3 1.9 collective-permute-start.15
  205.4 0.9 fusion.17
  206.3 27.9 %collective-permute-done.15 = f32[257,256]{1,0:T(8,128)S(1)} collective-permute-done((f32[257,256]{1,0:T(8,128)S(1)}, f32[257,256]{1,0:T(8,128)S(1)}, u32[]{:S(2)}, u32[]{:S(2)}) %collective-permute-start.15) | collective-permute-done | bytes 263200 | tf_op jit(solution)/shard_map/ppermute | solution.py:19
  234.4 5.4 %collective-permute-start.16 = (f32[257,256]{1,0:T(8,128)S(1)}, f32[257,256]{1,0:T(8,128)S(1)}, u32[]{:S(2)}, u32[]{:S(2)}) collective-permute-start(f32[257,256]{1,0:T(8,128)S(1)} %pad_maximum_fusion.13), channel_id=1, source_target_pairs={{0,256},{4,260},{8,264},{12,268},{16,272},{20,276},{24,280},{28,28... | collective-permute-start | bytes 789512 | tf_op jit(solution)/shard_map/ppermute | solution.py:19
  239.8 1.5 fusion.236
  241.4 22.9 %collective-permute-done.16 = f32[257,256]{1,0:T(8,128)S(1)} collective-permute-done((f32[257,256]{1,0:T(8,128)S(1)}, f32[257,256]{1,0:T(8,128)S(1)}, u32[]{:S(2)}, u32[]{:S(2)}) %collective-permute-start.16) | collective-permute-done | bytes 263200 | tf_op jit(solution)/shard_map/ppermute | solution.py:19
  264.4 0.7 fusion.235
  (273 shorter events, 39.4 us)
Async XLA Ops:
  1.5 11.5 %collective-permute-start.1 = (f32[2,64,256]{2,1,0:T(8,128)S(1)}, f32[2,64,256]{2,1,0:T(8,128)S(1)}, u32[]{:S(2)}, u32[]{:S(2)}) collective-permute-start(f32[2,64,256]{2,1,0:T(8,128)S(1)} %get-tuple-element.181), channel_id=1, source_target_pairs={{0,2},{1,3},{2,0},{3,1},{4,6},{5,7},{6,4},{7,5},{8,10},{9,11},{10,... | collective-permute-start | bytes 393224 | tf_op jit(solution)/shard_map/ppermute | solution.py:42
  6.6 6.9 %collective-permute-start = (f32[2,64,256]{2,1,0:T(8,128)S(1)}, f32[2,64,256]{2,1,0:T(8,128)S(1)}, u32[]{:S(2)}, u32[]{:S(2)}) collective-permute-start(f32[2,64,256]{2,1,0:T(8,128)S(1)} %get-tuple-element.181), channel_id=1, source_target_pairs={{0,1},{1,0},{2,3},{3,2},{4,5},{5,4},{6,7},{7,6},{8,9},{9,8},{10,11... | collective-permute-start | bytes 393224 | tf_op jit(solution)/shard_map/ppermute | solution.py:42
  9.2 8.1 %collective-permute-start.2 = (f32[2,64,256]{2,1,0:T(8,128)S(1)}, f32[2,64,256]{2,1,0:T(8,128)S(1)}, u32[]{:S(2)}, u32[]{:S(2)}) collective-permute-start(f32[2,64,256]{2,1,0:T(8,128)S(1)} %get-tuple-element.181), channel_id=1, source_target_pairs={{0,3},{1,2},{2,1},{3,0},{4,7},{5,6},{6,5},{7,4},{8,11},{9,10},{10,... | collective-permute-start | bytes 393224 | tf_op jit(solution)/shard_map/ppermute | solution.py:42
  17.5 8.0 %collective-permute-start.3 = (f32[257,256]{1,0:T(8,128)S(1)}, f32[257,256]{1,0:T(8,128)S(1)}, u32[]{:S(2)}, u32[]{:S(2)}) collective-permute-start(f32[257,256]{1,0:T(8,128)S(1)} %pad_maximum_fusion.1), channel_id=1, source_target_pairs={{0,4},{4,0},{8,12},{12,8},{16,20},{20,16},{24,28},{28,24},{32,36},... | collective-permute-start | bytes 789512 | tf_op jit(solution)/shard_map/ppermute | solution.py:19
  19.6 1.0 copy-start.12
  20.6 1.0 copy-start
  20.9 1.4 copy-start.23
  22.3 1.0 copy-start.2
  22.7 1.4 copy-start.25
  24.0 1.0 copy-start.4
  24.4 21.5 %copy-start.21 = (f32[4,64,256]{2,1,0:T(8,128)}, f32[4,64,256]{2,1,0:T(8,128)S(1)}, u32[]{:S(2)}) copy-start(f32[4,64,256]{2,1,0:T(8,128)S(1)} %get-tuple-element.187) | copy-start | bytes 786436
  24.4 1.1 copy-start.41
  25.6 0.7 copy-start.40
  28.2 12.3 %collective-permute-start.4 = (f32[257,256]{1,0:T(8,128)}, f32[257,256]{1,0:T(8,128)}, u32[]{:S(2)}, u32[]{:S(2)}) collective-permute-start(f32[257,256]{1,0:T(8,128)} %pad_maximum_fusion.2), channel_id=1, source_target_pairs={{0,8},{4,12},{8,0},{12,4},{16,24},{20,28},{24,16},{28,20},{32,40},... | collective-permute-start | bytes 789512 | tf_op jit(solution)/shard_map/ppermute | solution.py:19
  43.0 11.7 %collective-permute-start.5 = (f32[257,256]{1,0:T(8,128)S(1)}, f32[257,256]{1,0:T(8,128)S(1)}, u32[]{:S(2)}, u32[]{:S(2)}) collective-permute-start(f32[257,256]{1,0:T(8,128)S(1)} %pad_maximum_fusion.3), channel_id=1, source_target_pairs={{0,16},{4,20},{8,24},{12,28},{16,0},{20,4},{24,8},{28,12},{32,48},... | collective-permute-start | bytes 789512 | tf_op jit(solution)/shard_map/ppermute | solution.py:19
  46.2 9.9 %collective-permute-start.6 = (f32[4,64,256]{2,1,0:T(8,128)S(1)}, f32[4,64,256]{2,1,0:T(8,128)S(1)}, u32[]{:S(2)}, u32[]{:S(2)}) collective-permute-start(f32[4,64,256]{2,1,0:T(8,128)S(1)} %fusion.10), channel_id=1, source_target_pairs={{0,4},{4,8},{8,12},{12,16},{16,20},{20,24},{24,28},{28,32},{32,36}... | collective-permute-start | bytes 786440 | tf_op jit(solution)/shard_map/ppermute | solution.py:55
  57.3 6.2 %copy-start.13 = (f32[4,64,256]{2,1,0:T(8,128)}, f32[4,64,256]{2,1,0:T(8,128)S(1)}, u32[]{:S(2)}) copy-start(f32[4,64,256]{2,1,0:T(8,128)S(1)} %get-tuple-element.73) | copy-start | bytes 786436
  58.2 1.1 copy-start.6
  58.6 1.4 copy-start.27
  60.0 1.0 copy-start.8
  60.4 1.4 copy-start.29
  61.7 1.1 copy-start.10
  62.1 1.4 copy-start.31
  65.3 9.9 %collective-permute-start.7 = (f32[257,256]{1,0:T(8,128)}, f32[257,256]{1,0:T(8,128)}, u32[]{:S(2)}, u32[]{:S(2)}) collective-permute-start(f32[257,256]{1,0:T(8,128)} %pad_maximum_fusion.4), channel_id=1, source_target_pairs={{0,32},{4,36},{8,40},{12,44},{16,48},{20,52},{24,56},{28,60},{32,0... | collective-permute-start | bytes 789512 | tf_op jit(solution)/shard_map/ppermute | solution.py:19
  69.2 7.7 %copy-start.34 = (f32[4,64,256]{2,1,0:T(8,128)S(1)}, f32[4,64,256]{2,1,0:T(8,128)}, u32[]{:S(2)}) copy-start(f32[4,64,256]{2,1,0:T(8,128)} %get-tuple-element.38) | copy-start | bytes 786436
  70.2 7.5 %collective-permute-start.8 = (f32[257,256]{1,0:T(8,128)S(1)}, f32[257,256]{1,0:T(8,128)S(1)}, u32[]{:S(2)}, u32[]{:S(2)}) collective-permute-start(f32[257,256]{1,0:T(8,128)S(1)} %pad_maximum_fusion.5), channel_id=1, source_target_pairs={{0,4},{4,0},{8,12},{12,8},{16,20},{20,16},{24,28},{28,24},{32,36},... | collective-permute-start | bytes 789512 | tf_op jit(solution)/shard_map/ppermute | solution.py:19
  75.8 1.9 copy-start.20
  77.7 1.6 copy-start.16
  78.6 19.4 %copy-start.18 = (f32[4,64,256]{2,1,0:T(8,128)}, f32[4,64,256]{2,1,0:T(8,128)S(1)}, u32[]{:S(2)}) copy-start(f32[4,64,256]{2,1,0:T(8,128)S(1)} %get-tuple-element.48) | copy-start | bytes 786436
  80.0 16.2 %collective-permute-start.9 = (f32[257,256]{1,0:T(8,128)}, f32[257,256]{1,0:T(8,128)}, u32[]{:S(2)}, u32[]{:S(2)}) collective-permute-start(f32[257,256]{1,0:T(8,128)} %pad_maximum_fusion.6), channel_id=1, source_target_pairs={{0,64},{4,68},{8,72},{12,76},{16,80},{20,84},{24,88},{28,92},{32,9... | collective-permute-start | bytes 789512 | tf_op jit(solution)/shard_map/ppermute | solution.py:19
  85.2 12.7 %copy-start.17 = (f32[4,64,256]{2,1,0:T(8,128)S(1)}, f32[4,64,256]{2,1,0:T(8,128)}, u32[]{:S(2)}) copy-start(f32[4,64,256]{2,1,0:T(8,128)} %copy-done.16) | copy-start | bytes 786436
  85.2 12.7 %copy-start.37 = (f32[4,64,256]{2,1,0:T(8,128)S(1)}, f32[4,64,256]{2,1,0:T(8,128)}, u32[]{:S(2)}) copy-start(f32[4,64,256]{2,1,0:T(8,128)} %get-tuple-element.46) | copy-start | bytes 786436
  85.3 13.5 %collective-permute-start.10 = (f32[257,256]{1,0:T(8,128)S(1)}, f32[257,256]{1,0:T(8,128)S(1)}, u32[]{:S(2)}, u32[]{:S(2)}) collective-permute-start(f32[257,256]{1,0:T(8,128)S(1)} %pad_maximum_fusion.7), channel_id=1, source_target_pairs={{0,8},{4,12},{8,0},{12,4},{16,24},{20,28},{24,16},{28,20},{32,40},... | collective-permute-start | bytes 789512 | tf_op jit(solution)/shard_map/ppermute | solution.py:19
  96.9 1.9 copy-start.39
  97.9 1.0 copy-start.19
  101.2 31.4 %collective-permute-start.11 = (f32[257,256]{1,0:T(8,128)}, f32[257,256]{1,0:T(8,128)}, u32[]{:S(2)}, u32[]{:S(2)}) collective-permute-start(f32[257,256]{1,0:T(8,128)} %pad_maximum_fusion.8), channel_id=1, source_target_pairs={{0,128},{4,132},{8,136},{12,140},{16,144},{20,148},{24,152},{28,15... | collective-permute-start | bytes 789512 | tf_op jit(solution)/shard_map/ppermute | solution.py:19
  110.4 24.0 %copy-start.35 = (f32[4,64,256]{2,1,0:T(8,128)S(1)}, f32[4,64,256]{2,1,0:T(8,128)}, u32[]{:S(2)}) copy-start(f32[4,64,256]{2,1,0:T(8,128)} %get-tuple-element.54) | copy-start | bytes 786436
  111.4 23.7 %collective-permute-start.12 = (f32[257,256]{1,0:T(8,128)S(1)}, f32[257,256]{1,0:T(8,128)S(1)}, u32[]{:S(2)}, u32[]{:S(2)}) collective-permute-start(f32[257,256]{1,0:T(8,128)S(1)} %pad_maximum_fusion.9), channel_id=1, source_target_pairs={{0,16},{4,20},{8,24},{12,28},{16,0},{20,4},{24,8},{28,12},{32,48},... | collective-permute-start | bytes 789512 | tf_op jit(solution)/shard_map/ppermute | solution.py:19
  133.3 1.9 copy-start.15
  133.3 1.9 copy-start.36
  137.4 35.6 %collective-permute-start.17 = (f32[257,256]{1,0:T(8,128)}, f32[257,256]{1,0:T(8,128)}, u32[]{:S(2)}, u32[]{:S(2)}) collective-permute-start(f32[257,256]{1,0:T(8,128)} %pad_maximum_fusion.14), channel_id=1, source_target_pairs={{0,256},{4,260},{8,264},{12,268},{16,272},{20,276},{24,280},{28,28... | collective-permute-start | bytes 789512 | tf_op jit(solution)/shard_map/ppermute | solution.py:19
  150.7 23.3 %copy-start.38 = (f32[4,64,256]{2,1,0:T(8,128)S(1)}, f32[4,64,256]{2,1,0:T(8,128)}, u32[]{:S(2)}) copy-start(f32[4,64,256]{2,1,0:T(8,128)} %get-tuple-element.63) | copy-start | bytes 786436
  150.8 30.8 %collective-permute-start.13 = (f32[257,256]{1,0:T(8,128)S(1)}, f32[257,256]{1,0:T(8,128)S(1)}, u32[]{:S(2)}, u32[]{:S(2)}) collective-permute-start(f32[257,256]{1,0:T(8,128)S(1)} %pad_maximum_fusion.10), channel_id=1, source_target_pairs={{0,32},{4,36},{8,40},{12,44},{16,48},{20,52},{24,56},{28,60},{32,0... | collective-permute-start | bytes 789512 | tf_op jit(solution)/shard_map/ppermute | solution.py:19
  175.1 1.0 copy-start.32
  176.1 1.3 copy-start.11
  178.3 1.0 copy-start.30
  179.3 1.3 copy-start.9
  181.6 1.0 copy-start.28
  183.7 1.0 copy-start.14
  184.6 2.6 copy-start.33
  185.3 5.8 %collective-permute-start.18 = (f32[4,64,256]{2,1,0:T(8,128)S(1)}, f32[4,64,256]{2,1,0:T(8,128)S(1)}, u32[]{:S(2)}, u32[]{:S(2)}) collective-permute-start(f32[4,64,256]{2,1,0:T(8,128)S(1)} %fusion.82), channel_id=1, source_target_pairs={{4,0},{8,4},{12,8},{16,12},{20,16},{24,20},{28,24},{32,28},{36,32}... | collective-permute-start | bytes 786440 | tf_op jit(solution)/shard_map/ppermute | solution.py:55
  187.2 2.3 copy-start.7
  187.4 15.7 %collective-permute-start.14 = (f32[257,256]{1,0:T(8,128)S(1)}, f32[257,256]{1,0:T(8,128)S(1)}, u32[]{:S(2)}, u32[]{:S(2)}) collective-permute-start(f32[257,256]{1,0:T(8,128)S(1)} %pad_maximum_fusion.11), channel_id=1, source_target_pairs={{0,64},{4,68},{8,72},{12,76},{16,80},{20,84},{24,88},{28,92},{32,9... | collective-permute-start | bytes 789512 | tf_op jit(solution)/shard_map/ppermute | solution.py:19
  192.1 1.0 copy-start.22
  193.0 1.3 copy-start.5
  195.3 1.0 copy-start.26
  196.2 1.3 copy-start.3
  198.5 1.0 copy-start.24
  199.4 1.3 copy-start.1
  203.3 30.9 %collective-permute-start.15 = (f32[257,256]{1,0:T(8,128)S(1)}, f32[257,256]{1,0:T(8,128)S(1)}, u32[]{:S(2)}, u32[]{:S(2)}) collective-permute-start(f32[257,256]{1,0:T(8,128)S(1)} %pad_maximum_fusion.12), channel_id=1, source_target_pairs={{0,128},{4,132},{8,136},{12,140},{16,144},{20,148},{24,152},{28,15... | collective-permute-start | bytes 789512 | tf_op jit(solution)/shard_map/ppermute | solution.py:19
  234.4 29.9 %collective-permute-start.16 = (f32[257,256]{1,0:T(8,128)S(1)}, f32[257,256]{1,0:T(8,128)S(1)}, u32[]{:S(2)}, u32[]{:S(2)}) collective-permute-start(f32[257,256]{1,0:T(8,128)S(1)} %pad_maximum_fusion.13), channel_id=1, source_target_pairs={{0,256},{4,260},{8,264},{12,268},{16,272},{20,276},{24,280},{28,28... | collective-permute-start | bytes 789512 | tf_op jit(solution)/shard_map/ppermute | solution.py:19

commit v4 on v2

--- a/solution.py
+++ b/solution.py
@@ -9,16 +9,21 @@
 TAP_OFFSETS = [(-1, -1), (-1, 0), (-1, 1), (0, -1), (0, 0), (0, 1), (1, -1), (1, 0), (1, 1)]
 
 
-def pack(gain, state):
-    row = jnp.pad(gain, (0, state.shape[-1] - gain.shape[0]))
-    return jnp.concatenate([state.reshape(-1, state.shape[-1]), row[None]], axis=0)
+def pack(gains, states):
+    width = states.shape[-1]
+    rows = [jnp.pad(g, (0, width - g.shape[0]))[None] for g in gains]
+    return jnp.concatenate([states.reshape(-1, width)] + rows, axis=0)
 
 
-def exchange(gain, state, axis, bit):
+def exchange(gains, states, axis, bit):
     count = lax.axis_size(axis)
-    arrived = lax.ppermute(pack(gain, state), axis, [(i, i ^ (1 << bit)) for i in range(count)])
-    rows = state.shape[-2]
-    return arrived[rows, : gain.shape[0]], arrived[:rows].reshape(state.shape)
+    arrived = lax.ppermute(pack(gains, states), axis, [(i, i ^ (1 << bit)) for i in range(count)])
+    rows = states.size // states.shape[-1]
+    each = states.shape[1:]
+    got = arrived[:rows].reshape(states.shape)
+    return tuple(
+        (arrived[rows + k, : g.shape[0]], got[k].reshape(each)) for k, g in enumerate(gains)
+    )
 
 
 def scan_round(scan, arrived, partner_first, bit, last):
@@ -121,10 +126,6 @@
     def after(bit):
         return (place >> bit) % 2 == 0
 
-    reverse = (jnp.ones_like(rate_vec), jnp.zeros_like(cot_here), rate_vec, rate_vec[None, :, None] * cot_here)
-    lag = min(3, rounds - 1)
-    for bit in range(lag):
-        reverse = scan_round(reverse, exchange(reverse[2], reverse[3], "depth", bit), after, bit, bit == rounds - 1)
     relaxed, own_kept = run_block(own_state, weights, step_size)
     arriving = passed_along(relaxed, "depth", 1)
     start_state = jnp.where(leading, own_state, arriving)
@@ -132,27 +133,22 @@
     gained_start = rate_vec[None, :, None] * start_state
     offset = propagated - jnp.where(leading, jnp.zeros_like(gained_start), gained_start)
     forward = (rate_vec, offset, rate_vec, offset)
+    reverse = (jnp.ones_like(rate_vec), jnp.zeros_like(cot_here), rate_vec, rate_vec[None, :, None] * cot_here)
     for bit in range(rounds):
-        rbit = bit + lag
-        if rbit < rounds:
-            reverse, forward = lax.optimization_barrier((reverse, forward))
-            got_r = exchange(reverse[2], reverse[3], "depth", rbit)
-            got_f = exchange(forward[2], forward[3], "depth", bit)
-            reverse = scan_round(reverse, got_r, after, rbit, rbit == rounds - 1)
-        else:
-            got_f = exchange(forward[2], forward[3], "depth", bit)
+        got_f, got_r = exchange(
+            (forward[2], reverse[2]), jnp.stack([forward[3], reverse[3]]), "depth", bit
+        )
         forward = scan_round(forward, got_f, before, bit, bit == rounds - 1)
-        if rbit == rounds - 1:
-            passed_in = reverse[1]
-            adjoint_here = cot_here + passed_in
-            back_start, start_grads = back_block(start_kept, weights, adjoint_here, step_size)
-            start_sum = dp_sum(start_grads, "dp")
-            arriving_bar = passed_along(back_start, "depth", -1)
-            relaxed_bar = arriving_bar - passed_in
-            back_own, own_grads = back_block(own_kept, weights, relaxed_bar, step_size)
+        reverse = scan_round(reverse, got_r, after, bit, bit == rounds - 1)
+    passed_in = reverse[1]
+    adjoint_here = cot_here + passed_in
+    back_start, start_grads = back_block(start_kept, weights, adjoint_here, step_size)
+    arriving_bar = passed_along(back_start, "depth", -1)
+    relaxed_bar = arriving_bar - passed_in
+    back_own, own_grads = back_block(own_kept, weights, relaxed_bar, step_size)
     corrected = forward[1]
     grad_cpoints = jnp.where(leading, back_own + back_start, back_own)
-    grad_weights = start_sum + dp_sum(own_grads, "dp")
+    grad_weights = dp_sum(start_grads + own_grads, "dp")
     return (corrected[None], grad_cpoints[None], grad_weights)
 
 

time: 165 us -> 163 us (0.988)
  the two profiles are of different devices: /device:TPU:8 before, /device:TPU:2 now
where the time goes in v4:
time: 163 us; the launch traced here: 162 us
  waiting for transfers between devices  68.6 us (42%)
  starting transfers between devices  54.2 us (33%)
  other arithmetic  24.6 us (15%)
  local copies, waits for them, and re-layouts  6.9 us (4%)
  matrix products  5.47 us (3%)
  between operations  1.79 us (1%)
    ppermute x7, waiting for transfers between devices, exchange(): lax.ppermute(pack(gains, states), axis, [(i, i ^ 1 << bit) for i in range...  41.2 us
    ppermute x7, starting transfers between devices, exchange(): lax.ppermute(pack(gains, states), axis, [(i, i ^ 1 << bit) for i in range...  40.3 us
    ppermute x3, waiting for transfers between devices, dp_sum(): lax.ppermute(terms, axis, [(i, i ^ k) for i in range(count)])  23.8 us
    ppermute x3, starting transfers between devices, dp_sum(): lax.ppermute(terms, axis, [(i, i ^ k) for i in range(count)])  9.99 us
    unnamed x64, other arithmetic  4.68 us
    unnamed x34, local copies, waits for them, and re-layouts  4.25 us
    another operation x14, other arithmetic, body(): jnp.stack([forward[3], reverse[3]])  4.14 us
    ppermute x2, starting transfers between devices, passed_along(): return lax.ppermute(block, axis, route)  3.84 us
  transfers between devices with their start and end apart: 12, of which 10 were waited for; matrix products, arithmetic and copies ran while one was open for 2% of the time, Pallas kernels for 0%

profile of v4, /device:TPU:2, one launch (start us, length us, event | category | flops | bytes accessed | tf_op | source)
XLA Modules:
  0.0 161.6 jit_solution(8633468709169689757)
XLA Ops:
  0.7 0.9 fusion.202
  2.3 0.3 copy-done
  5.5 1.9 %collective-permute-start = (f32[1,64,256]{2,1,0:T(8,128)S(1)}, f32[1,64,256]{2,1,0:T(8,128)S(1)}, u32[]{:S(2)}, u32[]{:S(2)}) collective-permute-start(f32[1,64,256]{2,1,0:T(8,128)S(1)} %fusion.11), channel_id=1, source_target_pairs={{0,4},{4,8},{8,12},{12,16},{16,20},{20,24},{24,28},{28,32},{32,36}... | collective-permute-start | bytes 196616 | tf_op jit(solution)/shard_map/ppermute | solution.py:56
  7.6 3.5 %collective-permute-done = f32[1,64,256]{2,1,0:T(8,128)S(1)} collective-permute-done((f32[1,64,256]{2,1,0:T(8,128)S(1)}, f32[1,64,256]{2,1,0:T(8,128)S(1)}, u32[]{:S(2)}, u32[]{:S(2)}) %collective-permute-start) | collective-permute-done | bytes 65568 | tf_op jit(solution)/shard_map/ppermute | solution.py:56
  14.8 1.9 %collective-permute-start.1 = (f32[130,256]{1,0:T(8,128)S(1)}, f32[130,256]{1,0:T(8,128)S(1)}, u32[]{:S(2)}, u32[]{:S(2)}) collective-permute-start(f32[130,256]{1,0:T(8,128)S(1)} %pad_maximum_fusion), channel_id=1, source_target_pairs={{0,4},{4,0},{8,12},{12,8},{16,20},{20,16},{24,28},{28,24},{32,36},... | collective-permute-start | bytes 399368 | tf_op jit(solution)/shard_map/ppermute | solution.py:20
  16.7 1.3 collective-permute-done.1
  18.3 4.4 %collective-permute-start.2 = (f32[130,256]{1,0:T(8,128)S(1)}, f32[130,256]{1,0:T(8,128)S(1)}, u32[]{:S(2)}, u32[]{:S(2)}) collective-permute-start(f32[130,256]{1,0:T(8,128)S(1)} %pad_maximum_fusion.1), channel_id=1, source_target_pairs={{0,8},{4,12},{8,0},{12,4},{16,24},{20,28},{24,16},{28,20},{32,40},... | collective-permute-start | bytes 399368 | tf_op jit(solution)/shard_map/ppermute | solution.py:20
  22.7 4.2 %collective-permute-done.2 = f32[130,256]{1,0:T(8,128)S(1)} collective-permute-done((f32[130,256]{1,0:T(8,128)S(1)}, f32[130,256]{1,0:T(8,128)S(1)}, u32[]{:S(2)}, u32[]{:S(2)}) %collective-permute-start.2) | collective-permute-done | bytes 133152 | tf_op jit(solution)/shard_map/ppermute | solution.py:20
  27.2 0.7 pad_maximum_fusion.2
  27.8 3.0 %collective-permute-start.3 = (f32[130,256]{1,0:T(8,128)}, f32[130,256]{1,0:T(8,128)S(1)}, u32[]{:S(2)}, u32[]{:S(2)}) collective-permute-start(f32[130,256]{1,0:T(8,128)} %pad_maximum_fusion.2), channel_id=1, source_target_pairs={{0,16},{4,20},{8,24},{12,28},{16,0},{20,4},{24,8},{28,12},{32,48},... | collective-permute-start | bytes 399368 | tf_op jit(solution)/shard_map/ppermute | solution.py:20
  30.9 5.9 %collective-permute-done.3 = f32[130,256]{1,0:T(8,128)S(1)} collective-permute-done((f32[130,256]{1,0:T(8,128)}, f32[130,256]{1,0:T(8,128)S(1)}, u32[]{:S(2)}, u32[]{:S(2)}) %collective-permute-start.3) | collective-permute-done | bytes 133152 | tf_op jit(solution)/shard_map/ppermute | solution.py:20
  37.0 0.7 pad_maximum_fusion.3
  37.7 3.6 %collective-permute-start.4 = (f32[130,256]{1,0:T(8,128)}, f32[130,256]{1,0:T(8,128)}, u32[]{:S(2)}, u32[]{:S(2)}) collective-permute-start(f32[130,256]{1,0:T(8,128)} %pad_maximum_fusion.3), channel_id=1, source_target_pairs={{0,32},{4,36},{8,40},{12,44},{16,48},{20,52},{24,56},{28,60},{32,0... | collective-permute-start | bytes 399368 | tf_op jit(solution)/shard_map/ppermute | solution.py:20
  41.3 3.6 %collective-permute-done.4 = f32[130,256]{1,0:T(8,128)} collective-permute-done((f32[130,256]{1,0:T(8,128)}, f32[130,256]{1,0:T(8,128)}, u32[]{:S(2)}, u32[]{:S(2)}) %collective-permute-start.4) | collective-permute-done | bytes 133152 | tf_op jit(solution)/shard_map/ppermute | solution.py:20
  45.0 0.8 fusion.322
  45.7 0.8 slice_bitcast_fusion.5
  46.5 0.9 fusion.197
  47.5 0.9 fusion.329
  48.4 0.7 pad_maximum_fusion.4
  49.1 5.0 %collective-permute-start.5 = (f32[130,256]{1,0:T(8,128)}, f32[130,256]{1,0:T(8,128)}, u32[]{:S(2)}, u32[]{:S(2)}) collective-permute-start(f32[130,256]{1,0:T(8,128)} %pad_maximum_fusion.4), channel_id=1, source_target_pairs={{0,64},{4,68},{8,72},{12,76},{16,80},{20,84},{24,88},{28,92},{32,9... | collective-permute-start | bytes 399368 | tf_op jit(solution)/shard_map/ppermute | solution.py:20
  54.1 4.9 %collective-permute-done.5 = f32[130,256]{1,0:T(8,128)} collective-permute-done((f32[130,256]{1,0:T(8,128)}, f32[130,256]{1,0:T(8,128)}, u32[]{:S(2)}, u32[]{:S(2)}) %collective-permute-start.5) | collective-permute-done | bytes 133152 | tf_op jit(solution)/shard_map/ppermute | solution.py:20
  58.9 0.8 fusion.324
  59.7 0.8 slice_bitcast_fusion.3
  60.5 1.0 add_select_fusion.13
  61.4 0.9 fusion.332
  62.4 0.7 pad_maximum_fusion.5
  63.1 9.9 %collective-permute-start.6 = (f32[130,256]{1,0:T(8,128)}, f32[130,256]{1,0:T(8,128)}, u32[]{:S(2)}, u32[]{:S(2)}) collective-permute-start(f32[130,256]{1,0:T(8,128)} %pad_maximum_fusion.5), channel_id=1, source_target_pairs={{0,128},{4,132},{8,136},{12,140},{16,144},{20,148},{24,152},{28,15... | collective-permute-start | bytes 399368 | tf_op jit(solution)/shard_map/ppermute | solution.py:20
  73.0 9.5 %collective-permute-done.6 = f32[130,256]{1,0:T(8,128)} collective-permute-done((f32[130,256]{1,0:T(8,128)}, f32[130,256]{1,0:T(8,128)}, u32[]{:S(2)}, u32[]{:S(2)}) %collective-permute-start.6) | collective-permute-done | bytes 133152 | tf_op jit(solution)/shard_map/ppermute | solution.py:20
  82.5 0.8 broadcast_select_fusion
  83.3 0.8 slice_bitcast_fusion.1
  84.1 1.0 select_bitcast_fusion
  85.0 1.0 fusion.195
  86.1 12.5 %collective-permute-start.7 = (f32[130,256]{1,0:T(8,128)S(1)}, f32[130,256]{1,0:T(8,128)S(1)}, u32[]{:S(2)}, u32[]{:S(2)}) collective-permute-start(f32[130,256]{1,0:T(8,128)S(1)} %pad_maximum_fusion.6), channel_id=1, source_target_pairs={{0,256},{4,260},{8,264},{12,268},{16,272},{20,276},{24,280},{28,28... | collective-permute-start | bytes 399368 | tf_op jit(solution)/shard_map/ppermute | solution.py:20
  98.6 0.7 broadcast_select_fusion.6
  99.3 11.9 %collective-permute-done.7 = f32[130,256]{1,0:T(8,128)S(1)} collective-permute-done((f32[130,256]{1,0:T(8,128)S(1)}, f32[130,256]{1,0:T(8,128)S(1)}, u32[]{:S(2)}, u32[]{:S(2)}) %collective-permute-start.7) | collective-permute-done | bytes 133152 | tf_op jit(solution)/shard_map/ppermute | solution.py:20
  111.2 1.0 multiply_convert_fusion.7
  112.2 0.3 convolution_bitcast_fusion.7
  112.6 0.2 fusion.59
  113.0 0.3 convolution_bitcast_fusion.6
  113.3 0.8 copy-done.14
  114.1 0.2 fusion.77
  114.5 0.3 convolution_bitcast_fusion.5
  114.9 0.8 copy-done.12
  115.7 0.2 fusion.95
  116.1 0.3 convolution_bitcast_fusion.4
  116.5 0.2 fusion.113
  116.7 1.9 %collective-permute-start.8 = (f32[1,64,256]{2,1,0:T(8,128)S(1)}, f32[1,64,256]{2,1,0:T(8,128)S(1)}, u32[]{:S(2)}, u32[]{:S(2)}) collective-permute-start(f32[1,64,256]{2,1,0:T(8,128)S(1)} %fusion.113), channel_id=1, source_target_pairs={{4,0},{8,4},{12,8},{16,12},{20,16},{24,20},{28,24},{32,28},{36,32}... | collective-permute-start | bytes 196616 | tf_op jit(solution)/shard_map/ppermute | solution.py:56
  118.6 1.7 %fusion.48 = f32[1,1,64,256]{3,2,1,0:T(8,128)} fusion(f32[130,256]{1,0:T(8,128)S(1)} %collective-permute-done.7, f32[1,64,256]{2,1,0:T(8,128)S(1)} %select_subtract_fusion, f32[130,256]{1,0:T(8,128)} %collective-permute-done.6, f32[130,256]{1,0:T(8,128)} %collective-permute-done.5, f32[130,256]{1,0:T(8,128)} %collective-permute-done.4, ...), kind=kLoop, calls=%fused_computation.301 | loop fusion | flops 344064 | bytes 591623 | tf_op jit(solution)/shard_map/broadcast_in_dim | solution.py:152
  120.7 0.3 convolution_bitcast_fusion.3
  121.1 0.8 copy-done.10
  121.8 0.2 fusion.131
  122.3 0.3 convolution_bitcast_fusion.2
  122.6 0.8 copy-done.8
  123.4 0.2 fusion.149
  123.8 0.3 convolution_bitcast_fusion.1
  124.2 0.8 copy-done.6
  125.5 5.1 %collective-permute-start.10 = (f32[4,64,576]{2,1,0:T(8,128)S(1)}, f32[4,64,576]{2,1,0:T(8,128)S(1)}, u32[]{:S(2)}, u32[]{:S(2)}) collective-permute-start(f32[4,64,576]{2,1,0:T(8,128)S(1)} %maximum_add_fusion), channel_id=1, source_target_pairs={{0,2},{1,3},{2,0},{3,1},{4,6},{5,7},{6,4},{7,5},{8,10},{9,11},{10,... | collective-permute-start | bytes 1769480 | tf_op jit(solution)/shard_map/ppermute | solution.py:49
  130.6 3.0 %collective-permute-start.11 = (f32[4,64,576]{2,1,0:T(8,128)S(1)}, f32[4,64,576]{2,1,0:T(8,128)S(1)}, u32[]{:S(2)}, u32[]{:S(2)}) collective-permute-start(f32[4,64,576]{2,1,0:T(8,128)S(1)} %maximum_add_fusion), channel_id=1, source_target_pairs={{0,3},{1,2},{2,1},{3,0},{4,7},{5,6},{6,5},{7,4},{8,11},{9,10},{10,... | collective-permute-start | bytes 1769480 | tf_op jit(solution)/shard_map/ppermute | solution.py:49
  133.6 1.9 %collective-permute-start.9 = (f32[4,64,576]{2,1,0:T(8,128)S(1)}, f32[4,64,576]{2,1,0:T(8,128)S(1)}, u32[]{:S(2)}, u32[]{:S(2)}) collective-permute-start(f32[4,64,576]{2,1,0:T(8,128)S(1)} %maximum_add_fusion), channel_id=1, source_target_pairs={{0,1},{1,0},{2,3},{3,2},{4,5},{5,4},{6,7},{7,6},{8,9},{9,8},{10,11... | collective-permute-start | bytes 1769480 | tf_op jit(solution)/shard_map/ppermute | solution.py:49
  135.5 0.3 convolution_bitcast_fusion
  135.8 0.8 fusion.201
  136.7 9.1 %collective-permute-done.10 = f32[4,64,576]{2,1,0:T(8,128)S(1)} collective-permute-done((f32[4,64,576]{2,1,0:T(8,128)S(1)}, f32[4,64,576]{2,1,0:T(8,128)S(1)}, u32[]{:S(2)}, u32[]{:S(2)}) %collective-permute-start.10) | collective-permute-done | bytes 589856 | tf_op jit(solution)/shard_map/ppermute | solution.py:49
  145.8 14.7 %collective-permute-done.11 = f32[4,64,576]{2,1,0:T(8,128)S(1)} collective-permute-done((f32[4,64,576]{2,1,0:T(8,128)S(1)}, f32[4,64,576]{2,1,0:T(8,128)S(1)}, u32[]{:S(2)}, u32[]{:S(2)}) %collective-permute-start.11) | collective-permute-done | bytes 589856 | tf_op jit(solution)/shard_map/ppermute | solution.py:49
  160.5 1.1 add_add_fusion
  (168 shorter events, 10.0 us)
Async XLA Ops:
  0.7 1.3 copy-start.1
  1.6 1.0 copy-start
  2.8 0.7 copy-start.5
  3.7 0.7 copy-start.7
  4.6 0.7 copy-start.9
  5.3 2.1 %copy-start.2 = (f32[1,1,64,256]{3,2,1,0:T(8,128)S(1)}, f32[1,1,64,256]{3,2,1,0:T(8,128)}, u32[]{:S(2)}) copy-start(f32[1,1,64,256]{3,2,1,0:T(8,128)} %param.7) | copy-start | bytes 196612
  5.5 2.0 %copy-start.16 = (f32[1,64]{1,0:T(1,128)S(1)}, f32[1,64]{1,0:T(1,128)}, u32[]{:S(2)}) copy-start(f32[1,64]{1,0:T(1,128)} %param.6) | copy-start | bytes 772
  5.5 5.6 %collective-permute-start = (f32[1,64,256]{2,1,0:T(8,128)S(1)}, f32[1,64,256]{2,1,0:T(8,128)S(1)}, u32[]{:S(2)}, u32[]{:S(2)}) collective-permute-start(f32[1,64,256]{2,1,0:T(8,128)S(1)} %fusion.11), channel_id=1, source_target_pairs={{0,4},{4,8},{8,12},{12,16},{16,20},{20,24},{24,28},{28,32},{32,36}... | collective-permute-start | bytes 196616 | tf_op jit(solution)/shard_map/ppermute | solution.py:56
  12.0 0.7 copy-start.11
  12.9 0.7 copy-start.13
  14.8 3.3 %collective-permute-start.1 = (f32[130,256]{1,0:T(8,128)S(1)}, f32[130,256]{1,0:T(8,128)S(1)}, u32[]{:S(2)}, u32[]{:S(2)}) collective-permute-start(f32[130,256]{1,0:T(8,128)S(1)} %pad_maximum_fusion), channel_id=1, source_target_pairs={{0,4},{4,0},{8,12},{12,8},{16,20},{20,16},{24,28},{28,24},{32,36},... | collective-permute-start | bytes 399368 | tf_op jit(solution)/shard_map/ppermute | solution.py:20
  18.0 8.9 %copy-start.3 = (f32[130,256]{1,0:T(8,128)}, f32[130,256]{1,0:T(8,128)S(1)}, u32[]{:S(2)}) copy-start(f32[130,256]{1,0:T(8,128)S(1)} %collective-permute-done.1) | copy-start | bytes 399364
  18.3 8.6 %collective-permute-start.2 = (f32[130,256]{1,0:T(8,128)S(1)}, f32[130,256]{1,0:T(8,128)S(1)}, u32[]{:S(2)}, u32[]{:S(2)}) collective-permute-start(f32[130,256]{1,0:T(8,128)S(1)} %pad_maximum_fusion.1), channel_id=1, source_target_pairs={{0,8},{4,12},{8,0},{12,4},{16,24},{20,28},{24,16},{28,20},{32,40},... | collective-permute-start | bytes 399368 | tf_op jit(solution)/shard_map/ppermute | solution.py:20
  27.8 8.9 %collective-permute-start.3 = (f32[130,256]{1,0:T(8,128)}, f32[130,256]{1,0:T(8,128)S(1)}, u32[]{:S(2)}, u32[]{:S(2)}) collective-permute-start(f32[130,256]{1,0:T(8,128)} %pad_maximum_fusion.2), channel_id=1, source_target_pairs={{0,16},{4,20},{8,24},{12,28},{16,0},{20,4},{24,8},{28,12},{32,48},... | collective-permute-start | bytes 399368 | tf_op jit(solution)/shard_map/ppermute | solution.py:20
  37.7 7.3 %collective-permute-start.4 = (f32[130,256]{1,0:T(8,128)}, f32[130,256]{1,0:T(8,128)}, u32[]{:S(2)}, u32[]{:S(2)}) collective-permute-start(f32[130,256]{1,0:T(8,128)} %pad_maximum_fusion.3), channel_id=1, source_target_pairs={{0,32},{4,36},{8,40},{12,44},{16,48},{20,52},{24,56},{28,60},{32,0... | collective-permute-start | bytes 399368 | tf_op jit(solution)/shard_map/ppermute | solution.py:20
  49.1 9.9 %collective-permute-start.5 = (f32[130,256]{1,0:T(8,128)}, f32[130,256]{1,0:T(8,128)}, u32[]{:S(2)}, u32[]{:S(2)}) collective-permute-start(f32[130,256]{1,0:T(8,128)} %pad_maximum_fusion.4), channel_id=1, source_target_pairs={{0,64},{4,68},{8,72},{12,76},{16,80},{20,84},{24,88},{28,92},{32,9... | collective-permute-start | bytes 399368 | tf_op jit(solution)/shard_map/ppermute | solution.py:20
  61.4 1.0 copy-start.15
  62.4 20.1 %copy-start.4 = (f32[130,256]{1,0:T(8,128)S(1)}, f32[130,256]{1,0:T(8,128)}, u32[]{:S(2)}) copy-start(f32[130,256]{1,0:T(8,128)} %copy-done.3) | copy-start | bytes 399364
  63.1 19.4 %collective-permute-start.6 = (f32[130,256]{1,0:T(8,128)}, f32[130,256]{1,0:T(8,128)}, u32[]{:S(2)}, u32[]{:S(2)}) collective-permute-start(f32[130,256]{1,0:T(8,128)} %pad_maximum_fusion.5), channel_id=1, source_target_pairs={{0,128},{4,132},{8,136},{12,140},{16,144},{20,148},{24,152},{28,15... | collective-permute-start | bytes 399368 | tf_op jit(solution)/shard_map/ppermute | solution.py:20
  86.1 25.1 %collective-permute-start.7 = (f32[130,256]{1,0:T(8,128)S(1)}, f32[130,256]{1,0:T(8,128)S(1)}, u32[]{:S(2)}, u32[]{:S(2)}) collective-permute-start(f32[130,256]{1,0:T(8,128)S(1)} %pad_maximum_fusion.6), channel_id=1, source_target_pairs={{0,256},{4,260},{8,264},{12,268},{16,272},{20,276},{24,280},{28,28... | collective-permute-start | bytes 399368 | tf_op jit(solution)/shard_map/ppermute | solution.py:20
  113.3 0.8 copy-start.14
  114.8 0.8 copy-start.12
  116.7 3.8 %collective-permute-start.8 = (f32[1,64,256]{2,1,0:T(8,128)S(1)}, f32[1,64,256]{2,1,0:T(8,128)S(1)}, u32[]{:S(2)}, u32[]{:S(2)}) collective-permute-start(f32[1,64,256]{2,1,0:T(8,128)S(1)} %fusion.113), channel_id=1, source_target_pairs={{4,0},{8,4},{12,8},{16,12},{20,16},{24,20},{28,24},{32,28},{36,32}... | collective-permute-start | bytes 196616 | tf_op jit(solution)/shard_map/ppermute | solution.py:56
  121.0 0.8 copy-start.10
  122.6 0.8 copy-start.8
  124.1 0.8 copy-start.6
  125.5 20.3 %collective-permute-start.10 = (f32[4,64,576]{2,1,0:T(8,128)S(1)}, f32[4,64,576]{2,1,0:T(8,128)S(1)}, u32[]{:S(2)}, u32[]{:S(2)}) collective-permute-start(f32[4,64,576]{2,1,0:T(8,128)S(1)} %maximum_add_fusion), channel_id=1, source_target_pairs={{0,2},{1,3},{2,0},{3,1},{4,6},{5,7},{6,4},{7,5},{8,10},{9,11},{10,... | collective-permute-start | bytes 1769480 | tf_op jit(solution)/shard_map/ppermute | solution.py:49
  130.6 29.9 %collective-permute-start.11 = (f32[4,64,576]{2,1,0:T(8,128)S(1)}, f32[4,64,576]{2,1,0:T(8,128)S(1)}, u32[]{:S(2)}, u32[]{:S(2)}) collective-permute-start(f32[4,64,576]{2,1,0:T(8,128)S(1)} %maximum_add_fusion), channel_id=1, source_target_pairs={{0,3},{1,2},{2,1},{3,0},{4,7},{5,6},{6,5},{7,4},{8,11},{9,10},{10,... | collective-permute-start | bytes 1769480 | tf_op jit(solution)/shard_map/ppermute | solution.py:49
  133.6 26.9 %collective-permute-start.9 = (f32[4,64,576]{2,1,0:T(8,128)S(1)}, f32[4,64,576]{2,1,0:T(8,128)S(1)}, u32[]{:S(2)}, u32[]{:S(2)}) collective-permute-start(f32[4,64,576]{2,1,0:T(8,128)S(1)} %maximum_add_fusion), channel_id=1, source_target_pairs={{0,1},{1,0},{2,3},{3,2},{4,5},{5,4},{6,7},{7,6},{8,9},{9,8},{10,11... | collective-permute-start | bytes 1769480 | tf_op jit(solution)/shard_map/ppermute | solution.py:49

commit v5 on v4

--- a/solution.py
+++ b/solution.py
@@ -44,10 +44,19 @@
 
 def dp_sum(terms, axis):
     count = lax.axis_size(axis)
-    if count != 4:
+    if count != terms.shape[0] or count & (count - 1):
         return lax.psum(terms, axis)
-    got = [lax.ppermute(terms, axis, [(i, i ^ k) for i in range(count)]) for k in (1, 2, 3)]
-    return (terms + got[0]) + (got[1] + got[2])
+    place = lax.axis_index(axis)
+    pairs = lambda k: [(i, i ^ k) for i in range(count)]
+    got = [terms[place]] + [
+        lax.ppermute(lax.dynamic_index_in_dim(terms, place ^ k, 0, False), axis, pairs(k))
+        for k in range(1, count)
+    ]
+    total = got[0]
+    for piece in got[1:]:
+        total = total + piece
+    back = jnp.stack([total] + [lax.ppermute(total, axis, pairs(k)) for k in range(1, count)])
+    return jnp.take(back, jnp.arange(count) ^ place, axis=0)
 
 
 def passed_along(block, axis, distance):

time: 163 us -> 162 us (level)
  waiting for transfers between devices: 68.6 us -> 56.9 us
  starting transfers between devices: 54.2 us -> 64.2 us
    ppermute x3 -> x6, waiting for transfers between devices: 23.8 us -> 12.1 us  [the longest x3 7.5 us: dp_sum(): lax.ppermute(lax.dynamic_index_in_dim(terms, place ^ k, 0, False), axis,...]
    ppermute x3 -> x6, starting transfers between devices: 9.99 us -> 20 us  [the longest x3 10.2 us: dp_sum(): lax.ppermute(lax.dynamic_index_in_dim(terms, place ^ k, 0, False), axis,...]
  transfers between devices with their start and end apart: 12 -> 15, of which waited for: 10 -> 13; matrix products, arithmetic and copies ran while one was open for 2% -> 2% of each run, Pallas kernels for 0% -> 0%
where the time goes in v5:
time: 162 us; the launch traced here: 161 us
  starting transfers between devices  64.2 us (40%)
  waiting for transfers between devices  56.9 us (35%)
  other arithmetic  24.6 us (15%)
  local copies, waits for them, and re-layouts  7.52 us (5%)
  matrix products  5.47 us (3%)
  between operations  1.89 us (1%)
    ppermute x7, waiting for transfers between devices, exchange(): lax.ppermute(pack(gains, states), axis, [(i, i ^ 1 << bit) for i in range...  41.2 us
    ppermute x7, starting transfers between devices, exchange(): lax.ppermute(pack(gains, states), axis, [(i, i ^ 1 << bit) for i in range...  40.3 us
    ppermute x3, starting transfers between devices, dp_sum(): lax.ppermute(lax.dynamic_index_in_dim(terms, place ^ k, 0, False), axis,...  10.2 us
    ppermute x3, starting transfers between devices, dp_sum(): lax.ppermute(total, axis, pairs(k))  9.82 us
    ppermute x3, waiting for transfers between devices, dp_sum(): lax.ppermute(lax.dynamic_index_in_dim(terms, place ^ k, 0, False), axis,...  7.5 us
    unnamed x64, other arithmetic  4.68 us
    ppermute x3, waiting for transfers between devices, dp_sum(): lax.ppermute(total, axis, pairs(k))  4.64 us
    unnamed x34, local copies, waits for them, and re-layouts  4.25 us
  transfers between devices with their start and end apart: 15, of which 13 were waited for; matrix products, arithmetic and copies ran while one was open for 2% of the time, Pallas kernels for 0%

profile of v5, /device:TPU:2, one launch (start us, length us, event | category | flops | bytes accessed | tf_op | source)
XLA Modules:
  0.0 160.5 jit_solution(14566329502328013620)
XLA Ops:
  0.7 0.9 fusion.204
  5.5 1.9 %collective-permute-start = (f32[1,64,256]{2,1,0:T(8,128)S(1)}, f32[1,64,256]{2,1,0:T(8,128)S(1)}, u32[]{:S(2)}, u32[]{:S(2)}) collective-permute-start(f32[1,64,256]{2,1,0:T(8,128)S(1)} %fusion.11), channel_id=1, source_target_pairs={{0,4},{4,8},{8,12},{12,16},{16,20},{20,24},{24,28},{28,32},{32,36}... | collective-permute-start | bytes 196616 | tf_op jit(solution)/shard_map/ppermute | solution.py:65
  7.6 3.5 %collective-permute-done = f32[1,64,256]{2,1,0:T(8,128)S(1)} collective-permute-done((f32[1,64,256]{2,1,0:T(8,128)S(1)}, f32[1,64,256]{2,1,0:T(8,128)S(1)}, u32[]{:S(2)}, u32[]{:S(2)}) %collective-permute-start) | collective-permute-done | bytes 65568 | tf_op jit(solution)/shard_map/ppermute | solution.py:65
  14.8 1.9 %collective-permute-start.1 = (f32[130,256]{1,0:T(8,128)S(1)}, f32[130,256]{1,0:T(8,128)S(1)}, u32[]{:S(2)}, u32[]{:S(2)}) collective-permute-start(f32[130,256]{1,0:T(8,128)S(1)} %pad_maximum_fusion.1), channel_id=1, source_target_pairs={{0,4},{4,0},{8,12},{12,8},{16,20},{20,16},{24,28},{28,24},{32,36},... | collective-permute-start | bytes 399368 | tf_op jit(solution)/shard_map/ppermute | solution.py:20
  16.7 1.3 collective-permute-done.1
  18.3 4.4 %collective-permute-start.2 = (f32[130,256]{1,0:T(8,128)S(1)}, f32[130,256]{1,0:T(8,128)S(1)}, u32[]{:S(2)}, u32[]{:S(2)}) collective-permute-start(f32[130,256]{1,0:T(8,128)S(1)} %pad_maximum_fusion.2), channel_id=1, source_target_pairs={{0,8},{4,12},{8,0},{12,4},{16,24},{20,28},{24,16},{28,20},{32,40},... | collective-permute-start | bytes 399368 | tf_op jit(solution)/shard_map/ppermute | solution.py:20
  22.7 4.2 %collective-permute-done.2 = f32[130,256]{1,0:T(8,128)S(1)} collective-permute-done((f32[130,256]{1,0:T(8,128)S(1)}, f32[130,256]{1,0:T(8,128)S(1)}, u32[]{:S(2)}, u32[]{:S(2)}) %collective-permute-start.2) | collective-permute-done | bytes 133152 | tf_op jit(solution)/shard_map/ppermute | solution.py:20
  27.2 0.7 pad_maximum_fusion.3
  27.8 3.0 %collective-permute-start.3 = (f32[130,256]{1,0:T(8,128)}, f32[130,256]{1,0:T(8,128)S(1)}, u32[]{:S(2)}, u32[]{:S(2)}) collective-permute-start(f32[130,256]{1,0:T(8,128)} %pad_maximum_fusion.3), channel_id=1, source_target_pairs={{0,16},{4,20},{8,24},{12,28},{16,0},{20,4},{24,8},{28,12},{32,48},... | collective-permute-start | bytes 399368 | tf_op jit(solution)/shard_map/ppermute | solution.py:20
  30.9 5.9 %collective-permute-done.3 = f32[130,256]{1,0:T(8,128)S(1)} collective-permute-done((f32[130,256]{1,0:T(8,128)}, f32[130,256]{1,0:T(8,128)S(1)}, u32[]{:S(2)}, u32[]{:S(2)}) %collective-permute-start.3) | collective-permute-done | bytes 133152 | tf_op jit(solution)/shard_map/ppermute | solution.py:20
  37.0 0.7 pad_maximum_fusion.4
  37.7 3.6 %collective-permute-start.4 = (f32[130,256]{1,0:T(8,128)}, f32[130,256]{1,0:T(8,128)}, u32[]{:S(2)}, u32[]{:S(2)}) collective-permute-start(f32[130,256]{1,0:T(8,128)} %pad_maximum_fusion.4), channel_id=1, source_target_pairs={{0,32},{4,36},{8,40},{12,44},{16,48},{20,52},{24,56},{28,60},{32,0... | collective-permute-start | bytes 399368 | tf_op jit(solution)/shard_map/ppermute | solution.py:20
  41.3 3.6 %collective-permute-done.4 = f32[130,256]{1,0:T(8,128)} collective-permute-done((f32[130,256]{1,0:T(8,128)}, f32[130,256]{1,0:T(8,128)}, u32[]{:S(2)}, u32[]{:S(2)}) %collective-permute-start.4) | collective-permute-done | bytes 133152 | tf_op jit(solution)/shard_map/ppermute | solution.py:20
  45.0 0.8 fusion.325
  45.7 0.8 slice_bitcast_fusion.5
  46.5 0.9 fusion.199
  47.4 0.9 fusion.332
  48.4 0.7 pad_maximum_fusion.5
  49.1 5.0 %collective-permute-start.5 = (f32[130,256]{1,0:T(8,128)}, f32[130,256]{1,0:T(8,128)}, u32[]{:S(2)}, u32[]{:S(2)}) collective-permute-start(f32[130,256]{1,0:T(8,128)} %pad_maximum_fusion.5), channel_id=1, source_target_pairs={{0,64},{4,68},{8,72},{12,76},{16,80},{20,84},{24,88},{28,92},{32,9... | collective-permute-start | bytes 399368 | tf_op jit(solution)/shard_map/ppermute | solution.py:20
  54.1 4.9 %collective-permute-done.5 = f32[130,256]{1,0:T(8,128)} collective-permute-done((f32[130,256]{1,0:T(8,128)}, f32[130,256]{1,0:T(8,128)}, u32[]{:S(2)}, u32[]{:S(2)}) %collective-permute-start.5) | collective-permute-done | bytes 133152 | tf_op jit(solution)/shard_map/ppermute | solution.py:20
  58.9 0.8 fusion.327
  59.7 0.8 slice_bitcast_fusion.3
  60.4 1.0 add_select_fusion.13
  61.4 0.9 fusion.335
  62.4 0.7 pad_maximum_fusion.6
  63.1 9.9 %collective-permute-start.6 = (f32[130,256]{1,0:T(8,128)}, f32[130,256]{1,0:T(8,128)}, u32[]{:S(2)}, u32[]{:S(2)}) collective-permute-start(f32[130,256]{1,0:T(8,128)} %pad_maximum_fusion.6), channel_id=1, source_target_pairs={{0,128},{4,132},{8,136},{12,140},{16,144},{20,148},{24,152},{28,15... | collective-permute-start | bytes 399368 | tf_op jit(solution)/shard_map/ppermute | solution.py:20
  73.0 9.5 %collective-permute-done.6 = f32[130,256]{1,0:T(8,128)} collective-permute-done((f32[130,256]{1,0:T(8,128)}, f32[130,256]{1,0:T(8,128)}, u32[]{:S(2)}, u32[]{:S(2)}) %collective-permute-start.6) | collective-permute-done | bytes 133152 | tf_op jit(solution)/shard_map/ppermute | solution.py:20
  82.5 0.8 broadcast_select_fusion.1
  83.3 0.8 slice_bitcast_fusion.1
  84.0 1.0 select_bitcast_fusion
  85.0 1.0 fusion.197
  86.0 12.5 %collective-permute-start.7 = (f32[130,256]{1,0:T(8,128)S(1)}, f32[130,256]{1,0:T(8,128)S(1)}, u32[]{:S(2)}, u32[]{:S(2)}) collective-permute-start(f32[130,256]{1,0:T(8,128)S(1)} %pad_maximum_fusion.7), channel_id=1, source_target_pairs={{0,256},{4,260},{8,264},{12,268},{16,272},{20,276},{24,280},{28,28... | collective-permute-start | bytes 399368 | tf_op jit(solution)/shard_map/ppermute | solution.py:20
  98.5 0.7 broadcast_select_fusion.7
  99.2 11.9 %collective-permute-done.7 = f32[130,256]{1,0:T(8,128)S(1)} collective-permute-done((f32[130,256]{1,0:T(8,128)S(1)}, f32[130,256]{1,0:T(8,128)S(1)}, u32[]{:S(2)}, u32[]{:S(2)}) %collective-permute-start.7) | collective-permute-done | bytes 133152 | tf_op jit(solution)/shard_map/ppermute | solution.py:20
  111.1 1.0 multiply_convert_fusion.7
  112.2 0.3 convolution_bitcast_fusion.7
  112.9 0.3 convolution_bitcast_fusion.6
  113.3 0.8 copy-done.14
  114.5 0.3 convolution_bitcast_fusion.5
  114.9 0.8 copy-done.12
  116.1 0.3 convolution_bitcast_fusion.4
  116.6 1.9 %collective-permute-start.8 = (f32[1,64,256]{2,1,0:T(8,128)S(1)}, f32[1,64,256]{2,1,0:T(8,128)S(1)}, u32[]{:S(2)}, u32[]{:S(2)}) collective-permute-start(f32[1,64,256]{2,1,0:T(8,128)S(1)} %fusion.115), channel_id=1, source_target_pairs={{4,0},{8,4},{12,8},{16,12},{20,16},{24,20},{28,24},{32,28},{36,32}... | collective-permute-start | bytes 196616 | tf_op jit(solution)/shard_map/ppermute | solution.py:65
  118.5 1.7 %fusion.50 = f32[1,1,64,256]{3,2,1,0:T(8,128)} fusion(f32[130,256]{1,0:T(8,128)S(1)} %collective-permute-done.7, f32[1,64,256]{2,1,0:T(8,128)S(1)} %select_subtract_fusion, f32[130,256]{1,0:T(8,128)} %collective-permute-done.6, f32[130,256]{1,0:T(8,128)} %collective-permute-done.5, f32[130,256]{1,0:T(8,128)} %collective-permute-done.4, ...), kind=kLoop, calls=%fused_computation.309 | loop fusion | flops 344064 | bytes 591623 | tf_op jit(solution)/shard_map/broadcast_in_dim | solution.py:161
  120.7 0.3 convolution_bitcast_fusion.3
  121.0 0.8 copy-done.10
  122.2 0.3 convolution_bitcast_fusion.2
  122.6 0.8 copy-done.8
  123.8 0.3 convolution_bitcast_fusion.1
  124.1 0.8 copy-done.6
  125.3 0.3 convolution_bitcast_fusion
  125.8 3.5 %collective-permute-start.9 = (f32[64,576]{1,0:T(8,128)S(1)}, f32[64,576]{1,0:T(8,128)S(1)}, u32[]{:S(2)}, u32[]{:S(2)}) collective-permute-start(f32[64,576]{1,0:T(8,128)S(1)} %get-tuple-element.19), channel_id=1, source_target_pairs={{0,1},{1,0},{2,3},{3,2},{4,5},{5,4},{6,7},{7,6},{8,9},{9,8},{10,11... | collective-permute-start | bytes 442376 | tf_op jit(solution)/shard_map/ppermute | solution.py:52
  129.3 4.1 %collective-permute-start.11 = (f32[64,576]{1,0:T(8,128)S(1)}, f32[64,576]{1,0:T(8,128)S(1)}, u32[]{:S(2)}, u32[]{:S(2)}) collective-permute-start(f32[64,576]{1,0:T(8,128)S(1)} %get-tuple-element.20), channel_id=1, source_target_pairs={{0,3},{1,2},{2,1},{3,0},{4,7},{5,6},{6,5},{7,4},{8,11},{9,10},{10,... | collective-permute-start | bytes 442376 | tf_op jit(solution)/shard_map/ppermute | solution.py:52
  133.4 2.6 %collective-permute-start.10 = (f32[64,576]{1,0:T(8,128)S(1)}, f32[64,576]{1,0:T(8,128)S(1)}, u32[]{:S(2)}, u32[]{:S(2)}) collective-permute-start(f32[64,576]{1,0:T(8,128)S(1)} %get-tuple-element.21), channel_id=1, source_target_pairs={{0,2},{1,3},{2,0},{3,1},{4,6},{5,7},{6,4},{7,5},{8,10},{9,11},{10,... | collective-permute-start | bytes 442376 | tf_op jit(solution)/shard_map/ppermute | solution.py:52
  136.1 2.9 %collective-permute-done.11 = f32[64,576]{1,0:T(8,128)S(1)} collective-permute-done((f32[64,576]{1,0:T(8,128)S(1)}, f32[64,576]{1,0:T(8,128)S(1)}, u32[]{:S(2)}, u32[]{:S(2)}) %collective-permute-start.11) | collective-permute-done | bytes 147488 | tf_op jit(solution)/shard_map/ppermute | solution.py:52
  139.0 4.6 %collective-permute-done.10 = f32[64,576]{1,0:T(8,128)S(1)} collective-permute-done((f32[64,576]{1,0:T(8,128)S(1)}, f32[64,576]{1,0:T(8,128)S(1)}, u32[]{:S(2)}, u32[]{:S(2)}) %collective-permute-start.10) | collective-permute-done | bytes 147488 | tf_op jit(solution)/shard_map/ppermute | solution.py:52
  143.6 3.1 %collective-permute-start.14 = (f32[64,576]{1,0:T(8,128)S(1)}, f32[64,576]{1,0:T(8,128)S(1)}, u32[]{:S(2)}, u32[]{:S(2)}) collective-permute-start(f32[64,576]{1,0:T(8,128)S(1)} %fusion.33), channel_id=1, source_target_pairs={{0,3},{1,2},{2,1},{3,0},{4,7},{5,6},{6,5},{7,4},{8,11},{9,10},{10,... | collective-permute-start | bytes 442376 | tf_op jit(solution)/shard_map/ppermute | solution.py:58
  146.7 3.5 %collective-permute-start.13 = (f32[64,576]{1,0:T(8,128)S(1)}, f32[64,576]{1,0:T(8,128)S(1)}, u32[]{:S(2)}, u32[]{:S(2)}) collective-permute-start(f32[64,576]{1,0:T(8,128)S(1)} %fusion.33), channel_id=1, source_target_pairs={{0,2},{1,3},{2,0},{3,1},{4,6},{5,7},{6,4},{7,5},{8,10},{9,11},{10,... | collective-permute-start | bytes 442376 | tf_op jit(solution)/shard_map/ppermute | solution.py:58
  150.2 3.3 %collective-permute-start.12 = (f32[64,576]{1,0:T(8,128)S(1)}, f32[64,576]{1,0:T(8,128)S(1)}, u32[]{:S(2)}, u32[]{:S(2)}) collective-permute-start(f32[64,576]{1,0:T(8,128)S(1)} %fusion.33), channel_id=1, source_target_pairs={{0,1},{1,0},{2,3},{3,2},{4,5},{5,4},{6,7},{7,6},{8,9},{9,8},{10,11... | collective-permute-start | bytes 442376 | tf_op jit(solution)/shard_map/ppermute | solution.py:58
  153.4 0.8 fusion.203
  154.3 1.4 collective-permute-done.14
  155.7 1.4 collective-permute-done.13
  157.1 1.8 %collective-permute-done.12 = f32[64,576]{1,0:T(8,128)S(1)} collective-permute-done((f32[64,576]{1,0:T(8,128)S(1)}, f32[64,576]{1,0:T(8,128)S(1)}, u32[]{:S(2)}, u32[]{:S(2)}) %collective-permute-start.12) | collective-permute-done | bytes 147488 | tf_op jit(solution)/shard_map/ppermute | solution.py:58
  159.0 0.6 gather_fusion
  159.6 0.9 broadcast_select_fusion
  (181 shorter events, 11.7 us)
Async XLA Ops:
  0.7 1.3 copy-start.1
  1.6 1.0 copy-start
  2.8 0.7 copy-start.5
  3.7 0.7 copy-start.7
  4.6 0.7 copy-start.9
  5.3 2.1 %copy-start.2 = (f32[1,1,64,256]{3,2,1,0:T(8,128)S(1)}, f32[1,1,64,256]{3,2,1,0:T(8,128)}, u32[]{:S(2)}) copy-start(f32[1,1,64,256]{3,2,1,0:T(8,128)} %param.7) | copy-start | bytes 196612
  5.5 2.0 %copy-start.16 = (f32[1,64]{1,0:T(1,128)S(1)}, f32[1,64]{1,0:T(1,128)}, u32[]{:S(2)}) copy-start(f32[1,64]{1,0:T(1,128)} %param.6) | copy-start | bytes 772
  5.5 5.6 %collective-permute-start = (f32[1,64,256]{2,1,0:T(8,128)S(1)}, f32[1,64,256]{2,1,0:T(8,128)S(1)}, u32[]{:S(2)}, u32[]{:S(2)}) collective-permute-start(f32[1,64,256]{2,1,0:T(8,128)S(1)} %fusion.11), channel_id=1, source_target_pairs={{0,4},{4,8},{8,12},{12,16},{16,20},{20,24},{24,28},{28,32},{32,36}... | collective-permute-start | bytes 196616 | tf_op jit(solution)/shard_map/ppermute | solution.py:65
  12.0 0.7 copy-start.11
  12.9 0.7 copy-start.13
  14.8 3.3 %collective-permute-start.1 = (f32[130,256]{1,0:T(8,128)S(1)}, f32[130,256]{1,0:T(8,128)S(1)}, u32[]{:S(2)}, u32[]{:S(2)}) collective-permute-start(f32[130,256]{1,0:T(8,128)S(1)} %pad_maximum_fusion.1), channel_id=1, source_target_pairs={{0,4},{4,0},{8,12},{12,8},{16,20},{20,16},{24,28},{28,24},{32,36},... | collective-permute-start | bytes 399368 | tf_op jit(solution)/shard_map/ppermute | solution.py:20
  18.0 8.9 %copy-start.3 = (f32[130,256]{1,0:T(8,128)}, f32[130,256]{1,0:T(8,128)S(1)}, u32[]{:S(2)}) copy-start(f32[130,256]{1,0:T(8,128)S(1)} %collective-permute-done.1) | copy-start | bytes 399364
  18.3 8.6 %collective-permute-start.2 = (f32[130,256]{1,0:T(8,128)S(1)}, f32[130,256]{1,0:T(8,128)S(1)}, u32[]{:S(2)}, u32[]{:S(2)}) collective-permute-start(f32[130,256]{1,0:T(8,128)S(1)} %pad_maximum_fusion.2), channel_id=1, source_target_pairs={{0,8},{4,12},{8,0},{12,4},{16,24},{20,28},{24,16},{28,20},{32,40},... | collective-permute-start | bytes 399368 | tf_op jit(solution)/shard_map/ppermute | solution.py:20
  27.8 8.9 %collective-permute-start.3 = (f32[130,256]{1,0:T(8,128)}, f32[130,256]{1,0:T(8,128)S(1)}, u32[]{:S(2)}, u32[]{:S(2)}) collective-permute-start(f32[130,256]{1,0:T(8,128)} %pad_maximum_fusion.3), channel_id=1, source_target_pairs={{0,16},{4,20},{8,24},{12,28},{16,0},{20,4},{24,8},{28,12},{32,48},... | collective-permute-start | bytes 399368 | tf_op jit(solution)/shard_map/ppermute | solution.py:20
  37.7 7.3 %collective-permute-start.4 = (f32[130,256]{1,0:T(8,128)}, f32[130,256]{1,0:T(8,128)}, u32[]{:S(2)}, u32[]{:S(2)}) collective-permute-start(f32[130,256]{1,0:T(8,128)} %pad_maximum_fusion.4), channel_id=1, source_target_pairs={{0,32},{4,36},{8,40},{12,44},{16,48},{20,52},{24,56},{28,60},{32,0... | collective-permute-start | bytes 399368 | tf_op jit(solution)/shard_map/ppermute | solution.py:20
  49.1 9.9 %collective-permute-start.5 = (f32[130,256]{1,0:T(8,128)}, f32[130,256]{1,0:T(8,128)}, u32[]{:S(2)}, u32[]{:S(2)}) collective-permute-start(f32[130,256]{1,0:T(8,128)} %pad_maximum_fusion.5), channel_id=1, source_target_pairs={{0,64},{4,68},{8,72},{12,76},{16,80},{20,84},{24,88},{28,92},{32,9... | collective-permute-start | bytes 399368 | tf_op jit(solution)/shard_map/ppermute | solution.py:20
  61.4 1.0 copy-start.15
  62.4 20.1 %copy-start.4 = (f32[130,256]{1,0:T(8,128)S(1)}, f32[130,256]{1,0:T(8,128)}, u32[]{:S(2)}) copy-start(f32[130,256]{1,0:T(8,128)} %copy-done.3) | copy-start | bytes 399364
  63.1 19.4 %collective-permute-start.6 = (f32[130,256]{1,0:T(8,128)}, f32[130,256]{1,0:T(8,128)}, u32[]{:S(2)}, u32[]{:S(2)}) collective-permute-start(f32[130,256]{1,0:T(8,128)} %pad_maximum_fusion.6), channel_id=1, source_target_pairs={{0,128},{4,132},{8,136},{12,140},{16,144},{20,148},{24,152},{28,15... | collective-permute-start | bytes 399368 | tf_op jit(solution)/shard_map/ppermute | solution.py:20
  86.0 25.1 %collective-permute-start.7 = (f32[130,256]{1,0:T(8,128)S(1)}, f32[130,256]{1,0:T(8,128)S(1)}, u32[]{:S(2)}, u32[]{:S(2)}) collective-permute-start(f32[130,256]{1,0:T(8,128)S(1)} %pad_maximum_fusion.7), channel_id=1, source_target_pairs={{0,256},{4,260},{8,264},{12,268},{16,272},{20,276},{24,280},{28,28... | collective-permute-start | bytes 399368 | tf_op jit(solution)/shard_map/ppermute | solution.py:20
  113.2 0.8 copy-start.14
  114.8 0.8 copy-start.12
  116.6 3.8 %collective-permute-start.8 = (f32[1,64,256]{2,1,0:T(8,128)S(1)}, f32[1,64,256]{2,1,0:T(8,128)S(1)}, u32[]{:S(2)}, u32[]{:S(2)}) collective-permute-start(f32[1,64,256]{2,1,0:T(8,128)S(1)} %fusion.115), channel_id=1, source_target_pairs={{4,0},{8,4},{12,8},{16,12},{20,16},{24,20},{28,24},{32,28},{36,32}... | collective-permute-start | bytes 196616 | tf_op jit(solution)/shard_map/ppermute | solution.py:65
  121.0 0.8 copy-start.10
  122.5 0.8 copy-start.8
  124.1 0.8 copy-start.6
  125.8 10.3 %collective-permute-start.9 = (f32[64,576]{1,0:T(8,128)S(1)}, f32[64,576]{1,0:T(8,128)S(1)}, u32[]{:S(2)}, u32[]{:S(2)}) collective-permute-start(f32[64,576]{1,0:T(8,128)S(1)} %get-tuple-element.19), channel_id=1, source_target_pairs={{0,1},{1,0},{2,3},{3,2},{4,5},{5,4},{6,7},{7,6},{8,9},{9,8},{10,11... | collective-permute-start | bytes 442376 | tf_op jit(solution)/shard_map/ppermute | solution.py:52
  129.3 9.7 %collective-permute-start.11 = (f32[64,576]{1,0:T(8,128)S(1)}, f32[64,576]{1,0:T(8,128)S(1)}, u32[]{:S(2)}, u32[]{:S(2)}) collective-permute-start(f32[64,576]{1,0:T(8,128)S(1)} %get-tuple-element.20), channel_id=1, source_target_pairs={{0,3},{1,2},{2,1},{3,0},{4,7},{5,6},{6,5},{7,4},{8,11},{9,10},{10,... | collective-permute-start | bytes 442376 | tf_op jit(solution)/shard_map/ppermute | solution.py:52
  133.4 10.2 %collective-permute-start.10 = (f32[64,576]{1,0:T(8,128)S(1)}, f32[64,576]{1,0:T(8,128)S(1)}, u32[]{:S(2)}, u32[]{:S(2)}) collective-permute-start(f32[64,576]{1,0:T(8,128)S(1)} %get-tuple-element.21), channel_id=1, source_target_pairs={{0,2},{1,3},{2,0},{3,1},{4,6},{5,7},{6,4},{7,5},{8,10},{9,11},{10,... | collective-permute-start | bytes 442376 | tf_op jit(solution)/shard_map/ppermute | solution.py:52
  143.6 12.1 %collective-permute-start.14 = (f32[64,576]{1,0:T(8,128)S(1)}, f32[64,576]{1,0:T(8,128)S(1)}, u32[]{:S(2)}, u32[]{:S(2)}) collective-permute-start(f32[64,576]{1,0:T(8,128)S(1)} %fusion.33), channel_id=1, source_target_pairs={{0,3},{1,2},{2,1},{3,0},{4,7},{5,6},{6,5},{7,4},{8,11},{9,10},{10,... | collective-permute-start | bytes 442376 | tf_op jit(solution)/shard_map/ppermute | solution.py:58
  146.7 10.5 %collective-permute-start.13 = (f32[64,576]{1,0:T(8,128)S(1)}, f32[64,576]{1,0:T(8,128)S(1)}, u32[]{:S(2)}, u32[]{:S(2)}) collective-permute-start(f32[64,576]{1,0:T(8,128)S(1)} %fusion.33), channel_id=1, source_target_pairs={{0,2},{1,3},{2,0},{3,1},{4,6},{5,7},{6,4},{7,5},{8,10},{9,11},{10,... | collective-permute-start | bytes 442376 | tf_op jit(solution)/shard_map/ppermute | solution.py:58
  150.2 8.8 %collective-permute-start.12 = (f32[64,576]{1,0:T(8,128)S(1)}, f32[64,576]{1,0:T(8,128)S(1)}, u32[]{:S(2)}, u32[]{:S(2)}) collective-permute-start(f32[64,576]{1,0:T(8,128)S(1)} %fusion.33), channel_id=1, source_target_pairs={{0,1},{1,0},{2,3},{3,2},{4,5},{5,4},{6,7},{7,6},{8,9},{9,8},{10,11... | collective-permute-start | bytes 442376 | tf_op jit(solution)/shard_map/ppermute | solution.py:58

commit v6 on v5

--- a/solution.py
+++ b/solution.py
@@ -15,15 +15,37 @@
     return jnp.concatenate([states.reshape(-1, width)] + rows, axis=0)
 
 
-def exchange(gains, states, axis, bit):
+def exchange(gains, states, axis, bit, mask=None):
     count = lax.axis_size(axis)
-    arrived = lax.ppermute(pack(gains, states), axis, [(i, i ^ (1 << bit)) for i in range(count)])
+    mask = 1 << bit if mask is None else mask
+    arrived = lax.ppermute(pack(gains, states), axis, [(i, i ^ mask) for i in range(count)])
     rows = states.size // states.shape[-1]
     each = states.shape[1:]
     got = arrived[:rows].reshape(states.shape)
     return tuple(
         (arrived[rows + k, : g.shape[0]], got[k].reshape(each)) for k, g in enumerate(gains)
     )
+
+
+def last_two_rounds(forward, reverse, axis, bit, place):
+    quarter = (place >> bit) % 4
+    gains = (forward[2], reverse[2])
+    states = jnp.stack([forward[3], reverse[3]])
+    arrived = [exchange(gains, states, axis, bit, m << bit) for m in range(1, 4)]
+    order = jnp.arange(4) ^ quarter
+    results = []
+    for k, (scan, earlier) in enumerate(((forward, True), (reverse, False))):
+        slot_gain = jnp.take(jnp.stack([gains[k]] + [a[k][0] for a in arrived]), order, axis=0)
+        slot_state = jnp.take(jnp.stack([states[k]] + [a[k][1] for a in arrived]), order, axis=0)
+        steps = range(4) if earlier else reversed(range(4))
+        running = jnp.zeros_like(slot_state[0])
+        inner = [None] * 4
+        for q in steps:
+            inner[q] = running
+            running = slot_state[q] + slot_gain[q][:, None] * running
+        picked = lax.dynamic_index_in_dim(jnp.stack(inner), quarter, 0, False)
+        results.append(scan[1] + scan[0][:, None] * picked)
+    return results
 
 
 def scan_round(scan, arrived, partner_first, bit, last):
@@ -143,19 +165,22 @@
     offset = propagated - jnp.where(leading, jnp.zeros_like(gained_start), gained_start)
     forward = (rate_vec, offset, rate_vec, offset)
     reverse = (jnp.ones_like(rate_vec), jnp.zeros_like(cot_here), rate_vec, rate_vec[None, :, None] * cot_here)
-    for bit in range(rounds):
+    binary = rounds - 2 if rounds >= 2 and lax.axis_size("depth") == 1 << rounds else rounds
+    for bit in range(binary):
         got_f, got_r = exchange(
             (forward[2], reverse[2]), jnp.stack([forward[3], reverse[3]]), "depth", bit
         )
         forward = scan_round(forward, got_f, before, bit, bit == rounds - 1)
         reverse = scan_round(reverse, got_r, after, bit, bit == rounds - 1)
-    passed_in = reverse[1]
+    if binary < rounds:
+        corrected, passed_in = last_two_rounds(forward, reverse, "depth", binary, place)
+    else:
+        corrected, passed_in = forward[1], reverse[1]
     adjoint_here = cot_here + passed_in
     back_start, start_grads = back_block(start_kept, weights, adjoint_here, step_size)
     arriving_bar = passed_along(back_start, "depth", -1)
     relaxed_bar = arriving_bar - passed_in
     back_own, own_grads = back_block(own_kept, weights, relaxed_bar, step_size)
-    corrected = forward[1]
     grad_cpoints = jnp.where(leading, back_own + back_start, back_own)
     grad_weights = dp_sum(start_grads + own_grads, "dp")
     return (corrected[None], grad_cpoints[None], grad_weights)

time: 162 us -> 173 us (1.068)
  the two profiles are of different devices: /device:TPU:2 before, /device:TPU:64 now
where the time goes in v6:
time: 173 us; the launch traced here: 172 us
  waiting for transfers between devices  58.3 us (34%)
  starting transfers between devices  56.5 us (33%)
  other arithmetic  30.5 us (18%)
  local copies, waits for them, and re-layouts  19 us (11%)
  matrix products  5.47 us (3%)
  between operations  2 us (1%)
    ppermute x8, waiting for transfers between devices, exchange(): lax.ppermute(pack(gains, states), axis, [(i, i ^ mask) for i in range(cou...  41.9 us
    ppermute x8, starting transfers between devices, exchange(): lax.ppermute(pack(gains, states), axis, [(i, i ^ mask) for i in range(cou...  32.6 us
    ppermute x3, starting transfers between devices, dp_sum(): lax.ppermute(lax.dynamic_index_in_dim(terms, place ^ k, 0, False), axis,...  10.2 us
    ppermute x3, starting transfers between devices, dp_sum(): lax.ppermute(total, axis, pairs(k))  9.82 us
    unnamed x86, local copies, waits for them, and re-layouts  9.36 us
    ppermute x3, waiting for transfers between devices, dp_sum(): lax.ppermute(lax.dynamic_index_in_dim(terms, place ^ k, 0, False), axis,...  6.74 us
    ppermute x2, waiting for transfers between devices, passed_along(): return lax.ppermute(block, axis, route)  5.66 us
    unnamed x64, other arithmetic  4.68 us
  transfers between devices with their start and end apart: 16, of which 11 were waited for; matrix products, arithmetic and copies ran while one was open for 5% of the time, Pallas kernels for 0%

profile of v6, /device:TPU:64, one launch (start us, length us, event | category | flops | bytes accessed | tf_op | source)
XLA Modules:
  0.0 171.8 jit_solution(4231811633854096361)
XLA Ops:
  0.7 0.9 fusion.214
  5.5 1.9 %collective-permute-start = (f32[1,64,256]{2,1,0:T(8,128)S(1)}, f32[1,64,256]{2,1,0:T(8,128)S(1)}, u32[]{:S(2)}, u32[]{:S(2)}) collective-permute-start(f32[1,64,256]{2,1,0:T(8,128)S(1)} %fusion.11), channel_id=1, source_target_pairs={{0,4},{4,8},{8,12},{12,16},{16,20},{20,24},{24,28},{28,32},{32,36}... | collective-permute-start | bytes 196616 | tf_op jit(solution)/shard_map/ppermute | solution.py:87
  7.6 5.7 %collective-permute-done = f32[1,64,256]{2,1,0:T(8,128)S(1)} collective-permute-done((f32[1,64,256]{2,1,0:T(8,128)S(1)}, f32[1,64,256]{2,1,0:T(8,128)S(1)}, u32[]{:S(2)}, u32[]{:S(2)}) %collective-permute-start) | collective-permute-done | bytes 65568 | tf_op jit(solution)/shard_map/ppermute | solution.py:87
  16.9 1.9 %collective-permute-start.1 = (f32[130,256]{1,0:T(8,128)S(1)}, f32[130,256]{1,0:T(8,128)S(1)}, u32[]{:S(2)}, u32[]{:S(2)}) collective-permute-start(f32[130,256]{1,0:T(8,128)S(1)} %pad_maximum_fusion.1), channel_id=1, source_target_pairs={{0,4},{4,0},{8,12},{12,8},{16,20},{20,16},{24,28},{28,24},{32,36},... | collective-permute-start | bytes 399368 | tf_op jit(solution)/shard_map/ppermute | solution.py:21
  18.8 1.3 collective-permute-done.1
  20.4 0.7 pad_maximum_fusion.2
  21.1 1.9 %collective-permute-start.2 = (f32[130,256]{1,0:T(8,128)}, f32[130,256]{1,0:T(8,128)S(1)}, u32[]{:S(2)}, u32[]{:S(2)}) collective-permute-start(f32[130,256]{1,0:T(8,128)} %pad_maximum_fusion.2), channel_id=1, source_target_pairs={{0,8},{4,12},{8,0},{12,4},{16,24},{20,28},{24,16},{28,20},{32,40},... | collective-permute-start | bytes 399368 | tf_op jit(solution)/shard_map/ppermute | solution.py:21
  23.0 5.9 %collective-permute-done.2 = f32[130,256]{1,0:T(8,128)S(1)} collective-permute-done((f32[130,256]{1,0:T(8,128)}, f32[130,256]{1,0:T(8,128)S(1)}, u32[]{:S(2)}, u32[]{:S(2)}) %collective-permute-start.2) | collective-permute-done | bytes 133152 | tf_op jit(solution)/shard_map/ppermute | solution.py:21
  29.1 0.7 pad_maximum_fusion.3
  29.8 2.8 %collective-permute-start.3 = (f32[130,256]{1,0:T(8,128)}, f32[130,256]{1,0:T(8,128)S(1)}, u32[]{:S(2)}, u32[]{:S(2)}) collective-permute-start(f32[130,256]{1,0:T(8,128)} %pad_maximum_fusion.3), channel_id=1, source_target_pairs={{0,16},{4,20},{8,24},{12,28},{16,0},{20,4},{24,8},{28,12},{32,48},... | collective-permute-start | bytes 399368 | tf_op jit(solution)/shard_map/ppermute | solution.py:21
  33.7 4.8 %collective-permute-done.3 = f32[130,256]{1,0:T(8,128)S(1)} collective-permute-done((f32[130,256]{1,0:T(8,128)}, f32[130,256]{1,0:T(8,128)S(1)}, u32[]{:S(2)}, u32[]{:S(2)}) %collective-permute-start.3) | collective-permute-done | bytes 133152 | tf_op jit(solution)/shard_map/ppermute | solution.py:21
  38.7 0.7 pad_maximum_fusion.4
  39.4 3.8 %collective-permute-start.4 = (f32[130,256]{1,0:T(8,128)}, f32[130,256]{1,0:T(8,128)}, u32[]{:S(2)}, u32[]{:S(2)}) collective-permute-start(f32[130,256]{1,0:T(8,128)} %pad_maximum_fusion.4), channel_id=1, source_target_pairs={{0,32},{4,36},{8,40},{12,44},{16,48},{20,52},{24,56},{28,60},{32,0... | collective-permute-start | bytes 399368 | tf_op jit(solution)/shard_map/ppermute | solution.py:21
  44.5 2.2 %collective-permute-done.4 = f32[130,256]{1,0:T(8,128)} collective-permute-done((f32[130,256]{1,0:T(8,128)}, f32[130,256]{1,0:T(8,128)}, u32[]{:S(2)}, u32[]{:S(2)}) %collective-permute-start.4) | collective-permute-done | bytes 133152 | tf_op jit(solution)/shard_map/ppermute | solution.py:21
  46.6 0.8 fusion.335
  47.4 0.8 slice_bitcast_fusion.13
  48.2 0.9 fusion.209
  49.1 0.9 fusion.340
  50.1 0.7 pad_maximum_fusion.5
  50.7 1.9 %collective-permute-start.5 = (f32[130,256]{1,0:T(8,128)}, f32[130,256]{1,0:T(8,128)}, u32[]{:S(2)}, u32[]{:S(2)}) collective-permute-start(f32[130,256]{1,0:T(8,128)} %pad_maximum_fusion.5), channel_id=1, source_target_pairs={{0,64},{4,68},{8,72},{12,76},{16,80},{20,84},{24,88},{28,92},{32,9... | collective-permute-start | bytes 399368 | tf_op jit(solution)/shard_map/ppermute | solution.py:21
  53.8 5.2 %collective-permute-done.5 = f32[130,256]{1,0:T(8,128)} collective-permute-done((f32[130,256]{1,0:T(8,128)}, f32[130,256]{1,0:T(8,128)}, u32[]{:S(2)}, u32[]{:S(2)}) %collective-permute-start.5) | collective-permute-done | bytes 133152 | tf_op jit(solution)/shard_map/ppermute | solution.py:21
  59.0 1.4 broadcast_select_fusion.3
  60.4 1.3 multiply_multiply_fusion
  61.7 1.0 select_bitcast_fusion
  62.7 0.9 fusion.208
  64.3 11.1 %collective-permute-start.8 = (f32[130,256]{1,0:T(8,128)S(1)}, f32[130,256]{1,0:T(8,128)S(1)}, u32[]{:S(2)}, u32[]{:S(2)}) collective-permute-start(f32[130,256]{1,0:T(8,128)S(1)} %pad_maximum_fusion.6), channel_id=1, source_target_pairs={{0,384},{4,388},{8,392},{12,396},{16,400},{20,404},{24,408},{28,41... | collective-permute-start | bytes 399368 | tf_op jit(solution)/shard_map/ppermute | solution.py:21
  75.3 5.3 %collective-permute-start.7 = (f32[130,256]{1,0:T(8,128)S(1)}, f32[130,256]{1,0:T(8,128)S(1)}, u32[]{:S(2)}, u32[]{:S(2)}) collective-permute-start(f32[130,256]{1,0:T(8,128)S(1)} %pad_maximum_fusion.6), channel_id=1, source_target_pairs={{0,256},{4,260},{8,264},{12,268},{16,272},{20,276},{24,280},{28,28... | collective-permute-start | bytes 399368 | tf_op jit(solution)/shard_map/ppermute | solution.py:21
  80.6 3.9 %collective-permute-start.6 = (f32[130,256]{1,0:T(8,128)S(1)}, f32[130,256]{1,0:T(8,128)S(1)}, u32[]{:S(2)}, u32[]{:S(2)}) collective-permute-start(f32[130,256]{1,0:T(8,128)S(1)} %pad_maximum_fusion.6), channel_id=1, source_target_pairs={{0,128},{4,132},{8,136},{12,140},{16,144},{20,148},{24,152},{28,15... | collective-permute-start | bytes 399368 | tf_op jit(solution)/shard_map/ppermute | solution.py:21
  84.6 1.3 broadcast_select_fusion.8
  85.8 0.7 slice_bitcast_fusion
  86.5 22.5 %collective-permute-done.7 = f32[130,256]{1,0:T(8,128)S(1)} collective-permute-done((f32[130,256]{1,0:T(8,128)S(1)}, f32[130,256]{1,0:T(8,128)S(1)}, u32[]{:S(2)}, u32[]{:S(2)}) %collective-permute-start.7) | collective-permute-done | bytes 133152 | tf_op jit(solution)/shard_map/ppermute | solution.py:21
  109.0 0.7 slice_bitcast_fusion.1
  109.7 0.7 slice_bitcast_fusion.2
  110.4 0.7 gather_fusion.3
  111.1 0.8 fusion.354
  111.9 0.8 fusion.353
  112.7 0.8 fusion.352
  114.1 0.7 gather_fusion.4
  115.4 0.7 gather_fusion.2
  117.3 1.0 maximum_bitcast_fusion
  118.3 1.4 gather_fusion.1
  119.7 1.1 bitcast_select_fusion
  121.6 0.7 copy-done.4
  122.5 1.0 multiply_convert_fusion.7
  124.6 0.8 copy-done.18
  126.2 0.8 copy-done.16
  128.3 1.9 %collective-permute-start.9 = (f32[1,64,256]{2,1,0:T(8,128)S(1)}, f32[1,64,256]{2,1,0:T(8,128)S(1)}, u32[]{:S(2)}, u32[]{:S(2)}) collective-permute-start(f32[1,64,256]{2,1,0:T(8,128)S(1)} %fusion.117), channel_id=1, source_target_pairs={{4,0},{8,4},{12,8},{16,12},{20,16},{24,20},{28,24},{32,28},{36,32}... | collective-permute-start | bytes 196616 | tf_op jit(solution)/shard_map/ppermute | solution.py:87
  131.1 1.6 fusion.51
  133.5 0.8 copy-done.14
  135.0 0.8 copy-done.12
  136.6 0.8 copy-done.10
  138.2 3.5 %collective-permute-start.10 = (f32[64,576]{1,0:T(8,128)S(1)}, f32[64,576]{1,0:T(8,128)S(1)}, u32[]{:S(2)}, u32[]{:S(2)}) collective-permute-start(f32[64,576]{1,0:T(8,128)S(1)} %get-tuple-element.27), channel_id=1, source_target_pairs={{0,1},{1,0},{2,3},{3,2},{4,5},{5,4},{6,7},{7,6},{8,9},{9,8},{10,11... | collective-permute-start | bytes 442376 | tf_op jit(solution)/shard_map/ppermute | solution.py:74
  141.7 4.1 %collective-permute-start.12 = (f32[64,576]{1,0:T(8,128)S(1)}, f32[64,576]{1,0:T(8,128)S(1)}, u32[]{:S(2)}, u32[]{:S(2)}) collective-permute-start(f32[64,576]{1,0:T(8,128)S(1)} %get-tuple-element.28), channel_id=1, source_target_pairs={{0,3},{1,2},{2,1},{3,0},{4,7},{5,6},{6,5},{7,4},{8,11},{9,10},{10,... | collective-permute-start | bytes 442376 | tf_op jit(solution)/shard_map/ppermute | solution.py:74
  145.8 2.6 %collective-permute-start.11 = (f32[64,576]{1,0:T(8,128)S(1)}, f32[64,576]{1,0:T(8,128)S(1)}, u32[]{:S(2)}, u32[]{:S(2)}) collective-permute-start(f32[64,576]{1,0:T(8,128)S(1)} %get-tuple-element.29), channel_id=1, source_target_pairs={{0,2},{1,3},{2,0},{3,1},{4,6},{5,7},{6,4},{7,5},{8,10},{9,11},{10,... | collective-permute-start | bytes 442376 | tf_op jit(solution)/shard_map/ppermute | solution.py:74
  148.5 4.7 %collective-permute-done.12 = f32[64,576]{1,0:T(8,128)S(1)} collective-permute-done((f32[64,576]{1,0:T(8,128)S(1)}, f32[64,576]{1,0:T(8,128)S(1)}, u32[]{:S(2)}, u32[]{:S(2)}) %collective-permute-start.12) | collective-permute-done | bytes 147488 | tf_op jit(solution)/shard_map/ppermute | solution.py:74
  153.2 2.1 %collective-permute-done.11 = f32[64,576]{1,0:T(8,128)S(1)} collective-permute-done((f32[64,576]{1,0:T(8,128)S(1)}, f32[64,576]{1,0:T(8,128)S(1)}, u32[]{:S(2)}, u32[]{:S(2)}) %collective-permute-start.11) | collective-permute-done | bytes 147488 | tf_op jit(solution)/shard_map/ppermute | solution.py:74
  155.3 3.5 %collective-permute-start.15 = (f32[64,576]{1,0:T(8,128)S(1)}, f32[64,576]{1,0:T(8,128)S(1)}, u32[]{:S(2)}, u32[]{:S(2)}) collective-permute-start(f32[64,576]{1,0:T(8,128)S(1)} %fusion.33), channel_id=1, source_target_pairs={{0,3},{1,2},{2,1},{3,0},{4,7},{5,6},{6,5},{7,4},{8,11},{9,10},{10,... | collective-permute-start | bytes 442376 | tf_op jit(solution)/shard_map/ppermute | solution.py:80
  158.8 3.1 %collective-permute-start.14 = (f32[64,576]{1,0:T(8,128)S(1)}, f32[64,576]{1,0:T(8,128)S(1)}, u32[]{:S(2)}, u32[]{:S(2)}) collective-permute-start(f32[64,576]{1,0:T(8,128)S(1)} %fusion.33), channel_id=1, source_target_pairs={{0,2},{1,3},{2,0},{3,1},{4,6},{5,7},{6,4},{7,5},{8,10},{9,11},{10,... | collective-permute-start | bytes 442376 | tf_op jit(solution)/shard_map/ppermute | solution.py:80
  161.9 3.3 %collective-permute-start.13 = (f32[64,576]{1,0:T(8,128)S(1)}, f32[64,576]{1,0:T(8,128)S(1)}, u32[]{:S(2)}, u32[]{:S(2)}) collective-permute-start(f32[64,576]{1,0:T(8,128)S(1)} %fusion.33), channel_id=1, source_target_pairs={{0,1},{1,0},{2,3},{3,2},{4,5},{5,4},{6,7},{7,6},{8,9},{9,8},{10,11... | collective-permute-start | bytes 442376 | tf_op jit(solution)/shard_map/ppermute | solution.py:80
  165.1 0.8 fusion.213
  166.0 3.1 %collective-permute-done.14 = f32[64,576]{1,0:T(8,128)S(1)} collective-permute-done((f32[64,576]{1,0:T(8,128)S(1)}, f32[64,576]{1,0:T(8,128)S(1)}, u32[]{:S(2)}, u32[]{:S(2)}) %collective-permute-start.14) | collective-permute-done | bytes 147488 | tf_op jit(solution)/shard_map/ppermute | solution.py:80
  169.1 0.9 collective-permute-done.13
  170.1 0.7 gather_fusion
  170.8 1.0 broadcast_select_fusion
  (251 shorter events, 22.6 us)
Async XLA Ops:
  0.7 1.3 copy-start.1
  1.6 1.0 copy-start
  2.8 0.7 copy-start.9
  3.7 0.7 copy-start.11
  4.6 0.7 copy-start.13
  5.3 2.1 %copy-start.2 = (f32[1,1,64,256]{3,2,1,0:T(8,128)S(1)}, f32[1,1,64,256]{3,2,1,0:T(8,128)}, u32[]{:S(2)}) copy-start(f32[1,1,64,256]{3,2,1,0:T(8,128)} %param.11) | copy-start | bytes 196612
  5.5 2.0 %copy-start.23 = (f32[1,64]{1,0:T(1,128)S(1)}, f32[1,64]{1,0:T(1,128)}, u32[]{:S(2)}) copy-start(f32[1,64]{1,0:T(1,128)} %param.10) | copy-start | bytes 772
  5.5 7.7 %collective-permute-start = (f32[1,64,256]{2,1,0:T(8,128)S(1)}, f32[1,64,256]{2,1,0:T(8,128)S(1)}, u32[]{:S(2)}, u32[]{:S(2)}) collective-permute-start(f32[1,64,256]{2,1,0:T(8,128)S(1)} %fusion.11), channel_id=1, source_target_pairs={{0,4},{4,8},{8,12},{12,16},{16,20},{20,24},{24,28},{28,32},{32,36}... | collective-permute-start | bytes 196616 | tf_op jit(solution)/shard_map/ppermute | solution.py:87
  14.1 0.7 copy-start.15
  15.0 0.7 copy-start.17
  16.9 3.3 %collective-permute-start.1 = (f32[130,256]{1,0:T(8,128)S(1)}, f32[130,256]{1,0:T(8,128)S(1)}, u32[]{:S(2)}, u32[]{:S(2)}) collective-permute-start(f32[130,256]{1,0:T(8,128)S(1)} %pad_maximum_fusion.1), channel_id=1, source_target_pairs={{0,4},{4,0},{8,12},{12,8},{16,20},{20,16},{24,28},{28,24},{32,36},... | collective-permute-start | bytes 399368 | tf_op jit(solution)/shard_map/ppermute | solution.py:21
  20.1 8.8 %copy-start.7 = (f32[130,256]{1,0:T(8,128)}, f32[130,256]{1,0:T(8,128)S(1)}, u32[]{:S(2)}) copy-start(f32[130,256]{1,0:T(8,128)S(1)} %collective-permute-done.1) | copy-start | bytes 399364
  21.1 7.8 %collective-permute-start.2 = (f32[130,256]{1,0:T(8,128)}, f32[130,256]{1,0:T(8,128)S(1)}, u32[]{:S(2)}, u32[]{:S(2)}) collective-permute-start(f32[130,256]{1,0:T(8,128)} %pad_maximum_fusion.2), channel_id=1, source_target_pairs={{0,8},{4,12},{8,0},{12,4},{16,24},{20,28},{24,16},{28,20},{32,40},... | collective-permute-start | bytes 399368 | tf_op jit(solution)/shard_map/ppermute | solution.py:21
  28.9 55.7 %copy-start.3 = (f32[130,256]{1,0:T(8,128)}, f32[130,256]{1,0:T(8,128)S(1)}, u32[]{:S(2)}) copy-start(f32[130,256]{1,0:T(8,128)S(1)} %collective-permute-done.2) | copy-start | bytes 399364
  29.8 8.7 %collective-permute-start.3 = (f32[130,256]{1,0:T(8,128)}, f32[130,256]{1,0:T(8,128)S(1)}, u32[]{:S(2)}, u32[]{:S(2)}) collective-permute-start(f32[130,256]{1,0:T(8,128)} %pad_maximum_fusion.3), channel_id=1, source_target_pairs={{0,16},{4,20},{8,24},{12,28},{16,0},{20,4},{24,8},{28,12},{32,48},... | collective-permute-start | bytes 399368 | tf_op jit(solution)/shard_map/ppermute | solution.py:21
  38.5 46.1 %copy-start.5 = (f32[130,256]{1,0:T(8,128)}, f32[130,256]{1,0:T(8,128)S(1)}, u32[]{:S(2)}) copy-start(f32[130,256]{1,0:T(8,128)S(1)} %collective-permute-done.3) | copy-start | bytes 399364
  39.4 7.3 %collective-permute-start.4 = (f32[130,256]{1,0:T(8,128)}, f32[130,256]{1,0:T(8,128)}, u32[]{:S(2)}, u32[]{:S(2)}) collective-permute-start(f32[130,256]{1,0:T(8,128)} %pad_maximum_fusion.4), channel_id=1, source_target_pairs={{0,32},{4,36},{8,40},{12,44},{16,48},{20,52},{24,56},{28,60},{32,0... | collective-permute-start | bytes 399368 | tf_op jit(solution)/shard_map/ppermute | solution.py:21
  43.2 0.7 copy-start.42
  50.7 8.3 %collective-permute-start.5 = (f32[130,256]{1,0:T(8,128)}, f32[130,256]{1,0:T(8,128)}, u32[]{:S(2)}, u32[]{:S(2)}) collective-permute-start(f32[130,256]{1,0:T(8,128)} %pad_maximum_fusion.5), channel_id=1, source_target_pairs={{0,64},{4,68},{8,72},{12,76},{16,80},{20,84},{24,88},{28,92},{32,9... | collective-permute-start | bytes 399368 | tf_op jit(solution)/shard_map/ppermute | solution.py:21
  63.6 0.6 copy-start.19
  64.3 21.6 %collective-permute-start.8 = (f32[130,256]{1,0:T(8,128)S(1)}, f32[130,256]{1,0:T(8,128)S(1)}, u32[]{:S(2)}, u32[]{:S(2)}) collective-permute-start(f32[130,256]{1,0:T(8,128)S(1)} %pad_maximum_fusion.6), channel_id=1, source_target_pairs={{0,384},{4,388},{8,392},{12,396},{16,400},{20,404},{24,408},{28,41... | collective-permute-start | bytes 399368 | tf_op jit(solution)/shard_map/ppermute | solution.py:21
  75.3 33.7 %collective-permute-start.7 = (f32[130,256]{1,0:T(8,128)S(1)}, f32[130,256]{1,0:T(8,128)S(1)}, u32[]{:S(2)}, u32[]{:S(2)}) collective-permute-start(f32[130,256]{1,0:T(8,128)S(1)} %pad_maximum_fusion.6), channel_id=1, source_target_pairs={{0,256},{4,260},{8,264},{12,268},{16,272},{20,276},{24,280},{28,28... | collective-permute-start | bytes 399368 | tf_op jit(solution)/shard_map/ppermute | solution.py:21
  80.6 29.1 %collective-permute-start.6 = (f32[130,256]{1,0:T(8,128)S(1)}, f32[130,256]{1,0:T(8,128)S(1)}, u32[]{:S(2)}, u32[]{:S(2)}) collective-permute-start(f32[130,256]{1,0:T(8,128)S(1)} %pad_maximum_fusion.6), channel_id=1, source_target_pairs={{0,128},{4,132},{8,136},{12,140},{16,144},{20,148},{24,152},{28,15... | collective-permute-start | bytes 399368 | tf_op jit(solution)/shard_map/ppermute | solution.py:21
  85.8 23.9 %copy-start.20 = (f32[130,256]{1,0:T(8,128)}, f32[130,256]{1,0:T(8,128)S(1)}, u32[]{:S(2)}) copy-start(f32[130,256]{1,0:T(8,128)S(1)} %collective-permute-done.8) | copy-start | bytes 399364
  109.0 1.4 copy-start.21
  109.7 0.7 copy-start.22
  113.4 0.6 copy-start.30
  114.7 0.6 copy-start.29
  115.4 0.7 copy-start.25
  120.8 0.7 copy-start.26
  120.8 0.7 copy-start.27
  120.8 0.7 copy-start.28
  121.4 0.9 copy-start.4
  121.5 1.0 copy-start.6
  121.5 1.0 copy-start.8
  121.6 0.9 copy-start.36
  121.6 0.9 copy-start.37
  121.6 0.9 copy-start.38
  121.6 0.9 copy-start.39
  121.6 0.9 copy-start.40
  124.6 0.8 copy-start.18
  126.1 0.8 copy-start.16
  127.4 0.7 copy-start.24
  128.3 4.6 %collective-permute-start.9 = (f32[1,64,256]{2,1,0:T(8,128)S(1)}, f32[1,64,256]{2,1,0:T(8,128)S(1)}, u32[]{:S(2)}, u32[]{:S(2)}) collective-permute-start(f32[1,64,256]{2,1,0:T(8,128)S(1)} %fusion.117), channel_id=1, source_target_pairs={{4,0},{8,4},{12,8},{16,12},{20,16},{24,20},{28,24},{32,28},{36,32}... | collective-permute-start | bytes 196616 | tf_op jit(solution)/shard_map/ppermute | solution.py:87
  130.3 0.6 copy-start.34
  130.3 0.7 copy-start.35
  130.4 0.6 copy-start.31
  130.4 0.6 copy-start.32
  130.4 0.7 copy-start.33
  133.4 0.8 copy-start.14
  135.0 0.8 copy-start.12
  136.5 0.8 copy-start.10
  138.2 10.3 %collective-permute-start.10 = (f32[64,576]{1,0:T(8,128)S(1)}, f32[64,576]{1,0:T(8,128)S(1)}, u32[]{:S(2)}, u32[]{:S(2)}) collective-permute-start(f32[64,576]{1,0:T(8,128)S(1)} %get-tuple-element.27), channel_id=1, source_target_pairs={{0,1},{1,0},{2,3},{3,2},{4,5},{5,4},{6,7},{7,6},{8,9},{9,8},{10,11... | collective-permute-start | bytes 442376 | tf_op jit(solution)/shard_map/ppermute | solution.py:74
  141.7 11.5 %collective-permute-start.12 = (f32[64,576]{1,0:T(8,128)S(1)}, f32[64,576]{1,0:T(8,128)S(1)}, u32[]{:S(2)}, u32[]{:S(2)}) collective-permute-start(f32[64,576]{1,0:T(8,128)S(1)} %get-tuple-element.28), channel_id=1, source_target_pairs={{0,3},{1,2},{2,1},{3,0},{4,7},{5,6},{6,5},{7,4},{8,11},{9,10},{10,... | collective-permute-start | bytes 442376 | tf_op jit(solution)/shard_map/ppermute | solution.py:74
  145.8 9.4 %collective-permute-start.11 = (f32[64,576]{1,0:T(8,128)S(1)}, f32[64,576]{1,0:T(8,128)S(1)}, u32[]{:S(2)}, u32[]{:S(2)}) collective-permute-start(f32[64,576]{1,0:T(8,128)S(1)} %get-tuple-element.29), channel_id=1, source_target_pairs={{0,2},{1,3},{2,0},{3,1},{4,6},{5,7},{6,4},{7,5},{8,10},{9,11},{10,... | collective-permute-start | bytes 442376 | tf_op jit(solution)/shard_map/ppermute | solution.py:74
  155.3 10.7 %collective-permute-start.15 = (f32[64,576]{1,0:T(8,128)S(1)}, f32[64,576]{1,0:T(8,128)S(1)}, u32[]{:S(2)}, u32[]{:S(2)}) collective-permute-start(f32[64,576]{1,0:T(8,128)S(1)} %fusion.33), channel_id=1, source_target_pairs={{0,3},{1,2},{2,1},{3,0},{4,7},{5,6},{6,5},{7,4},{8,11},{9,10},{10,... | collective-permute-start | bytes 442376 | tf_op jit(solution)/shard_map/ppermute | solution.py:80
  158.8 10.3 %collective-permute-start.14 = (f32[64,576]{1,0:T(8,128)S(1)}, f32[64,576]{1,0:T(8,128)S(1)}, u32[]{:S(2)}, u32[]{:S(2)}) collective-permute-start(f32[64,576]{1,0:T(8,128)S(1)} %fusion.33), channel_id=1, source_target_pairs={{0,2},{1,3},{2,0},{3,1},{4,6},{5,7},{6,4},{7,5},{8,10},{9,11},{10,... | collective-permute-start | bytes 442376 | tf_op jit(solution)/shard_map/ppermute | solution.py:80
  161.9 8.1 %collective-permute-start.13 = (f32[64,576]{1,0:T(8,128)S(1)}, f32[64,576]{1,0:T(8,128)S(1)}, u32[]{:S(2)}, u32[]{:S(2)}) collective-permute-start(f32[64,576]{1,0:T(8,128)S(1)} %fusion.33), channel_id=1, source_target_pairs={{0,1},{1,0},{2,3},{3,2},{4,5},{5,4},{6,7},{7,6},{8,9},{9,8},{10,11... | collective-permute-start | bytes 442376 | tf_op jit(solution)/shard_map/ppermute | solution.py:80
  170.1 0.7 copy-start.41

commit v7 on v5

--- a/solution.py
+++ b/solution.py
@@ -157,7 +157,11 @@
     back_own, own_grads = back_block(own_kept, weights, relaxed_bar, step_size)
     corrected = forward[1]
     grad_cpoints = jnp.where(leading, back_own + back_start, back_own)
-    grad_weights = dp_sum(start_grads + own_grads, "dp")
+    grad_weights = lax.all_gather(
+        lax.psum_scatter(start_grads + own_grads, "dp", scatter_dimension=0, tiled=True),
+        "dp",
+        tiled=True,
+    )
     return (corrected[None], grad_cpoints[None], grad_weights)
 
 

time: 162 us -> 185 us (1.14)
  the two profiles are of different devices: /device:TPU:2 before, /device:TPU:4 now
where the time goes in v7:
time: 185 us; the launch traced here: 184 us
  waiting for transfers between devices  68.4 us (37%)
  starting transfers between devices  47.7 us (26%)
  other arithmetic  25.6 us (14%)
  between operations  15.1 us (8%)
  blocking collectives  13.6 us (7%)
  local copies, waits for them, and re-layouts  8.34 us (5%)
  matrix products  5.49 us (3%)
    ppermute x7, starting transfers between devices, exchange(): lax.ppermute(pack(gains, states), axis, [(i, i ^ 1 << bit) for i in range...  40.1 us
    ppermute x7, waiting for transfers between devices, exchange(): lax.ppermute(pack(gains, states), axis, [(i, i ^ 1 << bit) for i in range...  39 us
    reduce_scatter x1, waiting for transfers between devices, body(): lax.psum_scatter(start_grads + own_grads, 'dp', scatter_dimension=0, tile...  24.1 us
    all_gather x1, blocking collectives, body(): lax.all_gather(lax.psum_scatter(start_grads + own_grads, 'dp', scatter_di...  13.6 us
    ppermute x2, starting transfers between devices, passed_along(): return lax.ppermute(block, axis, route)  7.5 us
    unnamed x39, local copies, waits for them, and re-layouts  5.69 us
    ppermute x2, waiting for transfers between devices, passed_along(): return lax.ppermute(block, axis, route)  5.22 us
    unnamed x64, other arithmetic  4.68 us
  transfers between devices with their start and end apart: 10, of which 10 were waited for; matrix products, arithmetic and copies ran while one was open for 2% of the time, Pallas kernels for 0%

profile of v7, /device:TPU:4, one launch (start us, length us, event | category | flops | bytes accessed | tf_op | source)
XLA Modules:
  0.0 184.2 jit_solution(12041811993292943909)
XLA Ops:
  7.2 0.9 fusion.202
  8.9 0.3 copy-done
  12.1 1.9 %collective-permute-start = (f32[1,64,256]{2,1,0:T(8,128)S(1)}, f32[1,64,256]{2,1,0:T(8,128)S(1)}, u32[]{:S(2)}, u32[]{:S(2)}) collective-permute-start(f32[1,64,256]{2,1,0:T(8,128)S(1)} %fusion.11), channel_id=1, source_target_pairs={{0,4},{4,8},{8,12},{12,16},{16,20},{20,24},{24,28},{28,32},{32,36}... | collective-permute-start | bytes 196616 | tf_op jit(solution)/shard_map/ppermute | solution.py:65
  14.1 3.5 %collective-permute-done = f32[1,64,256]{2,1,0:T(8,128)S(1)} collective-permute-done((f32[1,64,256]{2,1,0:T(8,128)S(1)}, f32[1,64,256]{2,1,0:T(8,128)S(1)}, u32[]{:S(2)}, u32[]{:S(2)}) %collective-permute-start) | collective-permute-done | bytes 65568 | tf_op jit(solution)/shard_map/ppermute | solution.py:65
  21.4 1.9 %collective-permute-start.1 = (f32[130,256]{1,0:T(8,128)S(1)}, f32[130,256]{1,0:T(8,128)S(1)}, u32[]{:S(2)}, u32[]{:S(2)}) collective-permute-start(f32[130,256]{1,0:T(8,128)S(1)} %pad_maximum_fusion), channel_id=1, source_target_pairs={{0,4},{4,0},{8,12},{12,8},{16,20},{20,16},{24,28},{28,24},{32,36},... | collective-permute-start | bytes 399368 | tf_op jit(solution)/shard_map/ppermute | solution.py:20
  23.3 1.3 collective-permute-done.1
  24.9 3.1 %collective-permute-start.2 = (f32[130,256]{1,0:T(8,128)S(1)}, f32[130,256]{1,0:T(8,128)S(1)}, u32[]{:S(2)}, u32[]{:S(2)}) collective-permute-start(f32[130,256]{1,0:T(8,128)S(1)} %pad_maximum_fusion.1), channel_id=1, source_target_pairs={{0,8},{4,12},{8,0},{12,4},{16,24},{20,28},{24,16},{28,20},{32,40},... | collective-permute-start | bytes 399368 | tf_op jit(solution)/shard_map/ppermute | solution.py:20
  28.0 4.5 %collective-permute-done.2 = f32[130,256]{1,0:T(8,128)S(1)} collective-permute-done((f32[130,256]{1,0:T(8,128)S(1)}, f32[130,256]{1,0:T(8,128)S(1)}, u32[]{:S(2)}, u32[]{:S(2)}) %collective-permute-start.2) | collective-permute-done | bytes 133152 | tf_op jit(solution)/shard_map/ppermute | solution.py:20
  32.8 0.7 pad_maximum_fusion.2
  33.4 4.6 %collective-permute-start.3 = (f32[130,256]{1,0:T(8,128)}, f32[130,256]{1,0:T(8,128)S(1)}, u32[]{:S(2)}, u32[]{:S(2)}) collective-permute-start(f32[130,256]{1,0:T(8,128)} %pad_maximum_fusion.2), channel_id=1, source_target_pairs={{0,16},{4,20},{8,24},{12,28},{16,0},{20,4},{24,8},{28,12},{32,48},... | collective-permute-start | bytes 399368 | tf_op jit(solution)/shard_map/ppermute | solution.py:20
  38.0 4.0 %collective-permute-done.3 = f32[130,256]{1,0:T(8,128)S(1)} collective-permute-done((f32[130,256]{1,0:T(8,128)}, f32[130,256]{1,0:T(8,128)S(1)}, u32[]{:S(2)}, u32[]{:S(2)}) %collective-permute-start.3) | collective-permute-done | bytes 133152 | tf_op jit(solution)/shard_map/ppermute | solution.py:20
  42.4 0.7 pad_maximum_fusion.3
  43.0 3.8 %collective-permute-start.4 = (f32[130,256]{1,0:T(8,128)}, f32[130,256]{1,0:T(8,128)}, u32[]{:S(2)}, u32[]{:S(2)}) collective-permute-start(f32[130,256]{1,0:T(8,128)} %pad_maximum_fusion.3), channel_id=1, source_target_pairs={{0,32},{4,36},{8,40},{12,44},{16,48},{20,52},{24,56},{28,60},{32,0... | collective-permute-start | bytes 399368 | tf_op jit(solution)/shard_map/ppermute | solution.py:20
  46.9 3.4 %collective-permute-done.4 = f32[130,256]{1,0:T(8,128)} collective-permute-done((f32[130,256]{1,0:T(8,128)}, f32[130,256]{1,0:T(8,128)}, u32[]{:S(2)}, u32[]{:S(2)}) %collective-permute-start.4) | collective-permute-done | bytes 133152 | tf_op jit(solution)/shard_map/ppermute | solution.py:20
  50.3 0.8 fusion.322
  51.0 0.8 slice_bitcast_fusion.5
  51.8 0.9 fusion.197
  52.8 0.9 fusion.329
  53.7 0.7 pad_maximum_fusion.4
  54.4 5.2 %collective-permute-start.5 = (f32[130,256]{1,0:T(8,128)}, f32[130,256]{1,0:T(8,128)}, u32[]{:S(2)}, u32[]{:S(2)}) collective-permute-start(f32[130,256]{1,0:T(8,128)} %pad_maximum_fusion.4), channel_id=1, source_target_pairs={{0,64},{4,68},{8,72},{12,76},{16,80},{20,84},{24,88},{28,92},{32,9... | collective-permute-start | bytes 399368 | tf_op jit(solution)/shard_map/ppermute | solution.py:20
  59.6 3.3 %collective-permute-done.5 = f32[130,256]{1,0:T(8,128)} collective-permute-done((f32[130,256]{1,0:T(8,128)}, f32[130,256]{1,0:T(8,128)}, u32[]{:S(2)}, u32[]{:S(2)}) %collective-permute-start.5) | collective-permute-done | bytes 133152 | tf_op jit(solution)/shard_map/ppermute | solution.py:20
  62.9 0.8 fusion.324
  63.7 0.8 slice_bitcast_fusion.3
  64.4 1.0 add_select_fusion.13
  65.4 0.9 fusion.332
  66.4 0.7 pad_maximum_fusion.5
  67.1 9.1 %collective-permute-start.6 = (f32[130,256]{1,0:T(8,128)}, f32[130,256]{1,0:T(8,128)}, u32[]{:S(2)}, u32[]{:S(2)}) collective-permute-start(f32[130,256]{1,0:T(8,128)} %pad_maximum_fusion.5), channel_id=1, source_target_pairs={{0,128},{4,132},{8,136},{12,140},{16,144},{20,148},{24,152},{28,15... | collective-permute-start | bytes 399368 | tf_op jit(solution)/shard_map/ppermute | solution.py:20
  76.3 11.1 %collective-permute-done.6 = f32[130,256]{1,0:T(8,128)} collective-permute-done((f32[130,256]{1,0:T(8,128)}, f32[130,256]{1,0:T(8,128)}, u32[]{:S(2)}, u32[]{:S(2)}) %collective-permute-start.6) | collective-permute-done | bytes 133152 | tf_op jit(solution)/shard_map/ppermute | solution.py:20
  87.3 1.3 broadcast_select_fusion
  88.6 0.8 slice_bitcast_fusion.1
  89.4 1.0 select_bitcast_fusion
  90.3 1.0 fusion.195
  91.3 0.7 pad_maximum_fusion.6
  92.0 12.4 %collective-permute-start.7 = (f32[130,256]{1,0:T(8,128)}, f32[130,256]{1,0:T(8,128)}, u32[]{:S(2)}, u32[]{:S(2)}) collective-permute-start(f32[130,256]{1,0:T(8,128)} %pad_maximum_fusion.6), channel_id=1, source_target_pairs={{0,256},{4,260},{8,264},{12,268},{16,272},{20,276},{24,280},{28,28... | collective-permute-start | bytes 399368 | tf_op jit(solution)/shard_map/ppermute | solution.py:20
  104.4 11.3 %collective-permute-done.7 = f32[130,256]{1,0:T(8,128)} collective-permute-done((f32[130,256]{1,0:T(8,128)}, f32[130,256]{1,0:T(8,128)}, u32[]{:S(2)}, u32[]{:S(2)}) %collective-permute-start.7) | collective-permute-done | bytes 133152 | tf_op jit(solution)/shard_map/ppermute | solution.py:20
  115.7 0.6 copy-done.17
  116.3 1.1 multiply_convert_fusion.7
  117.4 0.3 convolution_bitcast_fusion.7
  117.7 0.2 fusion.59
  118.2 0.3 convolution_bitcast_fusion.6
  118.5 0.8 copy-done.14
  119.5 0.2 convolution_bitcast_fusion.14
  119.7 0.3 convolution_bitcast_fusion.5
  120.1 0.8 copy-done.12
  120.8 0.2 fusion.95
  121.3 0.3 convolution_bitcast_fusion.4
  121.6 0.2 fusion.113
  121.8 5.6 %collective-permute-start.8 = (f32[1,64,256]{2,1,0:T(8,128)S(1)}, f32[1,64,256]{2,1,0:T(8,128)S(1)}, u32[]{:S(2)}, u32[]{:S(2)}) collective-permute-start(f32[1,64,256]{2,1,0:T(8,128)S(1)} %fusion.113), channel_id=1, source_target_pairs={{4,0},{8,4},{12,8},{16,12},{20,16},{24,20},{28,24},{32,28},{36,32}... | collective-permute-start | bytes 196616 | tf_op jit(solution)/shard_map/ppermute | solution.py:65
  127.6 1.7 collective-permute-done.8
  129.5 0.3 convolution_bitcast_fusion.3
  129.9 0.8 copy-done.10
  130.7 0.2 fusion.131
  131.1 0.3 convolution_bitcast_fusion.2
  131.4 0.8 copy-done.8
  132.6 0.3 convolution_bitcast_fusion.1
  133.0 0.8 copy-done.6
  134.2 0.9 maximum_add_fusion
  135.1 0.7 broadcast_select_fusion.6
  135.9 1.7 fusion.48
  137.6 0.3 convolution_bitcast_fusion
  137.9 0.8 fusion.201
  138.7 24.1 %reduce-scatter.2.cloned.1.call-done = f32[1,64,576]{2,1,0:T(8,128)} async-done(((f32[4,64,576]{2,1,0:T(8,128)}), f32[1,64,576]{2,1,0:T(8,128)}) %reduce-scatter.2.cloned.1.call-update) | async-done | bytes 147472 | tf_op jit(solution)/shard_map/reduce_scatter | solution.py:161
  162.9 13.6 %all_gather.3 = f32[4,64,576]{2,1,0:T(8,128)S(1)} all-gather(f32[1,64,576]{2,1,0:T(8,128)} %reduce-scatter.2.cloned.1.call-done), channel_id=1, replica_groups=mesh['depth'=128,'dp'=4] {'dp'}, dimensions={0}, use_global_device_ids=true | all-gather | bytes 737280 | tf_op jit(solution)/shard_map/all_gather | solution.py:160
  176.5 0.8 copy.72
  (170 shorter events, 10.3 us)
Async XLA Ops:
  7.2 155.7 %reduce-scatter.2.cloned.1.call-start = ((), (), s32[]{:S(2)}) async-start(), calls=%async_computation.1 | async-start | bytes 819200 | tf_op jit(solution)/shard_map/reduce_scatter | solution.py:161
  7.2 1.3 copy-start.1
  8.2 1.0 copy-start
  9.3 0.7 copy-start.5
  10.3 0.7 copy-start.7
  11.2 0.7 copy-start.9
  11.9 2.1 %copy-start.2 = (f32[1,1,64,256]{3,2,1,0:T(8,128)S(1)}, f32[1,1,64,256]{3,2,1,0:T(8,128)}, u32[]{:S(2)}) copy-start(f32[1,1,64,256]{3,2,1,0:T(8,128)} %param.7) | copy-start | bytes 196612
  12.1 2.0 %copy-start.16 = (f32[1,64]{1,0:T(1,128)S(1)}, f32[1,64]{1,0:T(1,128)}, u32[]{:S(2)}) copy-start(f32[1,64]{1,0:T(1,128)} %param.6) | copy-start | bytes 772
  12.1 5.6 %collective-permute-start = (f32[1,64,256]{2,1,0:T(8,128)S(1)}, f32[1,64,256]{2,1,0:T(8,128)S(1)}, u32[]{:S(2)}, u32[]{:S(2)}) collective-permute-start(f32[1,64,256]{2,1,0:T(8,128)S(1)} %fusion.11), channel_id=1, source_target_pairs={{0,4},{4,8},{8,12},{12,16},{16,20},{20,24},{24,28},{28,32},{32,36}... | collective-permute-start | bytes 196616 | tf_op jit(solution)/shard_map/ppermute | solution.py:65
  18.6 0.7 copy-start.11
  19.5 0.7 copy-start.13
  21.4 3.3 %collective-permute-start.1 = (f32[130,256]{1,0:T(8,128)S(1)}, f32[130,256]{1,0:T(8,128)S(1)}, u32[]{:S(2)}, u32[]{:S(2)}) collective-permute-start(f32[130,256]{1,0:T(8,128)S(1)} %pad_maximum_fusion), channel_id=1, source_target_pairs={{0,4},{4,0},{8,12},{12,8},{16,20},{20,16},{24,28},{28,24},{32,36},... | collective-permute-start | bytes 399368 | tf_op jit(solution)/shard_map/ppermute | solution.py:20
  24.6 7.9 %copy-start.3 = (f32[130,256]{1,0:T(8,128)}, f32[130,256]{1,0:T(8,128)S(1)}, u32[]{:S(2)}) copy-start(f32[130,256]{1,0:T(8,128)S(1)} %collective-permute-done.1) | copy-start | bytes 399364
  24.9 7.6 %collective-permute-start.2 = (f32[130,256]{1,0:T(8,128)S(1)}, f32[130,256]{1,0:T(8,128)S(1)}, u32[]{:S(2)}, u32[]{:S(2)}) collective-permute-start(f32[130,256]{1,0:T(8,128)S(1)} %pad_maximum_fusion.1), channel_id=1, source_target_pairs={{0,8},{4,12},{8,0},{12,4},{16,24},{20,28},{24,16},{28,20},{32,40},... | collective-permute-start | bytes 399368 | tf_op jit(solution)/shard_map/ppermute | solution.py:20
  33.4 8.7 %collective-permute-start.3 = (f32[130,256]{1,0:T(8,128)}, f32[130,256]{1,0:T(8,128)S(1)}, u32[]{:S(2)}, u32[]{:S(2)}) collective-permute-start(f32[130,256]{1,0:T(8,128)} %pad_maximum_fusion.2), channel_id=1, source_target_pairs={{0,16},{4,20},{8,24},{12,28},{16,0},{20,4},{24,8},{28,12},{32,48},... | collective-permute-start | bytes 399368 | tf_op jit(solution)/shard_map/ppermute | solution.py:20
  43.0 7.3 %collective-permute-start.4 = (f32[130,256]{1,0:T(8,128)}, f32[130,256]{1,0:T(8,128)}, u32[]{:S(2)}, u32[]{:S(2)}) collective-permute-start(f32[130,256]{1,0:T(8,128)} %pad_maximum_fusion.3), channel_id=1, source_target_pairs={{0,32},{4,36},{8,40},{12,44},{16,48},{20,52},{24,56},{28,60},{32,0... | collective-permute-start | bytes 399368 | tf_op jit(solution)/shard_map/ppermute | solution.py:20
  54.4 8.5 %collective-permute-start.5 = (f32[130,256]{1,0:T(8,128)}, f32[130,256]{1,0:T(8,128)}, u32[]{:S(2)}, u32[]{:S(2)}) collective-permute-start(f32[130,256]{1,0:T(8,128)} %pad_maximum_fusion.4), channel_id=1, source_target_pairs={{0,64},{4,68},{8,72},{12,76},{16,80},{20,84},{24,88},{28,92},{32,9... | collective-permute-start | bytes 399368 | tf_op jit(solution)/shard_map/ppermute | solution.py:20
  65.4 1.0 copy-start.15
  66.4 20.9 %copy-start.4 = (f32[130,256]{1,0:T(8,128)S(1)}, f32[130,256]{1,0:T(8,128)}, u32[]{:S(2)}) copy-start(f32[130,256]{1,0:T(8,128)} %copy-done.3) | copy-start | bytes 399364
  67.1 20.2 %collective-permute-start.6 = (f32[130,256]{1,0:T(8,128)}, f32[130,256]{1,0:T(8,128)}, u32[]{:S(2)}, u32[]{:S(2)}) collective-permute-start(f32[130,256]{1,0:T(8,128)} %pad_maximum_fusion.5), channel_id=1, source_target_pairs={{0,128},{4,132},{8,136},{12,140},{16,144},{20,148},{24,152},{28,15... | collective-permute-start | bytes 399368 | tf_op jit(solution)/shard_map/ppermute | solution.py:20
  92.0 23.7 %collective-permute-start.7 = (f32[130,256]{1,0:T(8,128)}, f32[130,256]{1,0:T(8,128)}, u32[]{:S(2)}, u32[]{:S(2)}) collective-permute-start(f32[130,256]{1,0:T(8,128)} %pad_maximum_fusion.6), channel_id=1, source_target_pairs={{0,256},{4,260},{8,264},{12,268},{16,272},{20,276},{24,280},{28,28... | collective-permute-start | bytes 399368 | tf_op jit(solution)/shard_map/ppermute | solution.py:20
  115.7 0.6 copy-start.17
  115.7 0.6 copy-start.18
  118.5 0.8 copy-start.14
  120.0 0.8 copy-start.12
  121.8 7.5 %collective-permute-start.8 = (f32[1,64,256]{2,1,0:T(8,128)S(1)}, f32[1,64,256]{2,1,0:T(8,128)S(1)}, u32[]{:S(2)}, u32[]{:S(2)}) collective-permute-start(f32[1,64,256]{2,1,0:T(8,128)S(1)} %fusion.113), channel_id=1, source_target_pairs={{4,0},{8,4},{12,8},{16,12},{20,16},{24,20},{28,24},{32,28},{36,32}... | collective-permute-start | bytes 196616 | tf_op jit(solution)/shard_map/ppermute | solution.py:65
  129.8 0.8 copy-start.10
  131.4 0.8 copy-start.8
  132.9 0.8 copy-start.6
Sparse Core Ops, SparseCore 0:
  135.3 27.5 reduce-scatter.1

commit v8 on v5

--- a/solution.py
+++ b/solution.py
@@ -2,6 +2,8 @@
 import jax.numpy as jnp
 from jax import lax
 from jax.sharding import PartitionSpec as P
+from jax.experimental import pallas as pl
+from jax.experimental.pallas import tpu as pltpu
 
 WID = 16
 
@@ -40,6 +42,43 @@
         )
         whole_gain = whole_gain * got_gain
     return (part_gain, part_state, whole_gain, whole_state)
+
+
+def round_kernel(take_ref, got_ref, part_ref, whole_ref, part_out, whole_out):
+    channels = (got_ref.shape[0] - 2) // 2
+    width = got_ref.shape[1]
+    first = take_ref[0] == 1
+    rows = lax.broadcasted_iota(jnp.int32, (channels, width), 0)
+    lanes = lax.broadcasted_iota(jnp.int32, (channels, width), 1)
+
+    def column(row):
+        return jnp.sum(jnp.where(rows == lanes, jnp.broadcast_to(row, (channels, width)), 0.0), axis=1, keepdims=True)
+
+    for k, take in enumerate((first, jnp.logical_not(first))):
+        band = pl.ds(k * channels, channels)
+        grow = pl.ds(2 * channels + k, 1)
+        got_state, got_row = got_ref[band, :], got_ref[grow, :]
+        part_state, part_row = part_ref[band, :], part_ref[grow, :]
+        whole_state, whole_row = whole_ref[band, :], whole_ref[grow, :]
+        part_out[band, :] = jnp.where(take, part_state + column(part_row) * got_state, part_state)
+        part_out[grow, :] = jnp.where(take, part_row * got_row, part_row)
+        whole_out[band, :] = jnp.where(
+            take,
+            whole_state + column(whole_row) * got_state,
+            got_state + column(got_row) * whole_state,
+        )
+        whole_out[grow, :] = whole_row * got_row
+
+
+def packed_round(take, got, part, whole):
+    spec = pl.BlockSpec(memory_space=pltpu.VMEM)
+    return pl.pallas_call(
+        round_kernel,
+        out_shape=(jax.ShapeDtypeStruct(part.shape, part.dtype),) * 2,
+        in_specs=[pl.BlockSpec(memory_space=pltpu.SMEM), spec, spec, spec],
+        out_specs=(spec, spec),
+        cost_estimate=pl.CostEstimate(flops=12 * part.size, transcendentals=0, bytes_accessed=20 * part.size),
+    )(take.astype(jnp.int32).reshape(1), got, part, whole)
 
 
 def dp_sum(terms, axis):
@@ -141,21 +180,20 @@
     propagated, start_kept = run_block(start_state, weights, step_size)
     gained_start = rate_vec[None, :, None] * start_state
     offset = propagated - jnp.where(leading, jnp.zeros_like(gained_start), gained_start)
-    forward = (rate_vec, offset, rate_vec, offset)
-    reverse = (jnp.ones_like(rate_vec), jnp.zeros_like(cot_here), rate_vec, rate_vec[None, :, None] * cot_here)
+    channels = offset.shape[-2]
+    pair = lambda a, b: jnp.stack([a, b]).reshape(2 * channels, -1)
+    part = pack((rate_vec, jnp.ones_like(rate_vec)), pair(offset, jnp.zeros_like(cot_here)))
+    whole = pack((rate_vec, rate_vec), pair(offset, rate_vec[None, :, None] * cot_here))
     for bit in range(rounds):
-        got_f, got_r = exchange(
-            (forward[2], reverse[2]), jnp.stack([forward[3], reverse[3]]), "depth", bit
-        )
-        forward = scan_round(forward, got_f, before, bit, bit == rounds - 1)
-        reverse = scan_round(reverse, got_r, after, bit, bit == rounds - 1)
-    passed_in = reverse[1]
+        got = lax.ppermute(whole, "depth", [(i, i ^ (1 << bit)) for i in range(lax.axis_size("depth"))])
+        part, whole = packed_round(before(bit), got, part, whole)
+    corrected = part[:channels].reshape(offset.shape)
+    passed_in = part[channels : 2 * channels].reshape(cot_here.shape)
     adjoint_here = cot_here + passed_in
     back_start, start_grads = back_block(start_kept, weights, adjoint_here, step_size)
     arriving_bar = passed_along(back_start, "depth", -1)
     relaxed_bar = arriving_bar - passed_in
     back_own, own_grads = back_block(own_kept, weights, relaxed_bar, step_size)
-    corrected = forward[1]
     grad_cpoints = jnp.where(leading, back_own + back_start, back_own)
     grad_weights = dp_sum(start_grads + own_grads, "dp")
     return (corrected[None], grad_cpoints[None], grad_weights)

time: 162 us -> 163 us (level)
  Pallas kernels: 0 us -> 13.1 us
  other arithmetic: 24.6 us -> 12 us
  waiting for transfers between devices: 56.9 us -> 59.6 us
    pallas_call x0 -> x7, Pallas kernels: none -> 13.1 us  [packed_round(): pl.pallas_call(round_kernel, out_shape=(jax.ShapeDtypeStruct(part.shape,...]
    another operation x15 -> x2, other arithmetic: 4.16 us -> 0.03 us  [the longest x1 0.02 us: body(): pair = lambda a, b: jnp.stack([a, b]).reshape(2 * channels, -1)]
    select_n x7 -> x0, other arithmetic: 3.67 us -> none  [the longest x5 2.21 us: scan_round(): jnp.where(take, whole_state + whole_gain[:, None] * got_state, got_state...]
    squeeze x6 -> x0, local copies, waits for them, and re-layouts: 2.28 us -> none  [exchange(): arrived[rows + k, :g.shape[0]]]
    concatenate x7 -> x1, other arithmetic: 2.72 us -> 0.68 us  [pack(): return jnp.concatenate([states.reshape(-1, width)] + rows, axis=0)]
    broadcast_in_dim x2 -> x1, other arithmetic: 2.52 us -> 0.84 us  [body(): return (corrected[None], grad_cpoints[None], grad_weights)]
    ppermute x2, waiting for transfers between devices: 3.55 us -> 5.2 us  [passed_along(): return lax.ppermute(block, axis, route)]
    unnamed x34 -> x24, local copies, waits for them, and re-layouts: 4.25 us -> 5.08 us
  transfers between devices with their start and end apart: 15 -> 15, of which waited for: 13 -> 14; matrix products, arithmetic and copies ran while one was open for 2% -> 1% of each run, Pallas kernels for 0% -> 0%
where the time goes in v8:
time: 163 us; the launch traced here: 162 us
  starting transfers between devices  64.2 us (39%)
  waiting for transfers between devices  59.6 us (37%)
  Pallas kernels  13.1 us (8%)
  other arithmetic  12 us (7%)
  local copies, waits for them, and re-layouts  6.03 us (4%)
  matrix products  5.5 us (3%)
    ppermute x7, waiting for transfers between devices, body(): lax.ppermute(whole, 'depth', [(i, i ^ 1 << bit) for i in range(lax.axis_s...  42.2 us
    ppermute x7, starting transfers between devices, body(): lax.ppermute(whole, 'depth', [(i, i ^ 1 << bit) for i in range(lax.axis_s...  40.3 us
    pallas_call x7, Pallas kernels, packed_round(): pl.pallas_call(round_kernel, out_shape=(jax.ShapeDtypeStruct(part.shape,...  13.1 us
    ppermute x3, starting transfers between devices, dp_sum(): lax.ppermute(lax.dynamic_index_in_dim(terms, place ^ k, 0, False), axis,...  10.2 us
    ppermute x3, starting transfers between devices, dp_sum(): lax.ppermute(total, axis, pairs(k))  9.82 us
    ppermute x3, waiting for transfers between devices, dp_sum(): lax.ppermute(lax.dynamic_index_in_dim(terms, place ^ k, 0, False), axis,...  7.48 us
    ppermute x2, waiting for transfers between devices, passed_along(): return lax.ppermute(block, axis, route)  5.2 us
    unnamed x24, local copies, waits for them, and re-layouts  5.08 us
  transfers between devices with their start and end apart: 15, of which 14 were waited for; matrix products, arithmetic and copies ran while one was open for 1% of the time, Pallas kernels for 0%

profile of v8, /device:TPU:2, one launch (start us, length us, event | category | flops | bytes accessed | tf_op | source)
XLA Modules:
  0.0 161.8 jit_solution(8515594148597979216)
XLA Ops:
  0.7 0.9 fusion.197
  2.3 0.3 copy-done
  5.5 1.9 %collective-permute-start = (f32[1,64,256]{2,1,0:T(8,128)S(1)}, f32[1,64,256]{2,1,0:T(8,128)S(1)}, u32[]{:S(2)}, u32[]{:S(2)}) collective-permute-start(f32[1,64,256]{2,1,0:T(8,128)S(1)} %fusion.11), channel_id=1, source_target_pairs={{0,4},{4,8},{8,12},{12,16},{16,20},{20,24},{24,28},{28,32},{32,36}... | collective-permute-start | bytes 196616 | tf_op jit(solution)/shard_map/ppermute | solution.py:104
  7.5 3.5 %collective-permute-done = f32[1,64,256]{2,1,0:T(8,128)S(1)} collective-permute-done((f32[1,64,256]{2,1,0:T(8,128)S(1)}, f32[1,64,256]{2,1,0:T(8,128)S(1)}, u32[]{:S(2)}, u32[]{:S(2)}) %collective-permute-start) | collective-permute-done | bytes 65568 | tf_op jit(solution)/shard_map/ppermute | solution.py:104
  14.7 0.7 fusion.35
  15.4 1.9 %collective-permute-start.1 = (f32[130,256]{1,0:T(8,128)S(1)}, f32[130,256]{1,0:T(8,128)}, u32[]{:S(2)}, u32[]{:S(2)}) collective-permute-start(f32[130,256]{1,0:T(8,128)S(1)} %get-tuple-element.103.whole_ref), channel_id=1, source_target_pairs={{0,4},{4,0},{8,12},{12,8},{16,20},{20,16},{24,28},{28,24},{32,36},... | collective-permute-start | bytes 399368 | tf_op jit(solution)/shard_map/ppermute | solution.py:188
  17.3 1.4 collective-permute-done.1.got_ref
  18.7 1.9 %shard_map.67 = (f32[130,256]{1,0:T(8,128)}, f32[130,256]{1,0:T(8,128)}) custom-call(s32[1]{0:T(128)} %bitcast.6.take_ref, f32[130,256]{1,0:T(8,128)} %collective-permute-done.1.got_ref, f32[130,256]{1,0:T(8,128)} %get-tuple-element.102.part_ref, f32[130,256]{1,0:T(8,128)} %copy-done.4), custom_call_target="tpu_custom_call" | custom-call | flops 399360 | bytes 665600 | tf_op jit(solution)/shard_map/pallas_call | solution.py:75
  20.6 4.4 %collective-permute-start.2 = (f32[130,256]{1,0:T(8,128)}, f32[130,256]{1,0:T(8,128)S(1)}, u32[]{:S(2)}, u32[]{:S(2)}) collective-permute-start(f32[130,256]{1,0:T(8,128)} %get-tuple-element.16.whole_ref), channel_id=1, source_target_pairs={{0,8},{4,12},{8,0},{12,4},{16,24},{20,28},{24,16},{28,20},{32,40},... | collective-permute-start | bytes 399368 | tf_op jit(solution)/shard_map/ppermute | solution.py:188
  25.0 4.4 %collective-permute-done.2.got_ref = f32[130,256]{1,0:T(8,128)S(1)} collective-permute-done((f32[130,256]{1,0:T(8,128)}, f32[130,256]{1,0:T(8,128)S(1)}, u32[]{:S(2)}, u32[]{:S(2)}) %collective-permute-start.2) | collective-permute-done | bytes 133152 | tf_op jit(solution)/shard_map/ppermute | solution.py:188
  29.4 0.7 copy-done.7
  30.0 1.9 %shard_map.68 = (f32[130,256]{1,0:T(8,128)}, f32[130,256]{1,0:T(8,128)}) custom-call(s32[1]{0:T(128)} %bitcast.5.take_ref, f32[130,256]{1,0:T(8,128)} %copy-done.7, f32[130,256]{1,0:T(8,128)} %get-tuple-element.17.part_ref, f32[130,256]{1,0:T(8,128)} %get-tuple-element.16.whole_ref), custom_call_target="tpu_custom_call" | custom-call | flops 399360 | bytes 665600 | tf_op jit(solution)/shard_map/pallas_call | solution.py:75
  31.9 3.0 %collective-permute-start.3 = (f32[130,256]{1,0:T(8,128)}, f32[130,256]{1,0:T(8,128)S(1)}, u32[]{:S(2)}, u32[]{:S(2)}) collective-permute-start(f32[130,256]{1,0:T(8,128)} %get-tuple-element.18.whole_ref), channel_id=1, source_target_pairs={{0,16},{4,20},{8,24},{12,28},{16,0},{20,4},{24,8},{28,12},{32,48},... | collective-permute-start | bytes 399368 | tf_op jit(solution)/shard_map/ppermute | solution.py:188
  35.0 5.9 %collective-permute-done.3.got_ref = f32[130,256]{1,0:T(8,128)S(1)} collective-permute-done((f32[130,256]{1,0:T(8,128)}, f32[130,256]{1,0:T(8,128)S(1)}, u32[]{:S(2)}, u32[]{:S(2)}) %collective-permute-start.3) | collective-permute-done | bytes 133152 | tf_op jit(solution)/shard_map/ppermute | solution.py:188
  40.9 0.7 copy-done.8
  41.5 1.9 %shard_map.69 = (f32[130,256]{1,0:T(8,128)}, f32[130,256]{1,0:T(8,128)}) custom-call(s32[1]{0:T(128)} %bitcast.4.take_ref, f32[130,256]{1,0:T(8,128)} %copy-done.8, f32[130,256]{1,0:T(8,128)} %get-tuple-element.19.part_ref, f32[130,256]{1,0:T(8,128)} %get-tuple-element.18.whole_ref), custom_call_target="tpu_custom_call" | custom-call | flops 399360 | bytes 665600 | tf_op jit(solution)/shard_map/pallas_call | solution.py:75
  43.4 3.6 %collective-permute-start.4 = (f32[130,256]{1,0:T(8,128)}, f32[130,256]{1,0:T(8,128)S(1)}, u32[]{:S(2)}, u32[]{:S(2)}) collective-permute-start(f32[130,256]{1,0:T(8,128)} %get-tuple-element.20.whole_ref), channel_id=1, source_target_pairs={{0,32},{4,36},{8,40},{12,44},{16,48},{20,52},{24,56},{28,60},{32,0... | collective-permute-start | bytes 399368 | tf_op jit(solution)/shard_map/ppermute | solution.py:188
  47.0 3.5 %collective-permute-done.4.got_ref = f32[130,256]{1,0:T(8,128)S(1)} collective-permute-done((f32[130,256]{1,0:T(8,128)}, f32[130,256]{1,0:T(8,128)S(1)}, u32[]{:S(2)}, u32[]{:S(2)}) %collective-permute-start.4) | collective-permute-done | bytes 133152 | tf_op jit(solution)/shard_map/ppermute | solution.py:188
  50.5 0.7 copy-done.9
  51.2 1.9 %shard_map.70 = (f32[130,256]{1,0:T(8,128)}, f32[130,256]{1,0:T(8,128)}) custom-call(s32[1]{0:T(128)} %bitcast.3.take_ref, f32[130,256]{1,0:T(8,128)} %copy-done.9, f32[130,256]{1,0:T(8,128)} %get-tuple-element.21.part_ref, f32[130,256]{1,0:T(8,128)} %get-tuple-element.20.whole_ref), custom_call_target="tpu_custom_call" | custom-call | flops 399360 | bytes 665600 | tf_op jit(solution)/shard_map/pallas_call | solution.py:75
  53.1 5.0 %collective-permute-start.5 = (f32[130,256]{1,0:T(8,128)}, f32[130,256]{1,0:T(8,128)S(1)}, u32[]{:S(2)}, u32[]{:S(2)}) collective-permute-start(f32[130,256]{1,0:T(8,128)} %get-tuple-element.22.whole_ref), channel_id=1, source_target_pairs={{0,64},{4,68},{8,72},{12,76},{16,80},{20,84},{24,88},{28,92},{32,9... | collective-permute-start | bytes 399368 | tf_op jit(solution)/shard_map/ppermute | solution.py:188
  58.0 4.8 %collective-permute-done.5.got_ref = f32[130,256]{1,0:T(8,128)S(1)} collective-permute-done((f32[130,256]{1,0:T(8,128)}, f32[130,256]{1,0:T(8,128)S(1)}, u32[]{:S(2)}, u32[]{:S(2)}) %collective-permute-start.5) | collective-permute-done | bytes 133152 | tf_op jit(solution)/shard_map/ppermute | solution.py:188
  62.8 0.7 copy-done.10
  63.5 1.9 %shard_map.71 = (f32[130,256]{1,0:T(8,128)}, f32[130,256]{1,0:T(8,128)}) custom-call(s32[1]{0:T(128)} %bitcast.2.take_ref, f32[130,256]{1,0:T(8,128)} %copy-done.10, f32[130,256]{1,0:T(8,128)} %get-tuple-element.23.part_ref, f32[130,256]{1,0:T(8,128)} %get-tuple-element.22.whole_ref), custom_call_target="tpu_custom_call" | custom-call | flops 399360 | bytes 665600 | tf_op jit(solution)/shard_map/pallas_call | solution.py:75
  65.3 9.9 %collective-permute-start.6 = (f32[130,256]{1,0:T(8,128)}, f32[130,256]{1,0:T(8,128)S(1)}, u32[]{:S(2)}, u32[]{:S(2)}) collective-permute-start(f32[130,256]{1,0:T(8,128)} %get-tuple-element.24.whole_ref), channel_id=1, source_target_pairs={{0,128},{4,132},{8,136},{12,140},{16,144},{20,148},{24,152},{28,15... | collective-permute-start | bytes 399368 | tf_op jit(solution)/shard_map/ppermute | solution.py:188
  75.2 9.4 %collective-permute-done.6.got_ref = f32[130,256]{1,0:T(8,128)S(1)} collective-permute-done((f32[130,256]{1,0:T(8,128)}, f32[130,256]{1,0:T(8,128)S(1)}, u32[]{:S(2)}, u32[]{:S(2)}) %collective-permute-start.6) | collective-permute-done | bytes 133152 | tf_op jit(solution)/shard_map/ppermute | solution.py:188
  84.6 0.7 copy-done.6
  85.3 1.9 %shard_map.72 = (f32[130,256]{1,0:T(8,128)}, f32[130,256]{1,0:T(8,128)}) custom-call(s32[1]{0:T(128)} %bitcast.1.take_ref, f32[130,256]{1,0:T(8,128)} %copy-done.6, f32[130,256]{1,0:T(8,128)} %get-tuple-element.25.part_ref, f32[130,256]{1,0:T(8,128)} %get-tuple-element.24.whole_ref), custom_call_target="tpu_custom_call" | custom-call | flops 399360 | bytes 665600 | tf_op jit(solution)/shard_map/pallas_call | solution.py:75
  87.2 12.5 %collective-permute-start.7 = (f32[130,256]{1,0:T(8,128)}, f32[130,256]{1,0:T(8,128)S(1)}, u32[]{:S(2)}, u32[]{:S(2)}) collective-permute-start(f32[130,256]{1,0:T(8,128)} %get-tuple-element.26.whole_ref), channel_id=1, source_target_pairs={{0,256},{4,260},{8,264},{12,268},{16,272},{20,276},{24,280},{28,28... | collective-permute-start | bytes 399368 | tf_op jit(solution)/shard_map/ppermute | solution.py:188
  99.7 12.9 %collective-permute-done.7.got_ref = f32[130,256]{1,0:T(8,128)S(1)} collective-permute-done((f32[130,256]{1,0:T(8,128)}, f32[130,256]{1,0:T(8,128)S(1)}, u32[]{:S(2)}, u32[]{:S(2)}) %collective-permute-start.7) | collective-permute-done | bytes 133152 | tf_op jit(solution)/shard_map/ppermute | solution.py:188
  112.6 0.7 copy-done.5
  113.2 1.9 %shard_map.73 = (f32[130,256]{1,0:T(8,128)}, f32[130,256]{1,0:T(8,128)}) custom-call(s32[1]{0:T(128)} %bitcast.take_ref, f32[130,256]{1,0:T(8,128)} %copy-done.5, f32[130,256]{1,0:T(8,128)} %get-tuple-element.27.part_ref, f32[130,256]{1,0:T(8,128)} %get-tuple-element.26.whole_ref), custom_call_target="tpu_custom_call" | custom-call | flops 399360 | bytes 665600 | tf_op jit(solution)/shard_map/pallas_call | solution.py:75
  115.1 1.5 multiply_convert_fusion.7
  116.6 0.3 convolution_bitcast_fusion.7
  117.0 0.9 copy-done.2
  118.2 0.3 convolution_bitcast_fusion.6
  118.6 0.2 fusion.80
  119.0 0.3 convolution_bitcast_fusion.5
  119.3 0.2 fusion.98
  119.8 0.3 convolution_bitcast_fusion.4
  120.1 0.2 fusion.116
  120.3 1.9 %collective-permute-start.8 = (f32[1,64,256]{2,1,0:T(8,128)S(1)}, f32[1,64,256]{2,1,0:T(8,128)S(1)}, u32[]{:S(2)}, u32[]{:S(2)}) collective-permute-start(f32[1,64,256]{2,1,0:T(8,128)S(1)} %fusion.116), channel_id=1, source_target_pairs={{4,0},{8,4},{12,8},{16,12},{20,16},{24,20},{28,24},{32,28},{36,32}... | collective-permute-start | bytes 196616 | tf_op jit(solution)/shard_map/ppermute | solution.py:104
  122.5 1.7 %collective-permute-done.8 = f32[1,64,256]{2,1,0:T(8,128)S(1)} collective-permute-done((f32[1,64,256]{2,1,0:T(8,128)S(1)}, f32[1,64,256]{2,1,0:T(8,128)S(1)}, u32[]{:S(2)}, u32[]{:S(2)}) %collective-permute-start.8) | collective-permute-done | bytes 65568 | tf_op jit(solution)/shard_map/ppermute | solution.py:104
  124.4 0.3 convolution_bitcast_fusion.3
  124.7 0.2 fusion.134
  125.1 0.3 convolution_bitcast_fusion.2
  125.5 0.2 fusion.152
  125.9 0.3 convolution_bitcast_fusion.1
  126.2 0.2 fusion.170
  126.7 0.3 convolution_bitcast_fusion
  127.1 3.5 %collective-permute-start.9 = (f32[64,576]{1,0:T(8,128)S(1)}, f32[64,576]{1,0:T(8,128)S(1)}, u32[]{:S(2)}, u32[]{:S(2)}) collective-permute-start(f32[64,576]{1,0:T(8,128)S(1)} %get-tuple-element.31), channel_id=1, source_target_pairs={{0,1},{1,0},{2,3},{3,2},{4,5},{5,4},{6,7},{7,6},{8,9},{9,8},{10,11... | collective-permute-start | bytes 442376 | tf_op jit(solution)/shard_map/ppermute | solution.py:91
  130.6 4.1 %collective-permute-start.11 = (f32[64,576]{1,0:T(8,128)S(1)}, f32[64,576]{1,0:T(8,128)S(1)}, u32[]{:S(2)}, u32[]{:S(2)}) collective-permute-start(f32[64,576]{1,0:T(8,128)S(1)} %get-tuple-element.32), channel_id=1, source_target_pairs={{0,3},{1,2},{2,1},{3,0},{4,7},{5,6},{6,5},{7,4},{8,11},{9,10},{10,... | collective-permute-start | bytes 442376 | tf_op jit(solution)/shard_map/ppermute | solution.py:91
  134.7 2.6 %collective-permute-start.10 = (f32[64,576]{1,0:T(8,128)S(1)}, f32[64,576]{1,0:T(8,128)S(1)}, u32[]{:S(2)}, u32[]{:S(2)}) collective-permute-start(f32[64,576]{1,0:T(8,128)S(1)} %get-tuple-element.33), channel_id=1, source_target_pairs={{0,2},{1,3},{2,0},{3,1},{4,6},{5,7},{6,4},{7,5},{8,10},{9,11},{10,... | collective-permute-start | bytes 442376 | tf_op jit(solution)/shard_map/ppermute | solution.py:91
  137.4 2.9 %collective-permute-done.11 = f32[64,576]{1,0:T(8,128)S(1)} collective-permute-done((f32[64,576]{1,0:T(8,128)S(1)}, f32[64,576]{1,0:T(8,128)S(1)}, u32[]{:S(2)}, u32[]{:S(2)}) %collective-permute-start.11) | collective-permute-done | bytes 147488 | tf_op jit(solution)/shard_map/ppermute | solution.py:91
  140.3 4.6 %collective-permute-done.10 = f32[64,576]{1,0:T(8,128)S(1)} collective-permute-done((f32[64,576]{1,0:T(8,128)S(1)}, f32[64,576]{1,0:T(8,128)S(1)}, u32[]{:S(2)}, u32[]{:S(2)}) %collective-permute-start.10) | collective-permute-done | bytes 147488 | tf_op jit(solution)/shard_map/ppermute | solution.py:91
  144.9 3.1 %collective-permute-start.14 = (f32[64,576]{1,0:T(8,128)S(1)}, f32[64,576]{1,0:T(8,128)S(1)}, u32[]{:S(2)}, u32[]{:S(2)}) collective-permute-start(f32[64,576]{1,0:T(8,128)S(1)} %fusion.33), channel_id=1, source_target_pairs={{0,3},{1,2},{2,1},{3,0},{4,7},{5,6},{6,5},{7,4},{8,11},{9,10},{10,... | collective-permute-start | bytes 442376 | tf_op jit(solution)/shard_map/ppermute | solution.py:97
  148.0 3.5 %collective-permute-start.13 = (f32[64,576]{1,0:T(8,128)S(1)}, f32[64,576]{1,0:T(8,128)S(1)}, u32[]{:S(2)}, u32[]{:S(2)}) collective-permute-start(f32[64,576]{1,0:T(8,128)S(1)} %fusion.33), channel_id=1, source_target_pairs={{0,2},{1,3},{2,0},{3,1},{4,6},{5,7},{6,4},{7,5},{8,10},{9,11},{10,... | collective-permute-start | bytes 442376 | tf_op jit(solution)/shard_map/ppermute | solution.py:97
  151.5 3.3 %collective-permute-start.12 = (f32[64,576]{1,0:T(8,128)S(1)}, f32[64,576]{1,0:T(8,128)S(1)}, u32[]{:S(2)}, u32[]{:S(2)}) collective-permute-start(f32[64,576]{1,0:T(8,128)S(1)} %fusion.33), channel_id=1, source_target_pairs={{0,1},{1,0},{2,3},{3,2},{4,5},{5,4},{6,7},{7,6},{8,9},{9,8},{10,11... | collective-permute-start | bytes 442376 | tf_op jit(solution)/shard_map/ppermute | solution.py:97
  154.8 0.8 fusion.196
  155.6 1.4 collective-permute-done.14
  157.0 1.5 collective-permute-done.13
  158.5 1.8 %collective-permute-done.12 = f32[64,576]{1,0:T(8,128)S(1)} collective-permute-done((f32[64,576]{1,0:T(8,128)S(1)}, f32[64,576]{1,0:T(8,128)S(1)}, u32[]{:S(2)}, u32[]{:S(2)}) %collective-permute-start.12) | collective-permute-done | bytes 147488 | tf_op jit(solution)/shard_map/ppermute | solution.py:97
  160.3 0.6 gather_fusion
  160.9 1.0 broadcast_select_fusion
  (130 shorter events, 9.4 us)
Async XLA Ops:
  0.7 1.3 copy-start.1
  1.6 1.0 copy-start
  5.2 2.1 %copy-start.3 = (f32[1,1,64,256]{3,2,1,0:T(8,128)S(1)}, f32[1,1,64,256]{3,2,1,0:T(8,128)}, u32[]{:S(2)}) copy-start(f32[1,1,64,256]{3,2,1,0:T(8,128)} %param.7) | copy-start | bytes 196612
  5.4 2.0 %copy-start.11 = (f32[1,64]{1,0:T(1,128)S(1)}, f32[1,64]{1,0:T(1,128)}, u32[]{:S(2)}) copy-start(f32[1,64]{1,0:T(1,128)} %param.6) | copy-start | bytes 772
  5.5 5.6 %collective-permute-start = (f32[1,64,256]{2,1,0:T(8,128)S(1)}, f32[1,64,256]{2,1,0:T(8,128)S(1)}, u32[]{:S(2)}, u32[]{:S(2)}) collective-permute-start(f32[1,64,256]{2,1,0:T(8,128)S(1)} %fusion.11), channel_id=1, source_target_pairs={{0,4},{4,8},{8,12},{12,16},{16,20},{20,24},{24,28},{28,32},{32,36}... | collective-permute-start | bytes 196616 | tf_op jit(solution)/shard_map/ppermute | solution.py:104
  15.3 3.4 %copy-start.4 = (f32[130,256]{1,0:T(8,128)}, f32[130,256]{1,0:T(8,128)S(1)}, u32[]{:S(2)}) copy-start(f32[130,256]{1,0:T(8,128)S(1)} %get-tuple-element.103.whole_ref) | copy-start | bytes 399364
  15.4 3.4 %collective-permute-start.1 = (f32[130,256]{1,0:T(8,128)S(1)}, f32[130,256]{1,0:T(8,128)}, u32[]{:S(2)}, u32[]{:S(2)}) collective-permute-start(f32[130,256]{1,0:T(8,128)S(1)} %get-tuple-element.103.whole_ref), channel_id=1, source_target_pairs={{0,4},{4,0},{8,12},{12,8},{16,20},{20,16},{24,28},{28,24},{32,36},... | collective-permute-start | bytes 399368 | tf_op jit(solution)/shard_map/ppermute | solution.py:188
  20.6 8.8 %collective-permute-start.2 = (f32[130,256]{1,0:T(8,128)}, f32[130,256]{1,0:T(8,128)S(1)}, u32[]{:S(2)}, u32[]{:S(2)}) collective-permute-start(f32[130,256]{1,0:T(8,128)} %get-tuple-element.16.whole_ref), channel_id=1, source_target_pairs={{0,8},{4,12},{8,0},{12,4},{16,24},{20,28},{24,16},{28,20},{32,40},... | collective-permute-start | bytes 399368 | tf_op jit(solution)/shard_map/ppermute | solution.py:188
  29.4 0.7 copy-start.7
  31.9 8.9 %collective-permute-start.3 = (f32[130,256]{1,0:T(8,128)}, f32[130,256]{1,0:T(8,128)S(1)}, u32[]{:S(2)}, u32[]{:S(2)}) collective-permute-start(f32[130,256]{1,0:T(8,128)} %get-tuple-element.18.whole_ref), channel_id=1, source_target_pairs={{0,16},{4,20},{8,24},{12,28},{16,0},{20,4},{24,8},{28,12},{32,48},... | collective-permute-start | bytes 399368 | tf_op jit(solution)/shard_map/ppermute | solution.py:188
  40.9 0.7 copy-start.8
  43.4 7.1 %collective-permute-start.4 = (f32[130,256]{1,0:T(8,128)}, f32[130,256]{1,0:T(8,128)S(1)}, u32[]{:S(2)}, u32[]{:S(2)}) collective-permute-start(f32[130,256]{1,0:T(8,128)} %get-tuple-element.20.whole_ref), channel_id=1, source_target_pairs={{0,32},{4,36},{8,40},{12,44},{16,48},{20,52},{24,56},{28,60},{32,0... | collective-permute-start | bytes 399368 | tf_op jit(solution)/shard_map/ppermute | solution.py:188
  50.5 0.7 copy-start.9
  53.1 9.8 %collective-permute-start.5 = (f32[130,256]{1,0:T(8,128)}, f32[130,256]{1,0:T(8,128)S(1)}, u32[]{:S(2)}, u32[]{:S(2)}) collective-permute-start(f32[130,256]{1,0:T(8,128)} %get-tuple-element.22.whole_ref), channel_id=1, source_target_pairs={{0,64},{4,68},{8,72},{12,76},{16,80},{20,84},{24,88},{28,92},{32,9... | collective-permute-start | bytes 399368 | tf_op jit(solution)/shard_map/ppermute | solution.py:188
  62.8 0.7 copy-start.10
  65.3 19.3 %collective-permute-start.6 = (f32[130,256]{1,0:T(8,128)}, f32[130,256]{1,0:T(8,128)S(1)}, u32[]{:S(2)}, u32[]{:S(2)}) collective-permute-start(f32[130,256]{1,0:T(8,128)} %get-tuple-element.24.whole_ref), channel_id=1, source_target_pairs={{0,128},{4,132},{8,136},{12,140},{16,144},{20,148},{24,152},{28,15... | collective-permute-start | bytes 399368 | tf_op jit(solution)/shard_map/ppermute | solution.py:188
  84.6 0.7 copy-start.6
  87.2 25.4 %collective-permute-start.7 = (f32[130,256]{1,0:T(8,128)}, f32[130,256]{1,0:T(8,128)S(1)}, u32[]{:S(2)}, u32[]{:S(2)}) collective-permute-start(f32[130,256]{1,0:T(8,128)} %get-tuple-element.26.whole_ref), channel_id=1, source_target_pairs={{0,256},{4,260},{8,264},{12,268},{16,272},{20,276},{24,280},{28,28... | collective-permute-start | bytes 399368 | tf_op jit(solution)/shard_map/ppermute | solution.py:188
  112.6 0.7 copy-start.5
  116.9 0.9 copy-start.2
  120.3 3.8 %collective-permute-start.8 = (f32[1,64,256]{2,1,0:T(8,128)S(1)}, f32[1,64,256]{2,1,0:T(8,128)S(1)}, u32[]{:S(2)}, u32[]{:S(2)}) collective-permute-start(f32[1,64,256]{2,1,0:T(8,128)S(1)} %fusion.116), channel_id=1, source_target_pairs={{4,0},{8,4},{12,8},{16,12},{20,16},{24,20},{28,24},{32,28},{36,32}... | collective-permute-start | bytes 196616 | tf_op jit(solution)/shard_map/ppermute | solution.py:104
  127.1 10.3 %collective-permute-start.9 = (f32[64,576]{1,0:T(8,128)S(1)}, f32[64,576]{1,0:T(8,128)S(1)}, u32[]{:S(2)}, u32[]{:S(2)}) collective-permute-start(f32[64,576]{1,0:T(8,128)S(1)} %get-tuple-element.31), channel_id=1, source_target_pairs={{0,1},{1,0},{2,3},{3,2},{4,5},{5,4},{6,7},{7,6},{8,9},{9,8},{10,11... | collective-permute-start | bytes 442376 | tf_op jit(solution)/shard_map/ppermute | solution.py:91
  130.6 9.7 %collective-permute-start.11 = (f32[64,576]{1,0:T(8,128)S(1)}, f32[64,576]{1,0:T(8,128)S(1)}, u32[]{:S(2)}, u32[]{:S(2)}) collective-permute-start(f32[64,576]{1,0:T(8,128)S(1)} %get-tuple-element.32), channel_id=1, source_target_pairs={{0,3},{1,2},{2,1},{3,0},{4,7},{5,6},{6,5},{7,4},{8,11},{9,10},{10,... | collective-permute-start | bytes 442376 | tf_op jit(solution)/shard_map/ppermute | solution.py:91
  134.7 10.2 %collective-permute-start.10 = (f32[64,576]{1,0:T(8,128)S(1)}, f32[64,576]{1,0:T(8,128)S(1)}, u32[]{:S(2)}, u32[]{:S(2)}) collective-permute-start(f32[64,576]{1,0:T(8,128)S(1)} %get-tuple-element.33), channel_id=1, source_target_pairs={{0,2},{1,3},{2,0},{3,1},{4,6},{5,7},{6,4},{7,5},{8,10},{9,11},{10,... | collective-permute-start | bytes 442376 | tf_op jit(solution)/shard_map/ppermute | solution.py:91
  144.9 12.1 %collective-permute-start.14 = (f32[64,576]{1,0:T(8,128)S(1)}, f32[64,576]{1,0:T(8,128)S(1)}, u32[]{:S(2)}, u32[]{:S(2)}) collective-permute-start(f32[64,576]{1,0:T(8,128)S(1)} %fusion.33), channel_id=1, source_target_pairs={{0,3},{1,2},{2,1},{3,0},{4,7},{5,6},{6,5},{7,4},{8,11},{9,10},{10,... | collective-permute-start | bytes 442376 | tf_op jit(solution)/shard_map/ppermute | solution.py:97
  148.0 10.5 %collective-permute-start.13 = (f32[64,576]{1,0:T(8,128)S(1)}, f32[64,576]{1,0:T(8,128)S(1)}, u32[]{:S(2)}, u32[]{:S(2)}) collective-permute-start(f32[64,576]{1,0:T(8,128)S(1)} %fusion.33), channel_id=1, source_target_pairs={{0,2},{1,3},{2,0},{3,1},{4,6},{5,7},{6,4},{7,5},{8,10},{9,11},{10,... | collective-permute-start | bytes 442376 | tf_op jit(solution)/shard_map/ppermute | solution.py:97
  151.5 8.8 %collective-permute-start.12 = (f32[64,576]{1,0:T(8,128)S(1)}, f32[64,576]{1,0:T(8,128)S(1)}, u32[]{:S(2)}, u32[]{:S(2)}) collective-permute-start(f32[64,576]{1,0:T(8,128)S(1)} %fusion.33), channel_id=1, source_target_pairs={{0,1},{1,0},{2,3},{3,2},{4,5},{5,4},{6,7},{7,6},{8,9},{9,8},{10,11... | collective-permute-start | bytes 442376 | tf_op jit(solution)/shard_map/ppermute | solution.py:97

commit v9 on v8

--- a/solution.py
+++ b/solution.py
@@ -45,29 +45,23 @@
 
 
 def round_kernel(take_ref, got_ref, part_ref, whole_ref, part_out, whole_out):
-    channels = (got_ref.shape[0] - 2) // 2
-    width = got_ref.shape[1]
+    channels = got_ref.shape[0] // 2
+    width = got_ref.shape[1] - 128
     first = take_ref[0] == 1
-    rows = lax.broadcasted_iota(jnp.int32, (channels, width), 0)
-    lanes = lax.broadcasted_iota(jnp.int32, (channels, width), 1)
-
-    def column(row):
-        return jnp.sum(jnp.where(rows == lanes, jnp.broadcast_to(row, (channels, width)), 0.0), axis=1, keepdims=True)
-
     for k, take in enumerate((first, jnp.logical_not(first))):
         band = pl.ds(k * channels, channels)
-        grow = pl.ds(2 * channels + k, 1)
-        got_state, got_row = got_ref[band, :], got_ref[grow, :]
-        part_state, part_row = part_ref[band, :], part_ref[grow, :]
-        whole_state, whole_row = whole_ref[band, :], whole_ref[grow, :]
-        part_out[band, :] = jnp.where(take, part_state + column(part_row) * got_state, part_state)
-        part_out[grow, :] = jnp.where(take, part_row * got_row, part_row)
-        whole_out[band, :] = jnp.where(
+        state, gain, col = pl.ds(0, width), pl.ds(width, 128), pl.ds(width, 1)
+        got_state, got_gain = got_ref[band, state], got_ref[band, gain]
+        part_state, part_gain = part_ref[band, state], part_ref[band, gain]
+        whole_state, whole_gain = whole_ref[band, state], whole_ref[band, gain]
+        part_out[band, state] = jnp.where(take, part_state + part_ref[band, col] * got_state, part_state)
+        part_out[band, gain] = jnp.where(take, part_gain * got_gain, part_gain)
+        whole_out[band, state] = jnp.where(
             take,
-            whole_state + column(whole_row) * got_state,
-            got_state + column(got_row) * whole_state,
-        )
-        whole_out[grow, :] = whole_row * got_row
+            whole_state + whole_ref[band, col] * got_state,
+            got_state + got_ref[band, col] * whole_state,
+        )
+        whole_out[band, gain] = whole_gain * got_gain
 
 
 def packed_round(take, got, part, whole):
@@ -181,14 +175,21 @@
     gained_start = rate_vec[None, :, None] * start_state
     offset = propagated - jnp.where(leading, jnp.zeros_like(gained_start), gained_start)
     channels = offset.shape[-2]
-    pair = lambda a, b: jnp.stack([a, b]).reshape(2 * channels, -1)
-    part = pack((rate_vec, jnp.ones_like(rate_vec)), pair(offset, jnp.zeros_like(cot_here)))
-    whole = pack((rate_vec, rate_vec), pair(offset, rate_vec[None, :, None] * cot_here))
+    def pair(gains, states):
+        rows = [
+            jnp.concatenate([s.reshape(channels, -1), jnp.broadcast_to(g[:, None], (channels, 128))], axis=1)
+            for g, s in zip(gains, states)
+        ]
+        return jnp.concatenate(rows, axis=0)
+
+    part = pair((rate_vec, jnp.ones_like(rate_vec)), (offset, jnp.zeros_like(cot_here)))
+    whole = pair((rate_vec, rate_vec), (offset, rate_vec[None, :, None] * cot_here))
     for bit in range(rounds):
         got = lax.ppermute(whole, "depth", [(i, i ^ (1 << bit)) for i in range(lax.axis_size("depth"))])
         part, whole = packed_round(before(bit), got, part, whole)
-    corrected = part[:channels].reshape(offset.shape)
-    passed_in = part[channels : 2 * channels].reshape(cot_here.shape)
+    pixels = offset.shape[-1]
+    corrected = part[:channels, :pixels].reshape(offset.shape)
+    passed_in = part[channels : 2 * channels, :pixels].reshape(cot_here.shape)
     adjoint_here = cot_here + passed_in
     back_start, start_grads = back_block(start_kept, weights, adjoint_here, step_size)
     arriving_bar = passed_along(back_start, "depth", -1)

time: 163 us -> 180 us (1.10)
  waiting for transfers between devices: 59.6 us -> 76.2 us
    ppermute x7, waiting for transfers between devices: 42.2 us -> 59.2 us  [body(): lax.ppermute(whole, 'depth', [(i, i ^ 1 << bit) for i in range(lax.axis_s...]
    unnamed x24 -> x26, local copies, waits for them, and re-layouts: 5.08 us -> 5.84 us
  transfers between devices with their start and end apart: 15 -> 15, of which waited for: 14 -> 13; matrix products, arithmetic and copies ran while one was open for 1% -> 1% of each run, Pallas kernels for 0% -> 0%
where the time goes in v9:
time: 180 us
  waiting for transfers between devices  76.2 us (42%)
  starting transfers between devices  63.8 us (35%)
  Pallas kernels  13.8 us (8%)
  other arithmetic  12 us (7%)
  local copies, waits for them, and re-layouts  6.85 us (4%)
  matrix products  5.49 us (3%)
    ppermute x7, waiting for transfers between devices, body(): lax.ppermute(whole, 'depth', [(i, i ^ 1 << bit) for i in range(lax.axis_s...  59.2 us
    ppermute x7, starting transfers between devices, body(): lax.ppermute(whole, 'depth', [(i, i ^ 1 << bit) for i in range(lax.axis_s...  39.9 us
    pallas_call x7, Pallas kernels, packed_round(): pl.pallas_call(round_kernel, out_shape=(jax.ShapeDtypeStruct(part.shape,...  13.8 us
    ppermute x3, starting transfers between devices, dp_sum(): lax.ppermute(lax.dynamic_index_in_dim(terms, place ^ k, 0, False), axis,...  10.2 us
    ppermute x3, starting transfers between devices, dp_sum(): lax.ppermute(total, axis, pairs(k))  9.82 us
    ppermute x3, waiting for transfers between devices, dp_sum(): lax.ppermute(lax.dynamic_index_in_dim(terms, place ^ k, 0, False), axis,...  7.38 us
    unnamed x26, local copies, waits for them, and re-layouts  5.84 us
    ppermute x2, waiting for transfers between devices, passed_along(): return lax.ppermute(block, axis, route)  5.24 us
  transfers between devices with their start and end apart: 15, of which 13 were waited for; matrix products, arithmetic and copies ran while one was open for 1% of the time, Pallas kernels for 0%

profile of v9, /device:TPU:2, one launch (start us, length us, event | category | flops | bytes accessed | tf_op | source)
XLA Modules:
  0.0 179.6 jit_solution(13070139626952283947)
XLA Ops:
  0.7 0.9 fusion.196
  2.3 0.3 copy-done
  5.5 1.9 %collective-permute-start = (f32[1,64,256]{2,1,0:T(8,128)S(1)}, f32[1,64,256]{2,1,0:T(8,128)S(1)}, u32[]{:S(2)}, u32[]{:S(2)}) collective-permute-start(f32[1,64,256]{2,1,0:T(8,128)S(1)} %fusion.11), channel_id=1, source_target_pairs={{0,4},{4,8},{8,12},{12,16},{16,20},{20,24},{24,28},{28,32},{32,36}... | collective-permute-start | bytes 196616 | tf_op jit(solution)/shard_map/ppermute | solution.py:98
  7.5 3.6 %collective-permute-done = f32[1,64,256]{2,1,0:T(8,128)S(1)} collective-permute-done((f32[1,64,256]{2,1,0:T(8,128)S(1)}, f32[1,64,256]{2,1,0:T(8,128)S(1)}, u32[]{:S(2)}, u32[]{:S(2)}) %collective-permute-start) | collective-permute-done | bytes 65568 | tf_op jit(solution)/shard_map/ppermute | solution.py:98
  14.7 0.6 copy-done.11
  15.3 0.7 fusion.32
  16.1 1.9 %collective-permute-start.1 = (f32[128,384]{1,0:T(8,128)S(1)}, f32[128,384]{1,0:T(8,128)}, u32[]{:S(2)}, u32[]{:S(2)}) collective-permute-start(f32[128,384]{1,0:T(8,128)S(1)} %get-tuple-element.101.whole_ref), channel_id=1, source_target_pairs={{0,4},{4,0},{8,12},{12,8},{16,20},{20,16},{24,28},{28,24},{32,36},... | collective-permute-start | bytes 589832 | tf_op jit(solution)/shard_map/ppermute | solution.py:188
  18.0 1.5 collective-permute-done.1.got_ref
  19.5 2.0 %shard_map.67 = (f32[128,384]{1,0:T(8,128)}, f32[128,384]{1,0:T(8,128)}) custom-call(s32[1]{0:T(128)} %bitcast.6.take_ref, f32[128,384]{1,0:T(8,128)} %collective-permute-done.1.got_ref, f32[128,384]{1,0:T(8,128)} %get-tuple-element.100.part_ref, f32[128,384]{1,0:T(8,128)} %copy-done.2), custom_call_target="tpu_custom_call" | custom-call | flops 589824 | bytes 983040 | tf_op jit(solution)/shard_map/pallas_call | solution.py:69
  21.5 4.4 %collective-permute-start.2 = (f32[128,384]{1,0:T(8,128)}, f32[128,384]{1,0:T(8,128)S(1)}, u32[]{:S(2)}, u32[]{:S(2)}) collective-permute-start(f32[128,384]{1,0:T(8,128)} %get-tuple-element.16.whole_ref), channel_id=1, source_target_pairs={{0,8},{4,12},{8,0},{12,4},{16,24},{20,28},{24,16},{28,20},{32,40},... | collective-permute-start | bytes 589832 | tf_op jit(solution)/shard_map/ppermute | solution.py:188
  25.9 5.6 %collective-permute-done.2.got_ref = f32[128,384]{1,0:T(8,128)S(1)} collective-permute-done((f32[128,384]{1,0:T(8,128)}, f32[128,384]{1,0:T(8,128)S(1)}, u32[]{:S(2)}, u32[]{:S(2)}) %collective-permute-start.2) | collective-permute-done | bytes 196640 | tf_op jit(solution)/shard_map/ppermute | solution.py:188
  31.5 0.7 copy-done.6
  32.2 2.0 %shard_map.68 = (f32[128,384]{1,0:T(8,128)}, f32[128,384]{1,0:T(8,128)}) custom-call(s32[1]{0:T(128)} %bitcast.5.take_ref, f32[128,384]{1,0:T(8,128)} %copy-done.6, f32[128,384]{1,0:T(8,128)} %get-tuple-element.17.part_ref, f32[128,384]{1,0:T(8,128)} %get-tuple-element.16.whole_ref), custom_call_target="tpu_custom_call" | custom-call | flops 589824 | bytes 983040 | tf_op jit(solution)/shard_map/pallas_call | solution.py:69
  34.2 3.0 %collective-permute-start.3 = (f32[128,384]{1,0:T(8,128)}, f32[128,384]{1,0:T(8,128)S(1)}, u32[]{:S(2)}, u32[]{:S(2)}) collective-permute-start(f32[128,384]{1,0:T(8,128)} %get-tuple-element.18.whole_ref), channel_id=1, source_target_pairs={{0,16},{4,20},{8,24},{12,28},{16,0},{20,4},{24,8},{28,12},{32,48},... | collective-permute-start | bytes 589832 | tf_op jit(solution)/shard_map/ppermute | solution.py:188
  37.2 7.1 %collective-permute-done.3.got_ref = f32[128,384]{1,0:T(8,128)S(1)} collective-permute-done((f32[128,384]{1,0:T(8,128)}, f32[128,384]{1,0:T(8,128)S(1)}, u32[]{:S(2)}, u32[]{:S(2)}) %collective-permute-start.3) | collective-permute-done | bytes 196640 | tf_op jit(solution)/shard_map/ppermute | solution.py:188
  44.3 0.7 copy-done.7
  45.0 2.0 %shard_map.69 = (f32[128,384]{1,0:T(8,128)}, f32[128,384]{1,0:T(8,128)}) custom-call(s32[1]{0:T(128)} %bitcast.4.take_ref, f32[128,384]{1,0:T(8,128)} %copy-done.7, f32[128,384]{1,0:T(8,128)} %get-tuple-element.19.part_ref, f32[128,384]{1,0:T(8,128)} %get-tuple-element.18.whole_ref), custom_call_target="tpu_custom_call" | custom-call | flops 589824 | bytes 983040 | tf_op jit(solution)/shard_map/pallas_call | solution.py:69
  47.0 3.6 %collective-permute-start.4 = (f32[128,384]{1,0:T(8,128)}, f32[128,384]{1,0:T(8,128)S(1)}, u32[]{:S(2)}, u32[]{:S(2)}) collective-permute-start(f32[128,384]{1,0:T(8,128)} %get-tuple-element.20.whole_ref), channel_id=1, source_target_pairs={{0,32},{4,36},{8,40},{12,44},{16,48},{20,52},{24,56},{28,60},{32,0... | collective-permute-start | bytes 589832 | tf_op jit(solution)/shard_map/ppermute | solution.py:188
  50.6 4.2 %collective-permute-done.4.got_ref = f32[128,384]{1,0:T(8,128)S(1)} collective-permute-done((f32[128,384]{1,0:T(8,128)}, f32[128,384]{1,0:T(8,128)S(1)}, u32[]{:S(2)}, u32[]{:S(2)}) %collective-permute-start.4) | collective-permute-done | bytes 196640 | tf_op jit(solution)/shard_map/ppermute | solution.py:188
  54.8 0.7 copy-done.8
  55.5 2.0 %shard_map.70 = (f32[128,384]{1,0:T(8,128)}, f32[128,384]{1,0:T(8,128)}) custom-call(s32[1]{0:T(128)} %bitcast.3.take_ref, f32[128,384]{1,0:T(8,128)} %copy-done.8, f32[128,384]{1,0:T(8,128)} %get-tuple-element.21.part_ref, f32[128,384]{1,0:T(8,128)} %get-tuple-element.20.whole_ref), custom_call_target="tpu_custom_call" | custom-call | flops 589824 | bytes 983040 | tf_op jit(solution)/shard_map/pallas_call | solution.py:69
  57.4 5.0 %collective-permute-start.5 = (f32[128,384]{1,0:T(8,128)}, f32[128,384]{1,0:T(8,128)S(1)}, u32[]{:S(2)}, u32[]{:S(2)}) collective-permute-start(f32[128,384]{1,0:T(8,128)} %get-tuple-element.22.whole_ref), channel_id=1, source_target_pairs={{0,64},{4,68},{8,72},{12,76},{16,80},{20,84},{24,88},{28,92},{32,9... | collective-permute-start | bytes 589832 | tf_op jit(solution)/shard_map/ppermute | solution.py:188
  62.4 7.2 %collective-permute-done.5.got_ref = f32[128,384]{1,0:T(8,128)S(1)} collective-permute-done((f32[128,384]{1,0:T(8,128)}, f32[128,384]{1,0:T(8,128)S(1)}, u32[]{:S(2)}, u32[]{:S(2)}) %collective-permute-start.5) | collective-permute-done | bytes 196640 | tf_op jit(solution)/shard_map/ppermute | solution.py:188
  69.6 0.7 copy-done.9
  70.3 2.0 %shard_map.71 = (f32[128,384]{1,0:T(8,128)}, f32[128,384]{1,0:T(8,128)}) custom-call(s32[1]{0:T(128)} %bitcast.2.take_ref, f32[128,384]{1,0:T(8,128)} %copy-done.9, f32[128,384]{1,0:T(8,128)} %get-tuple-element.23.part_ref, f32[128,384]{1,0:T(8,128)} %get-tuple-element.22.whole_ref), custom_call_target="tpu_custom_call" | custom-call | flops 589824 | bytes 983040 | tf_op jit(solution)/shard_map/pallas_call | solution.py:69
  72.2 9.5 %collective-permute-start.6 = (f32[128,384]{1,0:T(8,128)}, f32[128,384]{1,0:T(8,128)S(1)}, u32[]{:S(2)}, u32[]{:S(2)}) collective-permute-start(f32[128,384]{1,0:T(8,128)} %get-tuple-element.24.whole_ref), channel_id=1, source_target_pairs={{0,128},{4,132},{8,136},{12,140},{16,144},{20,148},{24,152},{28,15... | collective-permute-start | bytes 589832 | tf_op jit(solution)/shard_map/ppermute | solution.py:188
  81.8 15.7 %collective-permute-done.6.got_ref = f32[128,384]{1,0:T(8,128)S(1)} collective-permute-done((f32[128,384]{1,0:T(8,128)}, f32[128,384]{1,0:T(8,128)S(1)}, u32[]{:S(2)}, u32[]{:S(2)}) %collective-permute-start.6) | collective-permute-done | bytes 196640 | tf_op jit(solution)/shard_map/ppermute | solution.py:188
  97.5 0.7 copy-done.5
  98.2 2.0 %shard_map.72 = (f32[128,384]{1,0:T(8,128)}, f32[128,384]{1,0:T(8,128)}) custom-call(s32[1]{0:T(128)} %bitcast.1.take_ref, f32[128,384]{1,0:T(8,128)} %copy-done.5, f32[128,384]{1,0:T(8,128)} %get-tuple-element.25.part_ref, f32[128,384]{1,0:T(8,128)} %get-tuple-element.24.whole_ref), custom_call_target="tpu_custom_call" | custom-call | flops 589824 | bytes 983040 | tf_op jit(solution)/shard_map/pallas_call | solution.py:69
  100.1 12.5 %collective-permute-start.7 = (f32[128,384]{1,0:T(8,128)}, f32[128,384]{1,0:T(8,128)S(1)}, u32[]{:S(2)}, u32[]{:S(2)}) collective-permute-start(f32[128,384]{1,0:T(8,128)} %get-tuple-element.26.whole_ref), channel_id=1, source_target_pairs={{0,256},{4,260},{8,264},{12,268},{16,272},{20,276},{24,280},{28,28... | collective-permute-start | bytes 589832 | tf_op jit(solution)/shard_map/ppermute | solution.py:188
  112.7 17.9 %collective-permute-done.7.got_ref = f32[128,384]{1,0:T(8,128)S(1)} collective-permute-done((f32[128,384]{1,0:T(8,128)}, f32[128,384]{1,0:T(8,128)S(1)}, u32[]{:S(2)}, u32[]{:S(2)}) %collective-permute-start.7) | collective-permute-done | bytes 196640 | tf_op jit(solution)/shard_map/ppermute | solution.py:188
  130.6 0.7 copy-done.10
  131.3 2.0 %shard_map.73 = (f32[128,384]{1,0:T(8,128)}, f32[128,384]{1,0:T(8,128)}) custom-call(s32[1]{0:T(128)} %bitcast.take_ref, f32[128,384]{1,0:T(8,128)} %copy-done.10, f32[128,384]{1,0:T(8,128)} %get-tuple-element.27.part_ref, f32[128,384]{1,0:T(8,128)} %get-tuple-element.26.whole_ref), custom_call_target="tpu_custom_call" | custom-call | flops 589824 | bytes 983040 | tf_op jit(solution)/shard_map/pallas_call | solution.py:69
  133.2 1.5 multiply_convert_fusion.7
  134.7 0.3 convolution_bitcast_fusion.7
  135.1 0.9 copy-done.4
  136.4 0.3 convolution_bitcast_fusion.6
  136.7 0.2 fusion.79
  137.1 0.3 convolution_bitcast_fusion.5
  137.5 0.2 fusion.97
  137.9 0.3 convolution_bitcast_fusion.4
  138.2 0.2 fusion.115
  138.5 1.9 %collective-permute-start.8 = (f32[1,64,256]{2,1,0:T(8,128)S(1)}, f32[1,64,256]{2,1,0:T(8,128)S(1)}, u32[]{:S(2)}, u32[]{:S(2)}) collective-permute-start(f32[1,64,256]{2,1,0:T(8,128)S(1)} %fusion.115), channel_id=1, source_target_pairs={{4,0},{8,4},{12,8},{16,12},{20,16},{24,20},{28,24},{32,28},{36,32}... | collective-permute-start | bytes 196616 | tf_op jit(solution)/shard_map/ppermute | solution.py:98
  140.6 1.7 collective-permute-done.8
  142.5 0.3 convolution_bitcast_fusion.3
  142.8 0.2 fusion.133
  143.3 0.3 convolution_bitcast_fusion.2
  143.6 0.2 fusion.151
  144.0 0.3 convolution_bitcast_fusion.1
  144.4 0.2 fusion.169
  144.8 0.3 convolution_bitcast_fusion
  145.2 3.5 %collective-permute-start.9 = (f32[64,576]{1,0:T(8,128)S(1)}, f32[64,576]{1,0:T(8,128)S(1)}, u32[]{:S(2)}, u32[]{:S(2)}) collective-permute-start(f32[64,576]{1,0:T(8,128)S(1)} %get-tuple-element.31), channel_id=1, source_target_pairs={{0,1},{1,0},{2,3},{3,2},{4,5},{5,4},{6,7},{7,6},{8,9},{9,8},{10,11... | collective-permute-start | bytes 442376 | tf_op jit(solution)/shard_map/ppermute | solution.py:85
  148.7 4.1 %collective-permute-start.11 = (f32[64,576]{1,0:T(8,128)S(1)}, f32[64,576]{1,0:T(8,128)S(1)}, u32[]{:S(2)}, u32[]{:S(2)}) collective-permute-start(f32[64,576]{1,0:T(8,128)S(1)} %get-tuple-element.32), channel_id=1, source_target_pairs={{0,3},{1,2},{2,1},{3,0},{4,7},{5,6},{6,5},{7,4},{8,11},{9,10},{10,... | collective-permute-start | bytes 442376 | tf_op jit(solution)/shard_map/ppermute | solution.py:85
  152.8 2.6 %collective-permute-start.10 = (f32[64,576]{1,0:T(8,128)S(1)}, f32[64,576]{1,0:T(8,128)S(1)}, u32[]{:S(2)}, u32[]{:S(2)}) collective-permute-start(f32[64,576]{1,0:T(8,128)S(1)} %get-tuple-element.33), channel_id=1, source_target_pairs={{0,2},{1,3},{2,0},{3,1},{4,6},{5,7},{6,4},{7,5},{8,10},{9,11},{10,... | collective-permute-start | bytes 442376 | tf_op jit(solution)/shard_map/ppermute | solution.py:85
  155.5 5.3 %collective-permute-done.11 = f32[64,576]{1,0:T(8,128)S(1)} collective-permute-done((f32[64,576]{1,0:T(8,128)S(1)}, f32[64,576]{1,0:T(8,128)S(1)}, u32[]{:S(2)}, u32[]{:S(2)}) %collective-permute-start.11) | collective-permute-done | bytes 147488 | tf_op jit(solution)/shard_map/ppermute | solution.py:85
  160.8 2.1 %collective-permute-done.10 = f32[64,576]{1,0:T(8,128)S(1)} collective-permute-done((f32[64,576]{1,0:T(8,128)S(1)}, f32[64,576]{1,0:T(8,128)S(1)}, u32[]{:S(2)}, u32[]{:S(2)}) %collective-permute-start.10) | collective-permute-done | bytes 147488 | tf_op jit(solution)/shard_map/ppermute | solution.py:85
  162.9 3.5 %collective-permute-start.14 = (f32[64,576]{1,0:T(8,128)S(1)}, f32[64,576]{1,0:T(8,128)S(1)}, u32[]{:S(2)}, u32[]{:S(2)}) collective-permute-start(f32[64,576]{1,0:T(8,128)S(1)} %fusion.34), channel_id=1, source_target_pairs={{0,3},{1,2},{2,1},{3,0},{4,7},{5,6},{6,5},{7,4},{8,11},{9,10},{10,... | collective-permute-start | bytes 442376 | tf_op jit(solution)/shard_map/ppermute | solution.py:91
  166.4 3.1 %collective-permute-start.13 = (f32[64,576]{1,0:T(8,128)S(1)}, f32[64,576]{1,0:T(8,128)S(1)}, u32[]{:S(2)}, u32[]{:S(2)}) collective-permute-start(f32[64,576]{1,0:T(8,128)S(1)} %fusion.34), channel_id=1, source_target_pairs={{0,2},{1,3},{2,0},{3,1},{4,6},{5,7},{6,4},{7,5},{8,10},{9,11},{10,... | collective-permute-start | bytes 442376 | tf_op jit(solution)/shard_map/ppermute | solution.py:91
  169.5 3.3 %collective-permute-start.12 = (f32[64,576]{1,0:T(8,128)S(1)}, f32[64,576]{1,0:T(8,128)S(1)}, u32[]{:S(2)}, u32[]{:S(2)}) collective-permute-start(f32[64,576]{1,0:T(8,128)S(1)} %fusion.34), channel_id=1, source_target_pairs={{0,1},{1,0},{2,3},{3,2},{4,5},{5,4},{6,7},{7,6},{8,9},{9,8},{10,11... | collective-permute-start | bytes 442376 | tf_op jit(solution)/shard_map/ppermute | solution.py:91
  172.8 0.8 fusion.195
  173.6 3.3 %collective-permute-done.13 = f32[64,576]{1,0:T(8,128)S(1)} collective-permute-done((f32[64,576]{1,0:T(8,128)S(1)}, f32[64,576]{1,0:T(8,128)S(1)}, u32[]{:S(2)}, u32[]{:S(2)}) %collective-permute-start.13) | collective-permute-done | bytes 147488 | tf_op jit(solution)/shard_map/ppermute | solution.py:91
  176.9 1.1 collective-permute-done.12
  178.1 0.6 gather_fusion
  178.7 1.0 broadcast_select_fusion
  (129 shorter events, 9.5 us)
Async XLA Ops:
  0.7 1.3 copy-start.1
  1.6 1.0 copy-start
  5.2 2.1 %copy-start.3 = (f32[1,1,64,256]{3,2,1,0:T(8,128)S(1)}, f32[1,1,64,256]{3,2,1,0:T(8,128)}, u32[]{:S(2)}) copy-start(f32[1,1,64,256]{3,2,1,0:T(8,128)} %param.7) | copy-start | bytes 196612
  5.4 2.0 %copy-start.12 = (f32[1,64]{1,0:T(1,128)S(1)}, f32[1,64]{1,0:T(1,128)}, u32[]{:S(2)}) copy-start(f32[1,64]{1,0:T(1,128)} %param.6) | copy-start | bytes 772
  5.5 5.6 %collective-permute-start = (f32[1,64,256]{2,1,0:T(8,128)S(1)}, f32[1,64,256]{2,1,0:T(8,128)S(1)}, u32[]{:S(2)}, u32[]{:S(2)}) collective-permute-start(f32[1,64,256]{2,1,0:T(8,128)S(1)} %fusion.11), channel_id=1, source_target_pairs={{0,4},{4,8},{8,12},{12,16},{16,20},{20,24},{24,28},{28,32},{32,36}... | collective-permute-start | bytes 196616 | tf_op jit(solution)/shard_map/ppermute | solution.py:98
  14.4 0.9 copy-start.11
  16.1 3.5 %copy-start.2 = (f32[128,384]{1,0:T(8,128)}, f32[128,384]{1,0:T(8,128)S(1)}, u32[]{:S(2)}) copy-start(f32[128,384]{1,0:T(8,128)S(1)} %get-tuple-element.101.whole_ref) | copy-start | bytes 589828
  16.1 3.5 %collective-permute-start.1 = (f32[128,384]{1,0:T(8,128)S(1)}, f32[128,384]{1,0:T(8,128)}, u32[]{:S(2)}, u32[]{:S(2)}) collective-permute-start(f32[128,384]{1,0:T(8,128)S(1)} %get-tuple-element.101.whole_ref), channel_id=1, source_target_pairs={{0,4},{4,0},{8,12},{12,8},{16,20},{20,16},{24,28},{28,24},{32,36},... | collective-permute-start | bytes 589832 | tf_op jit(solution)/shard_map/ppermute | solution.py:188
  21.5 10.0 %collective-permute-start.2 = (f32[128,384]{1,0:T(8,128)}, f32[128,384]{1,0:T(8,128)S(1)}, u32[]{:S(2)}, u32[]{:S(2)}) collective-permute-start(f32[128,384]{1,0:T(8,128)} %get-tuple-element.16.whole_ref), channel_id=1, source_target_pairs={{0,8},{4,12},{8,0},{12,4},{16,24},{20,28},{24,16},{28,20},{32,40},... | collective-permute-start | bytes 589832 | tf_op jit(solution)/shard_map/ppermute | solution.py:188
  31.5 0.7 copy-start.6
  34.2 10.2 %collective-permute-start.3 = (f32[128,384]{1,0:T(8,128)}, f32[128,384]{1,0:T(8,128)S(1)}, u32[]{:S(2)}, u32[]{:S(2)}) collective-permute-start(f32[128,384]{1,0:T(8,128)} %get-tuple-element.18.whole_ref), channel_id=1, source_target_pairs={{0,16},{4,20},{8,24},{12,28},{16,0},{20,4},{24,8},{28,12},{32,48},... | collective-permute-start | bytes 589832 | tf_op jit(solution)/shard_map/ppermute | solution.py:188
  44.3 0.7 copy-start.7
  47.0 7.8 %collective-permute-start.4 = (f32[128,384]{1,0:T(8,128)}, f32[128,384]{1,0:T(8,128)S(1)}, u32[]{:S(2)}, u32[]{:S(2)}) collective-permute-start(f32[128,384]{1,0:T(8,128)} %get-tuple-element.20.whole_ref), channel_id=1, source_target_pairs={{0,32},{4,36},{8,40},{12,44},{16,48},{20,52},{24,56},{28,60},{32,0... | collective-permute-start | bytes 589832 | tf_op jit(solution)/shard_map/ppermute | solution.py:188
  54.8 0.7 copy-start.8
  57.4 12.2 %collective-permute-start.5 = (f32[128,384]{1,0:T(8,128)}, f32[128,384]{1,0:T(8,128)S(1)}, u32[]{:S(2)}, u32[]{:S(2)}) collective-permute-start(f32[128,384]{1,0:T(8,128)} %get-tuple-element.22.whole_ref), channel_id=1, source_target_pairs={{0,64},{4,68},{8,72},{12,76},{16,80},{20,84},{24,88},{28,92},{32,9... | collective-permute-start | bytes 589832 | tf_op jit(solution)/shard_map/ppermute | solution.py:188
  69.6 0.7 copy-start.9
  72.2 25.2 %collective-permute-start.6 = (f32[128,384]{1,0:T(8,128)}, f32[128,384]{1,0:T(8,128)S(1)}, u32[]{:S(2)}, u32[]{:S(2)}) collective-permute-start(f32[128,384]{1,0:T(8,128)} %get-tuple-element.24.whole_ref), channel_id=1, source_target_pairs={{0,128},{4,132},{8,136},{12,140},{16,144},{20,148},{24,152},{28,15... | collective-permute-start | bytes 589832 | tf_op jit(solution)/shard_map/ppermute | solution.py:188
  97.5 0.7 copy-start.5
  100.1 30.4 %collective-permute-start.7 = (f32[128,384]{1,0:T(8,128)}, f32[128,384]{1,0:T(8,128)S(1)}, u32[]{:S(2)}, u32[]{:S(2)}) collective-permute-start(f32[128,384]{1,0:T(8,128)} %get-tuple-element.26.whole_ref), channel_id=1, source_target_pairs={{0,256},{4,260},{8,264},{12,268},{16,272},{20,276},{24,280},{28,28... | collective-permute-start | bytes 589832 | tf_op jit(solution)/shard_map/ppermute | solution.py:188
  130.6 0.7 copy-start.10
  135.0 0.9 copy-start.4
  138.5 3.8 %collective-permute-start.8 = (f32[1,64,256]{2,1,0:T(8,128)S(1)}, f32[1,64,256]{2,1,0:T(8,128)S(1)}, u32[]{:S(2)}, u32[]{:S(2)}) collective-permute-start(f32[1,64,256]{2,1,0:T(8,128)S(1)} %fusion.115), channel_id=1, source_target_pairs={{4,0},{8,4},{12,8},{16,12},{20,16},{24,20},{28,24},{32,28},{36,32}... | collective-permute-start | bytes 196616 | tf_op jit(solution)/shard_map/ppermute | solution.py:98
  145.2 10.3 %collective-permute-start.9 = (f32[64,576]{1,0:T(8,128)S(1)}, f32[64,576]{1,0:T(8,128)S(1)}, u32[]{:S(2)}, u32[]{:S(2)}) collective-permute-start(f32[64,576]{1,0:T(8,128)S(1)} %get-tuple-element.31), channel_id=1, source_target_pairs={{0,1},{1,0},{2,3},{3,2},{4,5},{5,4},{6,7},{7,6},{8,9},{9,8},{10,11... | collective-permute-start | bytes 442376 | tf_op jit(solution)/shard_map/ppermute | solution.py:85
  148.7 12.1 %collective-permute-start.11 = (f32[64,576]{1,0:T(8,128)S(1)}, f32[64,576]{1,0:T(8,128)S(1)}, u32[]{:S(2)}, u32[]{:S(2)}) collective-permute-start(f32[64,576]{1,0:T(8,128)S(1)} %get-tuple-element.32), channel_id=1, source_target_pairs={{0,3},{1,2},{2,1},{3,0},{4,7},{5,6},{6,5},{7,4},{8,11},{9,10},{10,... | collective-permute-start | bytes 442376 | tf_op jit(solution)/shard_map/ppermute | solution.py:85
  152.8 10.1 %collective-permute-start.10 = (f32[64,576]{1,0:T(8,128)S(1)}, f32[64,576]{1,0:T(8,128)S(1)}, u32[]{:S(2)}, u32[]{:S(2)}) collective-permute-start(f32[64,576]{1,0:T(8,128)S(1)} %get-tuple-element.33), channel_id=1, source_target_pairs={{0,2},{1,3},{2,0},{3,1},{4,6},{5,7},{6,4},{7,5},{8,10},{9,11},{10,... | collective-permute-start | bytes 442376 | tf_op jit(solution)/shard_map/ppermute | solution.py:85
  162.9 10.7 %collective-permute-start.14 = (f32[64,576]{1,0:T(8,128)S(1)}, f32[64,576]{1,0:T(8,128)S(1)}, u32[]{:S(2)}, u32[]{:S(2)}) collective-permute-start(f32[64,576]{1,0:T(8,128)S(1)} %fusion.34), channel_id=1, source_target_pairs={{0,3},{1,2},{2,1},{3,0},{4,7},{5,6},{6,5},{7,4},{8,11},{9,10},{10,... | collective-permute-start | bytes 442376 | tf_op jit(solution)/shard_map/ppermute | solution.py:91
  166.4 10.5 %collective-permute-start.13 = (f32[64,576]{1,0:T(8,128)S(1)}, f32[64,576]{1,0:T(8,128)S(1)}, u32[]{:S(2)}, u32[]{:S(2)}) collective-permute-start(f32[64,576]{1,0:T(8,128)S(1)} %fusion.34), channel_id=1, source_target_pairs={{0,2},{1,3},{2,0},{3,1},{4,6},{5,7},{6,4},{7,5},{8,10},{9,11},{10,... | collective-permute-start | bytes 442376 | tf_op jit(solution)/shard_map/ppermute | solution.py:91
  169.5 8.5 %collective-permute-start.12 = (f32[64,576]{1,0:T(8,128)S(1)}, f32[64,576]{1,0:T(8,128)S(1)}, u32[]{:S(2)}, u32[]{:S(2)}) collective-permute-start(f32[64,576]{1,0:T(8,128)S(1)} %fusion.34), channel_id=1, source_target_pairs={{0,1},{1,0},{2,3},{3,2},{4,5},{5,4},{6,7},{7,6},{8,9},{9,8},{10,11... | collective-permute-start | bytes 442376 | tf_op jit(solution)/shard_map/ppermute | solution.py:91

commit v10 on v4

--- a/solution.py
+++ b/solution.py
@@ -44,10 +44,13 @@
 
 def dp_sum(terms, axis):
     count = lax.axis_size(axis)
-    if count != 4:
+    if count & (count - 1):
         return lax.psum(terms, axis)
-    got = [lax.ppermute(terms, axis, [(i, i ^ k) for i in range(count)]) for k in (1, 2, 3)]
-    return (terms + got[0]) + (got[1] + got[2])
+    step = 1
+    while step < count:
+        terms = terms + lax.ppermute(terms, axis, [(i, i ^ step) for i in range(count)])
+        step *= 2
+    return terms
 
 
 def passed_along(block, axis, distance):

time: 163 us -> 172 us (1.055)
  waiting for transfers between devices: 68.6 us -> 74.3 us
  other arithmetic: 24.6 us -> 28.3 us
    ppermute x3 -> x2, waiting for transfers between devices: 23.8 us -> 26.3 us  [dp_sum(): lax.ppermute(terms, axis, [(i, i ^ step) for i in range(count)])]
    concatenate x7, other arithmetic: 2.72 us -> 4.69 us  [pack(): return jnp.concatenate([states.reshape(-1, width)] + rows, axis=0)]
    ppermute x3 -> x2, starting transfers between devices: 9.99 us -> 8.57 us  [dp_sum(): lax.ppermute(terms, axis, [(i, i ^ step) for i in range(count)])]
    unnamed x34 -> x40, local copies, waits for them, and re-layouts: 4.25 us -> 5.58 us
  transfers between devices with their start and end apart: 12 -> 11, of which waited for: 10 -> 11; matrix products, arithmetic and copies ran while one was open for 2% -> 2% of each run, Pallas kernels for 0% -> 0%
where the time goes in v10:
time: 172 us; the launch traced here: 171 us
  waiting for transfers between devices  74.3 us (43%)
  starting transfers between devices  52.7 us (31%)
  other arithmetic  28.3 us (16%)
  local copies, waits for them, and re-layouts  8.21 us (5%)
  matrix products  5.47 us (3%)
  between operations  1.76 us (1%)
    ppermute x7, waiting for transfers between devices, exchange(): lax.ppermute(pack(gains, states), axis, [(i, i ^ 1 << bit) for i in range...  42.8 us
    ppermute x7, starting transfers between devices, exchange(): lax.ppermute(pack(gains, states), axis, [(i, i ^ 1 << bit) for i in range...  40.3 us
    ppermute x2, waiting for transfers between devices, dp_sum(): lax.ppermute(terms, axis, [(i, i ^ step) for i in range(count)])  26.3 us
    ppermute x2, starting transfers between devices, dp_sum(): lax.ppermute(terms, axis, [(i, i ^ step) for i in range(count)])  8.57 us
    unnamed x40, local copies, waits for them, and re-layouts  5.58 us
    ppermute x2, waiting for transfers between devices, passed_along(): return lax.ppermute(block, axis, route)  5.21 us
    concatenate x7, other arithmetic, pack(): return jnp.concatenate([states.reshape(-1, width)] + rows, axis=0)  4.69 us
    unnamed x64, other arithmetic  4.68 us
  transfers between devices with their start and end apart: 11, of which 11 were waited for; matrix products, arithmetic and copies ran while one was open for 2% of the time, Pallas kernels for 0%

profile of v10, /device:TPU:2, one launch (start us, length us, event | category | flops | bytes accessed | tf_op | source)
XLA Modules:
  0.0 170.8 jit_solution(8317528601540299521)
XLA Ops:
  0.7 0.9 fusion.202
  5.5 1.9 %collective-permute-start = (f32[1,64,256]{2,1,0:T(8,128)S(1)}, f32[1,64,256]{2,1,0:T(8,128)S(1)}, u32[]{:S(2)}, u32[]{:S(2)}) collective-permute-start(f32[1,64,256]{2,1,0:T(8,128)S(1)} %fusion.11), channel_id=1, source_target_pairs={{0,4},{4,8},{8,12},{12,16},{16,20},{20,24},{24,28},{28,32},{32,36}... | collective-permute-start | bytes 196616 | tf_op jit(solution)/shard_map/ppermute | solution.py:59
  7.6 3.5 %collective-permute-done = f32[1,64,256]{2,1,0:T(8,128)S(1)} collective-permute-done((f32[1,64,256]{2,1,0:T(8,128)S(1)}, f32[1,64,256]{2,1,0:T(8,128)S(1)}, u32[]{:S(2)}, u32[]{:S(2)}) %collective-permute-start) | collective-permute-done | bytes 65568 | tf_op jit(solution)/shard_map/ppermute | solution.py:59
  14.7 0.7 pad_maximum_fusion
  15.4 1.9 %collective-permute-start.1 = (f32[130,256]{1,0:T(8,128)}, f32[130,256]{1,0:T(8,128)S(1)}, u32[]{:S(2)}, u32[]{:S(2)}) collective-permute-start(f32[130,256]{1,0:T(8,128)} %pad_maximum_fusion), channel_id=1, source_target_pairs={{0,4},{4,0},{8,12},{12,8},{16,20},{20,16},{24,28},{28,24},{32,36},... | collective-permute-start | bytes 399368 | tf_op jit(solution)/shard_map/ppermute | solution.py:20
  17.3 1.5 collective-permute-done.1
  19.1 0.7 pad_maximum_fusion.1
  19.8 4.4 %collective-permute-start.2 = (f32[130,256]{1,0:T(8,128)}, f32[130,256]{1,0:T(8,128)S(1)}, u32[]{:S(2)}, u32[]{:S(2)}) collective-permute-start(f32[130,256]{1,0:T(8,128)} %pad_maximum_fusion.1), channel_id=1, source_target_pairs={{0,8},{4,12},{8,0},{12,4},{16,24},{20,28},{24,16},{28,20},{32,40},... | collective-permute-start | bytes 399368 | tf_op jit(solution)/shard_map/ppermute | solution.py:20
  24.2 4.4 %collective-permute-done.2 = f32[130,256]{1,0:T(8,128)S(1)} collective-permute-done((f32[130,256]{1,0:T(8,128)}, f32[130,256]{1,0:T(8,128)S(1)}, u32[]{:S(2)}, u32[]{:S(2)}) %collective-permute-start.2) | collective-permute-done | bytes 133152 | tf_op jit(solution)/shard_map/ppermute | solution.py:20
  28.6 0.9 fusion.199
  29.7 0.7 pad_maximum_fusion.2
  30.4 3.0 %collective-permute-start.3 = (f32[130,256]{1,0:T(8,128)}, f32[130,256]{1,0:T(8,128)}, u32[]{:S(2)}, u32[]{:S(2)}) collective-permute-start(f32[130,256]{1,0:T(8,128)} %pad_maximum_fusion.2), channel_id=1, source_target_pairs={{0,16},{4,20},{8,24},{12,28},{16,0},{20,4},{24,8},{28,12},{32,48},... | collective-permute-start | bytes 399368 | tf_op jit(solution)/shard_map/ppermute | solution.py:20
  33.4 6.0 %collective-permute-done.3 = f32[130,256]{1,0:T(8,128)} collective-permute-done((f32[130,256]{1,0:T(8,128)}, f32[130,256]{1,0:T(8,128)}, u32[]{:S(2)}, u32[]{:S(2)}) %collective-permute-start.3) | collective-permute-done | bytes 133152 | tf_op jit(solution)/shard_map/ppermute | solution.py:20
  39.4 0.8 fusion.320
  40.2 0.8 slice_bitcast_fusion.7
  40.9 0.9 add_select_fusion.15
  41.9 0.9 fusion.331
  42.8 0.7 pad_maximum_fusion.3
  43.5 3.6 %collective-permute-start.4 = (f32[130,256]{1,0:T(8,128)}, f32[130,256]{1,0:T(8,128)}, u32[]{:S(2)}, u32[]{:S(2)}) collective-permute-start(f32[130,256]{1,0:T(8,128)} %pad_maximum_fusion.3), channel_id=1, source_target_pairs={{0,32},{4,36},{8,40},{12,44},{16,48},{20,52},{24,56},{28,60},{32,0... | collective-permute-start | bytes 399368 | tf_op jit(solution)/shard_map/ppermute | solution.py:20
  47.1 3.6 %collective-permute-done.4 = f32[130,256]{1,0:T(8,128)} collective-permute-done((f32[130,256]{1,0:T(8,128)}, f32[130,256]{1,0:T(8,128)}, u32[]{:S(2)}, u32[]{:S(2)}) %collective-permute-start.4) | collective-permute-done | bytes 133152 | tf_op jit(solution)/shard_map/ppermute | solution.py:20
  50.8 0.8 fusion.322
  51.5 0.8 slice_bitcast_fusion.5
  52.3 1.0 fusion.197
  53.3 0.9 fusion.329
  54.2 0.7 pad_maximum_fusion.4
  54.9 5.0 %collective-permute-start.5 = (f32[130,256]{1,0:T(8,128)}, f32[130,256]{1,0:T(8,128)S(1)}, u32[]{:S(2)}, u32[]{:S(2)}) collective-permute-start(f32[130,256]{1,0:T(8,128)} %pad_maximum_fusion.4), channel_id=1, source_target_pairs={{0,64},{4,68},{8,72},{12,76},{16,80},{20,84},{24,88},{28,92},{32,9... | collective-permute-start | bytes 399368 | tf_op jit(solution)/shard_map/ppermute | solution.py:20
  59.9 4.8 %collective-permute-done.5 = f32[130,256]{1,0:T(8,128)S(1)} collective-permute-done((f32[130,256]{1,0:T(8,128)}, f32[130,256]{1,0:T(8,128)S(1)}, u32[]{:S(2)}, u32[]{:S(2)}) %collective-permute-start.5) | collective-permute-done | bytes 133152 | tf_op jit(solution)/shard_map/ppermute | solution.py:20
  64.7 1.0 add_select_fusion.13
  65.7 0.5 copy-done.15
  66.3 0.7 pad_maximum_fusion.5
  67.0 9.9 %collective-permute-start.6 = (f32[130,256]{1,0:T(8,128)}, f32[130,256]{1,0:T(8,128)}, u32[]{:S(2)}, u32[]{:S(2)}) collective-permute-start(f32[130,256]{1,0:T(8,128)} %pad_maximum_fusion.5), channel_id=1, source_target_pairs={{0,128},{4,132},{8,136},{12,140},{16,144},{20,148},{24,152},{28,15... | collective-permute-start | bytes 399368 | tf_op jit(solution)/shard_map/ppermute | solution.py:20
  76.9 9.5 %collective-permute-done.6 = f32[130,256]{1,0:T(8,128)} collective-permute-done((f32[130,256]{1,0:T(8,128)}, f32[130,256]{1,0:T(8,128)}, u32[]{:S(2)}, u32[]{:S(2)}) %collective-permute-start.6) | collective-permute-done | bytes 133152 | tf_op jit(solution)/shard_map/ppermute | solution.py:20
  86.4 0.8 broadcast_select_fusion
  87.2 0.8 slice_bitcast_fusion.1
  87.9 0.9 select_bitcast_fusion
  88.9 0.9 fusion.195
  89.8 0.7 pad_maximum_fusion.6
  90.5 12.5 %collective-permute-start.7 = (f32[130,256]{1,0:T(8,128)}, f32[130,256]{1,0:T(8,128)}, u32[]{:S(2)}, u32[]{:S(2)}) collective-permute-start(f32[130,256]{1,0:T(8,128)} %pad_maximum_fusion.6), channel_id=1, source_target_pairs={{0,256},{4,260},{8,264},{12,268},{16,272},{20,276},{24,280},{28,28... | collective-permute-start | bytes 399368 | tf_op jit(solution)/shard_map/ppermute | solution.py:20
  103.0 13.0 %collective-permute-done.7 = f32[130,256]{1,0:T(8,128)} collective-permute-done((f32[130,256]{1,0:T(8,128)}, f32[130,256]{1,0:T(8,128)}, u32[]{:S(2)}, u32[]{:S(2)}) %collective-permute-start.7) | collective-permute-done | bytes 133152 | tf_op jit(solution)/shard_map/ppermute | solution.py:20
  116.0 1.1 multiply_convert_fusion.7
  117.1 0.3 convolution_bitcast_fusion.7
  117.9 0.3 convolution_bitcast_fusion.6
  118.2 0.8 copy-done.14
  119.5 0.3 convolution_bitcast_fusion.5
  119.8 0.8 copy-done.12
  121.0 0.3 convolution_bitcast_fusion.4
  121.6 1.9 %collective-permute-start.8 = (f32[1,64,256]{2,1,0:T(8,128)S(1)}, f32[1,64,256]{2,1,0:T(8,128)S(1)}, u32[]{:S(2)}, u32[]{:S(2)}) collective-permute-start(f32[1,64,256]{2,1,0:T(8,128)S(1)} %fusion.113), channel_id=1, source_target_pairs={{4,0},{8,4},{12,8},{16,12},{20,16},{24,20},{28,24},{32,28},{36,32}... | collective-permute-start | bytes 196616 | tf_op jit(solution)/shard_map/ppermute | solution.py:59
  123.7 1.7 collective-permute-done.8
  125.6 0.3 convolution_bitcast_fusion.3
  126.0 0.8 copy-done.10
  127.2 0.3 convolution_bitcast_fusion.2
  127.5 0.8 copy-done.8
  128.7 0.3 convolution_bitcast_fusion.1
  129.1 0.8 copy-done.6
  130.4 3.5 %collective-permute-start.9 = (f32[4,64,576]{2,1,0:T(8,128)S(1)}, f32[4,64,576]{2,1,0:T(8,128)S(1)}, u32[]{:S(2)}, u32[]{:S(2)}) collective-permute-start(f32[4,64,576]{2,1,0:T(8,128)S(1)} %maximum_add_fusion), channel_id=1, source_target_pairs={{0,1},{1,0},{2,3},{3,2},{4,5},{5,4},{6,7},{7,6},{8,9},{9,8},{10,11... | collective-permute-start | bytes 1769480 | tf_op jit(solution)/shard_map/ppermute | solution.py:51
  133.9 0.7 broadcast_select_fusion.6
  134.6 1.8 %fusion.48 = f32[1,1,64,256]{3,2,1,0:T(8,128)} fusion(f32[130,256]{1,0:T(8,128)} %collective-permute-done.7, f32[1,64,256]{2,1,0:T(8,128)S(1)} %select_subtract_fusion, f32[130,256]{1,0:T(8,128)} %collective-permute-done.6, f32[130,256]{1,0:T(8,128)} %copy-done.3, f32[130,256]{1,0:T(8,128)} %collective-permute-done.4, ...), kind=kLoop, calls=%fused_computation.300 | loop fusion | flops 344064 | bytes 591623 | tf_op jit(solution)/shard_map/broadcast_in_dim | solution.py:155
  136.4 12.7 %collective-permute-done.9 = f32[4,64,576]{2,1,0:T(8,128)S(1)} collective-permute-done((f32[4,64,576]{2,1,0:T(8,128)S(1)}, f32[4,64,576]{2,1,0:T(8,128)S(1)}, u32[]{:S(2)}, u32[]{:S(2)}) %collective-permute-start.9) | collective-permute-done | bytes 589856 | tf_op jit(solution)/shard_map/ppermute | solution.py:51
  149.2 5.1 %collective-permute-start.10 = (f32[4,64,576]{2,1,0:T(8,128)S(1)}, f32[4,64,576]{2,1,0:T(8,128)S(1)}, u32[]{:S(2)}, u32[]{:S(2)}) collective-permute-start(f32[4,64,576]{2,1,0:T(8,128)S(1)} %fusion.345), channel_id=1, source_target_pairs={{0,2},{1,3},{2,0},{3,1},{4,6},{5,7},{6,4},{7,5},{8,10},{9,11},{10,... | collective-permute-start | bytes 1769480 | tf_op jit(solution)/shard_map/ppermute | solution.py:51
  154.3 0.3 convolution_bitcast_fusion
  154.6 0.8 copy-done.18
  155.4 0.8 fusion.201
  156.2 13.6 %collective-permute-done.10 = f32[4,64,576]{2,1,0:T(8,128)S(1)} collective-permute-done((f32[4,64,576]{2,1,0:T(8,128)S(1)}, f32[4,64,576]{2,1,0:T(8,128)S(1)}, u32[]{:S(2)}, u32[]{:S(2)}) %collective-permute-start.10) | collective-permute-done | bytes 589856 | tf_op jit(solution)/shard_map/ppermute | solution.py:51
  169.8 1.0 fusion.346
  (173 shorter events, 11.4 us)
Async XLA Ops:
  0.7 1.3 copy-start.1
  1.6 1.0 copy-start
  2.8 0.7 copy-start.5
  3.7 0.7 copy-start.7
  4.6 0.7 copy-start.9
  5.3 2.1 %copy-start.2 = (f32[1,1,64,256]{3,2,1,0:T(8,128)S(1)}, f32[1,1,64,256]{3,2,1,0:T(8,128)}, u32[]{:S(2)}) copy-start(f32[1,1,64,256]{3,2,1,0:T(8,128)} %param.7) | copy-start | bytes 196612
  5.5 2.0 %copy-start.19 = (f32[1,64]{1,0:T(1,128)S(1)}, f32[1,64]{1,0:T(1,128)}, u32[]{:S(2)}) copy-start(f32[1,64]{1,0:T(1,128)} %param.6) | copy-start | bytes 772
  5.5 5.6 %collective-permute-start = (f32[1,64,256]{2,1,0:T(8,128)S(1)}, f32[1,64,256]{2,1,0:T(8,128)S(1)}, u32[]{:S(2)}, u32[]{:S(2)}) collective-permute-start(f32[1,64,256]{2,1,0:T(8,128)S(1)} %fusion.11), channel_id=1, source_target_pairs={{0,4},{4,8},{8,12},{12,16},{16,20},{20,24},{24,28},{28,32},{32,36}... | collective-permute-start | bytes 196616 | tf_op jit(solution)/shard_map/ppermute | solution.py:59
  12.0 0.7 copy-start.11
  12.9 0.7 copy-start.13
  15.4 3.5 %collective-permute-start.1 = (f32[130,256]{1,0:T(8,128)}, f32[130,256]{1,0:T(8,128)S(1)}, u32[]{:S(2)}, u32[]{:S(2)}) collective-permute-start(f32[130,256]{1,0:T(8,128)} %pad_maximum_fusion), channel_id=1, source_target_pairs={{0,4},{4,0},{8,12},{12,8},{16,20},{20,16},{24,28},{28,24},{32,36},... | collective-permute-start | bytes 399368 | tf_op jit(solution)/shard_map/ppermute | solution.py:20
  18.9 0.9 copy-start.4
  19.8 8.8 %collective-permute-start.2 = (f32[130,256]{1,0:T(8,128)}, f32[130,256]{1,0:T(8,128)S(1)}, u32[]{:S(2)}, u32[]{:S(2)}) collective-permute-start(f32[130,256]{1,0:T(8,128)} %pad_maximum_fusion.1), channel_id=1, source_target_pairs={{0,8},{4,12},{8,0},{12,4},{16,24},{20,28},{24,16},{28,20},{32,40},... | collective-permute-start | bytes 399368 | tf_op jit(solution)/shard_map/ppermute | solution.py:20
  30.4 9.1 %collective-permute-start.3 = (f32[130,256]{1,0:T(8,128)}, f32[130,256]{1,0:T(8,128)}, u32[]{:S(2)}, u32[]{:S(2)}) collective-permute-start(f32[130,256]{1,0:T(8,128)} %pad_maximum_fusion.2), channel_id=1, source_target_pairs={{0,16},{4,20},{8,24},{12,28},{16,0},{20,4},{24,8},{28,12},{32,48},... | collective-permute-start | bytes 399368 | tf_op jit(solution)/shard_map/ppermute | solution.py:20
  43.5 7.3 %collective-permute-start.4 = (f32[130,256]{1,0:T(8,128)}, f32[130,256]{1,0:T(8,128)}, u32[]{:S(2)}, u32[]{:S(2)}) collective-permute-start(f32[130,256]{1,0:T(8,128)} %pad_maximum_fusion.3), channel_id=1, source_target_pairs={{0,32},{4,36},{8,40},{12,44},{16,48},{20,52},{24,56},{28,60},{32,0... | collective-permute-start | bytes 399368 | tf_op jit(solution)/shard_map/ppermute | solution.py:20
  54.9 9.7 %collective-permute-start.5 = (f32[130,256]{1,0:T(8,128)}, f32[130,256]{1,0:T(8,128)S(1)}, u32[]{:S(2)}, u32[]{:S(2)}) collective-permute-start(f32[130,256]{1,0:T(8,128)} %pad_maximum_fusion.4), channel_id=1, source_target_pairs={{0,64},{4,68},{8,72},{12,76},{16,80},{20,84},{24,88},{28,92},{32,9... | collective-permute-start | bytes 399368 | tf_op jit(solution)/shard_map/ppermute | solution.py:20
  64.6 51.4 %copy-start.3 = (f32[130,256]{1,0:T(8,128)}, f32[130,256]{1,0:T(8,128)S(1)}, u32[]{:S(2)}) copy-start(f32[130,256]{1,0:T(8,128)S(1)} %collective-permute-done.5) | copy-start | bytes 399364
  65.6 0.6 copy-start.15
  66.3 21.6 %copy-start.16 = (f32[64,256]{1,0:T(8,128)S(1)}, f32[64,256]{1,0:T(8,128)}, u32[]{:S(2)}) copy-start(f32[64,256]{1,0:T(8,128)} %copy-done.15) | copy-start | bytes 196612
  67.0 19.4 %collective-permute-start.6 = (f32[130,256]{1,0:T(8,128)}, f32[130,256]{1,0:T(8,128)}, u32[]{:S(2)}, u32[]{:S(2)}) collective-permute-start(f32[130,256]{1,0:T(8,128)} %pad_maximum_fusion.5), channel_id=1, source_target_pairs={{0,128},{4,132},{8,136},{12,140},{16,144},{20,148},{24,152},{28,15... | collective-permute-start | bytes 399368 | tf_op jit(solution)/shard_map/ppermute | solution.py:20
  90.5 25.5 %collective-permute-start.7 = (f32[130,256]{1,0:T(8,128)}, f32[130,256]{1,0:T(8,128)}, u32[]{:S(2)}, u32[]{:S(2)}) collective-permute-start(f32[130,256]{1,0:T(8,128)} %pad_maximum_fusion.6), channel_id=1, source_target_pairs={{0,256},{4,260},{8,264},{12,268},{16,272},{20,276},{24,280},{28,28... | collective-permute-start | bytes 399368 | tf_op jit(solution)/shard_map/ppermute | solution.py:20
  118.2 0.8 copy-start.14
  119.7 0.8 copy-start.12
  121.6 2.2 %copy-start.17 = (f32[1,64,256]{2,1,0:T(8,128)}, f32[1,64,256]{2,1,0:T(8,128)S(1)}, u32[]{:S(2)}) copy-start(f32[1,64,256]{2,1,0:T(8,128)S(1)} %fusion.113) | copy-start | bytes 196612
  121.6 3.8 %collective-permute-start.8 = (f32[1,64,256]{2,1,0:T(8,128)S(1)}, f32[1,64,256]{2,1,0:T(8,128)S(1)}, u32[]{:S(2)}, u32[]{:S(2)}) collective-permute-start(f32[1,64,256]{2,1,0:T(8,128)S(1)} %fusion.113), channel_id=1, source_target_pairs={{4,0},{8,4},{12,8},{16,12},{20,16},{24,20},{28,24},{32,28},{36,32}... | collective-permute-start | bytes 196616 | tf_op jit(solution)/shard_map/ppermute | solution.py:59
  125.9 0.8 copy-start.10
  127.5 0.8 copy-start.8
  129.0 0.8 copy-start.6
  130.4 18.7 %collective-permute-start.9 = (f32[4,64,576]{2,1,0:T(8,128)S(1)}, f32[4,64,576]{2,1,0:T(8,128)S(1)}, u32[]{:S(2)}, u32[]{:S(2)}) collective-permute-start(f32[4,64,576]{2,1,0:T(8,128)S(1)} %maximum_add_fusion), channel_id=1, source_target_pairs={{0,1},{1,0},{2,3},{3,2},{4,5},{5,4},{6,7},{7,6},{8,9},{9,8},{10,11... | collective-permute-start | bytes 1769480 | tf_op jit(solution)/shard_map/ppermute | solution.py:51
  149.2 20.7 %collective-permute-start.10 = (f32[4,64,576]{2,1,0:T(8,128)S(1)}, f32[4,64,576]{2,1,0:T(8,128)S(1)}, u32[]{:S(2)}, u32[]{:S(2)}) collective-permute-start(f32[4,64,576]{2,1,0:T(8,128)S(1)} %fusion.345), channel_id=1, source_target_pairs={{0,2},{1,3},{2,0},{3,1},{4,6},{5,7},{6,4},{7,5},{8,10},{9,11},{10,... | collective-permute-start | bytes 1769480 | tf_op jit(solution)/shard_map/ppermute | solution.py:51
  154.6 0.8 copy-start.18

commit v11 on v5

--- a/solution.py
+++ b/solution.py
@@ -1,7 +1,11 @@
+import functools
+
 import jax
 import jax.numpy as jnp
 from jax import lax
 from jax.sharding import PartitionSpec as P
+from jax.experimental import pallas as pl
+from jax.experimental.pallas import tpu as pltpu
 
 WID = 16
 
@@ -90,17 +94,44 @@
     return accumulated
 
 
+def block_kernel(step_size, state_ref, weight_ref, out_ref, kept_ref):
+    current = state_ref[...]
+    pixels = current.shape[-1]
+    place = lax.broadcasted_iota(jnp.int32, (1, pixels), 1)
+    row, column = place // WID, place % WID
+    for layer in range(weight_ref.shape[0]):
+        kept_ref[layer] = current
+        squashed = jnp.tanh(current)
+        pieces = []
+        for down, right in TAP_OFFSETS:
+            shift = down * WID + right
+            moved = pltpu.roll(squashed, (-shift) % pixels, 1) if shift else squashed
+            inside = (row + down >= 0) & (row + down < WID) & (column + right >= 0) & (column + right < WID)
+            pieces.append(jnp.where(inside, moved, 0.0).astype(jnp.bfloat16))
+        patches = jnp.concatenate(pieces, axis=0)
+        mixed = jnp.dot(weight_ref[layer], patches, preferred_element_type=jnp.float32)
+        current = current + step_size * mixed
+    out_ref[...] = current
+
+
 def run_block(current, block_weights, step_size):
-    inputs_kept = []
-    for layer in range(block_weights.shape[0]):
-        inputs_kept.append(current)
-        squashed = jnp.tanh(current)
-        patches = unfold(squashed.astype(jnp.bfloat16), WID)
-        mixed = jnp.einsum(
-            "ok,bkp->bop", block_weights[layer], patches, preferred_element_type=jnp.float32
-        )
-        current = current + step_size * mixed
-    return (current, inputs_kept)
+    layers, channels, pixels = block_weights.shape[0], current.shape[-2], current.shape[-1]
+    spec = pl.BlockSpec(memory_space=pltpu.VMEM)
+    out, kept = pl.pallas_call(
+        functools.partial(block_kernel, step_size),
+        out_shape=(
+            jax.ShapeDtypeStruct((channels, pixels), jnp.float32),
+            jax.ShapeDtypeStruct((layers, channels, pixels), jnp.float32),
+        ),
+        in_specs=[spec, spec],
+        out_specs=(spec, spec),
+        cost_estimate=pl.CostEstimate(
+            flops=2 * layers * channels * block_weights.shape[-1] * pixels,
+            transcendentals=layers * channels * pixels,
+            bytes_accessed=4 * (layers + 2) * channels * pixels + 2 * block_weights.size,
+        ),
+    )(current.reshape(channels, pixels), block_weights)
+    return (out.reshape(current.shape), [kept[k].reshape(current.shape) for k in range(layers)])
 
 
 def back_block(inputs_kept, block_weights, upstream, step_size):

time: 162 us -> 145 us (0.90)
  other arithmetic: 24.6 us -> 9.86 us
  Pallas kernels: 0 us -> 5.66 us
  local copies, waits for them, and re-layouts: 7.52 us -> 2.84 us
  waiting for transfers between devices: 56.9 us -> 55 us
    pallas_call x0 -> x2, Pallas kernels: none -> 5.66 us  [run_block(): pl.pallas_call(functools.partial(block_kernel, step_size), out_shape=(jax...]
    another operation x14, other arithmetic: 4.14 us -> 0.7 us  [body(): jnp.stack([forward[3], reverse[3]])]
    concatenate x7, other arithmetic: 2.72 us -> 0.09 us  [pack(): return jnp.concatenate([states.reshape(-1, width)] + rows, axis=0)]
    unnamed x64 -> x27, other arithmetic: 4.68 us -> 2.21 us
    unnamed x34 -> x12, local copies, waits for them, and re-layouts: 4.25 us -> 1.82 us
    squeeze x6, local copies, waits for them, and re-layouts: 2.28 us -> 0.03 us  [exchange(): arrived[rows + k, :g.shape[0]]]
    ppermute x7, waiting for transfers between devices: 41.2 us -> 39.1 us  [exchange(): lax.ppermute(pack(gains, states), axis, [(i, i ^ 1 << bit) for i in range...]
    ppermute x7, starting transfers between devices: 40.3 us -> 42.1 us  [exchange(): lax.ppermute(pack(gains, states), axis, [(i, i ^ 1 << bit) for i in range...]
  transfers between devices with their start and end apart: 15 -> 15, of which waited for: 13 -> 14; matrix products, arithmetic and copies ran while one was open for 2% -> 1% of each run, Pallas kernels for 0% -> 0%
where the time goes in v11:
time: 145 us
  starting transfers between devices  65.7 us (45%)
  waiting for transfers between devices  55 us (38%)
  other arithmetic  9.86 us (7%)
  Pallas kernels  5.66 us (4%)
  matrix products  3.95 us (3%)
  local copies, waits for them, and re-layouts  2.84 us (2%)
  between operations  1.67 us (1%)
    ppermute x7, starting transfers between devices, exchange(): lax.ppermute(pack(gains, states), axis, [(i, i ^ 1 << bit) for i in range...  42.1 us
    ppermute x7, waiting for transfers between devices, exchange(): lax.ppermute(pack(gains, states), axis, [(i, i ^ 1 << bit) for i in range...  39.1 us
    ppermute x3, starting transfers between devices, dp_sum(): lax.ppermute(total, axis, pairs(k))  9.82 us
    ppermute x3, starting transfers between devices, dp_sum(): lax.ppermute(lax.dynamic_index_in_dim(terms, place ^ k, 0, False), axis,...  9.82 us
    ppermute x3, waiting for transfers between devices, dp_sum(): lax.ppermute(lax.dynamic_index_in_dim(terms, place ^ k, 0, False), axis,...  6.41 us
    pallas_call x2, Pallas kernels, run_block(): pl.pallas_call(functools.partial(block_kernel, step_size), out_shape=(jax...  5.66 us
    ppermute x2, waiting for transfers between devices, passed_along(): return lax.ppermute(block, axis, route)  4.86 us
    ppermute x3, waiting for transfers between devices, dp_sum(): lax.ppermute(total, axis, pairs(k))  4.69 us
  transfers between devices with their start and end apart: 15, of which 14 were waited for; matrix products, arithmetic and copies ran while one was open for 1% of the time, Pallas kernels for 0%

profile of v11, /device:TPU:2, one launch (start us, length us, event | category | flops | bytes accessed | tf_op | source)
XLA Modules:
  0.0 144.7 jit_solution(6528226651809661770)
XLA Ops:
  0.6 2.8 %shard_map.67 = (f32[64,256]{1,0:T(8,128)}, f32[4,64,256]{2,1,0:T(8,128)}) custom-call(f32[64,256]{1,0:T(8,128)} %bitcast.393, bf16[4,64,576]{2,1,0:T(8,128)(2,1)} %weight_ref.3), custom_call_target="tpu_custom_call" | custom-call | flops 75497472 | bytes 688128 | tf_op jit(solution)/shard_map/pallas_call | solution.py:120
  3.5 2.0 %collective-permute-start = (f32[1,64,256]{2,1,0:T(8,128)}, f32[1,64,256]{2,1,0:T(8,128)S(1)}, u32[]{:S(2)}, u32[]{:S(2)}) collective-permute-start(f32[1,64,256]{2,1,0:T(8,128)} %bitcast.425), channel_id=1, source_target_pairs={{0,4},{4,8},{8,12},{12,16},{16,20},{20,24},{24,28},{28,32},{32,36}... | collective-permute-start | bytes 196616 | tf_op jit(solution)/shard_map/ppermute | solution.py:69
  5.7 3.7 %collective-permute-done = f32[1,64,256]{2,1,0:T(8,128)S(1)} collective-permute-done((f32[1,64,256]{2,1,0:T(8,128)}, f32[1,64,256]{2,1,0:T(8,128)S(1)}, u32[]{:S(2)}, u32[]{:S(2)}) %collective-permute-start) | collective-permute-done | bytes 65568 | tf_op jit(solution)/shard_map/ppermute | solution.py:69
  9.4 0.6 fusion.259.state_ref
  10.0 2.8 %shard_map.68 = (f32[64,256]{1,0:T(8,128)}, f32[4,64,256]{2,1,0:T(8,128)}) custom-call(f32[64,256]{1,0:T(8,128)} %fusion.259.state_ref, bf16[4,64,576]{2,1,0:T(8,128)(2,1)} %weight_ref.3), custom_call_target="tpu_custom_call" | custom-call | flops 75497472 | bytes 688128 | tf_op jit(solution)/shard_map/pallas_call | solution.py:120
  12.9 0.9 bitcast_subtract_fusion.1
  13.8 1.9 %collective-permute-start.1 = (f32[130,256]{1,0:T(8,128)S(1)}, f32[130,256]{1,0:T(8,128)S(1)}, u32[]{:S(2)}, u32[]{:S(2)}) collective-permute-start(f32[130,256]{1,0:T(8,128)S(1)} %pad_maximum_fusion.1), channel_id=1, source_target_pairs={{0,4},{4,0},{8,12},{12,8},{16,20},{20,16},{24,28},{28,24},{32,36},... | collective-permute-start | bytes 399368 | tf_op jit(solution)/shard_map/ppermute | solution.py:24
  15.8 1.3 collective-permute-done.1
  17.3 4.4 %collective-permute-start.2 = (f32[130,256]{1,0:T(8,128)S(1)}, f32[130,256]{1,0:T(8,128)S(1)}, u32[]{:S(2)}, u32[]{:S(2)}) collective-permute-start(f32[130,256]{1,0:T(8,128)S(1)} %pad_maximum_fusion.2), channel_id=1, source_target_pairs={{0,8},{4,12},{8,0},{12,4},{16,24},{20,28},{24,16},{28,20},{32,40},... | collective-permute-start | bytes 399368 | tf_op jit(solution)/shard_map/ppermute | solution.py:24
  21.8 4.2 %collective-permute-done.2 = f32[130,256]{1,0:T(8,128)S(1)} collective-permute-done((f32[130,256]{1,0:T(8,128)S(1)}, f32[130,256]{1,0:T(8,128)S(1)}, u32[]{:S(2)}, u32[]{:S(2)}) %collective-permute-start.2) | collective-permute-done | bytes 133152 | tf_op jit(solution)/shard_map/ppermute | solution.py:24
  26.2 3.1 %collective-permute-start.3 = (f32[130,256]{1,0:T(8,128)S(1)}, f32[130,256]{1,0:T(8,128)S(1)}, u32[]{:S(2)}, u32[]{:S(2)}) collective-permute-start(f32[130,256]{1,0:T(8,128)S(1)} %pad_maximum_fusion.3), channel_id=1, source_target_pairs={{0,16},{4,20},{8,24},{12,28},{16,0},{20,4},{24,8},{28,12},{32,48},... | collective-permute-start | bytes 399368 | tf_op jit(solution)/shard_map/ppermute | solution.py:24
  29.3 5.7 %collective-permute-done.3 = f32[130,256]{1,0:T(8,128)S(1)} collective-permute-done((f32[130,256]{1,0:T(8,128)S(1)}, f32[130,256]{1,0:T(8,128)S(1)}, u32[]{:S(2)}, u32[]{:S(2)}) %collective-permute-start.3) | collective-permute-done | bytes 133152 | tf_op jit(solution)/shard_map/ppermute | solution.py:24
  35.2 3.6 %collective-permute-start.4 = (f32[130,256]{1,0:T(8,128)S(1)}, f32[130,256]{1,0:T(8,128)S(1)}, u32[]{:S(2)}, u32[]{:S(2)}) collective-permute-start(f32[130,256]{1,0:T(8,128)S(1)} %pad_maximum_fusion.4), channel_id=1, source_target_pairs={{0,32},{4,36},{8,40},{12,44},{16,48},{20,52},{24,56},{28,60},{32,0... | collective-permute-start | bytes 399368 | tf_op jit(solution)/shard_map/ppermute | solution.py:24
  38.9 3.3 %collective-permute-done.4 = f32[130,256]{1,0:T(8,128)S(1)} collective-permute-done((f32[130,256]{1,0:T(8,128)S(1)}, f32[130,256]{1,0:T(8,128)S(1)}, u32[]{:S(2)}, u32[]{:S(2)}) %collective-permute-start.4) | collective-permute-done | bytes 133152 | tf_op jit(solution)/shard_map/ppermute | solution.py:24
  42.5 5.0 %collective-permute-start.5 = (f32[130,256]{1,0:T(8,128)S(1)}, f32[130,256]{1,0:T(8,128)S(1)}, u32[]{:S(2)}, u32[]{:S(2)}) collective-permute-start(f32[130,256]{1,0:T(8,128)S(1)} %pad_maximum_fusion.5), channel_id=1, source_target_pairs={{0,64},{4,68},{8,72},{12,76},{16,80},{20,84},{24,88},{28,92},{32,9... | collective-permute-start | bytes 399368 | tf_op jit(solution)/shard_map/ppermute | solution.py:24
  47.5 4.5 %collective-permute-done.5 = f32[130,256]{1,0:T(8,128)S(1)} collective-permute-done((f32[130,256]{1,0:T(8,128)S(1)}, f32[130,256]{1,0:T(8,128)S(1)}, u32[]{:S(2)}, u32[]{:S(2)}) %collective-permute-start.5) | collective-permute-done | bytes 133152 | tf_op jit(solution)/shard_map/ppermute | solution.py:24
  52.3 9.9 %collective-permute-start.6 = (f32[130,256]{1,0:T(8,128)S(1)}, f32[130,256]{1,0:T(8,128)S(1)}, u32[]{:S(2)}, u32[]{:S(2)}) collective-permute-start(f32[130,256]{1,0:T(8,128)S(1)} %pad_maximum_fusion.6), channel_id=1, source_target_pairs={{0,128},{4,132},{8,136},{12,140},{16,144},{20,148},{24,152},{28,15... | collective-permute-start | bytes 399368 | tf_op jit(solution)/shard_map/ppermute | solution.py:24
  62.3 9.1 %collective-permute-done.6 = f32[130,256]{1,0:T(8,128)S(1)} collective-permute-done((f32[130,256]{1,0:T(8,128)S(1)}, f32[130,256]{1,0:T(8,128)S(1)}, u32[]{:S(2)}, u32[]{:S(2)}) %collective-permute-start.6) | collective-permute-done | bytes 133152 | tf_op jit(solution)/shard_map/ppermute | solution.py:24
  71.7 14.2 %collective-permute-start.7 = (f32[130,256]{1,0:T(8,128)S(1)}, f32[130,256]{1,0:T(8,128)S(1)}, u32[]{:S(2)}, u32[]{:S(2)}) collective-permute-start(f32[130,256]{1,0:T(8,128)S(1)} %pad_maximum_fusion.7), channel_id=1, source_target_pairs={{0,256},{4,260},{8,264},{12,268},{16,272},{20,276},{24,280},{28,28... | collective-permute-start | bytes 399368 | tf_op jit(solution)/shard_map/ppermute | solution.py:24
  86.0 11.0 %collective-permute-done.7 = f32[130,256]{1,0:T(8,128)S(1)} collective-permute-done((f32[130,256]{1,0:T(8,128)S(1)}, f32[130,256]{1,0:T(8,128)S(1)}, u32[]{:S(2)}, u32[]{:S(2)}) %collective-permute-start.7) | collective-permute-done | bytes 133152 | tf_op jit(solution)/shard_map/ppermute | solution.py:24
  97.1 0.3 convolution_bitcast_fusion.7
  97.4 0.9 copy-done.3
  98.3 0.2 fusion.37
  98.6 0.3 convolution_bitcast_fusion.6
  98.9 0.2 fusion.55
  99.1 0.3 convolution_bitcast_fusion.5
  99.4 0.2 fusion.73
  99.6 0.3 convolution_bitcast_fusion.4
  100.0 0.2 fusion.183
  100.2 1.9 %collective-permute-start.8 = (f32[1,64,256]{2,1,0:T(8,128)S(1)}, f32[1,64,256]{2,1,0:T(8,128)S(1)}, u32[]{:S(2)}, u32[]{:S(2)}) collective-permute-start(f32[1,64,256]{2,1,0:T(8,128)S(1)} %get-tuple-element.101), channel_id=1, source_target_pairs={{4,0},{8,4},{12,8},{16,12},{20,16},{24,20},{28,24},{32,28},{36,32}... | collective-permute-start | bytes 196616 | tf_op jit(solution)/shard_map/ppermute | solution.py:69
  102.1 0.8 fusion.26
  102.9 1.1 collective-permute-done.8
  104.0 0.3 convolution_bitcast_fusion.3
  104.4 0.9 copy-done.2
  105.3 0.2 fusion.109
  105.5 0.3 convolution_bitcast_fusion.2
  105.8 0.2 fusion.127
  106.0 0.3 convolution_bitcast_fusion.1
  106.4 0.2 fusion.187
  106.6 0.3 convolution_bitcast_fusion
  108.1 0.1 constant_dynamic-update-slice_fusion.37
  108.7 0.1 constant_dynamic-update-slice_fusion.36
  108.8 0.2 convolution_bitcast_fusion.12
  109.0 0.2 convolution_bitcast_fusion.13
  110.0 0.2 convolution_bitcast_fusion.14
  110.2 0.2 convolution_bitcast_fusion.15
  110.4 0.2 convolution_bitcast_fusion.8
  110.6 0.2 convolution_bitcast_fusion.9
  110.8 0.2 convolution_bitcast_fusion.10
  111.0 0.2 convolution_bitcast_fusion.11
  111.4 4.9 %collective-permute-start.11 = (f32[64,576]{1,0:T(8,128)S(1)}, f32[64,576]{1,0:T(8,128)S(1)}, u32[]{:S(2)}, u32[]{:S(2)}) collective-permute-start(f32[64,576]{1,0:T(8,128)S(1)} %get-tuple-element.26), channel_id=1, source_target_pairs={{0,3},{1,2},{2,1},{3,0},{4,7},{5,6},{6,5},{7,4},{8,11},{9,10},{10,... | collective-permute-start | bytes 442376 | tf_op jit(solution)/shard_map/ppermute | solution.py:56
  116.3 2.5 %collective-permute-start.10 = (f32[64,576]{1,0:T(8,128)S(1)}, f32[64,576]{1,0:T(8,128)S(1)}, u32[]{:S(2)}, u32[]{:S(2)}) collective-permute-start(f32[64,576]{1,0:T(8,128)S(1)} %get-tuple-element.27), channel_id=1, source_target_pairs={{0,2},{1,3},{2,0},{3,1},{4,6},{5,7},{6,4},{7,5},{8,10},{9,11},{10,... | collective-permute-start | bytes 442376 | tf_op jit(solution)/shard_map/ppermute | solution.py:56
  118.9 2.4 %collective-permute-start.9 = (f32[64,576]{1,0:T(8,128)S(1)}, f32[64,576]{1,0:T(8,128)S(1)}, u32[]{:S(2)}, u32[]{:S(2)}) collective-permute-start(f32[64,576]{1,0:T(8,128)S(1)} %get-tuple-element.25), channel_id=1, source_target_pairs={{0,1},{1,0},{2,3},{3,2},{4,5},{5,4},{6,7},{7,6},{8,9},{9,8},{10,11... | collective-permute-start | bytes 442376 | tf_op jit(solution)/shard_map/ppermute | solution.py:56
  121.3 5.0 %collective-permute-done.10 = f32[64,576]{1,0:T(8,128)S(1)} collective-permute-done((f32[64,576]{1,0:T(8,128)S(1)}, f32[64,576]{1,0:T(8,128)S(1)}, u32[]{:S(2)}, u32[]{:S(2)}) %collective-permute-start.10) | collective-permute-done | bytes 147488 | tf_op jit(solution)/shard_map/ppermute | solution.py:56
  126.3 1.4 collective-permute-done.9
  127.7 4.6 %collective-permute-start.14 = (f32[64,576]{1,0:T(8,128)S(1)}, f32[64,576]{1,0:T(8,128)S(1)}, u32[]{:S(2)}, u32[]{:S(2)}) collective-permute-start(f32[64,576]{1,0:T(8,128)S(1)} %fusion.9), channel_id=1, source_target_pairs={{0,3},{1,2},{2,1},{3,0},{4,7},{5,6},{6,5},{7,4},{8,11},{9,10},{10,... | collective-permute-start | bytes 442376 | tf_op jit(solution)/shard_map/ppermute | solution.py:62
  132.3 2.6 %collective-permute-start.13 = (f32[64,576]{1,0:T(8,128)S(1)}, f32[64,576]{1,0:T(8,128)S(1)}, u32[]{:S(2)}, u32[]{:S(2)}) collective-permute-start(f32[64,576]{1,0:T(8,128)S(1)} %fusion.9), channel_id=1, source_target_pairs={{0,2},{1,3},{2,0},{3,1},{4,6},{5,7},{6,4},{7,5},{8,10},{9,11},{10,... | collective-permute-start | bytes 442376 | tf_op jit(solution)/shard_map/ppermute | solution.py:62
  134.9 2.7 %collective-permute-start.12 = (f32[64,576]{1,0:T(8,128)S(1)}, f32[64,576]{1,0:T(8,128)S(1)}, u32[]{:S(2)}, u32[]{:S(2)}) collective-permute-start(f32[64,576]{1,0:T(8,128)S(1)} %fusion.9), channel_id=1, source_target_pairs={{0,1},{1,0},{2,3},{3,2},{4,5},{5,4},{6,7},{7,6},{8,9},{9,8},{10,11... | collective-permute-start | bytes 442376 | tf_op jit(solution)/shard_map/ppermute | solution.py:62
  137.6 0.8 fusion.179
  138.4 1.4 collective-permute-done.14
  139.8 3.0 %collective-permute-done.13 = f32[64,576]{1,0:T(8,128)S(1)} collective-permute-done((f32[64,576]{1,0:T(8,128)S(1)}, f32[64,576]{1,0:T(8,128)S(1)}, u32[]{:S(2)}, u32[]{:S(2)}) %collective-permute-start.13) | collective-permute-done | bytes 147488 | tf_op jit(solution)/shard_map/ppermute | solution.py:62
  142.8 0.3 collective-permute-done.12
  143.2 0.6 gather_fusion
  143.8 0.9 broadcast_select_fusion
  (111 shorter events, 4.4 us)
Async XLA Ops:
  0.6 4.9 %copy-start.1 = (f32[1,1,64,256]{3,2,1,0:T(8,128)S(1)}, f32[1,1,64,256]{3,2,1,0:T(8,128)}, u32[]{:S(2)}) copy-start(f32[1,1,64,256]{3,2,1,0:T(8,128)} %param.7) | copy-start | bytes 196612
  3.5 2.1 %copy-start.5 = (f32[1,64]{1,0:T(1,128)S(1)}, f32[1,64]{1,0:T(1,128)}, u32[]{:S(2)}) copy-start(f32[1,64]{1,0:T(1,128)} %param.6) | copy-start | bytes 772
  3.5 5.9 %collective-permute-start = (f32[1,64,256]{2,1,0:T(8,128)}, f32[1,64,256]{2,1,0:T(8,128)S(1)}, u32[]{:S(2)}, u32[]{:S(2)}) collective-permute-start(f32[1,64,256]{2,1,0:T(8,128)} %bitcast.425), channel_id=1, source_target_pairs={{0,4},{4,8},{8,12},{12,16},{16,20},{20,24},{24,28},{28,32},{32,36}... | collective-permute-start | bytes 196616 | tf_op jit(solution)/shard_map/ppermute | solution.py:69
  5.6 3.8 %copy-start.4 = (f32[1,1,64,256]{3,2,1,0:T(8,128)S(1)}, f32[1,1,64,256]{3,2,1,0:T(8,128)}, u32[]{:S(2)}) copy-start(f32[1,1,64,256]{3,2,1,0:T(8,128)} %param.4) | copy-start | bytes 196612
  13.8 3.3 %collective-permute-start.1 = (f32[130,256]{1,0:T(8,128)S(1)}, f32[130,256]{1,0:T(8,128)S(1)}, u32[]{:S(2)}, u32[]{:S(2)}) collective-permute-start(f32[130,256]{1,0:T(8,128)S(1)} %pad_maximum_fusion.1), channel_id=1, source_target_pairs={{0,4},{4,0},{8,12},{12,8},{16,20},{20,16},{24,28},{28,24},{32,36},... | collective-permute-start | bytes 399368 | tf_op jit(solution)/shard_map/ppermute | solution.py:24
  17.3 8.6 %collective-permute-start.2 = (f32[130,256]{1,0:T(8,128)S(1)}, f32[130,256]{1,0:T(8,128)S(1)}, u32[]{:S(2)}, u32[]{:S(2)}) collective-permute-start(f32[130,256]{1,0:T(8,128)S(1)} %pad_maximum_fusion.2), channel_id=1, source_target_pairs={{0,8},{4,12},{8,0},{12,4},{16,24},{20,28},{24,16},{28,20},{32,40},... | collective-permute-start | bytes 399368 | tf_op jit(solution)/shard_map/ppermute | solution.py:24
  26.2 8.8 %collective-permute-start.3 = (f32[130,256]{1,0:T(8,128)S(1)}, f32[130,256]{1,0:T(8,128)S(1)}, u32[]{:S(2)}, u32[]{:S(2)}) collective-permute-start(f32[130,256]{1,0:T(8,128)S(1)} %pad_maximum_fusion.3), channel_id=1, source_target_pairs={{0,16},{4,20},{8,24},{12,28},{16,0},{20,4},{24,8},{28,12},{32,48},... | collective-permute-start | bytes 399368 | tf_op jit(solution)/shard_map/ppermute | solution.py:24
  35.2 6.9 %collective-permute-start.4 = (f32[130,256]{1,0:T(8,128)S(1)}, f32[130,256]{1,0:T(8,128)S(1)}, u32[]{:S(2)}, u32[]{:S(2)}) collective-permute-start(f32[130,256]{1,0:T(8,128)S(1)} %pad_maximum_fusion.4), channel_id=1, source_target_pairs={{0,32},{4,36},{8,40},{12,44},{16,48},{20,52},{24,56},{28,60},{32,0... | collective-permute-start | bytes 399368 | tf_op jit(solution)/shard_map/ppermute | solution.py:24
  42.5 9.6 %collective-permute-start.5 = (f32[130,256]{1,0:T(8,128)S(1)}, f32[130,256]{1,0:T(8,128)S(1)}, u32[]{:S(2)}, u32[]{:S(2)}) collective-permute-start(f32[130,256]{1,0:T(8,128)S(1)} %pad_maximum_fusion.5), channel_id=1, source_target_pairs={{0,64},{4,68},{8,72},{12,76},{16,80},{20,84},{24,88},{28,92},{32,9... | collective-permute-start | bytes 399368 | tf_op jit(solution)/shard_map/ppermute | solution.py:24
  52.3 19.1 %collective-permute-start.6 = (f32[130,256]{1,0:T(8,128)S(1)}, f32[130,256]{1,0:T(8,128)S(1)}, u32[]{:S(2)}, u32[]{:S(2)}) collective-permute-start(f32[130,256]{1,0:T(8,128)S(1)} %pad_maximum_fusion.6), channel_id=1, source_target_pairs={{0,128},{4,132},{8,136},{12,140},{16,144},{20,148},{24,152},{28,15... | collective-permute-start | bytes 399368 | tf_op jit(solution)/shard_map/ppermute | solution.py:24
  71.7 25.4 %copy-start = (bf16[4,64,576]{2,1,0:T(8,128)(2,1)S(1)}, bf16[4,64,576]{2,1,0:T(8,128)(2,1)}, u32[]{:S(2)}) copy-start(bf16[4,64,576]{2,1,0:T(8,128)(2,1)} %weight_ref.3) | copy-start | bytes 884740
  71.7 25.2 %collective-permute-start.7 = (f32[130,256]{1,0:T(8,128)S(1)}, f32[130,256]{1,0:T(8,128)S(1)}, u32[]{:S(2)}, u32[]{:S(2)}) collective-permute-start(f32[130,256]{1,0:T(8,128)S(1)} %pad_maximum_fusion.7), channel_id=1, source_target_pairs={{0,256},{4,260},{8,264},{12,268},{16,272},{20,276},{24,280},{28,28... | collective-permute-start | bytes 399368 | tf_op jit(solution)/shard_map/ppermute | solution.py:24
  97.4 1.0 copy-start.3
  100.2 3.8 %collective-permute-start.8 = (f32[1,64,256]{2,1,0:T(8,128)S(1)}, f32[1,64,256]{2,1,0:T(8,128)S(1)}, u32[]{:S(2)}, u32[]{:S(2)}) collective-permute-start(f32[1,64,256]{2,1,0:T(8,128)S(1)} %get-tuple-element.101), channel_id=1, source_target_pairs={{4,0},{8,4},{12,8},{16,12},{20,16},{24,20},{28,24},{32,28},{36,32}... | collective-permute-start | bytes 196616 | tf_op jit(solution)/shard_map/ppermute | solution.py:69
  104.3 1.0 copy-start.2
  111.4 9.9 %collective-permute-start.11 = (f32[64,576]{1,0:T(8,128)S(1)}, f32[64,576]{1,0:T(8,128)S(1)}, u32[]{:S(2)}, u32[]{:S(2)}) collective-permute-start(f32[64,576]{1,0:T(8,128)S(1)} %get-tuple-element.26), channel_id=1, source_target_pairs={{0,3},{1,2},{2,1},{3,0},{4,7},{5,6},{6,5},{7,4},{8,11},{9,10},{10,... | collective-permute-start | bytes 442376 | tf_op jit(solution)/shard_map/ppermute | solution.py:56
  116.3 10.0 %collective-permute-start.10 = (f32[64,576]{1,0:T(8,128)S(1)}, f32[64,576]{1,0:T(8,128)S(1)}, u32[]{:S(2)}, u32[]{:S(2)}) collective-permute-start(f32[64,576]{1,0:T(8,128)S(1)} %get-tuple-element.27), channel_id=1, source_target_pairs={{0,2},{1,3},{2,0},{3,1},{4,6},{5,7},{6,4},{7,5},{8,10},{9,11},{10,... | collective-permute-start | bytes 442376 | tf_op jit(solution)/shard_map/ppermute | solution.py:56
  118.9 8.8 %collective-permute-start.9 = (f32[64,576]{1,0:T(8,128)S(1)}, f32[64,576]{1,0:T(8,128)S(1)}, u32[]{:S(2)}, u32[]{:S(2)}) collective-permute-start(f32[64,576]{1,0:T(8,128)S(1)} %get-tuple-element.25), channel_id=1, source_target_pairs={{0,1},{1,0},{2,3},{3,2},{4,5},{5,4},{6,7},{7,6},{8,9},{9,8},{10,11... | collective-permute-start | bytes 442376 | tf_op jit(solution)/shard_map/ppermute | solution.py:56
  127.7 12.1 %collective-permute-start.14 = (f32[64,576]{1,0:T(8,128)S(1)}, f32[64,576]{1,0:T(8,128)S(1)}, u32[]{:S(2)}, u32[]{:S(2)}) collective-permute-start(f32[64,576]{1,0:T(8,128)S(1)} %fusion.9), channel_id=1, source_target_pairs={{0,3},{1,2},{2,1},{3,0},{4,7},{5,6},{6,5},{7,4},{8,11},{9,10},{10,... | collective-permute-start | bytes 442376 | tf_op jit(solution)/shard_map/ppermute | solution.py:62
  132.3 10.5 %collective-permute-start.13 = (f32[64,576]{1,0:T(8,128)S(1)}, f32[64,576]{1,0:T(8,128)S(1)}, u32[]{:S(2)}, u32[]{:S(2)}) collective-permute-start(f32[64,576]{1,0:T(8,128)S(1)} %fusion.9), channel_id=1, source_target_pairs={{0,2},{1,3},{2,0},{3,1},{4,6},{5,7},{6,4},{7,5},{8,10},{9,11},{10,... | collective-permute-start | bytes 442376 | tf_op jit(solution)/shard_map/ppermute | solution.py:62
  134.9 8.2 %collective-permute-start.12 = (f32[64,576]{1,0:T(8,128)S(1)}, f32[64,576]{1,0:T(8,128)S(1)}, u32[]{:S(2)}, u32[]{:S(2)}) collective-permute-start(f32[64,576]{1,0:T(8,128)S(1)} %fusion.9), channel_id=1, source_target_pairs={{0,1},{1,0},{2,3},{3,2},{4,5},{5,4},{6,7},{7,6},{8,9},{9,8},{10,11... | collective-permute-start | bytes 442376 | tf_op jit(solution)/shard_map/ppermute | solution.py:62

commit v12 on v11

--- a/solution.py
+++ b/solution.py
@@ -94,24 +94,54 @@
     return accumulated
 
 
+def unfold_taps(squashed, row, column):
+    pixels = squashed.shape[-1]
+    pieces = []
+    for down, right in TAP_OFFSETS:
+        shift = down * WID + right
+        moved = pltpu.roll(squashed, (-shift) % pixels, 1) if shift else squashed
+        inside = (row + down >= 0) & (row + down < WID) & (column + right >= 0) & (column + right < WID)
+        pieces.append(jnp.where(inside, moved, 0.0).astype(jnp.bfloat16))
+    return jnp.concatenate(pieces, axis=0)
+
+
+def pixel_grid(pixels):
+    place = lax.broadcasted_iota(jnp.int32, (1, pixels), 1)
+    return place // WID, place % WID
+
+
 def block_kernel(step_size, state_ref, weight_ref, out_ref, kept_ref):
     current = state_ref[...]
-    pixels = current.shape[-1]
-    place = lax.broadcasted_iota(jnp.int32, (1, pixels), 1)
-    row, column = place // WID, place % WID
+    row, column = pixel_grid(current.shape[-1])
     for layer in range(weight_ref.shape[0]):
         kept_ref[layer] = current
-        squashed = jnp.tanh(current)
-        pieces = []
-        for down, right in TAP_OFFSETS:
-            shift = down * WID + right
-            moved = pltpu.roll(squashed, (-shift) % pixels, 1) if shift else squashed
-            inside = (row + down >= 0) & (row + down < WID) & (column + right >= 0) & (column + right < WID)
-            pieces.append(jnp.where(inside, moved, 0.0).astype(jnp.bfloat16))
-        patches = jnp.concatenate(pieces, axis=0)
+        patches = unfold_taps(jnp.tanh(current), row, column)
         mixed = jnp.dot(weight_ref[layer], patches, preferred_element_type=jnp.float32)
         current = current + step_size * mixed
     out_ref[...] = current
+
+
+def back_kernel(step_size, kept_ref, flipped_ref, upstream_ref, out_ref, grads_ref):
+    upstream = upstream_ref[...]
+    channels, pixels = upstream.shape
+    row, column = pixel_grid(pixels)
+    for layer in reversed(range(kept_ref.shape[0])):
+        squashed = jnp.tanh(kept_ref[layer])
+        patches = unfold_taps(squashed, row, column)
+        scaled = (step_size * upstream).astype(jnp.bfloat16)
+        grads_ref[layer] = lax.dot_general(
+            scaled, patches, (((1,), (1,)), ((), ())), preferred_element_type=jnp.float32
+        )
+        spread = jnp.dot(flipped_ref[layer], scaled, preferred_element_type=jnp.float32)
+        folded = jnp.zeros((channels, pixels), jnp.float32)
+        for tap, (down, right) in enumerate(TAP_OFFSETS):
+            shift = down * WID + right
+            piece = spread[tap * channels : (tap + 1) * channels]
+            moved = pltpu.roll(piece, shift % pixels, 1) if shift else piece
+            inside = (row - down >= 0) & (row - down < WID) & (column - right >= 0) & (column - right < WID)
+            folded = folded + jnp.where(inside, moved, 0.0)
+        upstream = upstream + (1.0 - squashed * squashed) * folded
+    out_ref[...] = upstream
 
 
 def run_block(current, block_weights, step_size):
@@ -135,20 +165,25 @@
 
 
 def back_block(inputs_kept, block_weights, upstream, step_size):
-    layer_count = block_weights.shape[0]
-    layer_grads = [None] * layer_count
-    for layer in reversed(range(layer_count)):
-        squashed = jnp.tanh(inputs_kept[layer])
-        patches = unfold(squashed.astype(jnp.bfloat16), WID)
-        scaled = (step_size * upstream).astype(jnp.bfloat16)
-        layer_grads[layer] = jnp.einsum(
-            "bop,bkp->ok", scaled, patches, preferred_element_type=jnp.float32
-        )
-        spread = jnp.einsum(
-            "ok,bop->bkp", block_weights[layer], scaled, preferred_element_type=jnp.float32
-        )
-        upstream = upstream + (1.0 - squashed * squashed) * fold_taps(spread, WID)
-    return (upstream, jnp.stack(layer_grads))
+    layers, channels, pixels = block_weights.shape[0], upstream.shape[-2], upstream.shape[-1]
+    taps = block_weights.shape[-1]
+    flipped = jnp.swapaxes(block_weights, 1, 2)
+    spec = pl.BlockSpec(memory_space=pltpu.VMEM)
+    out, grads = pl.pallas_call(
+        functools.partial(back_kernel, step_size),
+        out_shape=(
+            jax.ShapeDtypeStruct((channels, pixels), jnp.float32),
+            jax.ShapeDtypeStruct((layers, channels, taps), jnp.float32),
+        ),
+        in_specs=[spec, spec, spec],
+        out_specs=(spec, spec),
+        cost_estimate=pl.CostEstimate(
+            flops=4 * layers * channels * taps * pixels,
+            transcendentals=layers * channels * pixels,
+            bytes_accessed=4 * (layers + 2) * channels * pixels + 2 * block_weights.size + 4 * layers * channels * taps,
+        ),
+    )(jnp.stack(inputs_kept).reshape(layers, channels, pixels), flipped, upstream.reshape(channels, pixels))
+    return (out.reshape(upstream.shape), grads)
 
 
 def body(cpoints, weights, coarse_gain, cotangent):

time: 145 us -> 145 us (level)
  Pallas kernels: 5.66 us -> 12.7 us
  matrix products: 3.95 us -> 0 us
  waiting for transfers between devices: 55 us -> 53.1 us
    pallas_call x0 -> x2, Pallas kernels: none -> 7.01 us  [back_block(): pl.pallas_call(functools.partial(back_kernel, step_size), out_shape=(jax....]
    dot_general x16 -> x0, matrix products: 3.95 us -> none  [the longest x8 2.25 us: back_block(): jnp.einsum('ok,bop->bkp', block_weights[layer], scaled, preferred_element...]
    ppermute x7, waiting for transfers between devices: 39.1 us -> 36.6 us  [exchange(): lax.ppermute(pack(gains, states), axis, [(i, i ^ 1 << bit) for i in range...]
    unnamed x27 -> x0, other arithmetic: 2.21 us -> none
    reshape x0 -> x3, other arithmetic: none -> 2.08 us  [the longest x2 1.45 us: back_block(): jnp.stack(inputs_kept).reshape(layers, channels, pixels)]
  transfers between devices with their start and end apart: 15 -> 15, of which waited for: 14 -> 14; matrix products, arithmetic and copies ran while one was open for 1% -> 3% of each run, Pallas kernels for 0% -> 0%
where the time goes in v12:
time: 145 us
  starting transfers between devices  66.1 us (46%)
  waiting for transfers between devices  53.1 us (37%)
  Pallas kernels  12.7 us (9%)
  other arithmetic  9.48 us (7%)
  local copies, waits for them, and re-layouts  1.86 us (1%)
    ppermute x7, starting transfers between devices, exchange(): lax.ppermute(pack(gains, states), axis, [(i, i ^ 1 << bit) for i in range...  42.4 us
    ppermute x7, waiting for transfers between devices, exchange(): lax.ppermute(pack(gains, states), axis, [(i, i ^ 1 << bit) for i in range...  36.6 us
    ppermute x3, starting transfers between devices, dp_sum(): lax.ppermute(lax.dynamic_index_in_dim(terms, place ^ k, 0, False), axis,...  9.82 us
    ppermute x3, starting transfers between devices, dp_sum(): lax.ppermute(total, axis, pairs(k))  9.81 us
    pallas_call x2, Pallas kernels, back_block(): pl.pallas_call(functools.partial(back_kernel, step_size), out_shape=(jax....  7.01 us
    ppermute x2, waiting for transfers between devices, passed_along(): return lax.ppermute(block, axis, route)  5.92 us
    ppermute x3, waiting for transfers between devices, dp_sum(): lax.ppermute(lax.dynamic_index_in_dim(terms, place ^ k, 0, False), axis,...  5.79 us
    pallas_call x2, Pallas kernels, run_block(): pl.pallas_call(functools.partial(block_kernel, step_size), out_shape=(jax...  5.66 us
  transfers between devices with their start and end apart: 15, of which 14 were waited for; matrix products, arithmetic and copies ran while one was open for 3% of the time, Pallas kernels for 0%

profile of v12, /device:TPU:2, one launch (start us, length us, event | category | flops | bytes accessed | tf_op | source)
XLA Modules:
  0.0 144.6 jit_solution(7727419293478812978)
XLA Ops:
  0.6 2.8 %shard_map.67 = (f32[64,256]{1,0:T(8,128)}, f32[4,64,256]{2,1,0:T(8,128)}) custom-call(f32[64,256]{1,0:T(8,128)} %bitcast.289, bf16[4,64,576]{2,1,0:T(8,128)(2,1)} %weight_ref.3), custom_call_target="tpu_custom_call" | custom-call | flops 75497472 | bytes 688128 | tf_op jit(solution)/shard_map/pallas_call | solution.py:150
  3.5 2.0 %collective-permute-start = (f32[1,64,256]{2,1,0:T(8,128)}, f32[1,64,256]{2,1,0:T(8,128)S(1)}, u32[]{:S(2)}, u32[]{:S(2)}) collective-permute-start(f32[1,64,256]{2,1,0:T(8,128)} %bitcast.322), channel_id=1, source_target_pairs={{0,4},{4,8},{8,12},{12,16},{16,20},{20,24},{24,28},{28,32},{32,36}... | collective-permute-start | bytes 196616 | tf_op jit(solution)/shard_map/ppermute | solution.py:69
  5.6 0.0 copy-start.3
  5.6 0.1 broadcast_multiply_fusion
  5.7 3.7 %collective-permute-done = f32[1,64,256]{2,1,0:T(8,128)S(1)} collective-permute-done((f32[1,64,256]{2,1,0:T(8,128)}, f32[1,64,256]{2,1,0:T(8,128)S(1)}, u32[]{:S(2)}, u32[]{:S(2)}) %collective-permute-start) | collective-permute-done | bytes 65568 | tf_op jit(solution)/shard_map/ppermute | solution.py:69
  9.4 0.6 fusion.13.state_ref
  10.0 2.8 %shard_map.68 = (f32[64,256]{1,0:T(8,128)}, f32[4,64,256]{2,1,0:T(8,128)}) custom-call(f32[64,256]{1,0:T(8,128)} %fusion.13.state_ref, bf16[4,64,576]{2,1,0:T(8,128)(2,1)} %weight_ref.3), custom_call_target="tpu_custom_call" | custom-call | flops 75497472 | bytes 688128 | tf_op jit(solution)/shard_map/pallas_call | solution.py:150
  12.9 0.9 bitcast_subtract_fusion.1
  13.8 1.9 %collective-permute-start.1 = (f32[130,256]{1,0:T(8,128)S(1)}, f32[130,256]{1,0:T(8,128)S(1)}, u32[]{:S(2)}, u32[]{:S(2)}) collective-permute-start(f32[130,256]{1,0:T(8,128)S(1)} %pad_maximum_fusion.1), channel_id=1, source_target_pairs={{0,4},{4,0},{8,12},{12,8},{16,20},{20,16},{24,28},{28,24},{32,36},... | collective-permute-start | bytes 399368 | tf_op jit(solution)/shard_map/ppermute | solution.py:24
  15.8 1.3 collective-permute-done.1
  17.1 0.1 add_select_fusion.17
  17.2 0.1 fusion.27
  17.3 4.4 %collective-permute-start.2 = (f32[130,256]{1,0:T(8,128)S(1)}, f32[130,256]{1,0:T(8,128)S(1)}, u32[]{:S(2)}, u32[]{:S(2)}) collective-permute-start(f32[130,256]{1,0:T(8,128)S(1)} %pad_maximum_fusion.2), channel_id=1, source_target_pairs={{0,8},{4,12},{8,0},{12,4},{16,24},{20,28},{24,16},{28,20},{32,40},... | collective-permute-start | bytes 399368 | tf_op jit(solution)/shard_map/ppermute | solution.py:24
  21.8 4.2 %collective-permute-done.2 = f32[130,256]{1,0:T(8,128)S(1)} collective-permute-done((f32[130,256]{1,0:T(8,128)S(1)}, f32[130,256]{1,0:T(8,128)S(1)}, u32[]{:S(2)}, u32[]{:S(2)}) %collective-permute-start.2) | collective-permute-done | bytes 133152 | tf_op jit(solution)/shard_map/ppermute | solution.py:24
  26.0 0.1 fusion.25
  26.1 0.1 fusion.11
  26.2 3.1 %collective-permute-start.3 = (f32[130,256]{1,0:T(8,128)S(1)}, f32[130,256]{1,0:T(8,128)S(1)}, u32[]{:S(2)}, u32[]{:S(2)}) collective-permute-start(f32[130,256]{1,0:T(8,128)S(1)} %pad_maximum_fusion.3), channel_id=1, source_target_pairs={{0,16},{4,20},{8,24},{12,28},{16,0},{20,4},{24,8},{28,12},{32,48},... | collective-permute-start | bytes 399368 | tf_op jit(solution)/shard_map/ppermute | solution.py:24
  29.3 5.7 %collective-permute-done.3 = f32[130,256]{1,0:T(8,128)S(1)} collective-permute-done((f32[130,256]{1,0:T(8,128)S(1)}, f32[130,256]{1,0:T(8,128)S(1)}, u32[]{:S(2)}, u32[]{:S(2)}) %collective-permute-start.3) | collective-permute-done | bytes 133152 | tf_op jit(solution)/shard_map/ppermute | solution.py:24
  35.0 0.1 add_select_fusion.15
  35.1 0.1 fusion.28
  35.2 0.0 copy-start.5
  35.3 3.8 %collective-permute-start.4 = (f32[130,256]{1,0:T(8,128)S(1)}, f32[130,256]{1,0:T(8,128)S(1)}, u32[]{:S(2)}, u32[]{:S(2)}) collective-permute-start(f32[130,256]{1,0:T(8,128)S(1)} %pad_maximum_fusion.4), channel_id=1, source_target_pairs={{0,32},{4,36},{8,40},{12,44},{16,48},{20,52},{24,56},{28,60},{32,0... | collective-permute-start | bytes 399368 | tf_op jit(solution)/shard_map/ppermute | solution.py:24
  39.1 3.3 %collective-permute-done.4 = f32[130,256]{1,0:T(8,128)S(1)} collective-permute-done((f32[130,256]{1,0:T(8,128)S(1)}, f32[130,256]{1,0:T(8,128)S(1)}, u32[]{:S(2)}, u32[]{:S(2)}) %collective-permute-start.4) | collective-permute-done | bytes 133152 | tf_op jit(solution)/shard_map/ppermute | solution.py:24
  42.4 0.1 fusion.26
  42.5 0.1 fusion.9
  42.6 5.0 %collective-permute-start.5 = (f32[130,256]{1,0:T(8,128)S(1)}, f32[130,256]{1,0:T(8,128)S(1)}, u32[]{:S(2)}, u32[]{:S(2)}) collective-permute-start(f32[130,256]{1,0:T(8,128)S(1)} %pad_maximum_fusion.5), channel_id=1, source_target_pairs={{0,64},{4,68},{8,72},{12,76},{16,80},{20,84},{24,88},{28,92},{32,9... | collective-permute-start | bytes 399368 | tf_op jit(solution)/shard_map/ppermute | solution.py:24
  47.6 4.5 %collective-permute-done.5 = f32[130,256]{1,0:T(8,128)S(1)} collective-permute-done((f32[130,256]{1,0:T(8,128)S(1)}, f32[130,256]{1,0:T(8,128)S(1)}, u32[]{:S(2)}, u32[]{:S(2)}) %collective-permute-start.5) | collective-permute-done | bytes 133152 | tf_op jit(solution)/shard_map/ppermute | solution.py:24
  52.2 0.1 add_select_fusion.13
  52.3 0.1 fusion.29
  52.4 0.0 copy-start
  52.5 10.0 %collective-permute-start.6 = (f32[130,256]{1,0:T(8,128)S(1)}, f32[130,256]{1,0:T(8,128)S(1)}, u32[]{:S(2)}, u32[]{:S(2)}) collective-permute-start(f32[130,256]{1,0:T(8,128)S(1)} %pad_maximum_fusion.6), channel_id=1, source_target_pairs={{0,128},{4,132},{8,136},{12,140},{16,144},{20,148},{24,152},{28,15... | collective-permute-start | bytes 399368 | tf_op jit(solution)/shard_map/ppermute | solution.py:24
  62.5 1.1 copy.8
  63.6 0.7 maximum_bitcast_fusion.kept_ref
  64.3 7.4 %collective-permute-done.6 = f32[130,256]{1,0:T(8,128)S(1)} collective-permute-done((f32[130,256]{1,0:T(8,128)S(1)}, f32[130,256]{1,0:T(8,128)S(1)}, u32[]{:S(2)}, u32[]{:S(2)}) %collective-permute-start.6) | collective-permute-done | bytes 133152 | tf_op jit(solution)/shard_map/ppermute | solution.py:24
  71.7 0.1 select_bitcast_fusion
  71.8 0.1 fusion.7
  72.0 0.0 copy-start.4
  72.0 14.2 %collective-permute-start.7 = (f32[130,256]{1,0:T(8,128)S(1)}, f32[130,256]{1,0:T(8,128)S(1)}, u32[]{:S(2)}, u32[]{:S(2)}) collective-permute-start(f32[130,256]{1,0:T(8,128)S(1)} %pad_maximum_fusion.7), channel_id=1, source_target_pairs={{0,256},{4,260},{8,264},{12,268},{16,272},{20,276},{24,280},{28,28... | collective-permute-start | bytes 399368 | tf_op jit(solution)/shard_map/ppermute | solution.py:24
  86.3 0.7 maximum_bitcast_fusion.1.kept_ref
  87.0 10.2 %collective-permute-done.7 = f32[130,256]{1,0:T(8,128)S(1)} collective-permute-done((f32[130,256]{1,0:T(8,128)S(1)}, f32[130,256]{1,0:T(8,128)S(1)}, u32[]{:S(2)}, u32[]{:S(2)}) %collective-permute-start.7) | collective-permute-done | bytes 133152 | tf_op jit(solution)/shard_map/ppermute | solution.py:24
  97.2 0.8 bitcast_add_fusion.11
  98.0 3.5 %shard_map.69 = (f32[64,256]{1,0:T(8,128)}, f32[4,64,576]{2,1,0:T(8,128)}) custom-call(f32[4,64,256]{2,1,0:T(8,128)} %maximum_bitcast_fusion.1.kept_ref, bf16[4,576,64]{2,1,0:T(8,128)(2,1)} %bitcast.281, f32[64,256]{1,0:T(8,128)} %get-tuple-element.19.upstream_ref), custom_call_target="tpu_custom_call" | custom-call | flops 150994944 | bytes 1277952 | tf_op jit(solution)/shard_map/pallas_call | solution.py:172
  101.5 2.0 %collective-permute-start.8 = (f32[1,64,256]{2,1,0:T(8,128)}, f32[1,64,256]{2,1,0:T(8,128)S(1)}, u32[]{:S(2)}, u32[]{:S(2)}) collective-permute-start(f32[1,64,256]{2,1,0:T(8,128)} %bitcast.301), channel_id=1, source_target_pairs={{4,0},{8,4},{12,8},{16,12},{20,16},{24,20},{28,24},{32,28},{36,32}... | collective-permute-start | bytes 196616 | tf_op jit(solution)/shard_map/ppermute | solution.py:69
  103.6 2.2 %collective-permute-done.8 = f32[1,64,256]{2,1,0:T(8,128)S(1)} collective-permute-done((f32[1,64,256]{2,1,0:T(8,128)}, f32[1,64,256]{2,1,0:T(8,128)S(1)}, u32[]{:S(2)}, u32[]{:S(2)}) %collective-permute-start.8) | collective-permute-done | bytes 65568 | tf_op jit(solution)/shard_map/ppermute | solution.py:69
  105.7 0.6 fusion.5.upstream_ref
  106.4 3.5 %shard_map.70 = (f32[64,256]{1,0:T(8,128)}, f32[4,64,576]{2,1,0:T(8,128)}) custom-call(f32[4,64,256]{2,1,0:T(8,128)} %maximum_bitcast_fusion.kept_ref, bf16[4,576,64]{2,1,0:T(8,128)(2,1)} %bitcast.282, f32[64,256]{1,0:T(8,128)} %fusion.5.upstream_ref), custom_call_target="tpu_custom_call" | custom-call | flops 150994944 | bytes 1277952 | tf_op jit(solution)/shard_map/pallas_call | solution.py:172
  109.9 1.2 add.276
  111.1 4.9 %collective-permute-start.11 = (f32[64,576]{1,0:T(8,128)S(1)}, f32[64,576]{1,0:T(8,128)S(1)}, u32[]{:S(2)}, u32[]{:S(2)}) collective-permute-start(f32[64,576]{1,0:T(8,128)S(1)} %get-tuple-element.34), channel_id=1, source_target_pairs={{0,3},{1,2},{2,1},{3,0},{4,7},{5,6},{6,5},{7,4},{8,11},{9,10},{10,... | collective-permute-start | bytes 442376 | tf_op jit(solution)/shard_map/ppermute | solution.py:56
  116.1 2.5 %collective-permute-start.10 = (f32[64,576]{1,0:T(8,128)S(1)}, f32[64,576]{1,0:T(8,128)S(1)}, u32[]{:S(2)}, u32[]{:S(2)}) collective-permute-start(f32[64,576]{1,0:T(8,128)S(1)} %get-tuple-element.35), channel_id=1, source_target_pairs={{0,2},{1,3},{2,0},{3,1},{4,6},{5,7},{6,4},{7,5},{8,10},{9,11},{10,... | collective-permute-start | bytes 442376 | tf_op jit(solution)/shard_map/ppermute | solution.py:56
  118.6 2.4 %collective-permute-start.9 = (f32[64,576]{1,0:T(8,128)S(1)}, f32[64,576]{1,0:T(8,128)S(1)}, u32[]{:S(2)}, u32[]{:S(2)}) collective-permute-start(f32[64,576]{1,0:T(8,128)S(1)} %get-tuple-element.33), channel_id=1, source_target_pairs={{0,1},{1,0},{2,3},{3,2},{4,5},{5,4},{6,7},{7,6},{8,9},{9,8},{10,11... | collective-permute-start | bytes 442376 | tf_op jit(solution)/shard_map/ppermute | solution.py:56
  121.0 0.8 fusion.2
  121.7 0.0 collective-permute-done.11
  121.8 4.4 %collective-permute-done.10 = f32[64,576]{1,0:T(8,128)S(1)} collective-permute-done((f32[64,576]{1,0:T(8,128)S(1)}, f32[64,576]{1,0:T(8,128)S(1)}, u32[]{:S(2)}, u32[]{:S(2)}) %collective-permute-start.10) | collective-permute-done | bytes 147488 | tf_op jit(solution)/shard_map/ppermute | solution.py:56
  126.2 1.4 collective-permute-done.9
  127.5 0.1 fusion.1
  127.6 4.6 %collective-permute-start.14 = (f32[64,576]{1,0:T(8,128)S(1)}, f32[64,576]{1,0:T(8,128)S(1)}, u32[]{:S(2)}, u32[]{:S(2)}) collective-permute-start(f32[64,576]{1,0:T(8,128)S(1)} %fusion.1), channel_id=1, source_target_pairs={{0,3},{1,2},{2,1},{3,0},{4,7},{5,6},{6,5},{7,4},{8,11},{9,10},{10,... | collective-permute-start | bytes 442376 | tf_op jit(solution)/shard_map/ppermute | solution.py:62
  132.2 2.6 %collective-permute-start.13 = (f32[64,576]{1,0:T(8,128)S(1)}, f32[64,576]{1,0:T(8,128)S(1)}, u32[]{:S(2)}, u32[]{:S(2)}) collective-permute-start(f32[64,576]{1,0:T(8,128)S(1)} %fusion.1), channel_id=1, source_target_pairs={{0,2},{1,3},{2,0},{3,1},{4,6},{5,7},{6,4},{7,5},{8,10},{9,11},{10,... | collective-permute-start | bytes 442376 | tf_op jit(solution)/shard_map/ppermute | solution.py:62
  134.8 2.7 %collective-permute-start.12 = (f32[64,576]{1,0:T(8,128)S(1)}, f32[64,576]{1,0:T(8,128)S(1)}, u32[]{:S(2)}, u32[]{:S(2)}) collective-permute-start(f32[64,576]{1,0:T(8,128)S(1)} %fusion.1), channel_id=1, source_target_pairs={{0,1},{1,0},{2,3},{3,2},{4,5},{5,4},{6,7},{7,6},{8,9},{9,8},{10,11... | collective-permute-start | bytes 442376 | tf_op jit(solution)/shard_map/ppermute | solution.py:62
  137.5 0.6 fusion.3
  138.1 1.4 %collective-permute-done.14 = f32[64,576]{1,0:T(8,128)S(1)} collective-permute-done((f32[64,576]{1,0:T(8,128)S(1)}, f32[64,576]{1,0:T(8,128)S(1)}, u32[]{:S(2)}, u32[]{:S(2)}) %collective-permute-start.14) | collective-permute-done | bytes 147488 | tf_op jit(solution)/shard_map/ppermute | solution.py:62
  139.6 3.1 %collective-permute-done.13 = f32[64,576]{1,0:T(8,128)S(1)} collective-permute-done((f32[64,576]{1,0:T(8,128)S(1)}, f32[64,576]{1,0:T(8,128)S(1)}, u32[]{:S(2)}, u32[]{:S(2)}) %collective-permute-start.13) | collective-permute-done | bytes 147488 | tf_op jit(solution)/shard_map/ppermute | solution.py:62
  142.7 0.3 collective-permute-done.12
  143.0 0.6 gather_fusion
  143.6 0.9 broadcast_select_fusion
  (61 shorter events, 0.5 us)
Async XLA Ops:
  0.6 4.9 %copy-start.2 = (f32[1,1,64,256]{3,2,1,0:T(8,128)S(1)}, f32[1,1,64,256]{3,2,1,0:T(8,128)}, u32[]{:S(2)}) copy-start(f32[1,1,64,256]{3,2,1,0:T(8,128)} %param.7) | copy-start | bytes 196612
  3.5 2.1 %copy-start.8 = (f32[1,64]{1,0:T(1,128)S(1)}, f32[1,64]{1,0:T(1,128)}, u32[]{:S(2)}) copy-start(f32[1,64]{1,0:T(1,128)} %param.6) | copy-start | bytes 772
  3.5 5.9 %collective-permute-start = (f32[1,64,256]{2,1,0:T(8,128)}, f32[1,64,256]{2,1,0:T(8,128)S(1)}, u32[]{:S(2)}, u32[]{:S(2)}) collective-permute-start(f32[1,64,256]{2,1,0:T(8,128)} %bitcast.322), channel_id=1, source_target_pairs={{0,4},{4,8},{8,12},{12,16},{16,20},{20,24},{24,28},{28,32},{32,36}... | collective-permute-start | bytes 196616 | tf_op jit(solution)/shard_map/ppermute | solution.py:69
  5.6 3.8 %copy-start.3 = (f32[1,1,64,256]{3,2,1,0:T(8,128)S(1)}, f32[1,1,64,256]{3,2,1,0:T(8,128)}, u32[]{:S(2)}) copy-start(f32[1,1,64,256]{3,2,1,0:T(8,128)} %param.4) | copy-start | bytes 196612
  13.8 3.3 %collective-permute-start.1 = (f32[130,256]{1,0:T(8,128)S(1)}, f32[130,256]{1,0:T(8,128)S(1)}, u32[]{:S(2)}, u32[]{:S(2)}) collective-permute-start(f32[130,256]{1,0:T(8,128)S(1)} %pad_maximum_fusion.1), channel_id=1, source_target_pairs={{0,4},{4,0},{8,12},{12,8},{16,20},{20,16},{24,28},{28,24},{32,36},... | collective-permute-start | bytes 399368 | tf_op jit(solution)/shard_map/ppermute | solution.py:24
  17.3 8.6 %collective-permute-start.2 = (f32[130,256]{1,0:T(8,128)S(1)}, f32[130,256]{1,0:T(8,128)S(1)}, u32[]{:S(2)}, u32[]{:S(2)}) collective-permute-start(f32[130,256]{1,0:T(8,128)S(1)} %pad_maximum_fusion.2), channel_id=1, source_target_pairs={{0,8},{4,12},{8,0},{12,4},{16,24},{20,28},{24,16},{28,20},{32,40},... | collective-permute-start | bytes 399368 | tf_op jit(solution)/shard_map/ppermute | solution.py:24
  26.2 8.8 %collective-permute-start.3 = (f32[130,256]{1,0:T(8,128)S(1)}, f32[130,256]{1,0:T(8,128)S(1)}, u32[]{:S(2)}, u32[]{:S(2)}) collective-permute-start(f32[130,256]{1,0:T(8,128)S(1)} %pad_maximum_fusion.3), channel_id=1, source_target_pairs={{0,16},{4,20},{8,24},{12,28},{16,0},{20,4},{24,8},{28,12},{32,48},... | collective-permute-start | bytes 399368 | tf_op jit(solution)/shard_map/ppermute | solution.py:24
  35.2 3.8 %copy-start.5 = (f32[4,64,256]{2,1,0:T(8,128)S(1)}, f32[4,64,256]{2,1,0:T(8,128)}, u32[]{:S(2)}) copy-start(f32[4,64,256]{2,1,0:T(8,128)} %get-tuple-element.13) | copy-start | bytes 786436
  35.3 7.1 %collective-permute-start.4 = (f32[130,256]{1,0:T(8,128)S(1)}, f32[130,256]{1,0:T(8,128)S(1)}, u32[]{:S(2)}, u32[]{:S(2)}) collective-permute-start(f32[130,256]{1,0:T(8,128)S(1)} %pad_maximum_fusion.4), channel_id=1, source_target_pairs={{0,32},{4,36},{8,40},{12,44},{16,48},{20,52},{24,56},{28,60},{32,0... | collective-permute-start | bytes 399368 | tf_op jit(solution)/shard_map/ppermute | solution.py:24
  42.6 9.6 %collective-permute-start.5 = (f32[130,256]{1,0:T(8,128)S(1)}, f32[130,256]{1,0:T(8,128)S(1)}, u32[]{:S(2)}, u32[]{:S(2)}) collective-permute-start(f32[130,256]{1,0:T(8,128)S(1)} %pad_maximum_fusion.5), channel_id=1, source_target_pairs={{0,64},{4,68},{8,72},{12,76},{16,80},{20,84},{24,88},{28,92},{32,9... | collective-permute-start | bytes 399368 | tf_op jit(solution)/shard_map/ppermute | solution.py:24
  52.4 10.1 %copy-start = (bf16[4,64,576]{2,1,0:T(8,128)(2,1)S(1)}, bf16[4,64,576]{2,1,0:T(8,128)(2,1)}, u32[]{:S(2)}) copy-start(bf16[4,64,576]{2,1,0:T(8,128)(2,1)} %weight_ref.3) | copy-start | bytes 884740
  52.5 19.2 %collective-permute-start.6 = (f32[130,256]{1,0:T(8,128)S(1)}, f32[130,256]{1,0:T(8,128)S(1)}, u32[]{:S(2)}, u32[]{:S(2)}) collective-permute-start(f32[130,256]{1,0:T(8,128)S(1)} %pad_maximum_fusion.6), channel_id=1, source_target_pairs={{0,128},{4,132},{8,136},{12,140},{16,144},{20,148},{24,152},{28,15... | collective-permute-start | bytes 399368 | tf_op jit(solution)/shard_map/ppermute | solution.py:24
  72.0 14.3 %copy-start.4 = (f32[4,64,256]{2,1,0:T(8,128)S(1)}, f32[4,64,256]{2,1,0:T(8,128)}, u32[]{:S(2)}) copy-start(f32[4,64,256]{2,1,0:T(8,128)} %get-tuple-element.14) | copy-start | bytes 786436
  72.0 25.2 %collective-permute-start.7 = (f32[130,256]{1,0:T(8,128)S(1)}, f32[130,256]{1,0:T(8,128)S(1)}, u32[]{:S(2)}, u32[]{:S(2)}) collective-permute-start(f32[130,256]{1,0:T(8,128)S(1)} %pad_maximum_fusion.7), channel_id=1, source_target_pairs={{0,256},{4,260},{8,264},{12,268},{16,272},{20,276},{24,280},{28,28... | collective-permute-start | bytes 399368 | tf_op jit(solution)/shard_map/ppermute | solution.py:24
  101.5 8.4 %copy-start.1 = (f32[4,64,576]{2,1,0:T(8,128)S(1)}, f32[4,64,576]{2,1,0:T(8,128)}, u32[]{:S(2)}) copy-start(f32[4,64,576]{2,1,0:T(8,128)} %get-tuple-element.17) | copy-start | bytes 1769476
  101.5 4.2 %collective-permute-start.8 = (f32[1,64,256]{2,1,0:T(8,128)}, f32[1,64,256]{2,1,0:T(8,128)S(1)}, u32[]{:S(2)}, u32[]{:S(2)}) collective-permute-start(f32[1,64,256]{2,1,0:T(8,128)} %bitcast.301), channel_id=1, source_target_pairs={{4,0},{8,4},{12,8},{16,12},{20,16},{24,20},{28,24},{32,28},{36,32}... | collective-permute-start | bytes 196616 | tf_op jit(solution)/shard_map/ppermute | solution.py:69
  111.1 10.6 %collective-permute-start.11 = (f32[64,576]{1,0:T(8,128)S(1)}, f32[64,576]{1,0:T(8,128)S(1)}, u32[]{:S(2)}, u32[]{:S(2)}) collective-permute-start(f32[64,576]{1,0:T(8,128)S(1)} %get-tuple-element.34), channel_id=1, source_target_pairs={{0,3},{1,2},{2,1},{3,0},{4,7},{5,6},{6,5},{7,4},{8,11},{9,10},{10,... | collective-permute-start | bytes 442376 | tf_op jit(solution)/shard_map/ppermute | solution.py:56
  116.1 10.1 %collective-permute-start.10 = (f32[64,576]{1,0:T(8,128)S(1)}, f32[64,576]{1,0:T(8,128)S(1)}, u32[]{:S(2)}, u32[]{:S(2)}) collective-permute-start(f32[64,576]{1,0:T(8,128)S(1)} %get-tuple-element.35), channel_id=1, source_target_pairs={{0,2},{1,3},{2,0},{3,1},{4,6},{5,7},{6,4},{7,5},{8,10},{9,11},{10,... | collective-permute-start | bytes 442376 | tf_op jit(solution)/shard_map/ppermute | solution.py:56
  118.6 8.9 %collective-permute-start.9 = (f32[64,576]{1,0:T(8,128)S(1)}, f32[64,576]{1,0:T(8,128)S(1)}, u32[]{:S(2)}, u32[]{:S(2)}) collective-permute-start(f32[64,576]{1,0:T(8,128)S(1)} %get-tuple-element.33), channel_id=1, source_target_pairs={{0,1},{1,0},{2,3},{3,2},{4,5},{5,4},{6,7},{7,6},{8,9},{9,8},{10,11... | collective-permute-start | bytes 442376 | tf_op jit(solution)/shard_map/ppermute | solution.py:56
  121.7 15.7 %copy-start.6 = (f32[64,256]{1,0:T(8,128)S(1)}, f32[64,256]{1,0:T(8,128)}, u32[]{:S(2)}) copy-start(f32[64,256]{1,0:T(8,128)} %get-tuple-element.15) | copy-start | bytes 196612
  121.7 15.7 %copy-start.7 = (f32[64,256]{1,0:T(8,128)S(1)}, f32[64,256]{1,0:T(8,128)}, u32[]{:S(2)}) copy-start(f32[64,256]{1,0:T(8,128)} %get-tuple-element.16) | copy-start | bytes 196612
  127.6 11.9 %collective-permute-start.14 = (f32[64,576]{1,0:T(8,128)S(1)}, f32[64,576]{1,0:T(8,128)S(1)}, u32[]{:S(2)}, u32[]{:S(2)}) collective-permute-start(f32[64,576]{1,0:T(8,128)S(1)} %fusion.1), channel_id=1, source_target_pairs={{0,3},{1,2},{2,1},{3,0},{4,7},{5,6},{6,5},{7,4},{8,11},{9,10},{10,... | collective-permute-start | bytes 442376 | tf_op jit(solution)/shard_map/ppermute | solution.py:62
  132.2 10.5 %collective-permute-start.13 = (f32[64,576]{1,0:T(8,128)S(1)}, f32[64,576]{1,0:T(8,128)S(1)}, u32[]{:S(2)}, u32[]{:S(2)}) collective-permute-start(f32[64,576]{1,0:T(8,128)S(1)} %fusion.1), channel_id=1, source_target_pairs={{0,2},{1,3},{2,0},{3,1},{4,6},{5,7},{6,4},{7,5},{8,10},{9,11},{10,... | collective-permute-start | bytes 442376 | tf_op jit(solution)/shard_map/ppermute | solution.py:62
  134.8 8.2 %collective-permute-start.12 = (f32[64,576]{1,0:T(8,128)S(1)}, f32[64,576]{1,0:T(8,128)S(1)}, u32[]{:S(2)}, u32[]{:S(2)}) collective-permute-start(f32[64,576]{1,0:T(8,128)S(1)} %fusion.1), channel_id=1, source_target_pairs={{0,1},{1,0},{2,3},{3,2},{4,5},{5,4},{6,7},{7,6},{8,9},{9,8},{10,11... | collective-permute-start | bytes 442376 | tf_op jit(solution)/shard_map/ppermute | solution.py:62

commit v13 on v12

--- a/solution.py
+++ b/solution.py
@@ -19,9 +19,9 @@
     return jnp.concatenate([states.reshape(-1, width)] + rows, axis=0)
 
 
-def exchange(gains, states, axis, bit):
+def exchange(gains, states, axis, mask):
     count = lax.axis_size(axis)
-    arrived = lax.ppermute(pack(gains, states), axis, [(i, i ^ (1 << bit)) for i in range(count)])
+    arrived = lax.ppermute(pack(gains, states), axis, [(i, i ^ mask) for i in range(count)])
     rows = states.size // states.shape[-1]
     each = states.shape[1:]
     got = arrived[:rows].reshape(states.shape)
@@ -210,8 +210,9 @@
     forward = (rate_vec, offset, rate_vec, offset)
     reverse = (jnp.ones_like(rate_vec), jnp.zeros_like(cot_here), rate_vec, rate_vec[None, :, None] * cot_here)
     for bit in range(rounds):
+        mask = 3 << (bit - 1) if bit == rounds - 1 and bit >= 1 else 1 << bit
         got_f, got_r = exchange(
-            (forward[2], reverse[2]), jnp.stack([forward[3], reverse[3]]), "depth", bit
+            (forward[2], reverse[2]), jnp.stack([forward[3], reverse[3]]), "depth", mask
         )
         forward = scan_round(forward, got_f, before, bit, bit == rounds - 1)
         reverse = scan_round(reverse, got_r, after, bit, bit == rounds - 1)

time: 145 us -> 136 us (0.938)
  the two profiles are of different devices: /device:TPU:2 before, /device:TPU:98 now
where the time goes in v13:
time: 136 us
  starting transfers between devices  58.3 us (43%)
  waiting for transfers between devices  51.8 us (38%)
  Pallas kernels  12.7 us (9%)
  other arithmetic  9.48 us (7%)
  local copies, waits for them, and re-layouts  1.86 us (1%)
    ppermute x7, waiting for transfers between devices, exchange(): lax.ppermute(pack(gains, states), axis, [(i, i ^ mask) for i in range(cou...  35.3 us
    ppermute x7, starting transfers between devices, exchange(): lax.ppermute(pack(gains, states), axis, [(i, i ^ mask) for i in range(cou...  34.6 us
    ppermute x3, starting transfers between devices, dp_sum(): lax.ppermute(lax.dynamic_index_in_dim(terms, place ^ k, 0, False), axis,...  9.82 us
    ppermute x3, starting transfers between devices, dp_sum(): lax.ppermute(total, axis, pairs(k))  9.81 us
    pallas_call x2, Pallas kernels, back_block(): pl.pallas_call(functools.partial(back_kernel, step_size), out_shape=(jax....  7.01 us
    ppermute x2, waiting for transfers between devices, passed_along(): return lax.ppermute(block, axis, route)  5.92 us
    ppermute x3, waiting for transfers between devices, dp_sum(): lax.ppermute(lax.dynamic_index_in_dim(terms, place ^ k, 0, False), axis,...  5.79 us
    pallas_call x2, Pallas kernels, run_block(): pl.pallas_call(functools.partial(block_kernel, step_size), out_shape=(jax...  5.67 us
  transfers between devices with their start and end apart: 15, of which 14 were waited for; matrix products, arithmetic and copies ran while one was open for 3% of the time, Pallas kernels for 0%

profile of v13, /device:TPU:98, one launch (start us, length us, event | category | flops | bytes accessed | tf_op | source)
XLA Modules:
  0.0 135.5 jit_solution(10391306825497078044)
XLA Ops:
  0.6 2.9 %shard_map.67 = (f32[64,256]{1,0:T(8,128)}, f32[4,64,256]{2,1,0:T(8,128)}) custom-call(f32[64,256]{1,0:T(8,128)} %bitcast.289, bf16[4,64,576]{2,1,0:T(8,128)(2,1)} %weight_ref.3), custom_call_target="tpu_custom_call" | custom-call | flops 75497472 | bytes 688128 | tf_op jit(solution)/shard_map/pallas_call | solution.py:150
  3.5 2.0 %collective-permute-start = (f32[1,64,256]{2,1,0:T(8,128)}, f32[1,64,256]{2,1,0:T(8,128)S(1)}, u32[]{:S(2)}, u32[]{:S(2)}) collective-permute-start(f32[1,64,256]{2,1,0:T(8,128)} %bitcast.322), channel_id=1, source_target_pairs={{0,4},{4,8},{8,12},{12,16},{16,20},{20,24},{24,28},{28,32},{32,36}... | collective-permute-start | bytes 196616 | tf_op jit(solution)/shard_map/ppermute | solution.py:69
  5.6 0.0 copy-start.3
  5.6 0.1 broadcast_multiply_fusion
  5.7 3.7 %collective-permute-done = f32[1,64,256]{2,1,0:T(8,128)S(1)} collective-permute-done((f32[1,64,256]{2,1,0:T(8,128)}, f32[1,64,256]{2,1,0:T(8,128)S(1)}, u32[]{:S(2)}, u32[]{:S(2)}) %collective-permute-start) | collective-permute-done | bytes 65568 | tf_op jit(solution)/shard_map/ppermute | solution.py:69
  9.4 0.0 copy-done.3
  9.4 0.6 fusion.13.state_ref
  10.0 2.8 %shard_map.68 = (f32[64,256]{1,0:T(8,128)}, f32[4,64,256]{2,1,0:T(8,128)}) custom-call(f32[64,256]{1,0:T(8,128)} %fusion.13.state_ref, bf16[4,64,576]{2,1,0:T(8,128)(2,1)} %weight_ref.3), custom_call_target="tpu_custom_call" | custom-call | flops 75497472 | bytes 688128 | tf_op jit(solution)/shard_map/pallas_call | solution.py:150
  12.9 0.9 bitcast_subtract_fusion.1
  13.8 1.9 %collective-permute-start.1 = (f32[130,256]{1,0:T(8,128)S(1)}, f32[130,256]{1,0:T(8,128)S(1)}, u32[]{:S(2)}, u32[]{:S(2)}) collective-permute-start(f32[130,256]{1,0:T(8,128)S(1)} %pad_maximum_fusion.1), channel_id=1, source_target_pairs={{0,4},{4,0},{8,12},{12,8},{16,20},{20,16},{24,28},{28,24},{32,36},... | collective-permute-start | bytes 399368 | tf_op jit(solution)/shard_map/ppermute | solution.py:24
  15.8 1.3 collective-permute-done.1
  17.1 0.1 add_select_fusion.17
  17.2 0.1 fusion.27
  17.3 4.6 %collective-permute-start.2 = (f32[130,256]{1,0:T(8,128)S(1)}, f32[130,256]{1,0:T(8,128)S(1)}, u32[]{:S(2)}, u32[]{:S(2)}) collective-permute-start(f32[130,256]{1,0:T(8,128)S(1)} %pad_maximum_fusion.2), channel_id=1, source_target_pairs={{0,8},{4,12},{8,0},{12,4},{16,24},{20,28},{24,16},{28,20},{32,40},... | collective-permute-start | bytes 399368 | tf_op jit(solution)/shard_map/ppermute | solution.py:24
  21.9 4.0 %collective-permute-done.2 = f32[130,256]{1,0:T(8,128)S(1)} collective-permute-done((f32[130,256]{1,0:T(8,128)S(1)}, f32[130,256]{1,0:T(8,128)S(1)}, u32[]{:S(2)}, u32[]{:S(2)}) %collective-permute-start.2) | collective-permute-done | bytes 133152 | tf_op jit(solution)/shard_map/ppermute | solution.py:24
  25.9 0.1 fusion.25
  26.0 0.1 fusion.11
  26.1 3.9 %collective-permute-start.3 = (f32[130,256]{1,0:T(8,128)S(1)}, f32[130,256]{1,0:T(8,128)S(1)}, u32[]{:S(2)}, u32[]{:S(2)}) collective-permute-start(f32[130,256]{1,0:T(8,128)S(1)} %pad_maximum_fusion.3), channel_id=1, source_target_pairs={{0,16},{4,20},{8,24},{12,28},{16,0},{20,4},{24,8},{28,12},{32,48},... | collective-permute-start | bytes 399368 | tf_op jit(solution)/shard_map/ppermute | solution.py:24
  30.1 4.7 %collective-permute-done.3 = f32[130,256]{1,0:T(8,128)S(1)} collective-permute-done((f32[130,256]{1,0:T(8,128)S(1)}, f32[130,256]{1,0:T(8,128)S(1)}, u32[]{:S(2)}, u32[]{:S(2)}) %collective-permute-start.3) | collective-permute-done | bytes 133152 | tf_op jit(solution)/shard_map/ppermute | solution.py:24
  34.8 0.1 add_select_fusion.15
  34.9 0.1 fusion.28
  35.0 0.0 copy-start.5
  35.0 2.1 %collective-permute-start.4 = (f32[130,256]{1,0:T(8,128)S(1)}, f32[130,256]{1,0:T(8,128)S(1)}, u32[]{:S(2)}, u32[]{:S(2)}) collective-permute-start(f32[130,256]{1,0:T(8,128)S(1)} %pad_maximum_fusion.4), channel_id=1, source_target_pairs={{0,32},{4,36},{8,40},{12,44},{16,48},{20,52},{24,56},{28,60},{32,0... | collective-permute-start | bytes 399368 | tf_op jit(solution)/shard_map/ppermute | solution.py:24
  37.2 4.9 %collective-permute-done.4 = f32[130,256]{1,0:T(8,128)S(1)} collective-permute-done((f32[130,256]{1,0:T(8,128)S(1)}, f32[130,256]{1,0:T(8,128)S(1)}, u32[]{:S(2)}, u32[]{:S(2)}) %collective-permute-start.4) | collective-permute-done | bytes 133152 | tf_op jit(solution)/shard_map/ppermute | solution.py:24
  42.2 0.1 fusion.26
  42.3 0.1 fusion.9
  42.4 1.9 %collective-permute-start.5 = (f32[130,256]{1,0:T(8,128)S(1)}, f32[130,256]{1,0:T(8,128)S(1)}, u32[]{:S(2)}, u32[]{:S(2)}) collective-permute-start(f32[130,256]{1,0:T(8,128)S(1)} %pad_maximum_fusion.5), channel_id=1, source_target_pairs={{0,64},{4,68},{8,72},{12,76},{16,80},{20,84},{24,88},{28,92},{32,9... | collective-permute-start | bytes 399368 | tf_op jit(solution)/shard_map/ppermute | solution.py:24
  44.4 6.9 %collective-permute-done.5 = f32[130,256]{1,0:T(8,128)S(1)} collective-permute-done((f32[130,256]{1,0:T(8,128)S(1)}, f32[130,256]{1,0:T(8,128)S(1)}, u32[]{:S(2)}, u32[]{:S(2)}) %collective-permute-start.5) | collective-permute-done | bytes 133152 | tf_op jit(solution)/shard_map/ppermute | solution.py:24
  51.3 0.1 add_select_fusion.13
  51.4 0.1 fusion.29
  51.5 0.0 copy-start
  51.6 9.2 %collective-permute-start.6 = (f32[130,256]{1,0:T(8,128)S(1)}, f32[130,256]{1,0:T(8,128)S(1)}, u32[]{:S(2)}, u32[]{:S(2)}) collective-permute-start(f32[130,256]{1,0:T(8,128)S(1)} %pad_maximum_fusion.6), channel_id=1, source_target_pairs={{0,128},{4,132},{8,136},{12,140},{16,144},{20,148},{24,152},{28,15... | collective-permute-start | bytes 399368 | tf_op jit(solution)/shard_map/ppermute | solution.py:24
  60.9 1.1 copy.8
  61.9 0.7 maximum_bitcast_fusion.kept_ref
  62.7 5.4 %collective-permute-done.6 = f32[130,256]{1,0:T(8,128)S(1)} collective-permute-done((f32[130,256]{1,0:T(8,128)S(1)}, f32[130,256]{1,0:T(8,128)S(1)}, u32[]{:S(2)}, u32[]{:S(2)}) %collective-permute-start.6) | collective-permute-done | bytes 133152 | tf_op jit(solution)/shard_map/ppermute | solution.py:24
  68.1 0.1 select_bitcast_fusion
  68.2 0.1 fusion.7
  68.4 11.0 %collective-permute-start.7 = (f32[130,256]{1,0:T(8,128)S(1)}, f32[130,256]{1,0:T(8,128)S(1)}, u32[]{:S(2)}, u32[]{:S(2)}) collective-permute-start(f32[130,256]{1,0:T(8,128)S(1)} %pad_maximum_fusion.7), channel_id=1, source_target_pairs={{0,384},{4,388},{8,392},{12,396},{16,400},{20,404},{24,408},{28,41... | collective-permute-start | bytes 399368 | tf_op jit(solution)/shard_map/ppermute | solution.py:24
  79.4 0.7 maximum_bitcast_fusion.1.kept_ref
  80.1 8.1 %collective-permute-done.7 = f32[130,256]{1,0:T(8,128)S(1)} collective-permute-done((f32[130,256]{1,0:T(8,128)S(1)}, f32[130,256]{1,0:T(8,128)S(1)}, u32[]{:S(2)}, u32[]{:S(2)}) %collective-permute-start.7) | collective-permute-done | bytes 133152 | tf_op jit(solution)/shard_map/ppermute | solution.py:24
  88.2 0.8 bitcast_add_fusion.11
  88.9 3.5 %shard_map.69 = (f32[64,256]{1,0:T(8,128)}, f32[4,64,576]{2,1,0:T(8,128)}) custom-call(f32[4,64,256]{2,1,0:T(8,128)} %maximum_bitcast_fusion.1.kept_ref, bf16[4,576,64]{2,1,0:T(8,128)(2,1)} %bitcast.281, f32[64,256]{1,0:T(8,128)} %get-tuple-element.19.upstream_ref), custom_call_target="tpu_custom_call" | custom-call | flops 150994944 | bytes 1277952 | tf_op jit(solution)/shard_map/pallas_call | solution.py:172
  92.4 2.0 %collective-permute-start.8 = (f32[1,64,256]{2,1,0:T(8,128)}, f32[1,64,256]{2,1,0:T(8,128)S(1)}, u32[]{:S(2)}, u32[]{:S(2)}) collective-permute-start(f32[1,64,256]{2,1,0:T(8,128)} %bitcast.301), channel_id=1, source_target_pairs={{4,0},{8,4},{12,8},{16,12},{20,16},{24,20},{28,24},{32,28},{36,32}... | collective-permute-start | bytes 196616 | tf_op jit(solution)/shard_map/ppermute | solution.py:69
  94.5 2.2 %collective-permute-done.8 = f32[1,64,256]{2,1,0:T(8,128)S(1)} collective-permute-done((f32[1,64,256]{2,1,0:T(8,128)}, f32[1,64,256]{2,1,0:T(8,128)S(1)}, u32[]{:S(2)}, u32[]{:S(2)}) %collective-permute-start.8) | collective-permute-done | bytes 65568 | tf_op jit(solution)/shard_map/ppermute | solution.py:69
  96.7 0.6 fusion.5.upstream_ref
  97.3 3.5 %shard_map.70 = (f32[64,256]{1,0:T(8,128)}, f32[4,64,576]{2,1,0:T(8,128)}) custom-call(f32[4,64,256]{2,1,0:T(8,128)} %maximum_bitcast_fusion.kept_ref, bf16[4,576,64]{2,1,0:T(8,128)(2,1)} %bitcast.282, f32[64,256]{1,0:T(8,128)} %fusion.5.upstream_ref), custom_call_target="tpu_custom_call" | custom-call | flops 150994944 | bytes 1277952 | tf_op jit(solution)/shard_map/pallas_call | solution.py:172
  100.8 1.2 add.276
  102.1 4.9 %collective-permute-start.11 = (f32[64,576]{1,0:T(8,128)S(1)}, f32[64,576]{1,0:T(8,128)S(1)}, u32[]{:S(2)}, u32[]{:S(2)}) collective-permute-start(f32[64,576]{1,0:T(8,128)S(1)} %get-tuple-element.34), channel_id=1, source_target_pairs={{0,3},{1,2},{2,1},{3,0},{4,7},{5,6},{6,5},{7,4},{8,11},{9,10},{10,... | collective-permute-start | bytes 442376 | tf_op jit(solution)/shard_map/ppermute | solution.py:56
  107.0 2.5 %collective-permute-start.10 = (f32[64,576]{1,0:T(8,128)S(1)}, f32[64,576]{1,0:T(8,128)S(1)}, u32[]{:S(2)}, u32[]{:S(2)}) collective-permute-start(f32[64,576]{1,0:T(8,128)S(1)} %get-tuple-element.35), channel_id=1, source_target_pairs={{0,2},{1,3},{2,0},{3,1},{4,6},{5,7},{6,4},{7,5},{8,10},{9,11},{10,... | collective-permute-start | bytes 442376 | tf_op jit(solution)/shard_map/ppermute | solution.py:56
  109.6 2.4 %collective-permute-start.9 = (f32[64,576]{1,0:T(8,128)S(1)}, f32[64,576]{1,0:T(8,128)S(1)}, u32[]{:S(2)}, u32[]{:S(2)}) collective-permute-start(f32[64,576]{1,0:T(8,128)S(1)} %get-tuple-element.33), channel_id=1, source_target_pairs={{0,1},{1,0},{2,3},{3,2},{4,5},{5,4},{6,7},{7,6},{8,9},{9,8},{10,11... | collective-permute-start | bytes 442376 | tf_op jit(solution)/shard_map/ppermute | solution.py:56
  111.9 0.8 fusion.2
  112.7 0.0 collective-permute-done.11
  112.7 4.4 %collective-permute-done.10 = f32[64,576]{1,0:T(8,128)S(1)} collective-permute-done((f32[64,576]{1,0:T(8,128)S(1)}, f32[64,576]{1,0:T(8,128)S(1)}, u32[]{:S(2)}, u32[]{:S(2)}) %collective-permute-start.10) | collective-permute-done | bytes 147488 | tf_op jit(solution)/shard_map/ppermute | solution.py:56
  117.1 1.4 %collective-permute-done.9 = f32[64,576]{1,0:T(8,128)S(1)} collective-permute-done((f32[64,576]{1,0:T(8,128)S(1)}, f32[64,576]{1,0:T(8,128)S(1)}, u32[]{:S(2)}, u32[]{:S(2)}) %collective-permute-start.9) | collective-permute-done | bytes 147488 | tf_op jit(solution)/shard_map/ppermute | solution.py:56
  118.5 0.1 fusion.1
  118.5 4.6 %collective-permute-start.14 = (f32[64,576]{1,0:T(8,128)S(1)}, f32[64,576]{1,0:T(8,128)S(1)}, u32[]{:S(2)}, u32[]{:S(2)}) collective-permute-start(f32[64,576]{1,0:T(8,128)S(1)} %fusion.1), channel_id=1, source_target_pairs={{0,3},{1,2},{2,1},{3,0},{4,7},{5,6},{6,5},{7,4},{8,11},{9,10},{10,... | collective-permute-start | bytes 442376 | tf_op jit(solution)/shard_map/ppermute | solution.py:62
  123.2 2.5 %collective-permute-start.13 = (f32[64,576]{1,0:T(8,128)S(1)}, f32[64,576]{1,0:T(8,128)S(1)}, u32[]{:S(2)}, u32[]{:S(2)}) collective-permute-start(f32[64,576]{1,0:T(8,128)S(1)} %fusion.1), channel_id=1, source_target_pairs={{0,2},{1,3},{2,0},{3,1},{4,6},{5,7},{6,4},{7,5},{8,10},{9,11},{10,... | collective-permute-start | bytes 442376 | tf_op jit(solution)/shard_map/ppermute | solution.py:62
  125.7 2.7 %collective-permute-start.12 = (f32[64,576]{1,0:T(8,128)S(1)}, f32[64,576]{1,0:T(8,128)S(1)}, u32[]{:S(2)}, u32[]{:S(2)}) collective-permute-start(f32[64,576]{1,0:T(8,128)S(1)} %fusion.1), channel_id=1, source_target_pairs={{0,1},{1,0},{2,3},{3,2},{4,5},{5,4},{6,7},{7,6},{8,9},{9,8},{10,11... | collective-permute-start | bytes 442376 | tf_op jit(solution)/shard_map/ppermute | solution.py:62
  128.4 0.6 fusion.3
  129.0 1.4 %collective-permute-done.14 = f32[64,576]{1,0:T(8,128)S(1)} collective-permute-done((f32[64,576]{1,0:T(8,128)S(1)}, f32[64,576]{1,0:T(8,128)S(1)}, u32[]{:S(2)}, u32[]{:S(2)}) %collective-permute-start.14) | collective-permute-done | bytes 147488 | tf_op jit(solution)/shard_map/ppermute | solution.py:62
  130.5 3.1 %collective-permute-done.13 = f32[64,576]{1,0:T(8,128)S(1)} collective-permute-done((f32[64,576]{1,0:T(8,128)S(1)}, f32[64,576]{1,0:T(8,128)S(1)}, u32[]{:S(2)}, u32[]{:S(2)}) %collective-permute-start.13) | collective-permute-done | bytes 147488 | tf_op jit(solution)/shard_map/ppermute | solution.py:62
  133.6 0.3 collective-permute-done.12
  134.0 0.6 gather_fusion
  134.6 0.9 broadcast_select_fusion
  (61 shorter events, 0.5 us)
Async XLA Ops:
  0.6 4.9 %copy-start.2 = (f32[1,1,64,256]{3,2,1,0:T(8,128)S(1)}, f32[1,1,64,256]{3,2,1,0:T(8,128)}, u32[]{:S(2)}) copy-start(f32[1,1,64,256]{3,2,1,0:T(8,128)} %param.7) | copy-start | bytes 196612
  3.5 2.1 %copy-start.8 = (f32[1,64]{1,0:T(1,128)S(1)}, f32[1,64]{1,0:T(1,128)}, u32[]{:S(2)}) copy-start(f32[1,64]{1,0:T(1,128)} %param.6) | copy-start | bytes 772
  3.5 5.9 %collective-permute-start = (f32[1,64,256]{2,1,0:T(8,128)}, f32[1,64,256]{2,1,0:T(8,128)S(1)}, u32[]{:S(2)}, u32[]{:S(2)}) collective-permute-start(f32[1,64,256]{2,1,0:T(8,128)} %bitcast.322), channel_id=1, source_target_pairs={{0,4},{4,8},{8,12},{12,16},{16,20},{20,24},{24,28},{28,32},{32,36}... | collective-permute-start | bytes 196616 | tf_op jit(solution)/shard_map/ppermute | solution.py:69
  5.6 3.8 %copy-start.3 = (f32[1,1,64,256]{3,2,1,0:T(8,128)S(1)}, f32[1,1,64,256]{3,2,1,0:T(8,128)}, u32[]{:S(2)}) copy-start(f32[1,1,64,256]{3,2,1,0:T(8,128)} %param.4) | copy-start | bytes 196612
  13.8 3.3 %collective-permute-start.1 = (f32[130,256]{1,0:T(8,128)S(1)}, f32[130,256]{1,0:T(8,128)S(1)}, u32[]{:S(2)}, u32[]{:S(2)}) collective-permute-start(f32[130,256]{1,0:T(8,128)S(1)} %pad_maximum_fusion.1), channel_id=1, source_target_pairs={{0,4},{4,0},{8,12},{12,8},{16,20},{20,16},{24,28},{28,24},{32,36},... | collective-permute-start | bytes 399368 | tf_op jit(solution)/shard_map/ppermute | solution.py:24
  17.3 8.5 %collective-permute-start.2 = (f32[130,256]{1,0:T(8,128)S(1)}, f32[130,256]{1,0:T(8,128)S(1)}, u32[]{:S(2)}, u32[]{:S(2)}) collective-permute-start(f32[130,256]{1,0:T(8,128)S(1)} %pad_maximum_fusion.2), channel_id=1, source_target_pairs={{0,8},{4,12},{8,0},{12,4},{16,24},{20,28},{24,16},{28,20},{32,40},... | collective-permute-start | bytes 399368 | tf_op jit(solution)/shard_map/ppermute | solution.py:24
  26.1 8.6 %collective-permute-start.3 = (f32[130,256]{1,0:T(8,128)S(1)}, f32[130,256]{1,0:T(8,128)S(1)}, u32[]{:S(2)}, u32[]{:S(2)}) collective-permute-start(f32[130,256]{1,0:T(8,128)S(1)} %pad_maximum_fusion.3), channel_id=1, source_target_pairs={{0,16},{4,20},{8,24},{12,28},{16,0},{20,4},{24,8},{28,12},{32,48},... | collective-permute-start | bytes 399368 | tf_op jit(solution)/shard_map/ppermute | solution.py:24
  35.0 2.2 %copy-start.5 = (f32[4,64,256]{2,1,0:T(8,128)S(1)}, f32[4,64,256]{2,1,0:T(8,128)}, u32[]{:S(2)}) copy-start(f32[4,64,256]{2,1,0:T(8,128)} %get-tuple-element.13) | copy-start | bytes 786436
  35.0 7.1 %collective-permute-start.4 = (f32[130,256]{1,0:T(8,128)S(1)}, f32[130,256]{1,0:T(8,128)S(1)}, u32[]{:S(2)}, u32[]{:S(2)}) collective-permute-start(f32[130,256]{1,0:T(8,128)S(1)} %pad_maximum_fusion.4), channel_id=1, source_target_pairs={{0,32},{4,36},{8,40},{12,44},{16,48},{20,52},{24,56},{28,60},{32,0... | collective-permute-start | bytes 399368 | tf_op jit(solution)/shard_map/ppermute | solution.py:24
  42.4 8.9 %collective-permute-start.5 = (f32[130,256]{1,0:T(8,128)S(1)}, f32[130,256]{1,0:T(8,128)S(1)}, u32[]{:S(2)}, u32[]{:S(2)}) collective-permute-start(f32[130,256]{1,0:T(8,128)S(1)} %pad_maximum_fusion.5), channel_id=1, source_target_pairs={{0,64},{4,68},{8,72},{12,76},{16,80},{20,84},{24,88},{28,92},{32,9... | collective-permute-start | bytes 399368 | tf_op jit(solution)/shard_map/ppermute | solution.py:24
  51.5 9.3 %copy-start = (bf16[4,64,576]{2,1,0:T(8,128)(2,1)S(1)}, bf16[4,64,576]{2,1,0:T(8,128)(2,1)}, u32[]{:S(2)}) copy-start(bf16[4,64,576]{2,1,0:T(8,128)(2,1)} %weight_ref.3) | copy-start | bytes 884740
  51.6 16.5 %collective-permute-start.6 = (f32[130,256]{1,0:T(8,128)S(1)}, f32[130,256]{1,0:T(8,128)S(1)}, u32[]{:S(2)}, u32[]{:S(2)}) collective-permute-start(f32[130,256]{1,0:T(8,128)S(1)} %pad_maximum_fusion.6), channel_id=1, source_target_pairs={{0,128},{4,132},{8,136},{12,140},{16,144},{20,148},{24,152},{28,15... | collective-permute-start | bytes 399368 | tf_op jit(solution)/shard_map/ppermute | solution.py:24
  68.3 11.0 %copy-start.4 = (f32[4,64,256]{2,1,0:T(8,128)S(1)}, f32[4,64,256]{2,1,0:T(8,128)}, u32[]{:S(2)}) copy-start(f32[4,64,256]{2,1,0:T(8,128)} %get-tuple-element.14) | copy-start | bytes 786436
  68.4 19.8 %collective-permute-start.7 = (f32[130,256]{1,0:T(8,128)S(1)}, f32[130,256]{1,0:T(8,128)S(1)}, u32[]{:S(2)}, u32[]{:S(2)}) collective-permute-start(f32[130,256]{1,0:T(8,128)S(1)} %pad_maximum_fusion.7), channel_id=1, source_target_pairs={{0,384},{4,388},{8,392},{12,396},{16,400},{20,404},{24,408},{28,41... | collective-permute-start | bytes 399368 | tf_op jit(solution)/shard_map/ppermute | solution.py:24
  92.4 8.4 %copy-start.1 = (f32[4,64,576]{2,1,0:T(8,128)S(1)}, f32[4,64,576]{2,1,0:T(8,128)}, u32[]{:S(2)}) copy-start(f32[4,64,576]{2,1,0:T(8,128)} %get-tuple-element.17) | copy-start | bytes 1769476
  92.4 4.2 %collective-permute-start.8 = (f32[1,64,256]{2,1,0:T(8,128)}, f32[1,64,256]{2,1,0:T(8,128)S(1)}, u32[]{:S(2)}, u32[]{:S(2)}) collective-permute-start(f32[1,64,256]{2,1,0:T(8,128)} %bitcast.301), channel_id=1, source_target_pairs={{4,0},{8,4},{12,8},{16,12},{20,16},{24,20},{28,24},{32,28},{36,32}... | collective-permute-start | bytes 196616 | tf_op jit(solution)/shard_map/ppermute | solution.py:69
  102.1 10.6 %collective-permute-start.11 = (f32[64,576]{1,0:T(8,128)S(1)}, f32[64,576]{1,0:T(8,128)S(1)}, u32[]{:S(2)}, u32[]{:S(2)}) collective-permute-start(f32[64,576]{1,0:T(8,128)S(1)} %get-tuple-element.34), channel_id=1, source_target_pairs={{0,3},{1,2},{2,1},{3,0},{4,7},{5,6},{6,5},{7,4},{8,11},{9,10},{10,... | collective-permute-start | bytes 442376 | tf_op jit(solution)/shard_map/ppermute | solution.py:56
  107.0 10.1 %collective-permute-start.10 = (f32[64,576]{1,0:T(8,128)S(1)}, f32[64,576]{1,0:T(8,128)S(1)}, u32[]{:S(2)}, u32[]{:S(2)}) collective-permute-start(f32[64,576]{1,0:T(8,128)S(1)} %get-tuple-element.35), channel_id=1, source_target_pairs={{0,2},{1,3},{2,0},{3,1},{4,6},{5,7},{6,4},{7,5},{8,10},{9,11},{10,... | collective-permute-start | bytes 442376 | tf_op jit(solution)/shard_map/ppermute | solution.py:56
  109.6 8.9 %collective-permute-start.9 = (f32[64,576]{1,0:T(8,128)S(1)}, f32[64,576]{1,0:T(8,128)S(1)}, u32[]{:S(2)}, u32[]{:S(2)}) collective-permute-start(f32[64,576]{1,0:T(8,128)S(1)} %get-tuple-element.33), channel_id=1, source_target_pairs={{0,1},{1,0},{2,3},{3,2},{4,5},{5,4},{6,7},{7,6},{8,9},{9,8},{10,11... | collective-permute-start | bytes 442376 | tf_op jit(solution)/shard_map/ppermute | solution.py:56
  112.7 15.7 %copy-start.6 = (f32[64,256]{1,0:T(8,128)S(1)}, f32[64,256]{1,0:T(8,128)}, u32[]{:S(2)}) copy-start(f32[64,256]{1,0:T(8,128)} %get-tuple-element.15) | copy-start | bytes 196612
  112.7 15.7 %copy-start.7 = (f32[64,256]{1,0:T(8,128)S(1)}, f32[64,256]{1,0:T(8,128)}, u32[]{:S(2)}) copy-start(f32[64,256]{1,0:T(8,128)} %get-tuple-element.16) | copy-start | bytes 196612
  118.5 11.9 %collective-permute-start.14 = (f32[64,576]{1,0:T(8,128)S(1)}, f32[64,576]{1,0:T(8,128)S(1)}, u32[]{:S(2)}, u32[]{:S(2)}) collective-permute-start(f32[64,576]{1,0:T(8,128)S(1)} %fusion.1), channel_id=1, source_target_pairs={{0,3},{1,2},{2,1},{3,0},{4,7},{5,6},{6,5},{7,4},{8,11},{9,10},{10,... | collective-permute-start | bytes 442376 | tf_op jit(solution)/shard_map/ppermute | solution.py:62
  123.2 10.5 %collective-permute-start.13 = (f32[64,576]{1,0:T(8,128)S(1)}, f32[64,576]{1,0:T(8,128)S(1)}, u32[]{:S(2)}, u32[]{:S(2)}) collective-permute-start(f32[64,576]{1,0:T(8,128)S(1)} %fusion.1), channel_id=1, source_target_pairs={{0,2},{1,3},{2,0},{3,1},{4,6},{5,7},{6,4},{7,5},{8,10},{9,11},{10,... | collective-permute-start | bytes 442376 | tf_op jit(solution)/shard_map/ppermute | solution.py:62
  125.7 8.2 %collective-permute-start.12 = (f32[64,576]{1,0:T(8,128)S(1)}, f32[64,576]{1,0:T(8,128)S(1)}, u32[]{:S(2)}, u32[]{:S(2)}) collective-permute-start(f32[64,576]{1,0:T(8,128)S(1)} %fusion.1), channel_id=1, source_target_pairs={{0,1},{1,0},{2,3},{3,2},{4,5},{5,4},{6,7},{7,6},{8,9},{9,8},{10,11... | collective-permute-start | bytes 442376 | tf_op jit(solution)/shard_map/ppermute | solution.py:62

commit v14 on v13

--- a/solution.py
+++ b/solution.py
@@ -210,7 +210,8 @@
     forward = (rate_vec, offset, rate_vec, offset)
     reverse = (jnp.ones_like(rate_vec), jnp.zeros_like(cot_here), rate_vec, rate_vec[None, :, None] * cot_here)
     for bit in range(rounds):
-        mask = 3 << (bit - 1) if bit == rounds - 1 and bit >= 1 else 1 << bit
+        wide = {rounds - 1, 2} if rounds >= 4 else {rounds - 1}
+        mask = 3 << (bit - 1) if bit in wide and bit >= 1 else 1 << bit
         got_f, got_r = exchange(
             (forward[2], reverse[2]), jnp.stack([forward[3], reverse[3]]), "depth", mask
         )

time: 136 us -> 135 us (level)
  the two profiles are of different devices: /device:TPU:98 before, /device:TPU:96 now
where the time goes in v14:
time: 135 us
  starting transfers between devices  55.1 us (41%)
  waiting for transfers between devices  54.4 us (40%)
  Pallas kernels  12.7 us (9%)
  other arithmetic  9.48 us (7%)
  local copies, waits for them, and re-layouts  1.86 us (1%)
    ppermute x7, waiting for transfers between devices, exchange(): lax.ppermute(pack(gains, states), axis, [(i, i ^ mask) for i in range(cou...  35.7 us
    ppermute x7, starting transfers between devices, exchange(): lax.ppermute(pack(gains, states), axis, [(i, i ^ mask) for i in range(cou...  31.4 us
    ppermute x3, starting transfers between devices, dp_sum(): lax.ppermute(lax.dynamic_index_in_dim(terms, place ^ k, 0, False), axis,...  9.82 us
    ppermute x3, starting transfers between devices, dp_sum(): lax.ppermute(total, axis, pairs(k))  9.81 us
    ppermute x2, waiting for transfers between devices, passed_along(): return lax.ppermute(block, axis, route)  8.03 us
    pallas_call x2, Pallas kernels, back_block(): pl.pallas_call(functools.partial(back_kernel, step_size), out_shape=(jax....  7.01 us
    ppermute x3, waiting for transfers between devices, dp_sum(): lax.ppermute(lax.dynamic_index_in_dim(terms, place ^ k, 0, False), axis,...  5.79 us
    pallas_call x2, Pallas kernels, run_block(): pl.pallas_call(functools.partial(block_kernel, step_size), out_shape=(jax...  5.66 us
  transfers between devices with their start and end apart: 15, of which 14 were waited for; matrix products, arithmetic and copies ran while one was open for 3% of the time, Pallas kernels for 0%

profile of v14, /device:TPU:96, one launch (start us, length us, event | category | flops | bytes accessed | tf_op | source)
XLA Modules:
  0.0 134.8 jit_solution(8425750149927331838)
XLA Ops:
  0.6 2.8 %shard_map.67 = (f32[64,256]{1,0:T(8,128)}, f32[4,64,256]{2,1,0:T(8,128)}) custom-call(f32[64,256]{1,0:T(8,128)} %bitcast.289, bf16[4,64,576]{2,1,0:T(8,128)(2,1)} %weight_ref.3), custom_call_target="tpu_custom_call" | custom-call | flops 75497472 | bytes 688128 | tf_op jit(solution)/shard_map/pallas_call | solution.py:150
  3.5 2.0 %collective-permute-start = (f32[1,64,256]{2,1,0:T(8,128)}, f32[1,64,256]{2,1,0:T(8,128)S(1)}, u32[]{:S(2)}, u32[]{:S(2)}) collective-permute-start(f32[1,64,256]{2,1,0:T(8,128)} %bitcast.322), channel_id=1, source_target_pairs={{0,4},{4,8},{8,12},{12,16},{16,20},{20,24},{24,28},{28,32},{32,36}... | collective-permute-start | bytes 196616 | tf_op jit(solution)/shard_map/ppermute | solution.py:69
  5.6 0.0 copy-start.3
  5.6 0.1 broadcast_multiply_fusion
  5.7 5.9 %collective-permute-done = f32[1,64,256]{2,1,0:T(8,128)S(1)} collective-permute-done((f32[1,64,256]{2,1,0:T(8,128)}, f32[1,64,256]{2,1,0:T(8,128)S(1)}, u32[]{:S(2)}, u32[]{:S(2)}) %collective-permute-start) | collective-permute-done | bytes 65568 | tf_op jit(solution)/shard_map/ppermute | solution.py:69
  11.5 0.6 fusion.13.state_ref
  12.2 2.8 %shard_map.68 = (f32[64,256]{1,0:T(8,128)}, f32[4,64,256]{2,1,0:T(8,128)}) custom-call(f32[64,256]{1,0:T(8,128)} %fusion.13.state_ref, bf16[4,64,576]{2,1,0:T(8,128)(2,1)} %weight_ref.3), custom_call_target="tpu_custom_call" | custom-call | flops 75497472 | bytes 688128 | tf_op jit(solution)/shard_map/pallas_call | solution.py:150
  15.0 0.9 bitcast_subtract_fusion.1
  15.9 1.9 %collective-permute-start.1 = (f32[130,256]{1,0:T(8,128)S(1)}, f32[130,256]{1,0:T(8,128)S(1)}, u32[]{:S(2)}, u32[]{:S(2)}) collective-permute-start(f32[130,256]{1,0:T(8,128)S(1)} %pad_maximum_fusion.1), channel_id=1, source_target_pairs={{0,4},{4,0},{8,12},{12,8},{16,20},{20,16},{24,28},{28,24},{32,36},... | collective-permute-start | bytes 399368 | tf_op jit(solution)/shard_map/ppermute | solution.py:24
  17.9 1.3 collective-permute-done.1
  19.2 0.1 add_select_fusion.17
  19.3 0.1 fusion.27
  19.4 1.9 %collective-permute-start.2 = (f32[130,256]{1,0:T(8,128)S(1)}, f32[130,256]{1,0:T(8,128)S(1)}, u32[]{:S(2)}, u32[]{:S(2)}) collective-permute-start(f32[130,256]{1,0:T(8,128)S(1)} %pad_maximum_fusion.2), channel_id=1, source_target_pairs={{0,8},{4,12},{8,0},{12,4},{16,24},{20,28},{24,16},{28,20},{32,40},... | collective-permute-start | bytes 399368 | tf_op jit(solution)/shard_map/ppermute | solution.py:24
  21.4 5.7 %collective-permute-done.2 = f32[130,256]{1,0:T(8,128)S(1)} collective-permute-done((f32[130,256]{1,0:T(8,128)S(1)}, f32[130,256]{1,0:T(8,128)S(1)}, u32[]{:S(2)}, u32[]{:S(2)}) %collective-permute-start.2) | collective-permute-done | bytes 133152 | tf_op jit(solution)/shard_map/ppermute | solution.py:24
  27.1 0.1 fusion.25
  27.2 0.1 fusion.11
  27.3 3.3 %collective-permute-start.3 = (f32[130,256]{1,0:T(8,128)S(1)}, f32[130,256]{1,0:T(8,128)S(1)}, u32[]{:S(2)}, u32[]{:S(2)}) collective-permute-start(f32[130,256]{1,0:T(8,128)S(1)} %pad_maximum_fusion.3), channel_id=1, source_target_pairs={{0,24},{4,28},{8,16},{12,20},{16,8},{20,12},{24,0},{28,4},{32,56},... | collective-permute-start | bytes 399368 | tf_op jit(solution)/shard_map/ppermute | solution.py:24
  30.7 4.8 %collective-permute-done.3 = f32[130,256]{1,0:T(8,128)S(1)} collective-permute-done((f32[130,256]{1,0:T(8,128)S(1)}, f32[130,256]{1,0:T(8,128)S(1)}, u32[]{:S(2)}, u32[]{:S(2)}) %collective-permute-start.3) | collective-permute-done | bytes 133152 | tf_op jit(solution)/shard_map/ppermute | solution.py:24
  35.5 0.1 add_select_fusion.15
  35.7 0.1 fusion.28
  35.7 0.0 copy-start.5
  35.8 2.1 %collective-permute-start.4 = (f32[130,256]{1,0:T(8,128)S(1)}, f32[130,256]{1,0:T(8,128)S(1)}, u32[]{:S(2)}, u32[]{:S(2)}) collective-permute-start(f32[130,256]{1,0:T(8,128)S(1)} %pad_maximum_fusion.4), channel_id=1, source_target_pairs={{0,32},{4,36},{8,40},{12,44},{16,48},{20,52},{24,56},{28,60},{32,0... | collective-permute-start | bytes 399368 | tf_op jit(solution)/shard_map/ppermute | solution.py:24
  38.0 0.0 copy-done.5
  38.0 4.9 %collective-permute-done.4 = f32[130,256]{1,0:T(8,128)S(1)} collective-permute-done((f32[130,256]{1,0:T(8,128)S(1)}, f32[130,256]{1,0:T(8,128)S(1)}, u32[]{:S(2)}, u32[]{:S(2)}) %collective-permute-start.4) | collective-permute-done | bytes 133152 | tf_op jit(solution)/shard_map/ppermute | solution.py:24
  42.9 0.1 fusion.26
  43.0 0.1 fusion.9
  43.2 1.9 %collective-permute-start.5 = (f32[130,256]{1,0:T(8,128)S(1)}, f32[130,256]{1,0:T(8,128)S(1)}, u32[]{:S(2)}, u32[]{:S(2)}) collective-permute-start(f32[130,256]{1,0:T(8,128)S(1)} %pad_maximum_fusion.5), channel_id=1, source_target_pairs={{0,64},{4,68},{8,72},{12,76},{16,80},{20,84},{24,88},{28,92},{32,9... | collective-permute-start | bytes 399368 | tf_op jit(solution)/shard_map/ppermute | solution.py:24
  45.1 6.9 %collective-permute-done.5 = f32[130,256]{1,0:T(8,128)S(1)} collective-permute-done((f32[130,256]{1,0:T(8,128)S(1)}, f32[130,256]{1,0:T(8,128)S(1)}, u32[]{:S(2)}, u32[]{:S(2)}) %collective-permute-start.5) | collective-permute-done | bytes 133152 | tf_op jit(solution)/shard_map/ppermute | solution.py:24
  52.1 0.1 add_select_fusion.13
  52.2 0.1 fusion.29
  52.3 0.0 copy-start
  52.3 9.2 %collective-permute-start.6 = (f32[130,256]{1,0:T(8,128)S(1)}, f32[130,256]{1,0:T(8,128)S(1)}, u32[]{:S(2)}, u32[]{:S(2)}) collective-permute-start(f32[130,256]{1,0:T(8,128)S(1)} %pad_maximum_fusion.6), channel_id=1, source_target_pairs={{0,128},{4,132},{8,136},{12,140},{16,144},{20,148},{24,152},{28,15... | collective-permute-start | bytes 399368 | tf_op jit(solution)/shard_map/ppermute | solution.py:24
  61.6 1.1 copy.8
  62.7 0.7 maximum_bitcast_fusion.kept_ref
  63.4 4.9 %collective-permute-done.6 = f32[130,256]{1,0:T(8,128)S(1)} collective-permute-done((f32[130,256]{1,0:T(8,128)S(1)}, f32[130,256]{1,0:T(8,128)S(1)}, u32[]{:S(2)}, u32[]{:S(2)}) %collective-permute-start.6) | collective-permute-done | bytes 133152 | tf_op jit(solution)/shard_map/ppermute | solution.py:24
  68.3 0.1 select_bitcast_fusion
  68.4 0.1 fusion.7
  68.6 10.9 %collective-permute-start.7 = (f32[130,256]{1,0:T(8,128)S(1)}, f32[130,256]{1,0:T(8,128)S(1)}, u32[]{:S(2)}, u32[]{:S(2)}) collective-permute-start(f32[130,256]{1,0:T(8,128)S(1)} %pad_maximum_fusion.7), channel_id=1, source_target_pairs={{0,384},{4,388},{8,392},{12,396},{16,400},{20,404},{24,408},{28,41... | collective-permute-start | bytes 399368 | tf_op jit(solution)/shard_map/ppermute | solution.py:24
  79.5 0.7 maximum_bitcast_fusion.1.kept_ref
  80.2 7.2 %collective-permute-done.7 = f32[130,256]{1,0:T(8,128)S(1)} collective-permute-done((f32[130,256]{1,0:T(8,128)S(1)}, f32[130,256]{1,0:T(8,128)S(1)}, u32[]{:S(2)}, u32[]{:S(2)}) %collective-permute-start.7) | collective-permute-done | bytes 133152 | tf_op jit(solution)/shard_map/ppermute | solution.py:24
  87.5 0.8 bitcast_add_fusion.11
  88.2 3.5 %shard_map.69 = (f32[64,256]{1,0:T(8,128)}, f32[4,64,576]{2,1,0:T(8,128)}) custom-call(f32[4,64,256]{2,1,0:T(8,128)} %maximum_bitcast_fusion.1.kept_ref, bf16[4,576,64]{2,1,0:T(8,128)(2,1)} %bitcast.281, f32[64,256]{1,0:T(8,128)} %get-tuple-element.19.upstream_ref), custom_call_target="tpu_custom_call" | custom-call | flops 150994944 | bytes 1277952 | tf_op jit(solution)/shard_map/pallas_call | solution.py:172
  91.7 2.0 %collective-permute-start.8 = (f32[1,64,256]{2,1,0:T(8,128)}, f32[1,64,256]{2,1,0:T(8,128)S(1)}, u32[]{:S(2)}, u32[]{:S(2)}) collective-permute-start(f32[1,64,256]{2,1,0:T(8,128)} %bitcast.301), channel_id=1, source_target_pairs={{4,0},{8,4},{12,8},{16,12},{20,16},{24,20},{28,24},{32,28},{36,32}... | collective-permute-start | bytes 196616 | tf_op jit(solution)/shard_map/ppermute | solution.py:69
  93.8 2.2 %collective-permute-done.8 = f32[1,64,256]{2,1,0:T(8,128)S(1)} collective-permute-done((f32[1,64,256]{2,1,0:T(8,128)}, f32[1,64,256]{2,1,0:T(8,128)S(1)}, u32[]{:S(2)}, u32[]{:S(2)}) %collective-permute-start.8) | collective-permute-done | bytes 65568 | tf_op jit(solution)/shard_map/ppermute | solution.py:69
  96.0 0.6 fusion.5.upstream_ref
  96.6 3.5 %shard_map.70 = (f32[64,256]{1,0:T(8,128)}, f32[4,64,576]{2,1,0:T(8,128)}) custom-call(f32[4,64,256]{2,1,0:T(8,128)} %maximum_bitcast_fusion.kept_ref, bf16[4,576,64]{2,1,0:T(8,128)(2,1)} %bitcast.282, f32[64,256]{1,0:T(8,128)} %fusion.5.upstream_ref), custom_call_target="tpu_custom_call" | custom-call | flops 150994944 | bytes 1277952 | tf_op jit(solution)/shard_map/pallas_call | solution.py:172
  100.1 1.2 add.276
  101.4 4.9 %collective-permute-start.11 = (f32[64,576]{1,0:T(8,128)S(1)}, f32[64,576]{1,0:T(8,128)S(1)}, u32[]{:S(2)}, u32[]{:S(2)}) collective-permute-start(f32[64,576]{1,0:T(8,128)S(1)} %get-tuple-element.34), channel_id=1, source_target_pairs={{0,3},{1,2},{2,1},{3,0},{4,7},{5,6},{6,5},{7,4},{8,11},{9,10},{10,... | collective-permute-start | bytes 442376 | tf_op jit(solution)/shard_map/ppermute | solution.py:56
  106.3 2.5 %collective-permute-start.10 = (f32[64,576]{1,0:T(8,128)S(1)}, f32[64,576]{1,0:T(8,128)S(1)}, u32[]{:S(2)}, u32[]{:S(2)}) collective-permute-start(f32[64,576]{1,0:T(8,128)S(1)} %get-tuple-element.35), channel_id=1, source_target_pairs={{0,2},{1,3},{2,0},{3,1},{4,6},{5,7},{6,4},{7,5},{8,10},{9,11},{10,... | collective-permute-start | bytes 442376 | tf_op jit(solution)/shard_map/ppermute | solution.py:56
  108.8 2.4 %collective-permute-start.9 = (f32[64,576]{1,0:T(8,128)S(1)}, f32[64,576]{1,0:T(8,128)S(1)}, u32[]{:S(2)}, u32[]{:S(2)}) collective-permute-start(f32[64,576]{1,0:T(8,128)S(1)} %get-tuple-element.33), channel_id=1, source_target_pairs={{0,1},{1,0},{2,3},{3,2},{4,5},{5,4},{6,7},{7,6},{8,9},{9,8},{10,11... | collective-permute-start | bytes 442376 | tf_op jit(solution)/shard_map/ppermute | solution.py:56
  111.2 0.8 fusion.2
  112.0 0.0 collective-permute-done.11
  112.0 4.4 %collective-permute-done.10 = f32[64,576]{1,0:T(8,128)S(1)} collective-permute-done((f32[64,576]{1,0:T(8,128)S(1)}, f32[64,576]{1,0:T(8,128)S(1)}, u32[]{:S(2)}, u32[]{:S(2)}) %collective-permute-start.10) | collective-permute-done | bytes 147488 | tf_op jit(solution)/shard_map/ppermute | solution.py:56
  116.4 1.4 %collective-permute-done.9 = f32[64,576]{1,0:T(8,128)S(1)} collective-permute-done((f32[64,576]{1,0:T(8,128)S(1)}, f32[64,576]{1,0:T(8,128)S(1)}, u32[]{:S(2)}, u32[]{:S(2)}) %collective-permute-start.9) | collective-permute-done | bytes 147488 | tf_op jit(solution)/shard_map/ppermute | solution.py:56
  117.8 0.1 fusion.1
  117.8 4.6 %collective-permute-start.14 = (f32[64,576]{1,0:T(8,128)S(1)}, f32[64,576]{1,0:T(8,128)S(1)}, u32[]{:S(2)}, u32[]{:S(2)}) collective-permute-start(f32[64,576]{1,0:T(8,128)S(1)} %fusion.1), channel_id=1, source_target_pairs={{0,3},{1,2},{2,1},{3,0},{4,7},{5,6},{6,5},{7,4},{8,11},{9,10},{10,... | collective-permute-start | bytes 442376 | tf_op jit(solution)/shard_map/ppermute | solution.py:62
  122.4 2.5 %collective-permute-start.13 = (f32[64,576]{1,0:T(8,128)S(1)}, f32[64,576]{1,0:T(8,128)S(1)}, u32[]{:S(2)}, u32[]{:S(2)}) collective-permute-start(f32[64,576]{1,0:T(8,128)S(1)} %fusion.1), channel_id=1, source_target_pairs={{0,2},{1,3},{2,0},{3,1},{4,6},{5,7},{6,4},{7,5},{8,10},{9,11},{10,... | collective-permute-start | bytes 442376 | tf_op jit(solution)/shard_map/ppermute | solution.py:62
  125.0 2.7 %collective-permute-start.12 = (f32[64,576]{1,0:T(8,128)S(1)}, f32[64,576]{1,0:T(8,128)S(1)}, u32[]{:S(2)}, u32[]{:S(2)}) collective-permute-start(f32[64,576]{1,0:T(8,128)S(1)} %fusion.1), channel_id=1, source_target_pairs={{0,1},{1,0},{2,3},{3,2},{4,5},{5,4},{6,7},{7,6},{8,9},{9,8},{10,11... | collective-permute-start | bytes 442376 | tf_op jit(solution)/shard_map/ppermute | solution.py:62
  127.7 0.6 fusion.3
  128.3 1.4 %collective-permute-done.14 = f32[64,576]{1,0:T(8,128)S(1)} collective-permute-done((f32[64,576]{1,0:T(8,128)S(1)}, f32[64,576]{1,0:T(8,128)S(1)}, u32[]{:S(2)}, u32[]{:S(2)}) %collective-permute-start.14) | collective-permute-done | bytes 147488 | tf_op jit(solution)/shard_map/ppermute | solution.py:62
  129.8 3.1 %collective-permute-done.13 = f32[64,576]{1,0:T(8,128)S(1)} collective-permute-done((f32[64,576]{1,0:T(8,128)S(1)}, f32[64,576]{1,0:T(8,128)S(1)}, u32[]{:S(2)}, u32[]{:S(2)}) %collective-permute-start.13) | collective-permute-done | bytes 147488 | tf_op jit(solution)/shard_map/ppermute | solution.py:62
  132.9 0.3 collective-permute-done.12
  133.3 0.6 gather_fusion
  133.8 0.9 broadcast_select_fusion
  (61 shorter events, 0.5 us)
Async XLA Ops:
  0.6 4.9 %copy-start.2 = (f32[1,1,64,256]{3,2,1,0:T(8,128)S(1)}, f32[1,1,64,256]{3,2,1,0:T(8,128)}, u32[]{:S(2)}) copy-start(f32[1,1,64,256]{3,2,1,0:T(8,128)} %param.7) | copy-start | bytes 196612
  3.5 2.1 %copy-start.8 = (f32[1,64]{1,0:T(1,128)S(1)}, f32[1,64]{1,0:T(1,128)}, u32[]{:S(2)}) copy-start(f32[1,64]{1,0:T(1,128)} %param.6) | copy-start | bytes 772
  3.5 8.0 %collective-permute-start = (f32[1,64,256]{2,1,0:T(8,128)}, f32[1,64,256]{2,1,0:T(8,128)S(1)}, u32[]{:S(2)}, u32[]{:S(2)}) collective-permute-start(f32[1,64,256]{2,1,0:T(8,128)} %bitcast.322), channel_id=1, source_target_pairs={{0,4},{4,8},{8,12},{12,16},{16,20},{20,24},{24,28},{28,32},{32,36}... | collective-permute-start | bytes 196616 | tf_op jit(solution)/shard_map/ppermute | solution.py:69
  5.6 6.0 %copy-start.3 = (f32[1,1,64,256]{3,2,1,0:T(8,128)S(1)}, f32[1,1,64,256]{3,2,1,0:T(8,128)}, u32[]{:S(2)}) copy-start(f32[1,1,64,256]{3,2,1,0:T(8,128)} %param.4) | copy-start | bytes 196612
  15.9 3.3 %collective-permute-start.1 = (f32[130,256]{1,0:T(8,128)S(1)}, f32[130,256]{1,0:T(8,128)S(1)}, u32[]{:S(2)}, u32[]{:S(2)}) collective-permute-start(f32[130,256]{1,0:T(8,128)S(1)} %pad_maximum_fusion.1), channel_id=1, source_target_pairs={{0,4},{4,0},{8,12},{12,8},{16,20},{20,16},{24,28},{28,24},{32,36},... | collective-permute-start | bytes 399368 | tf_op jit(solution)/shard_map/ppermute | solution.py:24
  19.4 7.6 %collective-permute-start.2 = (f32[130,256]{1,0:T(8,128)S(1)}, f32[130,256]{1,0:T(8,128)S(1)}, u32[]{:S(2)}, u32[]{:S(2)}) collective-permute-start(f32[130,256]{1,0:T(8,128)S(1)} %pad_maximum_fusion.2), channel_id=1, source_target_pairs={{0,8},{4,12},{8,0},{12,4},{16,24},{20,28},{24,16},{28,20},{32,40},... | collective-permute-start | bytes 399368 | tf_op jit(solution)/shard_map/ppermute | solution.py:24
  27.3 8.2 %collective-permute-start.3 = (f32[130,256]{1,0:T(8,128)S(1)}, f32[130,256]{1,0:T(8,128)S(1)}, u32[]{:S(2)}, u32[]{:S(2)}) collective-permute-start(f32[130,256]{1,0:T(8,128)S(1)} %pad_maximum_fusion.3), channel_id=1, source_target_pairs={{0,24},{4,28},{8,16},{12,20},{16,8},{20,12},{24,0},{28,4},{32,56},... | collective-permute-start | bytes 399368 | tf_op jit(solution)/shard_map/ppermute | solution.py:24
  35.7 2.2 %copy-start.5 = (f32[4,64,256]{2,1,0:T(8,128)S(1)}, f32[4,64,256]{2,1,0:T(8,128)}, u32[]{:S(2)}) copy-start(f32[4,64,256]{2,1,0:T(8,128)} %get-tuple-element.13) | copy-start | bytes 786436
  35.8 7.1 %collective-permute-start.4 = (f32[130,256]{1,0:T(8,128)S(1)}, f32[130,256]{1,0:T(8,128)S(1)}, u32[]{:S(2)}, u32[]{:S(2)}) collective-permute-start(f32[130,256]{1,0:T(8,128)S(1)} %pad_maximum_fusion.4), channel_id=1, source_target_pairs={{0,32},{4,36},{8,40},{12,44},{16,48},{20,52},{24,56},{28,60},{32,0... | collective-permute-start | bytes 399368 | tf_op jit(solution)/shard_map/ppermute | solution.py:24
  43.2 8.9 %collective-permute-start.5 = (f32[130,256]{1,0:T(8,128)S(1)}, f32[130,256]{1,0:T(8,128)S(1)}, u32[]{:S(2)}, u32[]{:S(2)}) collective-permute-start(f32[130,256]{1,0:T(8,128)S(1)} %pad_maximum_fusion.5), channel_id=1, source_target_pairs={{0,64},{4,68},{8,72},{12,76},{16,80},{20,84},{24,88},{28,92},{32,9... | collective-permute-start | bytes 399368 | tf_op jit(solution)/shard_map/ppermute | solution.py:24
  52.3 9.3 %copy-start = (bf16[4,64,576]{2,1,0:T(8,128)(2,1)S(1)}, bf16[4,64,576]{2,1,0:T(8,128)(2,1)}, u32[]{:S(2)}) copy-start(bf16[4,64,576]{2,1,0:T(8,128)(2,1)} %weight_ref.3) | copy-start | bytes 884740
  52.3 15.9 %collective-permute-start.6 = (f32[130,256]{1,0:T(8,128)S(1)}, f32[130,256]{1,0:T(8,128)S(1)}, u32[]{:S(2)}, u32[]{:S(2)}) collective-permute-start(f32[130,256]{1,0:T(8,128)S(1)} %pad_maximum_fusion.6), channel_id=1, source_target_pairs={{0,128},{4,132},{8,136},{12,140},{16,144},{20,148},{24,152},{28,15... | collective-permute-start | bytes 399368 | tf_op jit(solution)/shard_map/ppermute | solution.py:24
  68.5 11.0 %copy-start.4 = (f32[4,64,256]{2,1,0:T(8,128)S(1)}, f32[4,64,256]{2,1,0:T(8,128)}, u32[]{:S(2)}) copy-start(f32[4,64,256]{2,1,0:T(8,128)} %get-tuple-element.14) | copy-start | bytes 786436
  68.6 18.9 %collective-permute-start.7 = (f32[130,256]{1,0:T(8,128)S(1)}, f32[130,256]{1,0:T(8,128)S(1)}, u32[]{:S(2)}, u32[]{:S(2)}) collective-permute-start(f32[130,256]{1,0:T(8,128)S(1)} %pad_maximum_fusion.7), channel_id=1, source_target_pairs={{0,384},{4,388},{8,392},{12,396},{16,400},{20,404},{24,408},{28,41... | collective-permute-start | bytes 399368 | tf_op jit(solution)/shard_map/ppermute | solution.py:24
  91.7 8.4 %copy-start.1 = (f32[4,64,576]{2,1,0:T(8,128)S(1)}, f32[4,64,576]{2,1,0:T(8,128)}, u32[]{:S(2)}) copy-start(f32[4,64,576]{2,1,0:T(8,128)} %get-tuple-element.17) | copy-start | bytes 1769476
  91.7 4.2 %collective-permute-start.8 = (f32[1,64,256]{2,1,0:T(8,128)}, f32[1,64,256]{2,1,0:T(8,128)S(1)}, u32[]{:S(2)}, u32[]{:S(2)}) collective-permute-start(f32[1,64,256]{2,1,0:T(8,128)} %bitcast.301), channel_id=1, source_target_pairs={{4,0},{8,4},{12,8},{16,12},{20,16},{24,20},{28,24},{32,28},{36,32}... | collective-permute-start | bytes 196616 | tf_op jit(solution)/shard_map/ppermute | solution.py:69
  101.4 10.6 %collective-permute-start.11 = (f32[64,576]{1,0:T(8,128)S(1)}, f32[64,576]{1,0:T(8,128)S(1)}, u32[]{:S(2)}, u32[]{:S(2)}) collective-permute-start(f32[64,576]{1,0:T(8,128)S(1)} %get-tuple-element.34), channel_id=1, source_target_pairs={{0,3},{1,2},{2,1},{3,0},{4,7},{5,6},{6,5},{7,4},{8,11},{9,10},{10,... | collective-permute-start | bytes 442376 | tf_op jit(solution)/shard_map/ppermute | solution.py:56
  106.3 10.1 %collective-permute-start.10 = (f32[64,576]{1,0:T(8,128)S(1)}, f32[64,576]{1,0:T(8,128)S(1)}, u32[]{:S(2)}, u32[]{:S(2)}) collective-permute-start(f32[64,576]{1,0:T(8,128)S(1)} %get-tuple-element.35), channel_id=1, source_target_pairs={{0,2},{1,3},{2,0},{3,1},{4,6},{5,7},{6,4},{7,5},{8,10},{9,11},{10,... | collective-permute-start | bytes 442376 | tf_op jit(solution)/shard_map/ppermute | solution.py:56
  108.8 8.9 %collective-permute-start.9 = (f32[64,576]{1,0:T(8,128)S(1)}, f32[64,576]{1,0:T(8,128)S(1)}, u32[]{:S(2)}, u32[]{:S(2)}) collective-permute-start(f32[64,576]{1,0:T(8,128)S(1)} %get-tuple-element.33), channel_id=1, source_target_pairs={{0,1},{1,0},{2,3},{3,2},{4,5},{5,4},{6,7},{7,6},{8,9},{9,8},{10,11... | collective-permute-start | bytes 442376 | tf_op jit(solution)/shard_map/ppermute | solution.py:56
  112.0 15.7 %copy-start.6 = (f32[64,256]{1,0:T(8,128)S(1)}, f32[64,256]{1,0:T(8,128)}, u32[]{:S(2)}) copy-start(f32[64,256]{1,0:T(8,128)} %get-tuple-element.15) | copy-start | bytes 196612
  112.0 15.7 %copy-start.7 = (f32[64,256]{1,0:T(8,128)S(1)}, f32[64,256]{1,0:T(8,128)}, u32[]{:S(2)}) copy-start(f32[64,256]{1,0:T(8,128)} %get-tuple-element.16) | copy-start | bytes 196612
  117.8 11.9 %collective-permute-start.14 = (f32[64,576]{1,0:T(8,128)S(1)}, f32[64,576]{1,0:T(8,128)S(1)}, u32[]{:S(2)}, u32[]{:S(2)}) collective-permute-start(f32[64,576]{1,0:T(8,128)S(1)} %fusion.1), channel_id=1, source_target_pairs={{0,3},{1,2},{2,1},{3,0},{4,7},{5,6},{6,5},{7,4},{8,11},{9,10},{10,... | collective-permute-start | bytes 442376 | tf_op jit(solution)/shard_map/ppermute | solution.py:62
  122.4 10.5 %collective-permute-start.13 = (f32[64,576]{1,0:T(8,128)S(1)}, f32[64,576]{1,0:T(8,128)S(1)}, u32[]{:S(2)}, u32[]{:S(2)}) collective-permute-start(f32[64,576]{1,0:T(8,128)S(1)} %fusion.1), channel_id=1, source_target_pairs={{0,2},{1,3},{2,0},{3,1},{4,6},{5,7},{6,4},{7,5},{8,10},{9,11},{10,... | collective-permute-start | bytes 442376 | tf_op jit(solution)/shard_map/ppermute | solution.py:62
  125.0 8.2 %collective-permute-start.12 = (f32[64,576]{1,0:T(8,128)S(1)}, f32[64,576]{1,0:T(8,128)S(1)}, u32[]{:S(2)}, u32[]{:S(2)}) collective-permute-start(f32[64,576]{1,0:T(8,128)S(1)} %fusion.1), channel_id=1, source_target_pairs={{0,1},{1,0},{2,3},{3,2},{4,5},{5,4},{6,7},{7,6},{8,9},{9,8},{10,11... | collective-permute-start | bytes 442376 | tf_op jit(solution)/shard_map/ppermute | solution.py:62

commit v15 on v14

--- a/solution.py
+++ b/solution.py
@@ -48,19 +48,13 @@
 
 def dp_sum(terms, axis):
     count = lax.axis_size(axis)
-    if count != terms.shape[0] or count & (count - 1):
+    if count != terms.shape[0]:
         return lax.psum(terms, axis)
-    place = lax.axis_index(axis)
-    pairs = lambda k: [(i, i ^ k) for i in range(count)]
-    got = [terms[place]] + [
-        lax.ppermute(lax.dynamic_index_in_dim(terms, place ^ k, 0, False), axis, pairs(k))
-        for k in range(1, count)
-    ]
+    got = lax.all_to_all(terms, axis, 0, 0)
     total = got[0]
-    for piece in got[1:]:
-        total = total + piece
-    back = jnp.stack([total] + [lax.ppermute(total, axis, pairs(k)) for k in range(1, count)])
-    return jnp.take(back, jnp.arange(count) ^ place, axis=0)
+    for k in range(1, count):
+        total = total + got[k]
+    return lax.all_to_all(jnp.broadcast_to(total[None], terms.shape), axis, 0, 0)
 
 
 def passed_along(block, axis, distance):

time: 135 us -> 136 us (level)
  starting transfers between devices: 55.1 us -> 43.3 us
  waiting for transfers between devices: 54.4 us -> 65.6 us
    all_to_all x0 -> x2, waiting for transfers between devices: none -> 21.9 us  [the longest x1 11.9 us: dp_sum(): got = lax.all_to_all(terms, axis, 0, 0)]
    ppermute x6 -> x0, starting transfers between devices: 19.6 us -> none  [the longest x3 9.82 us: dp_sum(): lax.ppermute(lax.dynamic_index_in_dim(terms, place ^ k, 0, False), axis,...]
    ppermute x6 -> x0, waiting for transfers between devices: 10.7 us -> none  [the longest x3 5.79 us: dp_sum(): lax.ppermute(lax.dynamic_index_in_dim(terms, place ^ k, 0, False), axis,...]
    all_to_all x0 -> x2, starting transfers between devices: none -> 7.94 us  [the longest x1 4.46 us: dp_sum(): got = lax.all_to_all(terms, axis, 0, 0)]
  transfers between devices with their start and end apart: 15 -> 11, of which waited for: 14 -> 11; matrix products, arithmetic and copies ran while one was open for 3% -> 3% of each run, Pallas kernels for 0% -> 0%
where the time goes in v15:
time: 136 us; the launch traced here: 135 us
  waiting for transfers between devices  65.6 us (48%)
  starting transfers between devices  43.3 us (32%)
  Pallas kernels  12.7 us (9%)
  other arithmetic  9.23 us (7%)
  local copies, waits for them, and re-layouts  3.04 us (2%)
    ppermute x7, waiting for transfers between devices, exchange(): lax.ppermute(pack(gains, states), axis, [(i, i ^ mask) for i in range(cou...  36.4 us
    ppermute x7, starting transfers between devices, exchange(): lax.ppermute(pack(gains, states), axis, [(i, i ^ mask) for i in range(cou...  31.4 us
    all_to_all x1, waiting for transfers between devices, dp_sum(): got = lax.all_to_all(terms, axis, 0, 0)  11.9 us
    all_to_all x1, waiting for transfers between devices, dp_sum(): lax.all_to_all(jnp.broadcast_to(total[None], terms.shape), axis, 0, 0)  9.97 us
    ppermute x2, waiting for transfers between devices, passed_along(): return lax.ppermute(block, axis, route)  7.34 us
    pallas_call x2, Pallas kernels, back_block(): pl.pallas_call(functools.partial(back_kernel, step_size), out_shape=(jax....  7.04 us
    pallas_call x2, Pallas kernels, run_block(): pl.pallas_call(functools.partial(block_kernel, step_size), out_shape=(jax...  5.66 us
    all_to_all x1, starting transfers between devices, dp_sum(): got = lax.all_to_all(terms, axis, 0, 0)  4.46 us
  transfers between devices with their start and end apart: 11, of which 11 were waited for; matrix products, arithmetic and copies ran while one was open for 3% of the time, Pallas kernels for 0%

profile of v15, /device:TPU:96, one launch (start us, length us, event | category | flops | bytes accessed | tf_op | source)
XLA Modules:
  0.0 135.1 jit_solution(3149961191867583616)
XLA Ops:
  0.6 0.0 copy-start.2
  0.6 2.8 %shard_map.67 = (f32[64,256]{1,0:T(8,128)}, f32[4,64,256]{2,1,0:T(8,128)}) custom-call(f32[64,256]{1,0:T(8,128)} %bitcast.272, bf16[4,64,576]{2,1,0:T(8,128)(2,1)} %weight_ref.3), custom_call_target="tpu_custom_call" | custom-call | flops 75497472 | bytes 688128 | tf_op jit(solution)/shard_map/pallas_call | solution.py:144
  3.5 2.0 %collective-permute-start = (f32[1,64,256]{2,1,0:T(8,128)}, f32[1,64,256]{2,1,0:T(8,128)S(1)}, u32[]{:S(2)}, u32[]{:S(2)}) collective-permute-start(f32[1,64,256]{2,1,0:T(8,128)} %bitcast.302), channel_id=1, source_target_pairs={{0,4},{4,8},{8,12},{12,16},{16,20},{20,24},{24,28},{28,32},{32,36}... | collective-permute-start | bytes 196616 | tf_op jit(solution)/shard_map/ppermute | solution.py:63
  5.5 0.0 copy-done.2
  5.5 0.0 copy-done.8
  5.6 0.0 copy-start.3
  5.6 0.1 broadcast_multiply_fusion
  5.7 5.9 %collective-permute-done = f32[1,64,256]{2,1,0:T(8,128)S(1)} collective-permute-done((f32[1,64,256]{2,1,0:T(8,128)}, f32[1,64,256]{2,1,0:T(8,128)S(1)}, u32[]{:S(2)}, u32[]{:S(2)}) %collective-permute-start) | collective-permute-done | bytes 65568 | tf_op jit(solution)/shard_map/ppermute | solution.py:63
  11.5 0.0 copy-done.3
  11.5 0.6 fusion.12.state_ref
  12.2 2.8 %shard_map.68 = (f32[64,256]{1,0:T(8,128)}, f32[4,64,256]{2,1,0:T(8,128)}) custom-call(f32[64,256]{1,0:T(8,128)} %fusion.12.state_ref, bf16[4,64,576]{2,1,0:T(8,128)(2,1)} %weight_ref.3), custom_call_target="tpu_custom_call" | custom-call | flops 75497472 | bytes 688128 | tf_op jit(solution)/shard_map/pallas_call | solution.py:144
  15.0 0.9 bitcast_subtract_fusion.1
  15.9 1.9 %collective-permute-start.1 = (f32[130,256]{1,0:T(8,128)S(1)}, f32[130,256]{1,0:T(8,128)S(1)}, u32[]{:S(2)}, u32[]{:S(2)}) collective-permute-start(f32[130,256]{1,0:T(8,128)S(1)} %pad_maximum_fusion), channel_id=1, source_target_pairs={{0,4},{4,0},{8,12},{12,8},{16,20},{20,16},{24,28},{28,24},{32,36},... | collective-permute-start | bytes 399368 | tf_op jit(solution)/shard_map/ppermute | solution.py:24
  17.9 1.3 collective-permute-done.1
  19.2 0.1 add_select_fusion.17
  19.3 0.1 fusion.25
  19.4 1.9 %collective-permute-start.2 = (f32[130,256]{1,0:T(8,128)S(1)}, f32[130,256]{1,0:T(8,128)S(1)}, u32[]{:S(2)}, u32[]{:S(2)}) collective-permute-start(f32[130,256]{1,0:T(8,128)S(1)} %pad_maximum_fusion.1), channel_id=1, source_target_pairs={{0,8},{4,12},{8,0},{12,4},{16,24},{20,28},{24,16},{28,20},{32,40},... | collective-permute-start | bytes 399368 | tf_op jit(solution)/shard_map/ppermute | solution.py:24
  21.4 5.7 %collective-permute-done.2 = f32[130,256]{1,0:T(8,128)S(1)} collective-permute-done((f32[130,256]{1,0:T(8,128)S(1)}, f32[130,256]{1,0:T(8,128)S(1)}, u32[]{:S(2)}, u32[]{:S(2)}) %collective-permute-start.2) | collective-permute-done | bytes 133152 | tf_op jit(solution)/shard_map/ppermute | solution.py:24
  27.1 0.1 fusion.10
  27.2 0.1 fusion.23
  27.3 3.3 %collective-permute-start.3 = (f32[130,256]{1,0:T(8,128)S(1)}, f32[130,256]{1,0:T(8,128)S(1)}, u32[]{:S(2)}, u32[]{:S(2)}) collective-permute-start(f32[130,256]{1,0:T(8,128)S(1)} %pad_maximum_fusion.2), channel_id=1, source_target_pairs={{0,24},{4,28},{8,16},{12,20},{16,8},{20,12},{24,0},{28,4},{32,56},... | collective-permute-start | bytes 399368 | tf_op jit(solution)/shard_map/ppermute | solution.py:24
  30.7 4.8 %collective-permute-done.3 = f32[130,256]{1,0:T(8,128)S(1)} collective-permute-done((f32[130,256]{1,0:T(8,128)S(1)}, f32[130,256]{1,0:T(8,128)S(1)}, u32[]{:S(2)}, u32[]{:S(2)}) %collective-permute-start.3) | collective-permute-done | bytes 133152 | tf_op jit(solution)/shard_map/ppermute | solution.py:24
  35.5 0.1 add_select_fusion.15
  35.7 0.1 fusion.26
  35.8 2.0 %collective-permute-start.4 = (f32[130,256]{1,0:T(8,128)S(1)}, f32[130,256]{1,0:T(8,128)S(1)}, u32[]{:S(2)}, u32[]{:S(2)}) collective-permute-start(f32[130,256]{1,0:T(8,128)S(1)} %pad_maximum_fusion.3), channel_id=1, source_target_pairs={{0,32},{4,36},{8,40},{12,44},{16,48},{20,52},{24,56},{28,60},{32,0... | collective-permute-start | bytes 399368 | tf_op jit(solution)/shard_map/ppermute | solution.py:24
  37.8 4.9 %collective-permute-done.4 = f32[130,256]{1,0:T(8,128)S(1)} collective-permute-done((f32[130,256]{1,0:T(8,128)S(1)}, f32[130,256]{1,0:T(8,128)S(1)}, u32[]{:S(2)}, u32[]{:S(2)}) %collective-permute-start.4) | collective-permute-done | bytes 133152 | tf_op jit(solution)/shard_map/ppermute | solution.py:24
  42.8 0.1 fusion.8
  42.9 0.1 fusion.24
  43.0 0.0 copy-start
  43.0 2.1 %collective-permute-start.5 = (f32[130,256]{1,0:T(8,128)S(1)}, f32[130,256]{1,0:T(8,128)S(1)}, u32[]{:S(2)}, u32[]{:S(2)}) collective-permute-start(f32[130,256]{1,0:T(8,128)S(1)} %pad_maximum_fusion.4), channel_id=1, source_target_pairs={{0,64},{4,68},{8,72},{12,76},{16,80},{20,84},{24,88},{28,92},{32,9... | collective-permute-start | bytes 399368 | tf_op jit(solution)/shard_map/ppermute | solution.py:24
  45.1 0.0 copy-done
  45.1 1.1 copy.7
  46.2 5.8 %collective-permute-done.5 = f32[130,256]{1,0:T(8,128)S(1)} collective-permute-done((f32[130,256]{1,0:T(8,128)S(1)}, f32[130,256]{1,0:T(8,128)S(1)}, u32[]{:S(2)}, u32[]{:S(2)}) %collective-permute-start.5) | collective-permute-done | bytes 133152 | tf_op jit(solution)/shard_map/ppermute | solution.py:24
  52.1 0.1 add_select_fusion.13
  52.2 0.1 fusion.27
  52.3 0.0 copy-start.5
  52.3 9.2 %collective-permute-start.6 = (f32[130,256]{1,0:T(8,128)S(1)}, f32[130,256]{1,0:T(8,128)S(1)}, u32[]{:S(2)}, u32[]{:S(2)}) collective-permute-start(f32[130,256]{1,0:T(8,128)S(1)} %pad_maximum_fusion.5), channel_id=1, source_target_pairs={{0,128},{4,132},{8,136},{12,140},{16,144},{20,148},{24,152},{28,15... | collective-permute-start | bytes 399368 | tf_op jit(solution)/shard_map/ppermute | solution.py:24
  61.6 0.0 copy-done.5
  61.6 6.6 %collective-permute-done.6 = f32[130,256]{1,0:T(8,128)S(1)} collective-permute-done((f32[130,256]{1,0:T(8,128)S(1)}, f32[130,256]{1,0:T(8,128)S(1)}, u32[]{:S(2)}, u32[]{:S(2)}) %collective-permute-start.6) | collective-permute-done | bytes 133152 | tf_op jit(solution)/shard_map/ppermute | solution.py:24
  68.3 0.1 select_bitcast_fusion
  68.4 0.1 fusion.6
  68.5 0.0 copy-start.4
  68.6 10.9 %collective-permute-start.7 = (f32[130,256]{1,0:T(8,128)S(1)}, f32[130,256]{1,0:T(8,128)S(1)}, u32[]{:S(2)}, u32[]{:S(2)}) collective-permute-start(f32[130,256]{1,0:T(8,128)S(1)} %pad_maximum_fusion.6), channel_id=1, source_target_pairs={{0,384},{4,388},{8,392},{12,396},{16,400},{20,404},{24,408},{28,41... | collective-permute-start | bytes 399368 | tf_op jit(solution)/shard_map/ppermute | solution.py:24
  79.5 0.0 copy-done.4
  79.5 0.7 maximum_bitcast_fusion.1.kept_ref
  80.3 7.2 %collective-permute-done.7 = f32[130,256]{1,0:T(8,128)S(1)} collective-permute-done((f32[130,256]{1,0:T(8,128)S(1)}, f32[130,256]{1,0:T(8,128)S(1)}, u32[]{:S(2)}, u32[]{:S(2)}) %collective-permute-start.7) | collective-permute-done | bytes 133152 | tf_op jit(solution)/shard_map/ppermute | solution.py:24
  87.5 0.8 bitcast_add_fusion.10
  88.2 3.5 %shard_map.69 = (f32[64,256]{1,0:T(8,128)}, f32[4,64,576]{2,1,0:T(8,128)}) custom-call(f32[4,64,256]{2,1,0:T(8,128)} %maximum_bitcast_fusion.1.kept_ref, bf16[4,576,64]{2,1,0:T(8,128)(2,1)} %bitcast.265, f32[64,256]{1,0:T(8,128)} %get-tuple-element.19.upstream_ref), custom_call_target="tpu_custom_call" | custom-call | flops 150994944 | bytes 1277952 | tf_op jit(solution)/shard_map/pallas_call | solution.py:166
  91.7 1.9 %collective-permute-start.8 = (f32[1,64,256]{2,1,0:T(8,128)}, f32[1,64,256]{2,1,0:T(8,128)S(1)}, u32[]{:S(2)}, u32[]{:S(2)}) collective-permute-start(f32[1,64,256]{2,1,0:T(8,128)} %bitcast.281), channel_id=1, source_target_pairs={{4,0},{8,4},{12,8},{16,12},{20,16},{24,20},{28,24},{32,28},{36,32}... | collective-permute-start | bytes 196616 | tf_op jit(solution)/shard_map/ppermute | solution.py:63
  93.6 0.7 maximum_bitcast_fusion.kept_ref
  94.3 1.5 %collective-permute-done.8 = f32[1,64,256]{2,1,0:T(8,128)S(1)} collective-permute-done((f32[1,64,256]{2,1,0:T(8,128)}, f32[1,64,256]{2,1,0:T(8,128)S(1)}, u32[]{:S(2)}, u32[]{:S(2)}) %collective-permute-start.8) | collective-permute-done | bytes 65568 | tf_op jit(solution)/shard_map/ppermute | solution.py:63
  95.8 0.6 fusion.4.upstream_ref
  96.5 3.5 %shard_map.70 = (f32[64,256]{1,0:T(8,128)}, f32[4,64,576]{2,1,0:T(8,128)}) custom-call(f32[4,64,256]{2,1,0:T(8,128)} %maximum_bitcast_fusion.kept_ref, bf16[4,576,64]{2,1,0:T(8,128)(2,1)} %bitcast.266, f32[64,256]{1,0:T(8,128)} %fusion.4.upstream_ref), custom_call_target="tpu_custom_call" | custom-call | flops 150994944 | bytes 1277952 | tf_op jit(solution)/shard_map/pallas_call | solution.py:166
  100.0 2.0 %add.250 = f32[4,64,576]{2,1,0:T(8,128)} add(f32[4,64,576]{2,1,0:T(8,128)S(1)} %copy-done.1, f32[4,64,576]{2,1,0:T(8,128)} %get-tuple-element.18) | non-fusion elementwise | flops 147456 | bytes 1769472 | tf_op jit(solution)/shard_map/add | solution.py:222
  102.0 4.5 %all-to-all-start = ((f32[4,64,576]{2,1,0:T(8,128)}), f32[4,64,576]{2,1,0:T(8,128)S(1)}, u32[]{:S(2)}, u32[]{:S(2)}) async-start(f32[4,64,576]{2,1,0:T(8,128)} %add.250), calls=%async_computation | async-start | bytes 1310720 | tf_op jit(solution)/shard_map/all_to_all | solution.py:53
  106.5 11.9 %all-to-all-done = f32[4,64,576]{2,1,0:T(8,128)S(1)} async-done(((f32[4,64,576]{2,1,0:T(8,128)}), f32[4,64,576]{2,1,0:T(8,128)S(1)}, u32[]{:S(2)}, u32[]{:S(2)}) %all-to-all-start) | async-done | bytes 589856 | tf_op jit(solution)/shard_map/all_to_all | solution.py:53
  118.4 0.9 broadcast_in_dim.74
  119.3 3.5 %all-to-all-start.1 = ((f32[4,64,576]{2,1,0:T(8,128)}), f32[4,64,576]{2,1,0:T(8,128)S(1)}, u32[]{:S(2)}, u32[]{:S(2)}) async-start(f32[4,64,576]{2,1,0:T(8,128)} %broadcast_in_dim.74), calls=%async_computation.1 | async-start | bytes 1310720 | tf_op jit(solution)/shard_map/all_to_all | solution.py:57
  122.8 0.8 fusion.1
  123.6 0.1 copy-done.6
  123.6 0.0 copy-done.7
  123.7 0.6 fusion.2
  124.3 10.0 %all-to-all-done.1 = f32[4,64,576]{2,1,0:T(8,128)S(1)} async-done(((f32[4,64,576]{2,1,0:T(8,128)}), f32[4,64,576]{2,1,0:T(8,128)S(1)}, u32[]{:S(2)}, u32[]{:S(2)}) %all-to-all-start.1) | async-done | bytes 589856 | tf_op jit(solution)/shard_map/all_to_all | solution.py:57
  134.3 0.8 copy.9
  (48 shorter events, 0.4 us)
Async XLA Ops:
  0.6 4.9 %copy-start.2 = (f32[1,1,64,256]{3,2,1,0:T(8,128)S(1)}, f32[1,1,64,256]{3,2,1,0:T(8,128)}, u32[]{:S(2)}) copy-start(f32[1,1,64,256]{3,2,1,0:T(8,128)} %param.7) | copy-start | bytes 196612
  3.5 2.1 %copy-start.8 = (f32[1,64]{1,0:T(1,128)S(1)}, f32[1,64]{1,0:T(1,128)}, u32[]{:S(2)}) copy-start(f32[1,64]{1,0:T(1,128)} %param.6) | copy-start | bytes 772
  3.5 8.0 %collective-permute-start = (f32[1,64,256]{2,1,0:T(8,128)}, f32[1,64,256]{2,1,0:T(8,128)S(1)}, u32[]{:S(2)}, u32[]{:S(2)}) collective-permute-start(f32[1,64,256]{2,1,0:T(8,128)} %bitcast.302), channel_id=1, source_target_pairs={{0,4},{4,8},{8,12},{12,16},{16,20},{20,24},{24,28},{28,32},{32,36}... | collective-permute-start | bytes 196616 | tf_op jit(solution)/shard_map/ppermute | solution.py:63
  5.6 6.0 %copy-start.3 = (f32[1,1,64,256]{3,2,1,0:T(8,128)S(1)}, f32[1,1,64,256]{3,2,1,0:T(8,128)}, u32[]{:S(2)}) copy-start(f32[1,1,64,256]{3,2,1,0:T(8,128)} %param.4) | copy-start | bytes 196612
  15.9 3.3 %collective-permute-start.1 = (f32[130,256]{1,0:T(8,128)S(1)}, f32[130,256]{1,0:T(8,128)S(1)}, u32[]{:S(2)}, u32[]{:S(2)}) collective-permute-start(f32[130,256]{1,0:T(8,128)S(1)} %pad_maximum_fusion), channel_id=1, source_target_pairs={{0,4},{4,0},{8,12},{12,8},{16,20},{20,16},{24,28},{28,24},{32,36},... | collective-permute-start | bytes 399368 | tf_op jit(solution)/shard_map/ppermute | solution.py:24
  19.4 7.6 %collective-permute-start.2 = (f32[130,256]{1,0:T(8,128)S(1)}, f32[130,256]{1,0:T(8,128)S(1)}, u32[]{:S(2)}, u32[]{:S(2)}) collective-permute-start(f32[130,256]{1,0:T(8,128)S(1)} %pad_maximum_fusion.1), channel_id=1, source_target_pairs={{0,8},{4,12},{8,0},{12,4},{16,24},{20,28},{24,16},{28,20},{32,40},... | collective-permute-start | bytes 399368 | tf_op jit(solution)/shard_map/ppermute | solution.py:24
  27.3 8.2 %collective-permute-start.3 = (f32[130,256]{1,0:T(8,128)S(1)}, f32[130,256]{1,0:T(8,128)S(1)}, u32[]{:S(2)}, u32[]{:S(2)}) collective-permute-start(f32[130,256]{1,0:T(8,128)S(1)} %pad_maximum_fusion.2), channel_id=1, source_target_pairs={{0,24},{4,28},{8,16},{12,20},{16,8},{20,12},{24,0},{28,4},{32,56},... | collective-permute-start | bytes 399368 | tf_op jit(solution)/shard_map/ppermute | solution.py:24
  35.8 6.9 %collective-permute-start.4 = (f32[130,256]{1,0:T(8,128)S(1)}, f32[130,256]{1,0:T(8,128)S(1)}, u32[]{:S(2)}, u32[]{:S(2)}) collective-permute-start(f32[130,256]{1,0:T(8,128)S(1)} %pad_maximum_fusion.3), channel_id=1, source_target_pairs={{0,32},{4,36},{8,40},{12,44},{16,48},{20,52},{24,56},{28,60},{32,0... | collective-permute-start | bytes 399368 | tf_op jit(solution)/shard_map/ppermute | solution.py:24
  43.0 2.1 %copy-start = (bf16[4,64,576]{2,1,0:T(8,128)(2,1)S(1)}, bf16[4,64,576]{2,1,0:T(8,128)(2,1)}, u32[]{:S(2)}) copy-start(bf16[4,64,576]{2,1,0:T(8,128)(2,1)} %weight_ref.3) | copy-start | bytes 884740
  43.0 9.0 %collective-permute-start.5 = (f32[130,256]{1,0:T(8,128)S(1)}, f32[130,256]{1,0:T(8,128)S(1)}, u32[]{:S(2)}, u32[]{:S(2)}) collective-permute-start(f32[130,256]{1,0:T(8,128)S(1)} %pad_maximum_fusion.4), channel_id=1, source_target_pairs={{0,64},{4,68},{8,72},{12,76},{16,80},{20,84},{24,88},{28,92},{32,9... | collective-permute-start | bytes 399368 | tf_op jit(solution)/shard_map/ppermute | solution.py:24
  52.3 9.3 %copy-start.5 = (f32[4,64,256]{2,1,0:T(8,128)S(1)}, f32[4,64,256]{2,1,0:T(8,128)}, u32[]{:S(2)}) copy-start(f32[4,64,256]{2,1,0:T(8,128)} %get-tuple-element.13) | copy-start | bytes 786436
  52.3 15.9 %collective-permute-start.6 = (f32[130,256]{1,0:T(8,128)S(1)}, f32[130,256]{1,0:T(8,128)S(1)}, u32[]{:S(2)}, u32[]{:S(2)}) collective-permute-start(f32[130,256]{1,0:T(8,128)S(1)} %pad_maximum_fusion.5), channel_id=1, source_target_pairs={{0,128},{4,132},{8,136},{12,140},{16,144},{20,148},{24,152},{28,15... | collective-permute-start | bytes 399368 | tf_op jit(solution)/shard_map/ppermute | solution.py:24
  68.5 11.0 %copy-start.4 = (f32[4,64,256]{2,1,0:T(8,128)S(1)}, f32[4,64,256]{2,1,0:T(8,128)}, u32[]{:S(2)}) copy-start(f32[4,64,256]{2,1,0:T(8,128)} %get-tuple-element.14) | copy-start | bytes 786436
  68.6 18.9 %collective-permute-start.7 = (f32[130,256]{1,0:T(8,128)S(1)}, f32[130,256]{1,0:T(8,128)S(1)}, u32[]{:S(2)}, u32[]{:S(2)}) collective-permute-start(f32[130,256]{1,0:T(8,128)S(1)} %pad_maximum_fusion.6), channel_id=1, source_target_pairs={{0,384},{4,388},{8,392},{12,396},{16,400},{20,404},{24,408},{28,41... | collective-permute-start | bytes 399368 | tf_op jit(solution)/shard_map/ppermute | solution.py:24
  91.7 4.1 %collective-permute-start.8 = (f32[1,64,256]{2,1,0:T(8,128)}, f32[1,64,256]{2,1,0:T(8,128)S(1)}, u32[]{:S(2)}, u32[]{:S(2)}) collective-permute-start(f32[1,64,256]{2,1,0:T(8,128)} %bitcast.281), channel_id=1, source_target_pairs={{4,0},{8,4},{12,8},{16,12},{20,16},{24,20},{28,24},{32,28},{36,32}... | collective-permute-start | bytes 196616 | tf_op jit(solution)/shard_map/ppermute | solution.py:63
  94.3 5.7 %copy-start.1 = (f32[4,64,576]{2,1,0:T(8,128)S(1)}, f32[4,64,576]{2,1,0:T(8,128)}, u32[]{:S(2)}) copy-start(f32[4,64,576]{2,1,0:T(8,128)} %get-tuple-element.17) | copy-start | bytes 1769476
  102.0 16.4 %all-to-all-start = ((f32[4,64,576]{2,1,0:T(8,128)}), f32[4,64,576]{2,1,0:T(8,128)S(1)}, u32[]{:S(2)}, u32[]{:S(2)}) async-start(f32[4,64,576]{2,1,0:T(8,128)} %add.250), calls=%async_computation | async-start | bytes 1310720 | tf_op jit(solution)/shard_map/all_to_all | solution.py:53
  119.3 15.0 %all-to-all-start.1 = ((f32[4,64,576]{2,1,0:T(8,128)}), f32[4,64,576]{2,1,0:T(8,128)S(1)}, u32[]{:S(2)}, u32[]{:S(2)}) async-start(f32[4,64,576]{2,1,0:T(8,128)} %broadcast_in_dim.74), calls=%async_computation.1 | async-start | bytes 1310720 | tf_op jit(solution)/shard_map/all_to_all | solution.py:57
  122.8 0.8 copy-start.6
  122.8 0.9 copy-start.7

commit v16 on v14

--- a/solution.py
+++ b/solution.py
@@ -110,27 +110,28 @@
     return place // WID, place % WID
 
 
-def block_kernel(step_size, state_ref, weight_ref, out_ref, kept_ref):
+def block_kernel(step_size, state_ref, weight_ref, out_ref, squashed_ref, patches_ref):
     current = state_ref[...]
     row, column = pixel_grid(current.shape[-1])
     for layer in range(weight_ref.shape[0]):
-        kept_ref[layer] = current
-        patches = unfold_taps(jnp.tanh(current), row, column)
+        squashed = jnp.tanh(current)
+        patches = unfold_taps(squashed, row, column)
+        squashed_ref[layer] = squashed
+        patches_ref[layer] = patches
         mixed = jnp.dot(weight_ref[layer], patches, preferred_element_type=jnp.float32)
         current = current + step_size * mixed
     out_ref[...] = current
 
 
-def back_kernel(step_size, kept_ref, flipped_ref, upstream_ref, out_ref, grads_ref):
+def back_kernel(step_size, squashed_ref, patches_ref, flipped_ref, upstream_ref, earlier_ref, out_ref, grads_ref):
     upstream = upstream_ref[...]
     channels, pixels = upstream.shape
     row, column = pixel_grid(pixels)
-    for layer in reversed(range(kept_ref.shape[0])):
-        squashed = jnp.tanh(kept_ref[layer])
-        patches = unfold_taps(squashed, row, column)
+    for layer in reversed(range(squashed_ref.shape[0])):
+        squashed = squashed_ref[layer]
         scaled = (step_size * upstream).astype(jnp.bfloat16)
-        grads_ref[layer] = lax.dot_general(
-            scaled, patches, (((1,), (1,)), ((), ())), preferred_element_type=jnp.float32
+        grads_ref[layer] = earlier_ref[layer] + lax.dot_general(
+            scaled, patches_ref[layer], (((1,), (1,)), ((), ())), preferred_element_type=jnp.float32
         )
         spread = jnp.dot(flipped_ref[layer], scaled, preferred_element_type=jnp.float32)
         folded = jnp.zeros((channels, pixels), jnp.float32)
@@ -146,27 +147,32 @@
 
 def run_block(current, block_weights, step_size):
     layers, channels, pixels = block_weights.shape[0], current.shape[-2], current.shape[-1]
+    taps = block_weights.shape[-1]
     spec = pl.BlockSpec(memory_space=pltpu.VMEM)
-    out, kept = pl.pallas_call(
+    out, squashed, patches = pl.pallas_call(
         functools.partial(block_kernel, step_size),
         out_shape=(
             jax.ShapeDtypeStruct((channels, pixels), jnp.float32),
             jax.ShapeDtypeStruct((layers, channels, pixels), jnp.float32),
+            jax.ShapeDtypeStruct((layers, taps, pixels), jnp.bfloat16),
         ),
         in_specs=[spec, spec],
-        out_specs=(spec, spec),
+        out_specs=(spec, spec, spec),
         cost_estimate=pl.CostEstimate(
-            flops=2 * layers * channels * block_weights.shape[-1] * pixels,
+            flops=2 * layers * channels * taps * pixels,
             transcendentals=layers * channels * pixels,
-            bytes_accessed=4 * (layers + 2) * channels * pixels + 2 * block_weights.size,
+            bytes_accessed=4 * (layers + 2) * channels * pixels + 2 * block_weights.size + 2 * layers * taps * pixels,
         ),
     )(current.reshape(channels, pixels), block_weights)
-    return (out.reshape(current.shape), [kept[k].reshape(current.shape) for k in range(layers)])
-
-
-def back_block(inputs_kept, block_weights, upstream, step_size):
+    return (out.reshape(current.shape), (squashed, patches))
+
+
+def back_block(inputs_kept, block_weights, upstream, step_size, earlier=None):
+    squashed, patches = inputs_kept
     layers, channels, pixels = block_weights.shape[0], upstream.shape[-2], upstream.shape[-1]
     taps = block_weights.shape[-1]
+    if earlier is None:
+        earlier = jnp.zeros((layers, channels, taps), jnp.float32)
     flipped = jnp.swapaxes(block_weights, 1, 2)
     spec = pl.BlockSpec(memory_space=pltpu.VMEM)
     out, grads = pl.pallas_call(
@@ -175,14 +181,15 @@
             jax.ShapeDtypeStruct((channels, pixels), jnp.float32),
             jax.ShapeDtypeStruct((layers, channels, taps), jnp.float32),
         ),
-        in_specs=[spec, spec, spec],
+        in_specs=[spec] * 5,
         out_specs=(spec, spec),
         cost_estimate=pl.CostEstimate(
             flops=4 * layers * channels * taps * pixels,
-            transcendentals=layers * channels * pixels,
-            bytes_accessed=4 * (layers + 2) * channels * pixels + 2 * block_weights.size + 4 * layers * channels * taps,
-        ),
-    )(jnp.stack(inputs_kept).reshape(layers, channels, pixels), flipped, upstream.reshape(channels, pixels))
+            transcendentals=0,
+            bytes_accessed=4 * (layers + 2) * channels * pixels + 2 * block_weights.size
+            + 2 * layers * taps * pixels + 8 * layers * channels * taps,
+        ),
+    )(squashed, patches, flipped, upstream.reshape(channels, pixels), earlier)
     return (out.reshape(upstream.shape), grads)
 
 
@@ -222,10 +229,10 @@
     back_start, start_grads = back_block(start_kept, weights, adjoint_here, step_size)
     arriving_bar = passed_along(back_start, "depth", -1)
     relaxed_bar = arriving_bar - passed_in
-    back_own, own_grads = back_block(own_kept, weights, relaxed_bar, step_size)
+    back_own, both_grads = back_block(own_kept, weights, relaxed_bar, step_size, start_grads)
     corrected = forward[1]
     grad_cpoints = jnp.where(leading, back_own + back_start, back_own)
-    grad_weights = dp_sum(start_grads + own_grads, "dp")
+    grad_weights = dp_sum(both_grads, "dp")
     return (corrected[None], grad_cpoints[None], grad_weights)
 
 

time: 135 us -> 139 us (1.030)
  local copies, waits for them, and re-layouts: 1.86 us -> 4.44 us
  Pallas kernels: 12.7 us -> 14.1 us
    ppermute x2, waiting for transfers between devices: 8.03 us -> 6.57 us  [passed_along(): return lax.ppermute(block, axis, route)]
    ppermute x7, waiting for transfers between devices: 35.7 us -> 37.1 us  [exchange(): lax.ppermute(pack(gains, states), axis, [(i, i ^ mask) for i in range(cou...]
    reshape x2 -> x0, other arithmetic: 1.45 us -> none  [back_block(): jnp.stack(inputs_kept).reshape(layers, channels, pixels)]
where the time goes in v16:
time: 139 us; the launch traced here: 138 us
  starting transfers between devices  54.6 us (39%)
  waiting for transfers between devices  54.4 us (39%)
  Pallas kernels  14.1 us (10%)
  other arithmetic  9.44 us (7%)
  local copies, waits for them, and re-layouts  4.44 us (3%)
    ppermute x7, waiting for transfers between devices, exchange(): lax.ppermute(pack(gains, states), axis, [(i, i ^ mask) for i in range(cou...  37.1 us
    ppermute x7, starting transfers between devices, exchange(): lax.ppermute(pack(gains, states), axis, [(i, i ^ mask) for i in range(cou...  31.2 us
    ppermute x3, starting transfers between devices, dp_sum(): lax.ppermute(lax.dynamic_index_in_dim(terms, place ^ k, 0, False), axis,...  9.82 us
    ppermute x3, starting transfers between devices, dp_sum(): lax.ppermute(total, axis, pairs(k))  9.82 us
    pallas_call x2, Pallas kernels, back_block(): pl.pallas_call(functools.partial(back_kernel, step_size), out_shape=(jax....  7.84 us
    ppermute x2, waiting for transfers between devices, passed_along(): return lax.ppermute(block, axis, route)  6.57 us
    pallas_call x2, Pallas kernels, run_block(): pl.pallas_call(functools.partial(block_kernel, step_size), out_shape=(jax...  6.21 us
    ppermute x3, waiting for transfers between devices, dp_sum(): lax.ppermute(lax.dynamic_index_in_dim(terms, place ^ k, 0, False), axis,...  5.79 us
  transfers between devices with their start and end apart: 15, of which 14 were waited for; matrix products, arithmetic and copies ran while one was open for 3% of the time, Pallas kernels for 0%

profile of v16, /device:TPU:96, one launch (start us, length us, event | category | flops | bytes accessed | tf_op | source)
XLA Modules:
  0.0 138.2 jit_solution(11113297433449463687)
XLA Ops:
  0.6 0.0 copy-start.2
  0.6 0.0 copy-start.5
  0.7 0.0 copy-start.1
  0.7 3.1 %shard_map.67 = (f32[64,256]{1,0:T(8,128)}, f32[4,64,256]{2,1,0:T(8,128)}, bf16[4,576,256]{2,1,0:T(8,128)(2,1)}) custom-call(f32[64,256]{1,0:T(8,128)} %bitcast.269, bf16[4,64,576]{2,1,0:T(8,128)(2,1)} %weight_ref.3), custom_call_target="tpu_custom_call" | custom-call | flops 75497472 | bytes 1867776 | tf_op jit(solution)/shard_map/pallas_call | solution.py:152
  3.8 1.9 %collective-permute-start = (f32[1,64,256]{2,1,0:T(8,128)}, f32[1,64,256]{2,1,0:T(8,128)S(1)}, u32[]{:S(2)}, u32[]{:S(2)}) collective-permute-start(f32[1,64,256]{2,1,0:T(8,128)} %bitcast.302), channel_id=1, source_target_pairs={{0,4},{4,8},{8,12},{12,16},{16,20},{20,24},{24,28},{28,32},{32,36}... | collective-permute-start | bytes 196616 | tf_op jit(solution)/shard_map/ppermute | solution.py:69
  5.7 0.9 broadcast_multiply_fusion
  6.6 0.7 pad.41
  7.3 4.4 %collective-permute-done = f32[1,64,256]{2,1,0:T(8,128)S(1)} collective-permute-done((f32[1,64,256]{2,1,0:T(8,128)}, f32[1,64,256]{2,1,0:T(8,128)S(1)}, u32[]{:S(2)}, u32[]{:S(2)}) %collective-permute-start) | collective-permute-done | bytes 65568 | tf_op jit(solution)/shard_map/ppermute | solution.py:69
  11.7 1.5 %fusion.13.state_ref = f32[64,256]{1,0:T(8,128)} fusion(f32[1,64,256]{2,1,0:T(8,128)S(1)} %collective-permute-done, f32[1,1,64,256]{3,2,1,0:T(8,128)} %param.4, pred[]{:T(512)S(6)} %eq.67), kind=kLoop, calls=%fused_computation.73 | loop fusion | flops 16384 | bytes 196609 | tf_op jit(solution)/shard_map/reshape | solution.py:166
  13.2 3.1 %shard_map.68 = (f32[64,256]{1,0:T(8,128)}, f32[4,64,256]{2,1,0:T(8,128)}, bf16[4,576,256]{2,1,0:T(8,128)(2,1)}) custom-call(f32[64,256]{1,0:T(8,128)} %fusion.13.state_ref, bf16[4,64,576]{2,1,0:T(8,128)(2,1)} %weight_ref.3), custom_call_target="tpu_custom_call" | custom-call | flops 75497472 | bytes 1867776 | tf_op jit(solution)/shard_map/pallas_call | solution.py:152
  16.3 0.9 bitcast_subtract_fusion.1
  17.2 1.9 %collective-permute-start.1 = (f32[130,256]{1,0:T(8,128)S(1)}, f32[130,256]{1,0:T(8,128)S(1)}, u32[]{:S(2)}, u32[]{:S(2)}) collective-permute-start(f32[130,256]{1,0:T(8,128)S(1)} %pad_maximum_fusion.1), channel_id=1, source_target_pairs={{0,4},{4,0},{8,12},{12,8},{16,20},{20,16},{24,28},{28,24},{32,36},... | collective-permute-start | bytes 399368 | tf_op jit(solution)/shard_map/ppermute | solution.py:24
  19.2 1.3 collective-permute-done.1
  20.5 0.1 add_select_fusion.17
  20.6 0.1 fusion.27
  20.8 1.9 %collective-permute-start.2 = (f32[130,256]{1,0:T(8,128)S(1)}, f32[130,256]{1,0:T(8,128)S(1)}, u32[]{:S(2)}, u32[]{:S(2)}) collective-permute-start(f32[130,256]{1,0:T(8,128)S(1)} %pad_maximum_fusion.2), channel_id=1, source_target_pairs={{0,8},{4,12},{8,0},{12,4},{16,24},{20,28},{24,16},{28,20},{32,40},... | collective-permute-start | bytes 399368 | tf_op jit(solution)/shard_map/ppermute | solution.py:24
  22.7 5.7 %collective-permute-done.2 = f32[130,256]{1,0:T(8,128)S(1)} collective-permute-done((f32[130,256]{1,0:T(8,128)S(1)}, f32[130,256]{1,0:T(8,128)S(1)}, u32[]{:S(2)}, u32[]{:S(2)}) %collective-permute-start.2) | collective-permute-done | bytes 133152 | tf_op jit(solution)/shard_map/ppermute | solution.py:24
  28.4 0.1 fusion.25
  28.5 0.1 fusion.11
  28.6 3.3 %collective-permute-start.3 = (f32[130,256]{1,0:T(8,128)S(1)}, f32[130,256]{1,0:T(8,128)S(1)}, u32[]{:S(2)}, u32[]{:S(2)}) collective-permute-start(f32[130,256]{1,0:T(8,128)S(1)} %pad_maximum_fusion.3), channel_id=1, source_target_pairs={{0,24},{4,28},{8,16},{12,20},{16,8},{20,12},{24,0},{28,4},{32,56},... | collective-permute-start | bytes 399368 | tf_op jit(solution)/shard_map/ppermute | solution.py:24
  32.0 4.8 %collective-permute-done.3 = f32[130,256]{1,0:T(8,128)S(1)} collective-permute-done((f32[130,256]{1,0:T(8,128)S(1)}, f32[130,256]{1,0:T(8,128)S(1)}, u32[]{:S(2)}, u32[]{:S(2)}) %collective-permute-start.3) | collective-permute-done | bytes 133152 | tf_op jit(solution)/shard_map/ppermute | solution.py:24
  36.8 0.1 add_select_fusion.15
  37.0 0.1 fusion.28
  37.1 2.0 %collective-permute-start.4 = (f32[130,256]{1,0:T(8,128)S(1)}, f32[130,256]{1,0:T(8,128)S(1)}, u32[]{:S(2)}, u32[]{:S(2)}) collective-permute-start(f32[130,256]{1,0:T(8,128)S(1)} %pad_maximum_fusion.4), channel_id=1, source_target_pairs={{0,32},{4,36},{8,40},{12,44},{16,48},{20,52},{24,56},{28,60},{32,0... | collective-permute-start | bytes 399368 | tf_op jit(solution)/shard_map/ppermute | solution.py:24
  39.1 4.9 %collective-permute-done.4 = f32[130,256]{1,0:T(8,128)S(1)} collective-permute-done((f32[130,256]{1,0:T(8,128)S(1)}, f32[130,256]{1,0:T(8,128)S(1)}, u32[]{:S(2)}, u32[]{:S(2)}) %collective-permute-start.4) | collective-permute-done | bytes 133152 | tf_op jit(solution)/shard_map/ppermute | solution.py:24
  44.1 0.1 fusion.26
  44.2 0.1 fusion.9
  44.3 0.0 copy-start
  44.3 2.1 %collective-permute-start.5 = (f32[130,256]{1,0:T(8,128)S(1)}, f32[130,256]{1,0:T(8,128)S(1)}, u32[]{:S(2)}, u32[]{:S(2)}) collective-permute-start(f32[130,256]{1,0:T(8,128)S(1)} %pad_maximum_fusion.5), channel_id=1, source_target_pairs={{0,64},{4,68},{8,72},{12,76},{16,80},{20,84},{24,88},{28,92},{32,9... | collective-permute-start | bytes 399368 | tf_op jit(solution)/shard_map/ppermute | solution.py:24
  46.4 6.9 %collective-permute-done.5 = f32[130,256]{1,0:T(8,128)S(1)} collective-permute-done((f32[130,256]{1,0:T(8,128)S(1)}, f32[130,256]{1,0:T(8,128)S(1)}, u32[]{:S(2)}, u32[]{:S(2)}) %collective-permute-start.5) | collective-permute-done | bytes 133152 | tf_op jit(solution)/shard_map/ppermute | solution.py:24
  53.4 0.1 add_select_fusion.13
  53.5 0.1 fusion.29
  53.6 9.1 %collective-permute-start.6 = (f32[130,256]{1,0:T(8,128)S(1)}, f32[130,256]{1,0:T(8,128)S(1)}, u32[]{:S(2)}, u32[]{:S(2)}) collective-permute-start(f32[130,256]{1,0:T(8,128)S(1)} %pad_maximum_fusion.6), channel_id=1, source_target_pairs={{0,128},{4,132},{8,136},{12,140},{16,144},{20,148},{24,152},{28,15... | collective-permute-start | bytes 399368 | tf_op jit(solution)/shard_map/ppermute | solution.py:24
  62.8 6.7 %collective-permute-done.6 = f32[130,256]{1,0:T(8,128)S(1)} collective-permute-done((f32[130,256]{1,0:T(8,128)S(1)}, f32[130,256]{1,0:T(8,128)S(1)}, u32[]{:S(2)}, u32[]{:S(2)}) %collective-permute-start.6) | collective-permute-done | bytes 133152 | tf_op jit(solution)/shard_map/ppermute | solution.py:24
  69.5 0.1 select_bitcast_fusion
  69.6 0.1 fusion.7
  69.7 10.8 %collective-permute-start.7 = (f32[130,256]{1,0:T(8,128)S(1)}, f32[130,256]{1,0:T(8,128)S(1)}, u32[]{:S(2)}, u32[]{:S(2)}) collective-permute-start(f32[130,256]{1,0:T(8,128)S(1)} %pad_maximum_fusion.7), channel_id=1, source_target_pairs={{0,384},{4,388},{8,392},{12,396},{16,400},{20,404},{24,408},{28,41... | collective-permute-start | bytes 399368 | tf_op jit(solution)/shard_map/ppermute | solution.py:24
  80.6 1.1 copy.8
  81.6 6.8 %collective-permute-done.7 = f32[130,256]{1,0:T(8,128)S(1)} collective-permute-done((f32[130,256]{1,0:T(8,128)S(1)}, f32[130,256]{1,0:T(8,128)S(1)}, u32[]{:S(2)}, u32[]{:S(2)}) %collective-permute-start.7) | collective-permute-done | bytes 133152 | tf_op jit(solution)/shard_map/ppermute | solution.py:24
  88.5 0.8 bitcast_add_fusion.11
  89.2 0.9 broadcast_in_dim.77.earlier_ref
  90.1 3.9 %shard_map.69 = (f32[64,256]{1,0:T(8,128)}, f32[4,64,576]{2,1,0:T(8,128)}) custom-call(f32[4,64,256]{2,1,0:T(8,128)} %get-tuple-element.17.squashed_ref, bf16[4,576,256]{2,1,0:T(8,128)(2,1)} %get-tuple-element.18.patches_ref, bf16[4,576,64]{2,1,0:T(8,128)(2,1)} %bitcast.261, f32[64,256]{1,0:T(8,128)} %get-tuple-element.23.upstream_ref, ...), custom_call_target="tpu_custom_call" | custom-call | flops 150994944 | bytes 3047424 | tf_op jit(solution)/shard_map/pallas_call | solution.py:178
  94.1 1.9 %collective-permute-start.8 = (f32[1,64,256]{2,1,0:T(8,128)}, f32[1,64,256]{2,1,0:T(8,128)S(1)}, u32[]{:S(2)}, u32[]{:S(2)}) collective-permute-start(f32[1,64,256]{2,1,0:T(8,128)} %bitcast.281), channel_id=1, source_target_pairs={{4,0},{8,4},{12,8},{16,12},{20,16},{24,20},{28,24},{32,28},{36,32}... | collective-permute-start | bytes 196616 | tf_op jit(solution)/shard_map/ppermute | solution.py:69
  96.0 2.2 %collective-permute-done.8 = f32[1,64,256]{2,1,0:T(8,128)S(1)} collective-permute-done((f32[1,64,256]{2,1,0:T(8,128)}, f32[1,64,256]{2,1,0:T(8,128)S(1)}, u32[]{:S(2)}, u32[]{:S(2)}) %collective-permute-start.8) | collective-permute-done | bytes 65568 | tf_op jit(solution)/shard_map/ppermute | solution.py:69
  98.2 0.6 fusion.5.upstream_ref
  98.8 3.9 %shard_map.70 = (f32[64,256]{1,0:T(8,128)}, f32[4,64,576]{2,1,0:T(8,128)}) custom-call(f32[4,64,256]{2,1,0:T(8,128)} %get-tuple-element.15.squashed_ref, bf16[4,576,256]{2,1,0:T(8,128)(2,1)} %get-tuple-element.16.patches_ref, bf16[4,576,64]{2,1,0:T(8,128)(2,1)} %bitcast.262, f32[64,256]{1,0:T(8,128)} %fusion.5.upstream_ref, ...), custom_call_target="tpu_custom_call" | custom-call | flops 150994944 | bytes 3047424 | tf_op jit(solution)/shard_map/pallas_call | solution.py:178
  102.7 1.1 dynamic-slice_bitcast_fusion.2
  103.9 4.9 %collective-permute-start.11 = (f32[64,576]{1,0:T(8,128)S(1)}, f32[64,576]{1,0:T(8,128)S(1)}, u32[]{:S(2)}, u32[]{:S(2)}) collective-permute-start(f32[64,576]{1,0:T(8,128)S(1)} %get-tuple-element.38), channel_id=1, source_target_pairs={{0,3},{1,2},{2,1},{3,0},{4,7},{5,6},{6,5},{7,4},{8,11},{9,10},{10,... | collective-permute-start | bytes 442376 | tf_op jit(solution)/shard_map/ppermute | solution.py:56
  108.8 2.5 %collective-permute-start.10 = (f32[64,576]{1,0:T(8,128)S(1)}, f32[64,576]{1,0:T(8,128)S(1)}, u32[]{:S(2)}, u32[]{:S(2)}) collective-permute-start(f32[64,576]{1,0:T(8,128)S(1)} %get-tuple-element.39), channel_id=1, source_target_pairs={{0,2},{1,3},{2,0},{3,1},{4,6},{5,7},{6,4},{7,5},{8,10},{9,11},{10,... | collective-permute-start | bytes 442376 | tf_op jit(solution)/shard_map/ppermute | solution.py:56
  111.3 2.4 %collective-permute-start.9 = (f32[64,576]{1,0:T(8,128)S(1)}, f32[64,576]{1,0:T(8,128)S(1)}, u32[]{:S(2)}, u32[]{:S(2)}) collective-permute-start(f32[64,576]{1,0:T(8,128)S(1)} %get-tuple-element.37), channel_id=1, source_target_pairs={{0,1},{1,0},{2,3},{3,2},{4,5},{5,4},{6,7},{7,6},{8,9},{9,8},{10,11... | collective-permute-start | bytes 442376 | tf_op jit(solution)/shard_map/ppermute | solution.py:56
  113.7 0.8 fusion.2
  114.5 0.0 collective-permute-done.11
  114.5 4.4 %collective-permute-done.10 = f32[64,576]{1,0:T(8,128)S(1)} collective-permute-done((f32[64,576]{1,0:T(8,128)S(1)}, f32[64,576]{1,0:T(8,128)S(1)}, u32[]{:S(2)}, u32[]{:S(2)}) %collective-permute-start.10) | collective-permute-done | bytes 147488 | tf_op jit(solution)/shard_map/ppermute | solution.py:56
  118.9 1.4 collective-permute-done.9
  120.3 1.0 fusion.1
  121.2 4.6 %collective-permute-start.14 = (f32[64,576]{1,0:T(8,128)S(1)}, f32[64,576]{1,0:T(8,128)S(1)}, u32[]{:S(2)}, u32[]{:S(2)}) collective-permute-start(f32[64,576]{1,0:T(8,128)S(1)} %fusion.1), channel_id=1, source_target_pairs={{0,3},{1,2},{2,1},{3,0},{4,7},{5,6},{6,5},{7,4},{8,11},{9,10},{10,... | collective-permute-start | bytes 442376 | tf_op jit(solution)/shard_map/ppermute | solution.py:62
  125.8 2.6 %collective-permute-start.13 = (f32[64,576]{1,0:T(8,128)S(1)}, f32[64,576]{1,0:T(8,128)S(1)}, u32[]{:S(2)}, u32[]{:S(2)}) collective-permute-start(f32[64,576]{1,0:T(8,128)S(1)} %fusion.1), channel_id=1, source_target_pairs={{0,2},{1,3},{2,0},{3,1},{4,6},{5,7},{6,4},{7,5},{8,10},{9,11},{10,... | collective-permute-start | bytes 442376 | tf_op jit(solution)/shard_map/ppermute | solution.py:62
  128.4 2.7 %collective-permute-start.12 = (f32[64,576]{1,0:T(8,128)S(1)}, f32[64,576]{1,0:T(8,128)S(1)}, u32[]{:S(2)}, u32[]{:S(2)}) collective-permute-start(f32[64,576]{1,0:T(8,128)S(1)} %fusion.1), channel_id=1, source_target_pairs={{0,1},{1,0},{2,3},{3,2},{4,5},{5,4},{6,7},{7,6},{8,9},{9,8},{10,11... | collective-permute-start | bytes 442376 | tf_op jit(solution)/shard_map/ppermute | solution.py:62
  131.1 0.6 fusion.3
  131.7 1.4 %collective-permute-done.14 = f32[64,576]{1,0:T(8,128)S(1)} collective-permute-done((f32[64,576]{1,0:T(8,128)S(1)}, f32[64,576]{1,0:T(8,128)S(1)}, u32[]{:S(2)}, u32[]{:S(2)}) %collective-permute-start.14) | collective-permute-done | bytes 147488 | tf_op jit(solution)/shard_map/ppermute | solution.py:62
  133.2 3.1 %collective-permute-done.13 = f32[64,576]{1,0:T(8,128)S(1)} collective-permute-done((f32[64,576]{1,0:T(8,128)S(1)}, f32[64,576]{1,0:T(8,128)S(1)}, u32[]{:S(2)}, u32[]{:S(2)}) %collective-permute-start.13) | collective-permute-done | bytes 147488 | tf_op jit(solution)/shard_map/ppermute | solution.py:62
  136.3 0.3 collective-permute-done.12
  136.6 0.6 gather_fusion
  137.2 0.9 broadcast_select_fusion
  (51 shorter events, 0.4 us)
Async XLA Ops:
  0.6 15.6 %copy-start.2 = (f32[1,1,64,256]{3,2,1,0:T(8,128)S(1)}, f32[1,1,64,256]{3,2,1,0:T(8,128)}, u32[]{:S(2)}) copy-start(f32[1,1,64,256]{3,2,1,0:T(8,128)} %param.4) | copy-start | bytes 196612
  0.6 19.8 %copy-start.5 = (f32[1,64]{1,0:T(1,128)S(1)}, f32[1,64]{1,0:T(1,128)}, u32[]{:S(2)}) copy-start(f32[1,64]{1,0:T(1,128)} %param.6) | copy-start | bytes 772
  0.7 19.9 %copy-start.1 = (f32[1,1,64,256]{3,2,1,0:T(8,128)S(1)}, f32[1,1,64,256]{3,2,1,0:T(8,128)}, u32[]{:S(2)}) copy-start(f32[1,1,64,256]{3,2,1,0:T(8,128)} %param.7) | copy-start | bytes 196612
  3.8 7.9 %collective-permute-start = (f32[1,64,256]{2,1,0:T(8,128)}, f32[1,64,256]{2,1,0:T(8,128)S(1)}, u32[]{:S(2)}, u32[]{:S(2)}) collective-permute-start(f32[1,64,256]{2,1,0:T(8,128)} %bitcast.302), channel_id=1, source_target_pairs={{0,4},{4,8},{8,12},{12,16},{16,20},{20,24},{24,28},{28,32},{32,36}... | collective-permute-start | bytes 196616 | tf_op jit(solution)/shard_map/ppermute | solution.py:69
  17.2 3.3 %collective-permute-start.1 = (f32[130,256]{1,0:T(8,128)S(1)}, f32[130,256]{1,0:T(8,128)S(1)}, u32[]{:S(2)}, u32[]{:S(2)}) collective-permute-start(f32[130,256]{1,0:T(8,128)S(1)} %pad_maximum_fusion.1), channel_id=1, source_target_pairs={{0,4},{4,0},{8,12},{12,8},{16,20},{20,16},{24,28},{28,24},{32,36},... | collective-permute-start | bytes 399368 | tf_op jit(solution)/shard_map/ppermute | solution.py:24
  20.8 7.6 %collective-permute-start.2 = (f32[130,256]{1,0:T(8,128)S(1)}, f32[130,256]{1,0:T(8,128)S(1)}, u32[]{:S(2)}, u32[]{:S(2)}) collective-permute-start(f32[130,256]{1,0:T(8,128)S(1)} %pad_maximum_fusion.2), channel_id=1, source_target_pairs={{0,8},{4,12},{8,0},{12,4},{16,24},{20,28},{24,16},{28,20},{32,40},... | collective-permute-start | bytes 399368 | tf_op jit(solution)/shard_map/ppermute | solution.py:24
  28.6 8.2 %collective-permute-start.3 = (f32[130,256]{1,0:T(8,128)S(1)}, f32[130,256]{1,0:T(8,128)S(1)}, u32[]{:S(2)}, u32[]{:S(2)}) collective-permute-start(f32[130,256]{1,0:T(8,128)S(1)} %pad_maximum_fusion.3), channel_id=1, source_target_pairs={{0,24},{4,28},{8,16},{12,20},{16,8},{20,12},{24,0},{28,4},{32,56},... | collective-permute-start | bytes 399368 | tf_op jit(solution)/shard_map/ppermute | solution.py:24
  37.1 6.9 %collective-permute-start.4 = (f32[130,256]{1,0:T(8,128)S(1)}, f32[130,256]{1,0:T(8,128)S(1)}, u32[]{:S(2)}, u32[]{:S(2)}) collective-permute-start(f32[130,256]{1,0:T(8,128)S(1)} %pad_maximum_fusion.4), channel_id=1, source_target_pairs={{0,32},{4,36},{8,40},{12,44},{16,48},{20,52},{24,56},{28,60},{32,0... | collective-permute-start | bytes 399368 | tf_op jit(solution)/shard_map/ppermute | solution.py:24
  44.3 36.3 %copy-start = (bf16[4,64,576]{2,1,0:T(8,128)(2,1)S(1)}, bf16[4,64,576]{2,1,0:T(8,128)(2,1)}, u32[]{:S(2)}) copy-start(bf16[4,64,576]{2,1,0:T(8,128)(2,1)} %weight_ref.3) | copy-start | bytes 884740
  44.3 9.0 %collective-permute-start.5 = (f32[130,256]{1,0:T(8,128)S(1)}, f32[130,256]{1,0:T(8,128)S(1)}, u32[]{:S(2)}, u32[]{:S(2)}) collective-permute-start(f32[130,256]{1,0:T(8,128)S(1)} %pad_maximum_fusion.5), channel_id=1, source_target_pairs={{0,64},{4,68},{8,72},{12,76},{16,80},{20,84},{24,88},{28,92},{32,9... | collective-permute-start | bytes 399368 | tf_op jit(solution)/shard_map/ppermute | solution.py:24
  53.6 15.8 %collective-permute-start.6 = (f32[130,256]{1,0:T(8,128)S(1)}, f32[130,256]{1,0:T(8,128)S(1)}, u32[]{:S(2)}, u32[]{:S(2)}) collective-permute-start(f32[130,256]{1,0:T(8,128)S(1)} %pad_maximum_fusion.6), channel_id=1, source_target_pairs={{0,128},{4,132},{8,136},{12,140},{16,144},{20,148},{24,152},{28,15... | collective-permute-start | bytes 399368 | tf_op jit(solution)/shard_map/ppermute | solution.py:24
  69.7 18.8 %collective-permute-start.7 = (f32[130,256]{1,0:T(8,128)S(1)}, f32[130,256]{1,0:T(8,128)S(1)}, u32[]{:S(2)}, u32[]{:S(2)}) collective-permute-start(f32[130,256]{1,0:T(8,128)S(1)} %pad_maximum_fusion.7), channel_id=1, source_target_pairs={{0,384},{4,388},{8,392},{12,396},{16,400},{20,404},{24,408},{28,41... | collective-permute-start | bytes 399368 | tf_op jit(solution)/shard_map/ppermute | solution.py:24
  94.1 4.1 %collective-permute-start.8 = (f32[1,64,256]{2,1,0:T(8,128)}, f32[1,64,256]{2,1,0:T(8,128)S(1)}, u32[]{:S(2)}, u32[]{:S(2)}) collective-permute-start(f32[1,64,256]{2,1,0:T(8,128)} %bitcast.281), channel_id=1, source_target_pairs={{4,0},{8,4},{12,8},{16,12},{20,16},{24,20},{28,24},{32,28},{36,32}... | collective-permute-start | bytes 196616 | tf_op jit(solution)/shard_map/ppermute | solution.py:69
  102.7 28.4 %copy-start.3 = (f32[64,256]{1,0:T(8,128)S(1)}, f32[64,256]{1,0:T(8,128)}, u32[]{:S(2)}) copy-start(f32[64,256]{1,0:T(8,128)} %get-tuple-element.19) | copy-start | bytes 196612
  102.7 28.4 %copy-start.4 = (f32[64,256]{1,0:T(8,128)S(1)}, f32[64,256]{1,0:T(8,128)}, u32[]{:S(2)}) copy-start(f32[64,256]{1,0:T(8,128)} %get-tuple-element.21) | copy-start | bytes 196612
  103.9 10.6 %collective-permute-start.11 = (f32[64,576]{1,0:T(8,128)S(1)}, f32[64,576]{1,0:T(8,128)S(1)}, u32[]{:S(2)}, u32[]{:S(2)}) collective-permute-start(f32[64,576]{1,0:T(8,128)S(1)} %get-tuple-element.38), channel_id=1, source_target_pairs={{0,3},{1,2},{2,1},{3,0},{4,7},{5,6},{6,5},{7,4},{8,11},{9,10},{10,... | collective-permute-start | bytes 442376 | tf_op jit(solution)/shard_map/ppermute | solution.py:56
  108.8 10.1 %collective-permute-start.10 = (f32[64,576]{1,0:T(8,128)S(1)}, f32[64,576]{1,0:T(8,128)S(1)}, u32[]{:S(2)}, u32[]{:S(2)}) collective-permute-start(f32[64,576]{1,0:T(8,128)S(1)} %get-tuple-element.39), channel_id=1, source_target_pairs={{0,2},{1,3},{2,0},{3,1},{4,6},{5,7},{6,4},{7,5},{8,10},{9,11},{10,... | collective-permute-start | bytes 442376 | tf_op jit(solution)/shard_map/ppermute | solution.py:56
  111.3 8.9 %collective-permute-start.9 = (f32[64,576]{1,0:T(8,128)S(1)}, f32[64,576]{1,0:T(8,128)S(1)}, u32[]{:S(2)}, u32[]{:S(2)}) collective-permute-start(f32[64,576]{1,0:T(8,128)S(1)} %get-tuple-element.37), channel_id=1, source_target_pairs={{0,1},{1,0},{2,3},{3,2},{4,5},{5,4},{6,7},{7,6},{8,9},{9,8},{10,11... | collective-permute-start | bytes 442376 | tf_op jit(solution)/shard_map/ppermute | solution.py:56
  121.2 12.0 %collective-permute-start.14 = (f32[64,576]{1,0:T(8,128)S(1)}, f32[64,576]{1,0:T(8,128)S(1)}, u32[]{:S(2)}, u32[]{:S(2)}) collective-permute-start(f32[64,576]{1,0:T(8,128)S(1)} %fusion.1), channel_id=1, source_target_pairs={{0,3},{1,2},{2,1},{3,0},{4,7},{5,6},{6,5},{7,4},{8,11},{9,10},{10,... | collective-permute-start | bytes 442376 | tf_op jit(solution)/shard_map/ppermute | solution.py:62
  125.8 10.5 %collective-permute-start.13 = (f32[64,576]{1,0:T(8,128)S(1)}, f32[64,576]{1,0:T(8,128)S(1)}, u32[]{:S(2)}, u32[]{:S(2)}) collective-permute-start(f32[64,576]{1,0:T(8,128)S(1)} %fusion.1), channel_id=1, source_target_pairs={{0,2},{1,3},{2,0},{3,1},{4,6},{5,7},{6,4},{7,5},{8,10},{9,11},{10,... | collective-permute-start | bytes 442376 | tf_op jit(solution)/shard_map/ppermute | solution.py:62
  128.4 8.2 %collective-permute-start.12 = (f32[64,576]{1,0:T(8,128)S(1)}, f32[64,576]{1,0:T(8,128)S(1)}, u32[]{:S(2)}, u32[]{:S(2)}) collective-permute-start(f32[64,576]{1,0:T(8,128)S(1)} %fusion.1), channel_id=1, source_target_pairs={{0,1},{1,0},{2,3},{3,2},{4,5},{5,4},{6,7},{7,6},{8,9},{9,8},{10,11... | collective-permute-start | bytes 442376 | tf_op jit(solution)/shard_map/ppermute | solution.py:62

commit v17 on v14

--- a/solution.py
+++ b/solution.py
@@ -121,7 +121,7 @@
     out_ref[...] = current
 
 
-def back_kernel(step_size, kept_ref, flipped_ref, upstream_ref, out_ref, grads_ref):
+def back_kernel(step_size, kept_ref, flipped_ref, upstream_ref, earlier_ref, out_ref, grads_ref):
     upstream = upstream_ref[...]
     channels, pixels = upstream.shape
     row, column = pixel_grid(pixels)
@@ -129,7 +129,7 @@
         squashed = jnp.tanh(kept_ref[layer])
         patches = unfold_taps(squashed, row, column)
         scaled = (step_size * upstream).astype(jnp.bfloat16)
-        grads_ref[layer] = lax.dot_general(
+        grads_ref[layer] = earlier_ref[layer] + lax.dot_general(
             scaled, patches, (((1,), (1,)), ((), ())), preferred_element_type=jnp.float32
         )
         spread = jnp.dot(flipped_ref[layer], scaled, preferred_element_type=jnp.float32)
@@ -164,9 +164,11 @@
     return (out.reshape(current.shape), [kept[k].reshape(current.shape) for k in range(layers)])
 
 
-def back_block(inputs_kept, block_weights, upstream, step_size):
+def back_block(inputs_kept, block_weights, upstream, step_size, earlier=None):
     layers, channels, pixels = block_weights.shape[0], upstream.shape[-2], upstream.shape[-1]
     taps = block_weights.shape[-1]
+    if earlier is None:
+        earlier = jnp.zeros((layers, channels, taps), jnp.float32)
     flipped = jnp.swapaxes(block_weights, 1, 2)
     spec = pl.BlockSpec(memory_space=pltpu.VMEM)
     out, grads = pl.pallas_call(
@@ -175,14 +177,14 @@
             jax.ShapeDtypeStruct((channels, pixels), jnp.float32),
             jax.ShapeDtypeStruct((layers, channels, taps), jnp.float32),
         ),
-        in_specs=[spec, spec, spec],
+        in_specs=[spec] * 4,
         out_specs=(spec, spec),
         cost_estimate=pl.CostEstimate(
             flops=4 * layers * channels * taps * pixels,
             transcendentals=layers * channels * pixels,
             bytes_accessed=4 * (layers + 2) * channels * pixels + 2 * block_weights.size + 4 * layers * channels * taps,
         ),
-    )(jnp.stack(inputs_kept).reshape(layers, channels, pixels), flipped, upstream.reshape(channels, pixels))
+    )(jnp.stack(inputs_kept).reshape(layers, channels, pixels), flipped, upstream.reshape(channels, pixels), earlier)
     return (out.reshape(upstream.shape), grads)
 
 
@@ -222,10 +224,10 @@
     back_start, start_grads = back_block(start_kept, weights, adjoint_here, step_size)
     arriving_bar = passed_along(back_start, "depth", -1)
     relaxed_bar = arriving_bar - passed_in
-    back_own, own_grads = back_block(own_kept, weights, relaxed_bar, step_size)
+    back_own, both_grads = back_block(own_kept, weights, relaxed_bar, step_size, start_grads)
     corrected = forward[1]
     grad_cpoints = jnp.where(leading, back_own + back_start, back_own)
-    grad_weights = dp_sum(start_grads + own_grads, "dp")
+    grad_weights = dp_sum(both_grads, "dp")
     return (corrected[None], grad_cpoints[None], grad_weights)
 
 

time: 135 us -> 137 us (1.015)
  local copies, waits for them, and re-layouts: 1.86 us -> 3.81 us
where the time goes in v17:
time: 137 us
  starting transfers between devices  55 us (40%)
  waiting for transfers between devices  54.4 us (40%)
  Pallas kernels  13.2 us (10%)
  other arithmetic  9.19 us (7%)
  local copies, waits for them, and re-layouts  3.81 us (3%)
    ppermute x7, waiting for transfers between devices, exchange(): lax.ppermute(pack(gains, states), axis, [(i, i ^ mask) for i in range(cou...  35.7 us
    ppermute x7, starting transfers between devices, exchange(): lax.ppermute(pack(gains, states), axis, [(i, i ^ mask) for i in range(cou...  31.4 us
    ppermute x3, starting transfers between devices, dp_sum(): lax.ppermute(lax.dynamic_index_in_dim(terms, place ^ k, 0, False), axis,...  9.82 us
    ppermute x3, starting transfers between devices, dp_sum(): lax.ppermute(total, axis, pairs(k))  9.82 us
    ppermute x2, waiting for transfers between devices, passed_along(): return lax.ppermute(block, axis, route)  8.03 us
    pallas_call x2, Pallas kernels, back_block(): pl.pallas_call(functools.partial(back_kernel, step_size), out_shape=(jax....  7.49 us
    ppermute x3, waiting for transfers between devices, dp_sum(): lax.ppermute(lax.dynamic_index_in_dim(terms, place ^ k, 0, False), axis,...  5.79 us
    pallas_call x2, Pallas kernels, run_block(): pl.pallas_call(functools.partial(block_kernel, step_size), out_shape=(jax...  5.66 us
  transfers between devices with their start and end apart: 15, of which 14 were waited for; matrix products, arithmetic and copies ran while one was open for 3% of the time, Pallas kernels for 0%

profile of v17, /device:TPU:96, one launch (start us, length us, event | category | flops | bytes accessed | tf_op | source)
XLA Modules:
  0.0 136.8 jit_solution(6630930981445225684)
XLA Ops:
  0.6 2.8 %shard_map.67 = (f32[64,256]{1,0:T(8,128)}, f32[4,64,256]{2,1,0:T(8,128)}) custom-call(f32[64,256]{1,0:T(8,128)} %bitcast.289, bf16[4,64,576]{2,1,0:T(8,128)(2,1)} %weight_ref.3), custom_call_target="tpu_custom_call" | custom-call | flops 75497472 | bytes 688128 | tf_op jit(solution)/shard_map/pallas_call | solution.py:150
  3.5 2.0 %collective-permute-start = (f32[1,64,256]{2,1,0:T(8,128)}, f32[1,64,256]{2,1,0:T(8,128)S(1)}, u32[]{:S(2)}, u32[]{:S(2)}) collective-permute-start(f32[1,64,256]{2,1,0:T(8,128)} %bitcast.322), channel_id=1, source_target_pairs={{0,4},{4,8},{8,12},{12,16},{16,20},{20,24},{24,28},{28,32},{32,36}... | collective-permute-start | bytes 196616 | tf_op jit(solution)/shard_map/ppermute | solution.py:69
  5.6 0.0 copy-start.2
  5.6 0.1 broadcast_multiply_fusion
  5.7 5.9 %collective-permute-done = f32[1,64,256]{2,1,0:T(8,128)S(1)} collective-permute-done((f32[1,64,256]{2,1,0:T(8,128)}, f32[1,64,256]{2,1,0:T(8,128)S(1)}, u32[]{:S(2)}, u32[]{:S(2)}) %collective-permute-start) | collective-permute-done | bytes 65568 | tf_op jit(solution)/shard_map/ppermute | solution.py:69
  11.5 0.6 fusion.13.state_ref
  12.2 2.8 %shard_map.68 = (f32[64,256]{1,0:T(8,128)}, f32[4,64,256]{2,1,0:T(8,128)}) custom-call(f32[64,256]{1,0:T(8,128)} %fusion.13.state_ref, bf16[4,64,576]{2,1,0:T(8,128)(2,1)} %weight_ref.3), custom_call_target="tpu_custom_call" | custom-call | flops 75497472 | bytes 688128 | tf_op jit(solution)/shard_map/pallas_call | solution.py:150
  15.0 0.9 bitcast_subtract_fusion.1
  15.9 1.9 %collective-permute-start.1 = (f32[130,256]{1,0:T(8,128)S(1)}, f32[130,256]{1,0:T(8,128)S(1)}, u32[]{:S(2)}, u32[]{:S(2)}) collective-permute-start(f32[130,256]{1,0:T(8,128)S(1)} %pad_maximum_fusion.1), channel_id=1, source_target_pairs={{0,4},{4,0},{8,12},{12,8},{16,20},{20,16},{24,28},{28,24},{32,36},... | collective-permute-start | bytes 399368 | tf_op jit(solution)/shard_map/ppermute | solution.py:24
  17.9 1.3 collective-permute-done.1
  19.2 0.1 add_select_fusion.17
  19.3 0.1 fusion.27
  19.5 1.9 %collective-permute-start.2 = (f32[130,256]{1,0:T(8,128)S(1)}, f32[130,256]{1,0:T(8,128)S(1)}, u32[]{:S(2)}, u32[]{:S(2)}) collective-permute-start(f32[130,256]{1,0:T(8,128)S(1)} %pad_maximum_fusion.2), channel_id=1, source_target_pairs={{0,8},{4,12},{8,0},{12,4},{16,24},{20,28},{24,16},{28,20},{32,40},... | collective-permute-start | bytes 399368 | tf_op jit(solution)/shard_map/ppermute | solution.py:24
  21.4 5.7 %collective-permute-done.2 = f32[130,256]{1,0:T(8,128)S(1)} collective-permute-done((f32[130,256]{1,0:T(8,128)S(1)}, f32[130,256]{1,0:T(8,128)S(1)}, u32[]{:S(2)}, u32[]{:S(2)}) %collective-permute-start.2) | collective-permute-done | bytes 133152 | tf_op jit(solution)/shard_map/ppermute | solution.py:24
  27.1 0.1 fusion.25
  27.2 0.1 fusion.11
  27.3 3.3 %collective-permute-start.3 = (f32[130,256]{1,0:T(8,128)S(1)}, f32[130,256]{1,0:T(8,128)S(1)}, u32[]{:S(2)}, u32[]{:S(2)}) collective-permute-start(f32[130,256]{1,0:T(8,128)S(1)} %pad_maximum_fusion.3), channel_id=1, source_target_pairs={{0,24},{4,28},{8,16},{12,20},{16,8},{20,12},{24,0},{28,4},{32,56},... | collective-permute-start | bytes 399368 | tf_op jit(solution)/shard_map/ppermute | solution.py:24
  30.7 4.8 %collective-permute-done.3 = f32[130,256]{1,0:T(8,128)S(1)} collective-permute-done((f32[130,256]{1,0:T(8,128)S(1)}, f32[130,256]{1,0:T(8,128)S(1)}, u32[]{:S(2)}, u32[]{:S(2)}) %collective-permute-start.3) | collective-permute-done | bytes 133152 | tf_op jit(solution)/shard_map/ppermute | solution.py:24
  35.5 0.1 add_select_fusion.15
  35.7 0.1 fusion.28
  35.8 0.0 copy-start.4
  35.8 2.1 %collective-permute-start.4 = (f32[130,256]{1,0:T(8,128)S(1)}, f32[130,256]{1,0:T(8,128)S(1)}, u32[]{:S(2)}, u32[]{:S(2)}) collective-permute-start(f32[130,256]{1,0:T(8,128)S(1)} %pad_maximum_fusion.4), channel_id=1, source_target_pairs={{0,32},{4,36},{8,40},{12,44},{16,48},{20,52},{24,56},{28,60},{32,0... | collective-permute-start | bytes 399368 | tf_op jit(solution)/shard_map/ppermute | solution.py:24
  38.0 4.9 %collective-permute-done.4 = f32[130,256]{1,0:T(8,128)S(1)} collective-permute-done((f32[130,256]{1,0:T(8,128)S(1)}, f32[130,256]{1,0:T(8,128)S(1)}, u32[]{:S(2)}, u32[]{:S(2)}) %collective-permute-start.4) | collective-permute-done | bytes 133152 | tf_op jit(solution)/shard_map/ppermute | solution.py:24
  42.9 0.1 fusion.26
  43.0 0.1 fusion.9
  43.2 1.9 %collective-permute-start.5 = (f32[130,256]{1,0:T(8,128)S(1)}, f32[130,256]{1,0:T(8,128)S(1)}, u32[]{:S(2)}, u32[]{:S(2)}) collective-permute-start(f32[130,256]{1,0:T(8,128)S(1)} %pad_maximum_fusion.5), channel_id=1, source_target_pairs={{0,64},{4,68},{8,72},{12,76},{16,80},{20,84},{24,88},{28,92},{32,9... | collective-permute-start | bytes 399368 | tf_op jit(solution)/shard_map/ppermute | solution.py:24
  45.1 6.9 %collective-permute-done.5 = f32[130,256]{1,0:T(8,128)S(1)} collective-permute-done((f32[130,256]{1,0:T(8,128)S(1)}, f32[130,256]{1,0:T(8,128)S(1)}, u32[]{:S(2)}, u32[]{:S(2)}) %collective-permute-start.5) | collective-permute-done | bytes 133152 | tf_op jit(solution)/shard_map/ppermute | solution.py:24
  52.1 0.1 add_select_fusion.13
  52.2 0.1 fusion.29
  52.3 0.0 copy-start
  52.3 9.2 %collective-permute-start.6 = (f32[130,256]{1,0:T(8,128)S(1)}, f32[130,256]{1,0:T(8,128)S(1)}, u32[]{:S(2)}, u32[]{:S(2)}) collective-permute-start(f32[130,256]{1,0:T(8,128)S(1)} %pad_maximum_fusion.6), channel_id=1, source_target_pairs={{0,128},{4,132},{8,136},{12,140},{16,144},{20,148},{24,152},{28,15... | collective-permute-start | bytes 399368 | tf_op jit(solution)/shard_map/ppermute | solution.py:24
  61.6 1.1 copy.8
  62.7 0.7 maximum_bitcast_fusion.kept_ref
  63.4 4.8 %collective-permute-done.6 = f32[130,256]{1,0:T(8,128)S(1)} collective-permute-done((f32[130,256]{1,0:T(8,128)S(1)}, f32[130,256]{1,0:T(8,128)S(1)}, u32[]{:S(2)}, u32[]{:S(2)}) %collective-permute-start.6) | collective-permute-done | bytes 133152 | tf_op jit(solution)/shard_map/ppermute | solution.py:24
  68.3 0.1 select_bitcast_fusion
  68.4 0.1 fusion.7
  68.6 10.9 %collective-permute-start.7 = (f32[130,256]{1,0:T(8,128)S(1)}, f32[130,256]{1,0:T(8,128)S(1)}, u32[]{:S(2)}, u32[]{:S(2)}) collective-permute-start(f32[130,256]{1,0:T(8,128)S(1)} %pad_maximum_fusion.7), channel_id=1, source_target_pairs={{0,384},{4,388},{8,392},{12,396},{16,400},{20,404},{24,408},{28,41... | collective-permute-start | bytes 399368 | tf_op jit(solution)/shard_map/ppermute | solution.py:24
  79.5 0.7 maximum_bitcast_fusion.1.kept_ref
  80.2 7.2 %collective-permute-done.7 = f32[130,256]{1,0:T(8,128)S(1)} collective-permute-done((f32[130,256]{1,0:T(8,128)S(1)}, f32[130,256]{1,0:T(8,128)S(1)}, u32[]{:S(2)}, u32[]{:S(2)}) %collective-permute-start.7) | collective-permute-done | bytes 133152 | tf_op jit(solution)/shard_map/ppermute | solution.py:24
  87.5 0.8 bitcast_add_fusion.11
  88.2 0.9 broadcast_in_dim.77.earlier_ref
  89.1 3.8 %shard_map.69 = (f32[64,256]{1,0:T(8,128)}, f32[4,64,576]{2,1,0:T(8,128)}) custom-call(f32[4,64,256]{2,1,0:T(8,128)} %maximum_bitcast_fusion.1.kept_ref, bf16[4,576,64]{2,1,0:T(8,128)(2,1)} %bitcast.281, f32[64,256]{1,0:T(8,128)} %get-tuple-element.19.upstream_ref, f32[4,64,576]{2,1,0:T(8,128)} %broadcast_in_dim.77.earlier_ref), custom_call_target="tpu_custom_call" | custom-call | flops 150994944 | bytes 1277952 | tf_op jit(solution)/shard_map/pallas_call | solution.py:174
  92.9 1.9 %collective-permute-start.8 = (f32[1,64,256]{2,1,0:T(8,128)}, f32[1,64,256]{2,1,0:T(8,128)S(1)}, u32[]{:S(2)}, u32[]{:S(2)}) collective-permute-start(f32[1,64,256]{2,1,0:T(8,128)} %bitcast.301), channel_id=1, source_target_pairs={{4,0},{8,4},{12,8},{16,12},{20,16},{24,20},{28,24},{32,28},{36,32}... | collective-permute-start | bytes 196616 | tf_op jit(solution)/shard_map/ppermute | solution.py:69
  94.8 2.2 %collective-permute-done.8 = f32[1,64,256]{2,1,0:T(8,128)S(1)} collective-permute-done((f32[1,64,256]{2,1,0:T(8,128)}, f32[1,64,256]{2,1,0:T(8,128)S(1)}, u32[]{:S(2)}, u32[]{:S(2)}) %collective-permute-start.8) | collective-permute-done | bytes 65568 | tf_op jit(solution)/shard_map/ppermute | solution.py:69
  97.0 0.6 fusion.5.upstream_ref
  97.6 3.7 %shard_map.70 = (f32[64,256]{1,0:T(8,128)}, f32[4,64,576]{2,1,0:T(8,128)}) custom-call(f32[4,64,256]{2,1,0:T(8,128)} %maximum_bitcast_fusion.kept_ref, bf16[4,576,64]{2,1,0:T(8,128)(2,1)} %bitcast.282, f32[64,256]{1,0:T(8,128)} %fusion.5.upstream_ref, f32[4,64,576]{2,1,0:T(8,128)} %get-tuple-element.16.earlier_ref), custom_call_target="tpu_custom_call" | custom-call | flops 150994944 | bytes 1277952 | tf_op jit(solution)/shard_map/pallas_call | solution.py:174
  101.4 1.1 dynamic-slice_bitcast_fusion.2
  102.5 4.9 %collective-permute-start.11 = (f32[64,576]{1,0:T(8,128)S(1)}, f32[64,576]{1,0:T(8,128)S(1)}, u32[]{:S(2)}, u32[]{:S(2)}) collective-permute-start(f32[64,576]{1,0:T(8,128)S(1)} %get-tuple-element.34), channel_id=1, source_target_pairs={{0,3},{1,2},{2,1},{3,0},{4,7},{5,6},{6,5},{7,4},{8,11},{9,10},{10,... | collective-permute-start | bytes 442376 | tf_op jit(solution)/shard_map/ppermute | solution.py:56
  107.4 2.5 %collective-permute-start.10 = (f32[64,576]{1,0:T(8,128)S(1)}, f32[64,576]{1,0:T(8,128)S(1)}, u32[]{:S(2)}, u32[]{:S(2)}) collective-permute-start(f32[64,576]{1,0:T(8,128)S(1)} %get-tuple-element.35), channel_id=1, source_target_pairs={{0,2},{1,3},{2,0},{3,1},{4,6},{5,7},{6,4},{7,5},{8,10},{9,11},{10,... | collective-permute-start | bytes 442376 | tf_op jit(solution)/shard_map/ppermute | solution.py:56
  109.9 2.4 %collective-permute-start.9 = (f32[64,576]{1,0:T(8,128)S(1)}, f32[64,576]{1,0:T(8,128)S(1)}, u32[]{:S(2)}, u32[]{:S(2)}) collective-permute-start(f32[64,576]{1,0:T(8,128)S(1)} %get-tuple-element.33), channel_id=1, source_target_pairs={{0,1},{1,0},{2,3},{3,2},{4,5},{5,4},{6,7},{7,6},{8,9},{9,8},{10,11... | collective-permute-start | bytes 442376 | tf_op jit(solution)/shard_map/ppermute | solution.py:56
  112.3 0.8 fusion.2
  113.1 0.0 collective-permute-done.11
  113.1 4.4 %collective-permute-done.10 = f32[64,576]{1,0:T(8,128)S(1)} collective-permute-done((f32[64,576]{1,0:T(8,128)S(1)}, f32[64,576]{1,0:T(8,128)S(1)}, u32[]{:S(2)}, u32[]{:S(2)}) %collective-permute-start.10) | collective-permute-done | bytes 147488 | tf_op jit(solution)/shard_map/ppermute | solution.py:56
  117.5 1.4 %collective-permute-done.9 = f32[64,576]{1,0:T(8,128)S(1)} collective-permute-done((f32[64,576]{1,0:T(8,128)S(1)}, f32[64,576]{1,0:T(8,128)S(1)}, u32[]{:S(2)}, u32[]{:S(2)}) %collective-permute-start.9) | collective-permute-done | bytes 147488 | tf_op jit(solution)/shard_map/ppermute | solution.py:56
  118.9 1.0 fusion.1
  119.8 4.6 %collective-permute-start.14 = (f32[64,576]{1,0:T(8,128)S(1)}, f32[64,576]{1,0:T(8,128)S(1)}, u32[]{:S(2)}, u32[]{:S(2)}) collective-permute-start(f32[64,576]{1,0:T(8,128)S(1)} %fusion.1), channel_id=1, source_target_pairs={{0,3},{1,2},{2,1},{3,0},{4,7},{5,6},{6,5},{7,4},{8,11},{9,10},{10,... | collective-permute-start | bytes 442376 | tf_op jit(solution)/shard_map/ppermute | solution.py:62
  124.4 2.5 %collective-permute-start.13 = (f32[64,576]{1,0:T(8,128)S(1)}, f32[64,576]{1,0:T(8,128)S(1)}, u32[]{:S(2)}, u32[]{:S(2)}) collective-permute-start(f32[64,576]{1,0:T(8,128)S(1)} %fusion.1), channel_id=1, source_target_pairs={{0,2},{1,3},{2,0},{3,1},{4,6},{5,7},{6,4},{7,5},{8,10},{9,11},{10,... | collective-permute-start | bytes 442376 | tf_op jit(solution)/shard_map/ppermute | solution.py:62
  127.0 2.7 %collective-permute-start.12 = (f32[64,576]{1,0:T(8,128)S(1)}, f32[64,576]{1,0:T(8,128)S(1)}, u32[]{:S(2)}, u32[]{:S(2)}) collective-permute-start(f32[64,576]{1,0:T(8,128)S(1)} %fusion.1), channel_id=1, source_target_pairs={{0,1},{1,0},{2,3},{3,2},{4,5},{5,4},{6,7},{7,6},{8,9},{9,8},{10,11... | collective-permute-start | bytes 442376 | tf_op jit(solution)/shard_map/ppermute | solution.py:62
  129.7 0.6 fusion.3
  130.3 1.4 %collective-permute-done.14 = f32[64,576]{1,0:T(8,128)S(1)} collective-permute-done((f32[64,576]{1,0:T(8,128)S(1)}, f32[64,576]{1,0:T(8,128)S(1)}, u32[]{:S(2)}, u32[]{:S(2)}) %collective-permute-start.14) | collective-permute-done | bytes 147488 | tf_op jit(solution)/shard_map/ppermute | solution.py:62
  131.8 3.1 %collective-permute-done.13 = f32[64,576]{1,0:T(8,128)S(1)} collective-permute-done((f32[64,576]{1,0:T(8,128)S(1)}, f32[64,576]{1,0:T(8,128)S(1)}, u32[]{:S(2)}, u32[]{:S(2)}) %collective-permute-start.13) | collective-permute-done | bytes 147488 | tf_op jit(solution)/shard_map/ppermute | solution.py:62
  134.9 0.3 collective-permute-done.12
  135.3 0.6 gather_fusion
  135.9 0.9 broadcast_select_fusion
  (59 shorter events, 0.4 us)
Async XLA Ops:
  0.6 4.9 %copy-start.1 = (f32[1,1,64,256]{3,2,1,0:T(8,128)S(1)}, f32[1,1,64,256]{3,2,1,0:T(8,128)}, u32[]{:S(2)}) copy-start(f32[1,1,64,256]{3,2,1,0:T(8,128)} %param.7) | copy-start | bytes 196612
  3.5 2.1 %copy-start.7 = (f32[1,64]{1,0:T(1,128)S(1)}, f32[1,64]{1,0:T(1,128)}, u32[]{:S(2)}) copy-start(f32[1,64]{1,0:T(1,128)} %param.6) | copy-start | bytes 772
  3.5 8.0 %collective-permute-start = (f32[1,64,256]{2,1,0:T(8,128)}, f32[1,64,256]{2,1,0:T(8,128)S(1)}, u32[]{:S(2)}, u32[]{:S(2)}) collective-permute-start(f32[1,64,256]{2,1,0:T(8,128)} %bitcast.322), channel_id=1, source_target_pairs={{0,4},{4,8},{8,12},{12,16},{16,20},{20,24},{24,28},{28,32},{32,36}... | collective-permute-start | bytes 196616 | tf_op jit(solution)/shard_map/ppermute | solution.py:69
  5.6 6.0 %copy-start.2 = (f32[1,1,64,256]{3,2,1,0:T(8,128)S(1)}, f32[1,1,64,256]{3,2,1,0:T(8,128)}, u32[]{:S(2)}) copy-start(f32[1,1,64,256]{3,2,1,0:T(8,128)} %param.4) | copy-start | bytes 196612
  15.9 3.3 %collective-permute-start.1 = (f32[130,256]{1,0:T(8,128)S(1)}, f32[130,256]{1,0:T(8,128)S(1)}, u32[]{:S(2)}, u32[]{:S(2)}) collective-permute-start(f32[130,256]{1,0:T(8,128)S(1)} %pad_maximum_fusion.1), channel_id=1, source_target_pairs={{0,4},{4,0},{8,12},{12,8},{16,20},{20,16},{24,28},{28,24},{32,36},... | collective-permute-start | bytes 399368 | tf_op jit(solution)/shard_map/ppermute | solution.py:24
  19.5 7.6 %collective-permute-start.2 = (f32[130,256]{1,0:T(8,128)S(1)}, f32[130,256]{1,0:T(8,128)S(1)}, u32[]{:S(2)}, u32[]{:S(2)}) collective-permute-start(f32[130,256]{1,0:T(8,128)S(1)} %pad_maximum_fusion.2), channel_id=1, source_target_pairs={{0,8},{4,12},{8,0},{12,4},{16,24},{20,28},{24,16},{28,20},{32,40},... | collective-permute-start | bytes 399368 | tf_op jit(solution)/shard_map/ppermute | solution.py:24
  27.3 8.2 %collective-permute-start.3 = (f32[130,256]{1,0:T(8,128)S(1)}, f32[130,256]{1,0:T(8,128)S(1)}, u32[]{:S(2)}, u32[]{:S(2)}) collective-permute-start(f32[130,256]{1,0:T(8,128)S(1)} %pad_maximum_fusion.3), channel_id=1, source_target_pairs={{0,24},{4,28},{8,16},{12,20},{16,8},{20,12},{24,0},{28,4},{32,56},... | collective-permute-start | bytes 399368 | tf_op jit(solution)/shard_map/ppermute | solution.py:24
  35.8 2.2 %copy-start.4 = (f32[4,64,256]{2,1,0:T(8,128)S(1)}, f32[4,64,256]{2,1,0:T(8,128)}, u32[]{:S(2)}) copy-start(f32[4,64,256]{2,1,0:T(8,128)} %get-tuple-element.13) | copy-start | bytes 786436
  35.8 7.1 %collective-permute-start.4 = (f32[130,256]{1,0:T(8,128)S(1)}, f32[130,256]{1,0:T(8,128)S(1)}, u32[]{:S(2)}, u32[]{:S(2)}) collective-permute-start(f32[130,256]{1,0:T(8,128)S(1)} %pad_maximum_fusion.4), channel_id=1, source_target_pairs={{0,32},{4,36},{8,40},{12,44},{16,48},{20,52},{24,56},{28,60},{32,0... | collective-permute-start | bytes 399368 | tf_op jit(solution)/shard_map/ppermute | solution.py:24
  43.2 8.9 %collective-permute-start.5 = (f32[130,256]{1,0:T(8,128)S(1)}, f32[130,256]{1,0:T(8,128)S(1)}, u32[]{:S(2)}, u32[]{:S(2)}) collective-permute-start(f32[130,256]{1,0:T(8,128)S(1)} %pad_maximum_fusion.5), channel_id=1, source_target_pairs={{0,64},{4,68},{8,72},{12,76},{16,80},{20,84},{24,88},{28,92},{32,9... | collective-permute-start | bytes 399368 | tf_op jit(solution)/shard_map/ppermute | solution.py:24
  52.3 9.3 %copy-start = (bf16[4,64,576]{2,1,0:T(8,128)(2,1)S(1)}, bf16[4,64,576]{2,1,0:T(8,128)(2,1)}, u32[]{:S(2)}) copy-start(bf16[4,64,576]{2,1,0:T(8,128)(2,1)} %weight_ref.3) | copy-start | bytes 884740
  52.3 15.9 %collective-permute-start.6 = (f32[130,256]{1,0:T(8,128)S(1)}, f32[130,256]{1,0:T(8,128)S(1)}, u32[]{:S(2)}, u32[]{:S(2)}) collective-permute-start(f32[130,256]{1,0:T(8,128)S(1)} %pad_maximum_fusion.6), channel_id=1, source_target_pairs={{0,128},{4,132},{8,136},{12,140},{16,144},{20,148},{24,152},{28,15... | collective-permute-start | bytes 399368 | tf_op jit(solution)/shard_map/ppermute | solution.py:24
  68.5 11.0 %copy-start.3 = (f32[4,64,256]{2,1,0:T(8,128)S(1)}, f32[4,64,256]{2,1,0:T(8,128)}, u32[]{:S(2)}) copy-start(f32[4,64,256]{2,1,0:T(8,128)} %get-tuple-element.14) | copy-start | bytes 786436
  68.6 18.9 %collective-permute-start.7 = (f32[130,256]{1,0:T(8,128)S(1)}, f32[130,256]{1,0:T(8,128)S(1)}, u32[]{:S(2)}, u32[]{:S(2)}) collective-permute-start(f32[130,256]{1,0:T(8,128)S(1)} %pad_maximum_fusion.7), channel_id=1, source_target_pairs={{0,384},{4,388},{8,392},{12,396},{16,400},{20,404},{24,408},{28,41... | collective-permute-start | bytes 399368 | tf_op jit(solution)/shard_map/ppermute | solution.py:24
  92.9 4.1 %collective-permute-start.8 = (f32[1,64,256]{2,1,0:T(8,128)}, f32[1,64,256]{2,1,0:T(8,128)S(1)}, u32[]{:S(2)}, u32[]{:S(2)}) collective-permute-start(f32[1,64,256]{2,1,0:T(8,128)} %bitcast.301), channel_id=1, source_target_pairs={{4,0},{8,4},{12,8},{16,12},{20,16},{24,20},{28,24},{32,28},{36,32}... | collective-permute-start | bytes 196616 | tf_op jit(solution)/shard_map/ppermute | solution.py:69
  102.5 10.6 %collective-permute-start.11 = (f32[64,576]{1,0:T(8,128)S(1)}, f32[64,576]{1,0:T(8,128)S(1)}, u32[]{:S(2)}, u32[]{:S(2)}) collective-permute-start(f32[64,576]{1,0:T(8,128)S(1)} %get-tuple-element.34), channel_id=1, source_target_pairs={{0,3},{1,2},{2,1},{3,0},{4,7},{5,6},{6,5},{7,4},{8,11},{9,10},{10,... | collective-permute-start | bytes 442376 | tf_op jit(solution)/shard_map/ppermute | solution.py:56
  107.4 10.1 %collective-permute-start.10 = (f32[64,576]{1,0:T(8,128)S(1)}, f32[64,576]{1,0:T(8,128)S(1)}, u32[]{:S(2)}, u32[]{:S(2)}) collective-permute-start(f32[64,576]{1,0:T(8,128)S(1)} %get-tuple-element.35), channel_id=1, source_target_pairs={{0,2},{1,3},{2,0},{3,1},{4,6},{5,7},{6,4},{7,5},{8,10},{9,11},{10,... | collective-permute-start | bytes 442376 | tf_op jit(solution)/shard_map/ppermute | solution.py:56
  109.9 8.9 %collective-permute-start.9 = (f32[64,576]{1,0:T(8,128)S(1)}, f32[64,576]{1,0:T(8,128)S(1)}, u32[]{:S(2)}, u32[]{:S(2)}) collective-permute-start(f32[64,576]{1,0:T(8,128)S(1)} %get-tuple-element.33), channel_id=1, source_target_pairs={{0,1},{1,0},{2,3},{3,2},{4,5},{5,4},{6,7},{7,6},{8,9},{9,8},{10,11... | collective-permute-start | bytes 442376 | tf_op jit(solution)/shard_map/ppermute | solution.py:56
  113.1 16.6 %copy-start.5 = (f32[64,256]{1,0:T(8,128)S(1)}, f32[64,256]{1,0:T(8,128)}, u32[]{:S(2)}) copy-start(f32[64,256]{1,0:T(8,128)} %get-tuple-element.15) | copy-start | bytes 196612
  113.1 16.6 %copy-start.6 = (f32[64,256]{1,0:T(8,128)S(1)}, f32[64,256]{1,0:T(8,128)}, u32[]{:S(2)}) copy-start(f32[64,256]{1,0:T(8,128)} %get-tuple-element.17) | copy-start | bytes 196612
  119.8 11.9 %collective-permute-start.14 = (f32[64,576]{1,0:T(8,128)S(1)}, f32[64,576]{1,0:T(8,128)S(1)}, u32[]{:S(2)}, u32[]{:S(2)}) collective-permute-start(f32[64,576]{1,0:T(8,128)S(1)} %fusion.1), channel_id=1, source_target_pairs={{0,3},{1,2},{2,1},{3,0},{4,7},{5,6},{6,5},{7,4},{8,11},{9,10},{10,... | collective-permute-start | bytes 442376 | tf_op jit(solution)/shard_map/ppermute | solution.py:62
  124.4 10.5 %collective-permute-start.13 = (f32[64,576]{1,0:T(8,128)S(1)}, f32[64,576]{1,0:T(8,128)S(1)}, u32[]{:S(2)}, u32[]{:S(2)}) collective-permute-start(f32[64,576]{1,0:T(8,128)S(1)} %fusion.1), channel_id=1, source_target_pairs={{0,2},{1,3},{2,0},{3,1},{4,6},{5,7},{6,4},{7,5},{8,10},{9,11},{10,... | collective-permute-start | bytes 442376 | tf_op jit(solution)/shard_map/ppermute | solution.py:62
  127.0 8.2 %collective-permute-start.12 = (f32[64,576]{1,0:T(8,128)S(1)}, f32[64,576]{1,0:T(8,128)S(1)}, u32[]{:S(2)}, u32[]{:S(2)}) collective-permute-start(f32[64,576]{1,0:T(8,128)S(1)} %fusion.1), channel_id=1, source_target_pairs={{0,1},{1,0},{2,3},{3,2},{4,5},{5,4},{6,7},{7,6},{8,9},{9,8},{10,11... | collective-permute-start | bytes 442376 | tf_op jit(solution)/shard_map/ppermute | solution.py:62

commit v18 on v14

--- a/solution.py
+++ b/solution.py
@@ -161,7 +161,7 @@
             bytes_accessed=4 * (layers + 2) * channels * pixels + 2 * block_weights.size,
         ),
     )(current.reshape(channels, pixels), block_weights)
-    return (out.reshape(current.shape), [kept[k].reshape(current.shape) for k in range(layers)])
+    return (out.reshape(current.shape), kept)
 
 
 def back_block(inputs_kept, block_weights, upstream, step_size):
@@ -182,7 +182,7 @@
             transcendentals=layers * channels * pixels,
             bytes_accessed=4 * (layers + 2) * channels * pixels + 2 * block_weights.size + 4 * layers * channels * taps,
         ),
-    )(jnp.stack(inputs_kept).reshape(layers, channels, pixels), flipped, upstream.reshape(channels, pixels))
+    )(inputs_kept, flipped, upstream.reshape(channels, pixels))
     return (out.reshape(upstream.shape), grads)
 
 

time: 135 us -> 135 us (level)
  other arithmetic: 9.48 us -> 8.03 us
  waiting for transfers between devices: 54.4 us -> 55.8 us
    ppermute x7, waiting for transfers between devices: 35.7 us -> 37.1 us  [exchange(): lax.ppermute(pack(gains, states), axis, [(i, i ^ mask) for i in range(cou...]
    reshape x2 -> x0, other arithmetic: 1.45 us -> none  [back_block(): jnp.stack(inputs_kept).reshape(layers, channels, pixels)]
  transfers between devices with their start and end apart: 15 -> 15, of which waited for: 14 -> 14; matrix products, arithmetic and copies ran while one was open for 3% -> 2% of each run, Pallas kernels for 0% -> 0%
where the time goes in v18:
time: 135 us
  waiting for transfers between devices  55.8 us (41%)
  starting transfers between devices  54.9 us (41%)
  Pallas kernels  12.7 us (9%)
  other arithmetic  8.03 us (6%)
  local copies, waits for them, and re-layouts  1.83 us (1%)
    ppermute x7, waiting for transfers between devices, exchange(): lax.ppermute(pack(gains, states), axis, [(i, i ^ mask) for i in range(cou...  37.1 us
    ppermute x7, starting transfers between devices, exchange(): lax.ppermute(pack(gains, states), axis, [(i, i ^ mask) for i in range(cou...  31.2 us
    ppermute x3, starting transfers between devices, dp_sum(): lax.ppermute(lax.dynamic_index_in_dim(terms, place ^ k, 0, False), axis,...  9.82 us
    ppermute x3, starting transfers between devices, dp_sum(): lax.ppermute(total, axis, pairs(k))  9.81 us
    ppermute x2, waiting for transfers between devices, passed_along(): return lax.ppermute(block, axis, route)  8.03 us
    pallas_call x2, Pallas kernels, back_block(): pl.pallas_call(functools.partial(back_kernel, step_size), out_shape=(jax....  7.05 us
    ppermute x3, waiting for transfers between devices, dp_sum(): lax.ppermute(lax.dynamic_index_in_dim(terms, place ^ k, 0, False), axis,...  5.79 us
    pallas_call x2, Pallas kernels, run_block(): pl.pallas_call(functools.partial(block_kernel, step_size), out_shape=(jax...  5.66 us
  transfers between devices with their start and end apart: 15, of which 14 were waited for; matrix products, arithmetic and copies ran while one was open for 2% of the time, Pallas kernels for 0%

profile of v18, /device:TPU:96, one launch (start us, length us, event | category | flops | bytes accessed | tf_op | source)
XLA Modules:
  0.0 134.6 jit_solution(5921304558892804065)
XLA Ops:
  0.6 0.0 copy-start.2
  0.6 2.8 %shard_map.67 = (f32[64,256]{1,0:T(8,128)}, f32[4,64,256]{2,1,0:T(8,128)}) custom-call(f32[64,256]{1,0:T(8,128)} %bitcast.269, bf16[4,64,576]{2,1,0:T(8,128)(2,1)} %weight_ref.3), custom_call_target="tpu_custom_call" | custom-call | flops 75497472 | bytes 688128 | tf_op jit(solution)/shard_map/pallas_call | solution.py:150
  3.5 2.0 %collective-permute-start = (f32[1,64,256]{2,1,0:T(8,128)}, f32[1,64,256]{2,1,0:T(8,128)S(1)}, u32[]{:S(2)}, u32[]{:S(2)}) collective-permute-start(f32[1,64,256]{2,1,0:T(8,128)} %bitcast.302), channel_id=1, source_target_pairs={{0,4},{4,8},{8,12},{12,16},{16,20},{20,24},{24,28},{28,32},{32,36}... | collective-permute-start | bytes 196616 | tf_op jit(solution)/shard_map/ppermute | solution.py:69
  5.5 0.0 copy-done.2
  5.5 0.0 copy-done.6
  5.6 0.0 copy-start.3
  5.6 0.1 broadcast_multiply_fusion
  5.7 5.9 %collective-permute-done = f32[1,64,256]{2,1,0:T(8,128)S(1)} collective-permute-done((f32[1,64,256]{2,1,0:T(8,128)}, f32[1,64,256]{2,1,0:T(8,128)S(1)}, u32[]{:S(2)}, u32[]{:S(2)}) %collective-permute-start) | collective-permute-done | bytes 65568 | tf_op jit(solution)/shard_map/ppermute | solution.py:69
  11.5 0.6 fusion.13.state_ref
  12.2 2.8 %shard_map.68 = (f32[64,256]{1,0:T(8,128)}, f32[4,64,256]{2,1,0:T(8,128)}) custom-call(f32[64,256]{1,0:T(8,128)} %fusion.13.state_ref, bf16[4,64,576]{2,1,0:T(8,128)(2,1)} %weight_ref.3), custom_call_target="tpu_custom_call" | custom-call | flops 75497472 | bytes 688128 | tf_op jit(solution)/shard_map/pallas_call | solution.py:150
  15.0 0.9 bitcast_subtract_fusion.1
  15.9 1.9 %collective-permute-start.1 = (f32[130,256]{1,0:T(8,128)S(1)}, f32[130,256]{1,0:T(8,128)S(1)}, u32[]{:S(2)}, u32[]{:S(2)}) collective-permute-start(f32[130,256]{1,0:T(8,128)S(1)} %pad_maximum_fusion.1), channel_id=1, source_target_pairs={{0,4},{4,0},{8,12},{12,8},{16,20},{20,16},{24,28},{28,24},{32,36},... | collective-permute-start | bytes 399368 | tf_op jit(solution)/shard_map/ppermute | solution.py:24
  17.9 1.3 collective-permute-done.1
  19.2 0.1 add_select_fusion.17
  19.3 0.1 fusion.27
  19.5 1.9 %collective-permute-start.2 = (f32[130,256]{1,0:T(8,128)S(1)}, f32[130,256]{1,0:T(8,128)S(1)}, u32[]{:S(2)}, u32[]{:S(2)}) collective-permute-start(f32[130,256]{1,0:T(8,128)S(1)} %pad_maximum_fusion.2), channel_id=1, source_target_pairs={{0,8},{4,12},{8,0},{12,4},{16,24},{20,28},{24,16},{28,20},{32,40},... | collective-permute-start | bytes 399368 | tf_op jit(solution)/shard_map/ppermute | solution.py:24
  21.4 5.7 %collective-permute-done.2 = f32[130,256]{1,0:T(8,128)S(1)} collective-permute-done((f32[130,256]{1,0:T(8,128)S(1)}, f32[130,256]{1,0:T(8,128)S(1)}, u32[]{:S(2)}, u32[]{:S(2)}) %collective-permute-start.2) | collective-permute-done | bytes 133152 | tf_op jit(solution)/shard_map/ppermute | solution.py:24
  27.1 0.1 fusion.25
  27.2 0.1 fusion.11
  27.3 3.3 %collective-permute-start.3 = (f32[130,256]{1,0:T(8,128)S(1)}, f32[130,256]{1,0:T(8,128)S(1)}, u32[]{:S(2)}, u32[]{:S(2)}) collective-permute-start(f32[130,256]{1,0:T(8,128)S(1)} %pad_maximum_fusion.3), channel_id=1, source_target_pairs={{0,24},{4,28},{8,16},{12,20},{16,8},{20,12},{24,0},{28,4},{32,56},... | collective-permute-start | bytes 399368 | tf_op jit(solution)/shard_map/ppermute | solution.py:24
  30.7 4.8 %collective-permute-done.3 = f32[130,256]{1,0:T(8,128)S(1)} collective-permute-done((f32[130,256]{1,0:T(8,128)S(1)}, f32[130,256]{1,0:T(8,128)S(1)}, u32[]{:S(2)}, u32[]{:S(2)}) %collective-permute-start.3) | collective-permute-done | bytes 133152 | tf_op jit(solution)/shard_map/ppermute | solution.py:24
  35.5 0.1 add_select_fusion.15
  35.7 0.1 fusion.28
  35.8 2.0 %collective-permute-start.4 = (f32[130,256]{1,0:T(8,128)S(1)}, f32[130,256]{1,0:T(8,128)S(1)}, u32[]{:S(2)}, u32[]{:S(2)}) collective-permute-start(f32[130,256]{1,0:T(8,128)S(1)} %pad_maximum_fusion.4), channel_id=1, source_target_pairs={{0,32},{4,36},{8,40},{12,44},{16,48},{20,52},{24,56},{28,60},{32,0... | collective-permute-start | bytes 399368 | tf_op jit(solution)/shard_map/ppermute | solution.py:24
  37.8 4.9 %collective-permute-done.4 = f32[130,256]{1,0:T(8,128)S(1)} collective-permute-done((f32[130,256]{1,0:T(8,128)S(1)}, f32[130,256]{1,0:T(8,128)S(1)}, u32[]{:S(2)}, u32[]{:S(2)}) %collective-permute-start.4) | collective-permute-done | bytes 133152 | tf_op jit(solution)/shard_map/ppermute | solution.py:24
  42.8 0.1 fusion.26
  42.9 0.1 fusion.9
  43.0 1.9 %collective-permute-start.5 = (f32[130,256]{1,0:T(8,128)S(1)}, f32[130,256]{1,0:T(8,128)S(1)}, u32[]{:S(2)}, u32[]{:S(2)}) collective-permute-start(f32[130,256]{1,0:T(8,128)S(1)} %pad_maximum_fusion.5), channel_id=1, source_target_pairs={{0,64},{4,68},{8,72},{12,76},{16,80},{20,84},{24,88},{28,92},{32,9... | collective-permute-start | bytes 399368 | tf_op jit(solution)/shard_map/ppermute | solution.py:24
  45.0 6.9 %collective-permute-done.5 = f32[130,256]{1,0:T(8,128)S(1)} collective-permute-done((f32[130,256]{1,0:T(8,128)S(1)}, f32[130,256]{1,0:T(8,128)S(1)}, u32[]{:S(2)}, u32[]{:S(2)}) %collective-permute-start.5) | collective-permute-done | bytes 133152 | tf_op jit(solution)/shard_map/ppermute | solution.py:24
  51.9 0.1 add_select_fusion.13
  52.0 0.1 fusion.29
  52.2 9.1 %collective-permute-start.6 = (f32[130,256]{1,0:T(8,128)S(1)}, f32[130,256]{1,0:T(8,128)S(1)}, u32[]{:S(2)}, u32[]{:S(2)}) collective-permute-start(f32[130,256]{1,0:T(8,128)S(1)} %pad_maximum_fusion.6), channel_id=1, source_target_pairs={{0,128},{4,132},{8,136},{12,140},{16,144},{20,148},{24,152},{28,15... | collective-permute-start | bytes 399368 | tf_op jit(solution)/shard_map/ppermute | solution.py:24
  61.3 6.7 %collective-permute-done.6 = f32[130,256]{1,0:T(8,128)S(1)} collective-permute-done((f32[130,256]{1,0:T(8,128)S(1)}, f32[130,256]{1,0:T(8,128)S(1)}, u32[]{:S(2)}, u32[]{:S(2)}) %collective-permute-start.6) | collective-permute-done | bytes 133152 | tf_op jit(solution)/shard_map/ppermute | solution.py:24
  68.0 0.1 select_bitcast_fusion
  68.1 0.1 fusion.7
  68.2 0.0 copy-start
  68.3 11.0 %collective-permute-start.7 = (f32[130,256]{1,0:T(8,128)S(1)}, f32[130,256]{1,0:T(8,128)S(1)}, u32[]{:S(2)}, u32[]{:S(2)}) collective-permute-start(f32[130,256]{1,0:T(8,128)S(1)} %pad_maximum_fusion.7), channel_id=1, source_target_pairs={{0,384},{4,388},{8,392},{12,396},{16,400},{20,404},{24,408},{28,41... | collective-permute-start | bytes 399368 | tf_op jit(solution)/shard_map/ppermute | solution.py:24
  79.3 0.0 copy-done
  79.3 1.1 copy.8
  80.4 6.8 %collective-permute-done.7 = f32[130,256]{1,0:T(8,128)S(1)} collective-permute-done((f32[130,256]{1,0:T(8,128)S(1)}, f32[130,256]{1,0:T(8,128)S(1)}, u32[]{:S(2)}, u32[]{:S(2)}) %collective-permute-start.7) | collective-permute-done | bytes 133152 | tf_op jit(solution)/shard_map/ppermute | solution.py:24
  87.2 0.8 bitcast_add_fusion.11
  87.9 3.5 %shard_map.69 = (f32[64,256]{1,0:T(8,128)}, f32[4,64,576]{2,1,0:T(8,128)}) custom-call(f32[4,64,256]{2,1,0:T(8,128)} %get-tuple-element.14.kept_ref, bf16[4,576,64]{2,1,0:T(8,128)(2,1)} %bitcast.261, f32[64,256]{1,0:T(8,128)} %get-tuple-element.19.upstream_ref), custom_call_target="tpu_custom_call" | custom-call | flops 150994944 | bytes 1277952 | tf_op jit(solution)/shard_map/pallas_call | solution.py:172
  91.4 2.0 %collective-permute-start.8 = (f32[1,64,256]{2,1,0:T(8,128)}, f32[1,64,256]{2,1,0:T(8,128)S(1)}, u32[]{:S(2)}, u32[]{:S(2)}) collective-permute-start(f32[1,64,256]{2,1,0:T(8,128)} %bitcast.281), channel_id=1, source_target_pairs={{4,0},{8,4},{12,8},{16,12},{20,16},{24,20},{28,24},{32,28},{36,32}... | collective-permute-start | bytes 196616 | tf_op jit(solution)/shard_map/ppermute | solution.py:69
  93.5 2.2 %collective-permute-done.8 = f32[1,64,256]{2,1,0:T(8,128)S(1)} collective-permute-done((f32[1,64,256]{2,1,0:T(8,128)}, f32[1,64,256]{2,1,0:T(8,128)S(1)}, u32[]{:S(2)}, u32[]{:S(2)}) %collective-permute-start.8) | collective-permute-done | bytes 65568 | tf_op jit(solution)/shard_map/ppermute | solution.py:69
  95.7 0.6 fusion.5.upstream_ref
  96.3 3.5 %shard_map.70 = (f32[64,256]{1,0:T(8,128)}, f32[4,64,576]{2,1,0:T(8,128)}) custom-call(f32[4,64,256]{2,1,0:T(8,128)} %get-tuple-element.13.kept_ref, bf16[4,576,64]{2,1,0:T(8,128)(2,1)} %bitcast.262, f32[64,256]{1,0:T(8,128)} %fusion.5.upstream_ref), custom_call_target="tpu_custom_call" | custom-call | flops 150994944 | bytes 1277952 | tf_op jit(solution)/shard_map/pallas_call | solution.py:172
  99.9 1.2 add.276
  101.1 4.9 %collective-permute-start.11 = (f32[64,576]{1,0:T(8,128)S(1)}, f32[64,576]{1,0:T(8,128)S(1)}, u32[]{:S(2)}, u32[]{:S(2)}) collective-permute-start(f32[64,576]{1,0:T(8,128)S(1)} %get-tuple-element.34), channel_id=1, source_target_pairs={{0,3},{1,2},{2,1},{3,0},{4,7},{5,6},{6,5},{7,4},{8,11},{9,10},{10,... | collective-permute-start | bytes 442376 | tf_op jit(solution)/shard_map/ppermute | solution.py:56
  106.0 2.5 %collective-permute-start.10 = (f32[64,576]{1,0:T(8,128)S(1)}, f32[64,576]{1,0:T(8,128)S(1)}, u32[]{:S(2)}, u32[]{:S(2)}) collective-permute-start(f32[64,576]{1,0:T(8,128)S(1)} %get-tuple-element.35), channel_id=1, source_target_pairs={{0,2},{1,3},{2,0},{3,1},{4,6},{5,7},{6,4},{7,5},{8,10},{9,11},{10,... | collective-permute-start | bytes 442376 | tf_op jit(solution)/shard_map/ppermute | solution.py:56
  108.6 2.4 %collective-permute-start.9 = (f32[64,576]{1,0:T(8,128)S(1)}, f32[64,576]{1,0:T(8,128)S(1)}, u32[]{:S(2)}, u32[]{:S(2)}) collective-permute-start(f32[64,576]{1,0:T(8,128)S(1)} %get-tuple-element.33), channel_id=1, source_target_pairs={{0,1},{1,0},{2,3},{3,2},{4,5},{5,4},{6,7},{7,6},{8,9},{9,8},{10,11... | collective-permute-start | bytes 442376 | tf_op jit(solution)/shard_map/ppermute | solution.py:56
  111.0 0.8 fusion.2
  111.7 0.0 collective-permute-done.11
  111.7 4.4 %collective-permute-done.10 = f32[64,576]{1,0:T(8,128)S(1)} collective-permute-done((f32[64,576]{1,0:T(8,128)S(1)}, f32[64,576]{1,0:T(8,128)S(1)}, u32[]{:S(2)}, u32[]{:S(2)}) %collective-permute-start.10) | collective-permute-done | bytes 147488 | tf_op jit(solution)/shard_map/ppermute | solution.py:56
  116.1 1.4 %collective-permute-done.9 = f32[64,576]{1,0:T(8,128)S(1)} collective-permute-done((f32[64,576]{1,0:T(8,128)S(1)}, f32[64,576]{1,0:T(8,128)S(1)}, u32[]{:S(2)}, u32[]{:S(2)}) %collective-permute-start.9) | collective-permute-done | bytes 147488 | tf_op jit(solution)/shard_map/ppermute | solution.py:56
  117.5 0.1 fusion.1
  117.6 4.6 %collective-permute-start.14 = (f32[64,576]{1,0:T(8,128)S(1)}, f32[64,576]{1,0:T(8,128)S(1)}, u32[]{:S(2)}, u32[]{:S(2)}) collective-permute-start(f32[64,576]{1,0:T(8,128)S(1)} %fusion.1), channel_id=1, source_target_pairs={{0,3},{1,2},{2,1},{3,0},{4,7},{5,6},{6,5},{7,4},{8,11},{9,10},{10,... | collective-permute-start | bytes 442376 | tf_op jit(solution)/shard_map/ppermute | solution.py:62
  122.2 2.5 %collective-permute-start.13 = (f32[64,576]{1,0:T(8,128)S(1)}, f32[64,576]{1,0:T(8,128)S(1)}, u32[]{:S(2)}, u32[]{:S(2)}) collective-permute-start(f32[64,576]{1,0:T(8,128)S(1)} %fusion.1), channel_id=1, source_target_pairs={{0,2},{1,3},{2,0},{3,1},{4,6},{5,7},{6,4},{7,5},{8,10},{9,11},{10,... | collective-permute-start | bytes 442376 | tf_op jit(solution)/shard_map/ppermute | solution.py:62
  124.7 2.7 %collective-permute-start.12 = (f32[64,576]{1,0:T(8,128)S(1)}, f32[64,576]{1,0:T(8,128)S(1)}, u32[]{:S(2)}, u32[]{:S(2)}) collective-permute-start(f32[64,576]{1,0:T(8,128)S(1)} %fusion.1), channel_id=1, source_target_pairs={{0,1},{1,0},{2,3},{3,2},{4,5},{5,4},{6,7},{7,6},{8,9},{9,8},{10,11... | collective-permute-start | bytes 442376 | tf_op jit(solution)/shard_map/ppermute | solution.py:62
  127.4 0.6 fusion.3
  128.1 1.4 %collective-permute-done.14 = f32[64,576]{1,0:T(8,128)S(1)} collective-permute-done((f32[64,576]{1,0:T(8,128)S(1)}, f32[64,576]{1,0:T(8,128)S(1)}, u32[]{:S(2)}, u32[]{:S(2)}) %collective-permute-start.14) | collective-permute-done | bytes 147488 | tf_op jit(solution)/shard_map/ppermute | solution.py:62
  129.5 3.1 %collective-permute-done.13 = f32[64,576]{1,0:T(8,128)S(1)} collective-permute-done((f32[64,576]{1,0:T(8,128)S(1)}, f32[64,576]{1,0:T(8,128)S(1)}, u32[]{:S(2)}, u32[]{:S(2)}) %collective-permute-start.13) | collective-permute-done | bytes 147488 | tf_op jit(solution)/shard_map/ppermute | solution.py:62
  132.7 0.3 collective-permute-done.12
  133.0 0.6 gather_fusion
  133.6 0.9 broadcast_select_fusion
  (53 shorter events, 0.4 us)
Async XLA Ops:
  0.6 4.9 %copy-start.2 = (f32[1,1,64,256]{3,2,1,0:T(8,128)S(1)}, f32[1,1,64,256]{3,2,1,0:T(8,128)}, u32[]{:S(2)}) copy-start(f32[1,1,64,256]{3,2,1,0:T(8,128)} %param.7) | copy-start | bytes 196612
  3.5 2.1 %copy-start.6 = (f32[1,64]{1,0:T(1,128)S(1)}, f32[1,64]{1,0:T(1,128)}, u32[]{:S(2)}) copy-start(f32[1,64]{1,0:T(1,128)} %param.6) | copy-start | bytes 772
  3.5 8.0 %collective-permute-start = (f32[1,64,256]{2,1,0:T(8,128)}, f32[1,64,256]{2,1,0:T(8,128)S(1)}, u32[]{:S(2)}, u32[]{:S(2)}) collective-permute-start(f32[1,64,256]{2,1,0:T(8,128)} %bitcast.302), channel_id=1, source_target_pairs={{0,4},{4,8},{8,12},{12,16},{16,20},{20,24},{24,28},{28,32},{32,36}... | collective-permute-start | bytes 196616 | tf_op jit(solution)/shard_map/ppermute | solution.py:69
  5.6 6.0 %copy-start.3 = (f32[1,1,64,256]{3,2,1,0:T(8,128)S(1)}, f32[1,1,64,256]{3,2,1,0:T(8,128)}, u32[]{:S(2)}) copy-start(f32[1,1,64,256]{3,2,1,0:T(8,128)} %param.4) | copy-start | bytes 196612
  15.9 3.3 %collective-permute-start.1 = (f32[130,256]{1,0:T(8,128)S(1)}, f32[130,256]{1,0:T(8,128)S(1)}, u32[]{:S(2)}, u32[]{:S(2)}) collective-permute-start(f32[130,256]{1,0:T(8,128)S(1)} %pad_maximum_fusion.1), channel_id=1, source_target_pairs={{0,4},{4,0},{8,12},{12,8},{16,20},{20,16},{24,28},{28,24},{32,36},... | collective-permute-start | bytes 399368 | tf_op jit(solution)/shard_map/ppermute | solution.py:24
  19.5 7.6 %collective-permute-start.2 = (f32[130,256]{1,0:T(8,128)S(1)}, f32[130,256]{1,0:T(8,128)S(1)}, u32[]{:S(2)}, u32[]{:S(2)}) collective-permute-start(f32[130,256]{1,0:T(8,128)S(1)} %pad_maximum_fusion.2), channel_id=1, source_target_pairs={{0,8},{4,12},{8,0},{12,4},{16,24},{20,28},{24,16},{28,20},{32,40},... | collective-permute-start | bytes 399368 | tf_op jit(solution)/shard_map/ppermute | solution.py:24
  27.3 8.2 %collective-permute-start.3 = (f32[130,256]{1,0:T(8,128)S(1)}, f32[130,256]{1,0:T(8,128)S(1)}, u32[]{:S(2)}, u32[]{:S(2)}) collective-permute-start(f32[130,256]{1,0:T(8,128)S(1)} %pad_maximum_fusion.3), channel_id=1, source_target_pairs={{0,24},{4,28},{8,16},{12,20},{16,8},{20,12},{24,0},{28,4},{32,56},... | collective-permute-start | bytes 399368 | tf_op jit(solution)/shard_map/ppermute | solution.py:24
  35.8 6.9 %collective-permute-start.4 = (f32[130,256]{1,0:T(8,128)S(1)}, f32[130,256]{1,0:T(8,128)S(1)}, u32[]{:S(2)}, u32[]{:S(2)}) collective-permute-start(f32[130,256]{1,0:T(8,128)S(1)} %pad_maximum_fusion.4), channel_id=1, source_target_pairs={{0,32},{4,36},{8,40},{12,44},{16,48},{20,52},{24,56},{28,60},{32,0... | collective-permute-start | bytes 399368 | tf_op jit(solution)/shard_map/ppermute | solution.py:24
  43.0 8.9 %collective-permute-start.5 = (f32[130,256]{1,0:T(8,128)S(1)}, f32[130,256]{1,0:T(8,128)S(1)}, u32[]{:S(2)}, u32[]{:S(2)}) collective-permute-start(f32[130,256]{1,0:T(8,128)S(1)} %pad_maximum_fusion.5), channel_id=1, source_target_pairs={{0,64},{4,68},{8,72},{12,76},{16,80},{20,84},{24,88},{28,92},{32,9... | collective-permute-start | bytes 399368 | tf_op jit(solution)/shard_map/ppermute | solution.py:24
  52.2 15.8 %collective-permute-start.6 = (f32[130,256]{1,0:T(8,128)S(1)}, f32[130,256]{1,0:T(8,128)S(1)}, u32[]{:S(2)}, u32[]{:S(2)}) collective-permute-start(f32[130,256]{1,0:T(8,128)S(1)} %pad_maximum_fusion.6), channel_id=1, source_target_pairs={{0,128},{4,132},{8,136},{12,140},{16,144},{20,148},{24,152},{28,15... | collective-permute-start | bytes 399368 | tf_op jit(solution)/shard_map/ppermute | solution.py:24
  68.2 11.1 %copy-start = (bf16[4,64,576]{2,1,0:T(8,128)(2,1)S(1)}, bf16[4,64,576]{2,1,0:T(8,128)(2,1)}, u32[]{:S(2)}) copy-start(bf16[4,64,576]{2,1,0:T(8,128)(2,1)} %weight_ref.3) | copy-start | bytes 884740
  68.3 18.9 %collective-permute-start.7 = (f32[130,256]{1,0:T(8,128)S(1)}, f32[130,256]{1,0:T(8,128)S(1)}, u32[]{:S(2)}, u32[]{:S(2)}) collective-permute-start(f32[130,256]{1,0:T(8,128)S(1)} %pad_maximum_fusion.7), channel_id=1, source_target_pairs={{0,384},{4,388},{8,392},{12,396},{16,400},{20,404},{24,408},{28,41... | collective-permute-start | bytes 399368 | tf_op jit(solution)/shard_map/ppermute | solution.py:24
  91.4 8.4 %copy-start.1 = (f32[4,64,576]{2,1,0:T(8,128)S(1)}, f32[4,64,576]{2,1,0:T(8,128)}, u32[]{:S(2)}) copy-start(f32[4,64,576]{2,1,0:T(8,128)} %get-tuple-element.17) | copy-start | bytes 1769476
  91.4 4.2 %collective-permute-start.8 = (f32[1,64,256]{2,1,0:T(8,128)}, f32[1,64,256]{2,1,0:T(8,128)S(1)}, u32[]{:S(2)}, u32[]{:S(2)}) collective-permute-start(f32[1,64,256]{2,1,0:T(8,128)} %bitcast.281), channel_id=1, source_target_pairs={{4,0},{8,4},{12,8},{16,12},{20,16},{24,20},{28,24},{32,28},{36,32}... | collective-permute-start | bytes 196616 | tf_op jit(solution)/shard_map/ppermute | solution.py:69
  101.1 10.6 %collective-permute-start.11 = (f32[64,576]{1,0:T(8,128)S(1)}, f32[64,576]{1,0:T(8,128)S(1)}, u32[]{:S(2)}, u32[]{:S(2)}) collective-permute-start(f32[64,576]{1,0:T(8,128)S(1)} %get-tuple-element.34), channel_id=1, source_target_pairs={{0,3},{1,2},{2,1},{3,0},{4,7},{5,6},{6,5},{7,4},{8,11},{9,10},{10,... | collective-permute-start | bytes 442376 | tf_op jit(solution)/shard_map/ppermute | solution.py:56
  106.0 10.1 %collective-permute-start.10 = (f32[64,576]{1,0:T(8,128)S(1)}, f32[64,576]{1,0:T(8,128)S(1)}, u32[]{:S(2)}, u32[]{:S(2)}) collective-permute-start(f32[64,576]{1,0:T(8,128)S(1)} %get-tuple-element.35), channel_id=1, source_target_pairs={{0,2},{1,3},{2,0},{3,1},{4,6},{5,7},{6,4},{7,5},{8,10},{9,11},{10,... | collective-permute-start | bytes 442376 | tf_op jit(solution)/shard_map/ppermute | solution.py:56
  108.6 8.9 %collective-permute-start.9 = (f32[64,576]{1,0:T(8,128)S(1)}, f32[64,576]{1,0:T(8,128)S(1)}, u32[]{:S(2)}, u32[]{:S(2)}) collective-permute-start(f32[64,576]{1,0:T(8,128)S(1)} %get-tuple-element.33), channel_id=1, source_target_pairs={{0,1},{1,0},{2,3},{3,2},{4,5},{5,4},{6,7},{7,6},{8,9},{9,8},{10,11... | collective-permute-start | bytes 442376 | tf_op jit(solution)/shard_map/ppermute | solution.py:56
  111.7 15.7 %copy-start.4 = (f32[64,256]{1,0:T(8,128)S(1)}, f32[64,256]{1,0:T(8,128)}, u32[]{:S(2)}) copy-start(f32[64,256]{1,0:T(8,128)} %get-tuple-element.15) | copy-start | bytes 196612
  111.7 15.7 %copy-start.5 = (f32[64,256]{1,0:T(8,128)S(1)}, f32[64,256]{1,0:T(8,128)}, u32[]{:S(2)}) copy-start(f32[64,256]{1,0:T(8,128)} %get-tuple-element.16) | copy-start | bytes 196612
  117.6 11.9 %collective-permute-start.14 = (f32[64,576]{1,0:T(8,128)S(1)}, f32[64,576]{1,0:T(8,128)S(1)}, u32[]{:S(2)}, u32[]{:S(2)}) collective-permute-start(f32[64,576]{1,0:T(8,128)S(1)} %fusion.1), channel_id=1, source_target_pairs={{0,3},{1,2},{2,1},{3,0},{4,7},{5,6},{6,5},{7,4},{8,11},{9,10},{10,... | collective-permute-start | bytes 442376 | tf_op jit(solution)/shard_map/ppermute | solution.py:62
  122.2 10.5 %collective-permute-start.13 = (f32[64,576]{1,0:T(8,128)S(1)}, f32[64,576]{1,0:T(8,128)S(1)}, u32[]{:S(2)}, u32[]{:S(2)}) collective-permute-start(f32[64,576]{1,0:T(8,128)S(1)} %fusion.1), channel_id=1, source_target_pairs={{0,2},{1,3},{2,0},{3,1},{4,6},{5,7},{6,4},{7,5},{8,10},{9,11},{10,... | collective-permute-start | bytes 442376 | tf_op jit(solution)/shard_map/ppermute | solution.py:62
  124.7 8.2 %collective-permute-start.12 = (f32[64,576]{1,0:T(8,128)S(1)}, f32[64,576]{1,0:T(8,128)S(1)}, u32[]{:S(2)}, u32[]{:S(2)}) collective-permute-start(f32[64,576]{1,0:T(8,128)S(1)} %fusion.1), channel_id=1, source_target_pairs={{0,1},{1,0},{2,3},{3,2},{4,5},{5,4},{6,7},{7,6},{8,9},{9,8},{10,11... | collective-permute-start | bytes 442376 | tf_op jit(solution)/shard_map/ppermute | solution.py:62

commit v19 on v15

--- a/solution.py
+++ b/solution.py
@@ -155,7 +155,7 @@
             bytes_accessed=4 * (layers + 2) * channels * pixels + 2 * block_weights.size,
         ),
     )(current.reshape(channels, pixels), block_weights)
-    return (out.reshape(current.shape), [kept[k].reshape(current.shape) for k in range(layers)])
+    return (out.reshape(current.shape), kept)
 
 
 def back_block(inputs_kept, block_weights, upstream, step_size):
@@ -176,7 +176,7 @@
             transcendentals=layers * channels * pixels,
             bytes_accessed=4 * (layers + 2) * channels * pixels + 2 * block_weights.size + 4 * layers * channels * taps,
         ),
-    )(jnp.stack(inputs_kept).reshape(layers, channels, pixels), flipped, upstream.reshape(channels, pixels))
+    )(inputs_kept, flipped, upstream.reshape(channels, pixels))
     return (out.reshape(upstream.shape), grads)
 
 

time: 136 us -> 136 us (level)
  waiting for transfers between devices: 65.6 us -> 67.1 us
  other arithmetic: 9.23 us -> 7.79 us
    reshape x2 -> x0, other arithmetic: 1.44 us -> none  [back_block(): jnp.stack(inputs_kept).reshape(layers, channels, pixels)]
  transfers between devices with their start and end apart: 11 -> 11, of which waited for: 11 -> 11; matrix products, arithmetic and copies ran while one was open for 3% -> 2% of each run, Pallas kernels for 0% -> 0%
where the time goes in v19:
time: 136 us; the launch traced here: 135 us
  waiting for transfers between devices  67.1 us (49%)
  starting transfers between devices  43.2 us (32%)
  Pallas kernels  12.7 us (9%)
  other arithmetic  7.79 us (6%)
  local copies, waits for them, and re-layouts  3 us (2%)
    ppermute x7, waiting for transfers between devices, exchange(): lax.ppermute(pack(gains, states), axis, [(i, i ^ mask) for i in range(cou...  37.2 us
    ppermute x7, starting transfers between devices, exchange(): lax.ppermute(pack(gains, states), axis, [(i, i ^ mask) for i in range(cou...  31.2 us
    all_to_all x1, waiting for transfers between devices, dp_sum(): got = lax.all_to_all(terms, axis, 0, 0)  11.9 us
    all_to_all x1, waiting for transfers between devices, dp_sum(): lax.all_to_all(jnp.broadcast_to(total[None], terms.shape), axis, 0, 0)  9.97 us
    ppermute x2, waiting for transfers between devices, passed_along(): return lax.ppermute(block, axis, route)  8.05 us
    pallas_call x2, Pallas kernels, back_block(): pl.pallas_call(functools.partial(back_kernel, step_size), out_shape=(jax....  7.01 us
    pallas_call x2, Pallas kernels, run_block(): pl.pallas_call(functools.partial(block_kernel, step_size), out_shape=(jax...  5.66 us
    all_to_all x1, starting transfers between devices, dp_sum(): got = lax.all_to_all(terms, axis, 0, 0)  4.46 us
  transfers between devices with their start and end apart: 11, of which 11 were waited for; matrix products, arithmetic and copies ran while one was open for 2% of the time, Pallas kernels for 0%

profile of v19, /device:TPU:96, one launch (start us, length us, event | category | flops | bytes accessed | tf_op | source)
XLA Modules:
  0.0 135.0 jit_solution(13607592734317361439)
XLA Ops:
  0.6 0.0 copy-start.2
  0.6 2.8 %shard_map.67 = (f32[64,256]{1,0:T(8,128)}, f32[4,64,256]{2,1,0:T(8,128)}) custom-call(f32[64,256]{1,0:T(8,128)} %bitcast.252, bf16[4,64,576]{2,1,0:T(8,128)(2,1)} %weight_ref.3), custom_call_target="tpu_custom_call" | custom-call | flops 75497472 | bytes 688128 | tf_op jit(solution)/shard_map/pallas_call | solution.py:144
  3.5 0.0 copy-start.6
  3.5 2.0 %collective-permute-start = (f32[1,64,256]{2,1,0:T(8,128)}, f32[1,64,256]{2,1,0:T(8,128)S(1)}, u32[]{:S(2)}, u32[]{:S(2)}) collective-permute-start(f32[1,64,256]{2,1,0:T(8,128)} %bitcast.282), channel_id=1, source_target_pairs={{0,4},{4,8},{8,12},{12,16},{16,20},{20,24},{24,28},{28,32},{32,36}... | collective-permute-start | bytes 196616 | tf_op jit(solution)/shard_map/ppermute | solution.py:63
  5.5 0.0 copy-done.2
  5.5 0.0 copy-done.6
  5.6 0.0 copy-start.3
  5.6 0.1 broadcast_multiply_fusion
  5.7 5.9 %collective-permute-done = f32[1,64,256]{2,1,0:T(8,128)S(1)} collective-permute-done((f32[1,64,256]{2,1,0:T(8,128)}, f32[1,64,256]{2,1,0:T(8,128)S(1)}, u32[]{:S(2)}, u32[]{:S(2)}) %collective-permute-start) | collective-permute-done | bytes 65568 | tf_op jit(solution)/shard_map/ppermute | solution.py:63
  11.5 0.0 copy-done.3
  11.5 0.6 fusion.12.state_ref
  12.2 2.8 %shard_map.68 = (f32[64,256]{1,0:T(8,128)}, f32[4,64,256]{2,1,0:T(8,128)}) custom-call(f32[64,256]{1,0:T(8,128)} %fusion.12.state_ref, bf16[4,64,576]{2,1,0:T(8,128)(2,1)} %weight_ref.3), custom_call_target="tpu_custom_call" | custom-call | flops 75497472 | bytes 688128 | tf_op jit(solution)/shard_map/pallas_call | solution.py:144
  15.0 0.9 bitcast_subtract_fusion.1
  15.9 1.9 %collective-permute-start.1 = (f32[130,256]{1,0:T(8,128)S(1)}, f32[130,256]{1,0:T(8,128)S(1)}, u32[]{:S(2)}, u32[]{:S(2)}) collective-permute-start(f32[130,256]{1,0:T(8,128)S(1)} %pad_maximum_fusion), channel_id=1, source_target_pairs={{0,4},{4,0},{8,12},{12,8},{16,20},{20,16},{24,28},{28,24},{32,36},... | collective-permute-start | bytes 399368 | tf_op jit(solution)/shard_map/ppermute | solution.py:24
  17.9 1.3 collective-permute-done.1
  19.2 0.1 add_select_fusion.17
  19.3 0.1 fusion.25
  19.4 1.9 %collective-permute-start.2 = (f32[130,256]{1,0:T(8,128)S(1)}, f32[130,256]{1,0:T(8,128)S(1)}, u32[]{:S(2)}, u32[]{:S(2)}) collective-permute-start(f32[130,256]{1,0:T(8,128)S(1)} %pad_maximum_fusion.1), channel_id=1, source_target_pairs={{0,8},{4,12},{8,0},{12,4},{16,24},{20,28},{24,16},{28,20},{32,40},... | collective-permute-start | bytes 399368 | tf_op jit(solution)/shard_map/ppermute | solution.py:24
  21.4 5.7 %collective-permute-done.2 = f32[130,256]{1,0:T(8,128)S(1)} collective-permute-done((f32[130,256]{1,0:T(8,128)S(1)}, f32[130,256]{1,0:T(8,128)S(1)}, u32[]{:S(2)}, u32[]{:S(2)}) %collective-permute-start.2) | collective-permute-done | bytes 133152 | tf_op jit(solution)/shard_map/ppermute | solution.py:24
  27.1 0.1 fusion.10
  27.2 0.1 fusion.23
  27.3 3.3 %collective-permute-start.3 = (f32[130,256]{1,0:T(8,128)S(1)}, f32[130,256]{1,0:T(8,128)S(1)}, u32[]{:S(2)}, u32[]{:S(2)}) collective-permute-start(f32[130,256]{1,0:T(8,128)S(1)} %pad_maximum_fusion.2), channel_id=1, source_target_pairs={{0,24},{4,28},{8,16},{12,20},{16,8},{20,12},{24,0},{28,4},{32,56},... | collective-permute-start | bytes 399368 | tf_op jit(solution)/shard_map/ppermute | solution.py:24
  30.7 4.8 %collective-permute-done.3 = f32[130,256]{1,0:T(8,128)S(1)} collective-permute-done((f32[130,256]{1,0:T(8,128)S(1)}, f32[130,256]{1,0:T(8,128)S(1)}, u32[]{:S(2)}, u32[]{:S(2)}) %collective-permute-start.3) | collective-permute-done | bytes 133152 | tf_op jit(solution)/shard_map/ppermute | solution.py:24
  35.5 0.1 add_select_fusion.15
  35.7 0.1 fusion.26
  35.8 2.0 %collective-permute-start.4 = (f32[130,256]{1,0:T(8,128)S(1)}, f32[130,256]{1,0:T(8,128)S(1)}, u32[]{:S(2)}, u32[]{:S(2)}) collective-permute-start(f32[130,256]{1,0:T(8,128)S(1)} %pad_maximum_fusion.3), channel_id=1, source_target_pairs={{0,32},{4,36},{8,40},{12,44},{16,48},{20,52},{24,56},{28,60},{32,0... | collective-permute-start | bytes 399368 | tf_op jit(solution)/shard_map/ppermute | solution.py:24
  37.8 4.9 %collective-permute-done.4 = f32[130,256]{1,0:T(8,128)S(1)} collective-permute-done((f32[130,256]{1,0:T(8,128)S(1)}, f32[130,256]{1,0:T(8,128)S(1)}, u32[]{:S(2)}, u32[]{:S(2)}) %collective-permute-start.4) | collective-permute-done | bytes 133152 | tf_op jit(solution)/shard_map/ppermute | solution.py:24
  42.8 0.1 fusion.8
  42.9 0.1 fusion.24
  43.0 1.9 %collective-permute-start.5 = (f32[130,256]{1,0:T(8,128)S(1)}, f32[130,256]{1,0:T(8,128)S(1)}, u32[]{:S(2)}, u32[]{:S(2)}) collective-permute-start(f32[130,256]{1,0:T(8,128)S(1)} %pad_maximum_fusion.4), channel_id=1, source_target_pairs={{0,64},{4,68},{8,72},{12,76},{16,80},{20,84},{24,88},{28,92},{32,9... | collective-permute-start | bytes 399368 | tf_op jit(solution)/shard_map/ppermute | solution.py:24
  45.0 6.9 %collective-permute-done.5 = f32[130,256]{1,0:T(8,128)S(1)} collective-permute-done((f32[130,256]{1,0:T(8,128)S(1)}, f32[130,256]{1,0:T(8,128)S(1)}, u32[]{:S(2)}, u32[]{:S(2)}) %collective-permute-start.5) | collective-permute-done | bytes 133152 | tf_op jit(solution)/shard_map/ppermute | solution.py:24
  51.9 0.1 add_select_fusion.13
  52.0 0.1 fusion.27
  52.2 9.1 %collective-permute-start.6 = (f32[130,256]{1,0:T(8,128)S(1)}, f32[130,256]{1,0:T(8,128)S(1)}, u32[]{:S(2)}, u32[]{:S(2)}) collective-permute-start(f32[130,256]{1,0:T(8,128)S(1)} %pad_maximum_fusion.5), channel_id=1, source_target_pairs={{0,128},{4,132},{8,136},{12,140},{16,144},{20,148},{24,152},{28,15... | collective-permute-start | bytes 399368 | tf_op jit(solution)/shard_map/ppermute | solution.py:24
  61.3 6.7 %collective-permute-done.6 = f32[130,256]{1,0:T(8,128)S(1)} collective-permute-done((f32[130,256]{1,0:T(8,128)S(1)}, f32[130,256]{1,0:T(8,128)S(1)}, u32[]{:S(2)}, u32[]{:S(2)}) %collective-permute-start.6) | collective-permute-done | bytes 133152 | tf_op jit(solution)/shard_map/ppermute | solution.py:24
  68.0 0.1 select_bitcast_fusion
  68.1 0.1 fusion.6
  68.2 0.0 copy-start
  68.3 11.0 %collective-permute-start.7 = (f32[130,256]{1,0:T(8,128)S(1)}, f32[130,256]{1,0:T(8,128)S(1)}, u32[]{:S(2)}, u32[]{:S(2)}) collective-permute-start(f32[130,256]{1,0:T(8,128)S(1)} %pad_maximum_fusion.6), channel_id=1, source_target_pairs={{0,384},{4,388},{8,392},{12,396},{16,400},{20,404},{24,408},{28,41... | collective-permute-start | bytes 399368 | tf_op jit(solution)/shard_map/ppermute | solution.py:24
  79.3 0.0 copy-done
  79.3 1.1 copy.7
  80.4 6.8 %collective-permute-done.7 = f32[130,256]{1,0:T(8,128)S(1)} collective-permute-done((f32[130,256]{1,0:T(8,128)S(1)}, f32[130,256]{1,0:T(8,128)S(1)}, u32[]{:S(2)}, u32[]{:S(2)}) %collective-permute-start.7) | collective-permute-done | bytes 133152 | tf_op jit(solution)/shard_map/ppermute | solution.py:24
  87.2 0.8 bitcast_add_fusion.10
  87.9 3.5 %shard_map.69 = (f32[64,256]{1,0:T(8,128)}, f32[4,64,576]{2,1,0:T(8,128)}) custom-call(f32[4,64,256]{2,1,0:T(8,128)} %get-tuple-element.14.kept_ref, bf16[4,576,64]{2,1,0:T(8,128)(2,1)} %bitcast.245, f32[64,256]{1,0:T(8,128)} %get-tuple-element.19.upstream_ref), custom_call_target="tpu_custom_call" | custom-call | flops 150994944 | bytes 1277952 | tf_op jit(solution)/shard_map/pallas_call | solution.py:166
  91.4 0.0 copy-start.1
  91.4 2.0 %collective-permute-start.8 = (f32[1,64,256]{2,1,0:T(8,128)}, f32[1,64,256]{2,1,0:T(8,128)S(1)}, u32[]{:S(2)}, u32[]{:S(2)}) collective-permute-start(f32[1,64,256]{2,1,0:T(8,128)} %bitcast.261), channel_id=1, source_target_pairs={{4,0},{8,4},{12,8},{16,12},{20,16},{24,20},{28,24},{32,28},{36,32}... | collective-permute-start | bytes 196616 | tf_op jit(solution)/shard_map/ppermute | solution.py:63
  93.5 2.2 %collective-permute-done.8 = f32[1,64,256]{2,1,0:T(8,128)S(1)} collective-permute-done((f32[1,64,256]{2,1,0:T(8,128)}, f32[1,64,256]{2,1,0:T(8,128)S(1)}, u32[]{:S(2)}, u32[]{:S(2)}) %collective-permute-start.8) | collective-permute-done | bytes 65568 | tf_op jit(solution)/shard_map/ppermute | solution.py:63
  95.7 0.6 fusion.4.upstream_ref
  96.3 3.5 %shard_map.70 = (f32[64,256]{1,0:T(8,128)}, f32[4,64,576]{2,1,0:T(8,128)}) custom-call(f32[4,64,256]{2,1,0:T(8,128)} %get-tuple-element.13.kept_ref, bf16[4,576,64]{2,1,0:T(8,128)(2,1)} %bitcast.246, f32[64,256]{1,0:T(8,128)} %fusion.4.upstream_ref), custom_call_target="tpu_custom_call" | custom-call | flops 150994944 | bytes 1277952 | tf_op jit(solution)/shard_map/pallas_call | solution.py:166
  99.8 0.0 copy-done.1
  99.8 2.0 %add.250 = f32[4,64,576]{2,1,0:T(8,128)} add(f32[4,64,576]{2,1,0:T(8,128)S(1)} %copy-done.1, f32[4,64,576]{2,1,0:T(8,128)} %get-tuple-element.18) | non-fusion elementwise | flops 147456 | bytes 1769472 | tf_op jit(solution)/shard_map/add | solution.py:222
  101.8 4.5 %all-to-all-start = ((f32[4,64,576]{2,1,0:T(8,128)}), f32[4,64,576]{2,1,0:T(8,128)S(1)}, u32[]{:S(2)}, u32[]{:S(2)}) async-start(f32[4,64,576]{2,1,0:T(8,128)} %add.250), calls=%async_computation | async-start | bytes 1310720 | tf_op jit(solution)/shard_map/all_to_all | solution.py:53
  106.3 11.9 %all-to-all-done = f32[4,64,576]{2,1,0:T(8,128)S(1)} async-done(((f32[4,64,576]{2,1,0:T(8,128)}), f32[4,64,576]{2,1,0:T(8,128)S(1)}, u32[]{:S(2)}, u32[]{:S(2)}) %all-to-all-start) | async-done | bytes 589856 | tf_op jit(solution)/shard_map/all_to_all | solution.py:53
  118.3 0.9 broadcast_in_dim.74
  119.1 3.5 %all-to-all-start.1 = ((f32[4,64,576]{2,1,0:T(8,128)}), f32[4,64,576]{2,1,0:T(8,128)S(1)}, u32[]{:S(2)}, u32[]{:S(2)}) async-start(f32[4,64,576]{2,1,0:T(8,128)} %broadcast_in_dim.74), calls=%async_computation.1 | async-start | bytes 1310720 | tf_op jit(solution)/shard_map/all_to_all | solution.py:57
  122.6 0.0 copy-start.4
  122.6 0.0 copy-start.5
  122.7 0.8 fusion.1
  123.4 0.1 copy-done.4
  123.5 0.0 copy-done.5
  123.5 0.6 fusion.2
  124.2 10.0 %all-to-all-done.1 = f32[4,64,576]{2,1,0:T(8,128)S(1)} async-done(((f32[4,64,576]{2,1,0:T(8,128)}), f32[4,64,576]{2,1,0:T(8,128)S(1)}, u32[]{:S(2)}, u32[]{:S(2)}) %all-to-all-start.1) | async-done | bytes 589856 | tf_op jit(solution)/shard_map/all_to_all | solution.py:57
  134.1 0.8 copy.9
  (41 shorter events, 0.3 us)
Async XLA Ops:
  0.6 4.9 %copy-start.2 = (f32[1,1,64,256]{3,2,1,0:T(8,128)S(1)}, f32[1,1,64,256]{3,2,1,0:T(8,128)}, u32[]{:S(2)}) copy-start(f32[1,1,64,256]{3,2,1,0:T(8,128)} %param.7) | copy-start | bytes 196612
  3.5 2.1 %copy-start.6 = (f32[1,64]{1,0:T(1,128)S(1)}, f32[1,64]{1,0:T(1,128)}, u32[]{:S(2)}) copy-start(f32[1,64]{1,0:T(1,128)} %param.6) | copy-start | bytes 772
  3.5 8.0 %collective-permute-start = (f32[1,64,256]{2,1,0:T(8,128)}, f32[1,64,256]{2,1,0:T(8,128)S(1)}, u32[]{:S(2)}, u32[]{:S(2)}) collective-permute-start(f32[1,64,256]{2,1,0:T(8,128)} %bitcast.282), channel_id=1, source_target_pairs={{0,4},{4,8},{8,12},{12,16},{16,20},{20,24},{24,28},{28,32},{32,36}... | collective-permute-start | bytes 196616 | tf_op jit(solution)/shard_map/ppermute | solution.py:63
  5.6 6.0 %copy-start.3 = (f32[1,1,64,256]{3,2,1,0:T(8,128)S(1)}, f32[1,1,64,256]{3,2,1,0:T(8,128)}, u32[]{:S(2)}) copy-start(f32[1,1,64,256]{3,2,1,0:T(8,128)} %param.4) | copy-start | bytes 196612
  15.9 3.3 %collective-permute-start.1 = (f32[130,256]{1,0:T(8,128)S(1)}, f32[130,256]{1,0:T(8,128)S(1)}, u32[]{:S(2)}, u32[]{:S(2)}) collective-permute-start(f32[130,256]{1,0:T(8,128)S(1)} %pad_maximum_fusion), channel_id=1, source_target_pairs={{0,4},{4,0},{8,12},{12,8},{16,20},{20,16},{24,28},{28,24},{32,36},... | collective-permute-start | bytes 399368 | tf_op jit(solution)/shard_map/ppermute | solution.py:24
  19.4 7.6 %collective-permute-start.2 = (f32[130,256]{1,0:T(8,128)S(1)}, f32[130,256]{1,0:T(8,128)S(1)}, u32[]{:S(2)}, u32[]{:S(2)}) collective-permute-start(f32[130,256]{1,0:T(8,128)S(1)} %pad_maximum_fusion.1), channel_id=1, source_target_pairs={{0,8},{4,12},{8,0},{12,4},{16,24},{20,28},{24,16},{28,20},{32,40},... | collective-permute-start | bytes 399368 | tf_op jit(solution)/shard_map/ppermute | solution.py:24
  27.3 8.2 %collective-permute-start.3 = (f32[130,256]{1,0:T(8,128)S(1)}, f32[130,256]{1,0:T(8,128)S(1)}, u32[]{:S(2)}, u32[]{:S(2)}) collective-permute-start(f32[130,256]{1,0:T(8,128)S(1)} %pad_maximum_fusion.2), channel_id=1, source_target_pairs={{0,24},{4,28},{8,16},{12,20},{16,8},{20,12},{24,0},{28,4},{32,56},... | collective-permute-start | bytes 399368 | tf_op jit(solution)/shard_map/ppermute | solution.py:24
  35.8 6.9 %collective-permute-start.4 = (f32[130,256]{1,0:T(8,128)S(1)}, f32[130,256]{1,0:T(8,128)S(1)}, u32[]{:S(2)}, u32[]{:S(2)}) collective-permute-start(f32[130,256]{1,0:T(8,128)S(1)} %pad_maximum_fusion.3), channel_id=1, source_target_pairs={{0,32},{4,36},{8,40},{12,44},{16,48},{20,52},{24,56},{28,60},{32,0... | collective-permute-start | bytes 399368 | tf_op jit(solution)/shard_map/ppermute | solution.py:24
  43.0 8.9 %collective-permute-start.5 = (f32[130,256]{1,0:T(8,128)S(1)}, f32[130,256]{1,0:T(8,128)S(1)}, u32[]{:S(2)}, u32[]{:S(2)}) collective-permute-start(f32[130,256]{1,0:T(8,128)S(1)} %pad_maximum_fusion.4), channel_id=1, source_target_pairs={{0,64},{4,68},{8,72},{12,76},{16,80},{20,84},{24,88},{28,92},{32,9... | collective-permute-start | bytes 399368 | tf_op jit(solution)/shard_map/ppermute | solution.py:24
  52.2 15.8 %collective-permute-start.6 = (f32[130,256]{1,0:T(8,128)S(1)}, f32[130,256]{1,0:T(8,128)S(1)}, u32[]{:S(2)}, u32[]{:S(2)}) collective-permute-start(f32[130,256]{1,0:T(8,128)S(1)} %pad_maximum_fusion.5), channel_id=1, source_target_pairs={{0,128},{4,132},{8,136},{12,140},{16,144},{20,148},{24,152},{28,15... | collective-permute-start | bytes 399368 | tf_op jit(solution)/shard_map/ppermute | solution.py:24
  68.2 11.0 %copy-start = (bf16[4,64,576]{2,1,0:T(8,128)(2,1)S(1)}, bf16[4,64,576]{2,1,0:T(8,128)(2,1)}, u32[]{:S(2)}) copy-start(bf16[4,64,576]{2,1,0:T(8,128)(2,1)} %weight_ref.3) | copy-start | bytes 884740
  68.3 18.9 %collective-permute-start.7 = (f32[130,256]{1,0:T(8,128)S(1)}, f32[130,256]{1,0:T(8,128)S(1)}, u32[]{:S(2)}, u32[]{:S(2)}) collective-permute-start(f32[130,256]{1,0:T(8,128)S(1)} %pad_maximum_fusion.6), channel_id=1, source_target_pairs={{0,384},{4,388},{8,392},{12,396},{16,400},{20,404},{24,408},{28,41... | collective-permute-start | bytes 399368 | tf_op jit(solution)/shard_map/ppermute | solution.py:24
  91.4 8.4 %copy-start.1 = (f32[4,64,576]{2,1,0:T(8,128)S(1)}, f32[4,64,576]{2,1,0:T(8,128)}, u32[]{:S(2)}) copy-start(f32[4,64,576]{2,1,0:T(8,128)} %get-tuple-element.17) | copy-start | bytes 1769476
  91.4 4.2 %collective-permute-start.8 = (f32[1,64,256]{2,1,0:T(8,128)}, f32[1,64,256]{2,1,0:T(8,128)S(1)}, u32[]{:S(2)}, u32[]{:S(2)}) collective-permute-start(f32[1,64,256]{2,1,0:T(8,128)} %bitcast.261), channel_id=1, source_target_pairs={{4,0},{8,4},{12,8},{16,12},{20,16},{24,20},{28,24},{32,28},{36,32}... | collective-permute-start | bytes 196616 | tf_op jit(solution)/shard_map/ppermute | solution.py:63
  101.8 16.4 %all-to-all-start = ((f32[4,64,576]{2,1,0:T(8,128)}), f32[4,64,576]{2,1,0:T(8,128)S(1)}, u32[]{:S(2)}, u32[]{:S(2)}) async-start(f32[4,64,576]{2,1,0:T(8,128)} %add.250), calls=%async_computation | async-start | bytes 1310720 | tf_op jit(solution)/shard_map/all_to_all | solution.py:53
  119.1 15.0 %all-to-all-start.1 = ((f32[4,64,576]{2,1,0:T(8,128)}), f32[4,64,576]{2,1,0:T(8,128)S(1)}, u32[]{:S(2)}, u32[]{:S(2)}) async-start(f32[4,64,576]{2,1,0:T(8,128)} %broadcast_in_dim.74), calls=%async_computation.1 | async-start | bytes 1310720 | tf_op jit(solution)/shard_map/all_to_all | solution.py:57
  122.6 0.8 copy-start.4
  122.6 0.9 copy-start.5
